TPU v7x, 32 devices: a whole 2x2x4 slice. The times are simulated.
32 devices in a mesh: blk: 8 (over y, x, core), rep: 4 (over z).
Axes of the slice: x: 2, y: 2, z: 4, core: 2. Of those that a mesh axis runs over, the one named last changes fastest.
Arguments:
- picture_averaged_features: bfloat16 [4, 512, 1152], P('rep', 'blk'), may hold values from -0.23925781 to 0.23925781
- caption_averaged_features: bfloat16 [4, 512, 1152], P('rep', 'blk'), may hold values from -0.23925781 to 0.23925781
- picture_rescale_factor: float32 [1152], replicated, may hold values from 0.1 to 1.9
- caption_rescale_factor: float32 [1152], replicated, may hold values from 0.1 to 1.9
- exponent_of_sharpness: float32 [1], replicated, may hold values from 1.8 to 2.6
- score_shift_term: float32 [1], replicated, may hold values from -8 to -4
- objective_multiplier: float32 [1], replicated, may hold values from 512 to 2048
- matching_caption_index: int32 [4, 512], P('rep'), may hold values from 0 to 511, each once within a row
- genuine_entry_counts: int32 [4, 8], P('rep'), may hold values from 1 to 64, 384 in all within a row
Outputs:
- image_grad: bfloat16 [4, 512, 1152], P('rep', 'blk')
- text_grad: bfloat16 [4, 512, 1152], P('rep', 'blk')
- gain_grads: float32 [2, 1152], replicated
- group_loss: float32 [4], P('rep')
Inputs may be any that keep to these rules, and one draw needn't show every extreme that they name: `matching_caption_index`: each group's row of positives is a permutation of 0 to 511. `genuine_entry_counts`: each group's counts sum to 384, and some block of every group is full.
All inputs are finite; a program needn't handle non-finite values.
Results may differ from a plain program's by a relative error of at most 0.0058.
Values may be sent and summed in bfloat16 or wider, within the bound.
No kernel may reach another device: no remote copies, remote signals or barrier semaphores. Data moves between devices by JAX's collectives and lax.ppermute only.
A program may use at most 64 MiB of HBM per device.

v0:
```python
import jax
import jax.numpy as jnp
from jax import lax
from jax.sharding import PartitionSpec as P

epsilon = 1e-06


def from_behind(value, axis, steps):
    count = lax.axis_size(axis)
    pairs = [(source, (source + steps) % count) for source in range(count)]
    return lax.ppermute(value, axis, pairs)


def embed_rows(pooled, gain):
    values = pooled.astype(jnp.float32)
    centred = values - jnp.mean(values, axis=-1, keepdims=True)
    inverse = lax.rsqrt(jnp.mean(centred * centred, axis=-1, keepdims=True) + epsilon)
    normed = centred * inverse
    scaled = normed * gain
    inv_length = lax.rsqrt(jnp.sum(scaled * scaled, axis=-1, keepdims=True) + epsilon)
    return (scaled * inv_length, normed, inverse, inv_length)


def embed_back(direction, unit_rows, normed, inverse, inv_length, gain):
    tangent = (
        direction - unit_rows * jnp.sum(unit_rows * direction, axis=-1, keepdims=True)
    ) * inv_length
    gain_part = jnp.sum(tangent * normed, axis=0)
    scaled = tangent * gain
    gradient = (
        scaled
        - jnp.mean(scaled, axis=-1, keepdims=True)
        - normed * jnp.mean(scaled * normed, axis=-1, keepdims=True)
    ) * inverse
    return (gradient, gain_part)


def pair_tile(
    image_side,
    text_side,
    image_partner,
    text_start,
    image_count,
    text_count,
    score_sharpness_factor,
    score_shift_amount,
    grad_factor,
):
    angle_similarity_table = lax.dot_general(
        image_side, text_side, (((1,), (1,)), ((), ())), preferred_element_type=jnp.float32
    )
    score_similarity_table = score_sharpness_factor * angle_similarity_table + score_shift_amount
    index_row = lax.broadcasted_iota(jnp.int32, angle_similarity_table.shape, 0)
    index_col = lax.broadcasted_iota(jnp.int32, angle_similarity_table.shape, 1)
    labels = jnp.where(image_partner[:, None] == text_start + index_col, 1.0, -1.0).astype(
        jnp.float32
    )
    kept_pairs = (index_row < image_count) & (index_col < text_count)
    margin = -labels * score_similarity_table
    loss_sum = jnp.sum(jnp.where(kept_pairs, jax.nn.softplus(margin), 0.0))
    couple_importance_factor = (
        jnp.where(kept_pairs, -labels * jax.nn.sigmoid(margin), 0.0) * grad_factor
    )
    return (loss_sum, couple_importance_factor.astype(jnp.bfloat16))


def image_side_sum(couple_importance_factor, text_side):
    return jnp.dot(couple_importance_factor, text_side, preferred_element_type=jnp.float32)


def text_side_sum(couple_importance_factor, image_side):
    return lax.dot_general(
        couple_importance_factor,
        image_side,
        (((0,), (0,)), ((), ())),
        preferred_element_type=jnp.float32,
    )


def shards(
    picture_averaged_features,
    caption_averaged_features,
    picture_rescale_factor,
    caption_rescale_factor,
    exponent_of_sharpness,
    score_shift_term,
    objective_multiplier,
    matching_caption_index,
    genuine_entry_counts,
):
    block_rows = picture_averaged_features.shape[1]
    members = lax.axis_size("blk")
    own_block = lax.axis_index("blk")
    image_unit_rows, image_normalized, image_inverse_length, image_length = embed_rows(
        picture_averaged_features[0], picture_rescale_factor
    )
    text_unit_rows, text_normalized, text_inverse_length, text_length = embed_rows(
        caption_averaged_features[0], caption_rescale_factor
    )
    picture_feature_entries = image_unit_rows.astype(jnp.bfloat16)
    caption_feature_entries = text_unit_rows.astype(jnp.bfloat16)
    block_counts = genuine_entry_counts[0]
    partner = matching_caption_index[0]
    real_count = jnp.sum(block_counts).astype(jnp.float32)
    score_sharpness_factor = jnp.exp(exponent_of_sharpness[0])
    score_shift_amount = score_shift_term[0]
    grad_factor = objective_multiplier[0] / real_count

    def count_of(block):
        return lax.dynamic_index_in_dim(block_counts, block, keepdims=False)

    own_partner = lax.dynamic_slice_in_dim(partner, own_block * block_rows, block_rows)
    own_count = count_of(own_block)
    loss_sum, couple_importance_factor = pair_tile(
        picture_feature_entries,
        caption_feature_entries,
        own_partner,
        own_block * block_rows,
        own_count,
        own_count,
        score_sharpness_factor,
        score_shift_amount,
        grad_factor,
    )
    picture_running_total = image_side_sum(couple_importance_factor, caption_feature_entries)
    caption_running_total = text_side_sum(couple_importance_factor, picture_feature_entries)
    routes = ((1, members - 1),)
    state = (loss_sum, picture_running_total, caption_running_total)
    stride, turns = routes[0]

    def advance(turn, carry):
        partial_value, image_total, seen_text, carried = carry
        seen_text = from_behind(seen_text, "blk", stride)
        carried = from_behind(carried, "blk", stride)
        source = (own_block - stride * turn) % members
        part_loss, forward_weight = pair_tile(
            picture_feature_entries,
            seen_text,
            own_partner,
            source * block_rows,
            own_count,
            count_of(source),
            score_sharpness_factor,
            score_shift_amount,
            grad_factor,
        )
        image_total = image_total + image_side_sum(forward_weight, seen_text)
        carried = carried + text_side_sum(forward_weight, picture_feature_entries)
        return (partial_value + part_loss, image_total, seen_text, carried)

    partial_value, image_total, text_total = state
    carried = jnp.zeros(text_total.shape, jnp.float32)
    partial_value, image_total, unused, carried = lax.fori_loop(
        1, turns + 1, advance, (partial_value, image_total, caption_feature_entries, carried)
    )
    returned = from_behind(carried, "blk", -stride * turns)
    state = (partial_value, image_total, text_total + returned)
    loss_sum, picture_running_total, caption_running_total = state
    image_gradient, image_part = embed_back(
        score_sharpness_factor * picture_running_total,
        image_unit_rows,
        image_normalized,
        image_inverse_length,
        image_length,
        picture_rescale_factor,
    )
    text_gradient, text_part = embed_back(
        score_sharpness_factor * caption_running_total,
        text_unit_rows,
        text_normalized,
        text_inverse_length,
        text_length,
        caption_rescale_factor,
    )
    replicas = lax.axis_size("rep")
    group_index = lax.axis_index("rep")
    loss_vector = jnp.where(
        jnp.arange(replicas, dtype=jnp.int32) == group_index, loss_sum / real_count, 0.0
    )
    gain_grads, losses = lax.psum((jnp.stack([image_part, text_part]), loss_vector), ("blk", "rep"))
    group_loss = lax.dynamic_slice_in_dim(losses, group_index, 1)
    return (
        image_gradient.astype(jnp.bfloat16)[None],
        text_gradient.astype(jnp.bfloat16)[None],
        gain_grads,
        group_loss,
    )


def solution(mesh):
    placed = (
        P("rep", "blk", None),
        P("rep", "blk", None),
        P(),
        P(),
        P(),
        P(),
        P(),
        P("rep", None),
        P("rep", None),
    )
    return jax.shard_map(
        shards,
        mesh=mesh,
        in_specs=placed,
        out_specs=(P("rep", "blk", None), P("rep", "blk", None), P(), P("rep")),
        check_vma=False,
    )
```

profile of v0, /device:TPU:0, one launch (start us, length us, event | category | flops | bytes accessed | tf_op | source)
XLA Modules:
  0.0 126.7 jit_solution(3212492489369515872)
XLA Ops:
  10.0 67.0 %while.22 = (s32[]{:T(128)}, f32[]{:T(128)}, f32[64,1152]{1,0:T(8,128)S(1)}, bf16[64,1152]{1,0:T(8,128)(2,1)S(1)}, f32[64,1152]{1,0:T(8,128)S(1)}, /*index=5*/s3...) while((s32[]{:T(128)}, f32[]{:T(128)}, ...), condition=%wide.region_10.11_spmd.clone, body=%wide.region_8.10_spmd.clone.sunk | while | flops 28684496 | bytes 4475614 | solution.py:154
  10.6 2.6 %collective-permute-start.1 = (f32[64,1152]{1,0:T(8,128)S(1)}, f32[64,1152]{1,0:T(8,128)S(1)}, u32[]{:S(2)}, u32[]{:S(2)}) collective-permute-start(f32[64,1152]{1,0:T(8,128)S(1)} %broadcast_select_fusion.2), channel_id=1, source_target_pairs={{0,4},{4,8},{8,12},{12,16},{16,20},{20,24},{24,28},{28,0},{1,5},{5... | collective-permute-start | bytes 884744 | tf_op jit(solution)/shard_map/while/body/eval_jaxpr/ppermute | solution.py:12
  13.8 1.3 %iota_compare_fusion.4 = (pred[64]{0:T(512)(128)(4,1)S(1)}, pred[64]{0:T(512)(128)(4,1)S(1)}) fusion(s32[]{:T(128)} %bitcast.135, s32[]{:T(128)} %get-tuple-element.534), kind=kLoop, calls=%fused_computation.14.clone.1 | loop fusion | flops 128 | bytes 136 | tf_op jit(solution)/shard_map/while/body/eval_jaxpr/lt | solution.py:59
  16.3 1.5 %fusion.103 = (f32[]{:T(128)}, f32[64,64]{1,0:T(8,128)S(1)}) fusion(pred[64]{0:T(512)(128)(4,1)S(1)} %get-tuple-element.489, pred[64]{0:T(512)(128)(4,1)S(1)} %get-tuple-element.490, f32[]{:T(128)} %get-tuple-element.540, bf16[64,1152]{1,0:T(8,128)(2,1)S(1)} %get-tuple-element.539, bf16[64,1152]{1,0:T(8,128)(2,1)S(1)} %collective-permute-done, ...), kind=kOutput, calls=%fused_computation.9.clone.1 | convolution fusion | flops 9498623 | bytes 311948 | tf_op jit(solution)/shard_map/while/body/eval_jaxpr/dot_general | solution.py:50
  20.3 1.5 %collective-permute-start.1 = (f32[64,1152]{1,0:T(8,128)S(1)}, f32[64,1152]{1,0:T(8,128)S(1)}, u32[]{:S(2)}, u32[]{:S(2)}) collective-permute-start(f32[64,1152]{1,0:T(8,128)S(1)} %broadcast_select_fusion.2), channel_id=1, source_target_pairs={{0,4},{4,8},{8,12},{12,16},{16,20},{20,24},{24,28},{28,0},{1,5},{5... | collective-permute-start | bytes 884744 | tf_op jit(solution)/shard_map/while/body/eval_jaxpr/ppermute | solution.py:12
  22.4 1.3 %iota_compare_fusion.4 = (pred[64]{0:T(512)(128)(4,1)S(1)}, pred[64]{0:T(512)(128)(4,1)S(1)}) fusion(s32[]{:T(128)} %bitcast.135, s32[]{:T(128)} %get-tuple-element.534), kind=kLoop, calls=%fused_computation.14.clone.1 | loop fusion | flops 128 | bytes 136 | tf_op jit(solution)/shard_map/while/body/eval_jaxpr/lt | solution.py:59
  23.7 2.0 %collective-permute-done = bf16[64,1152]{1,0:T(8,128)(2,1)S(1)} collective-permute-done((bf16[64,1152]{1,0:T(8,128)(2,1)S(1)}, bf16[64,1152]{1,0:T(8,128)(2,1)S(1)}, u32[]{:S(2)}, u32[]{:S(2)}) %collective-permute-start) | collective-permute-done | bytes 147488 | tf_op jit(solution)/shard_map/while/body/eval_jaxpr/ppermute | solution.py:12
  25.7 1.5 %fusion.103 = (f32[]{:T(128)}, f32[64,64]{1,0:T(8,128)S(1)}) fusion(pred[64]{0:T(512)(128)(4,1)S(1)} %get-tuple-element.489, pred[64]{0:T(512)(128)(4,1)S(1)} %get-tuple-element.490, f32[]{:T(128)} %get-tuple-element.540, bf16[64,1152]{1,0:T(8,128)(2,1)S(1)} %get-tuple-element.539, bf16[64,1152]{1,0:T(8,128)(2,1)S(1)} %collective-permute-done, ...), kind=kOutput, calls=%fused_computation.9.clone.1 | convolution fusion | flops 9498623 | bytes 311948 | tf_op jit(solution)/shard_map/while/body/eval_jaxpr/dot_general | solution.py:50
  31.0 1.3 %iota_compare_fusion.4 = (pred[64]{0:T(512)(128)(4,1)S(1)}, pred[64]{0:T(512)(128)(4,1)S(1)}) fusion(s32[]{:T(128)} %bitcast.135, s32[]{:T(128)} %get-tuple-element.534), kind=kLoop, calls=%fused_computation.14.clone.1 | loop fusion | flops 128 | bytes 136 | tf_op jit(solution)/shard_map/while/body/eval_jaxpr/lt | solution.py:59
  32.3 2.9 %collective-permute-done = bf16[64,1152]{1,0:T(8,128)(2,1)S(1)} collective-permute-done((bf16[64,1152]{1,0:T(8,128)(2,1)S(1)}, bf16[64,1152]{1,0:T(8,128)(2,1)S(1)}, u32[]{:S(2)}, u32[]{:S(2)}) %collective-permute-start) | collective-permute-done | bytes 147488 | tf_op jit(solution)/shard_map/while/body/eval_jaxpr/ppermute | solution.py:12
  35.2 1.5 %fusion.103 = (f32[]{:T(128)}, f32[64,64]{1,0:T(8,128)S(1)}) fusion(pred[64]{0:T(512)(128)(4,1)S(1)} %get-tuple-element.489, pred[64]{0:T(512)(128)(4,1)S(1)} %get-tuple-element.490, f32[]{:T(128)} %get-tuple-element.540, bf16[64,1152]{1,0:T(8,128)(2,1)S(1)} %get-tuple-element.539, bf16[64,1152]{1,0:T(8,128)(2,1)S(1)} %collective-permute-done, ...), kind=kOutput, calls=%fused_computation.9.clone.1 | convolution fusion | flops 9498623 | bytes 311948 | tf_op jit(solution)/shard_map/while/body/eval_jaxpr/dot_general | solution.py:50
  40.2 1.3 %iota_compare_fusion.4 = (pred[64]{0:T(512)(128)(4,1)S(1)}, pred[64]{0:T(512)(128)(4,1)S(1)}) fusion(s32[]{:T(128)} %bitcast.135, s32[]{:T(128)} %get-tuple-element.534), kind=kLoop, calls=%fused_computation.14.clone.1 | loop fusion | flops 128 | bytes 136 | tf_op jit(solution)/shard_map/while/body/eval_jaxpr/lt | solution.py:59
  41.5 3.1 %collective-permute-done = bf16[64,1152]{1,0:T(8,128)(2,1)S(1)} collective-permute-done((bf16[64,1152]{1,0:T(8,128)(2,1)S(1)}, bf16[64,1152]{1,0:T(8,128)(2,1)S(1)}, u32[]{:S(2)}, u32[]{:S(2)}) %collective-permute-start) | collective-permute-done | bytes 147488 | tf_op jit(solution)/shard_map/while/body/eval_jaxpr/ppermute | solution.py:12
  44.7 1.5 %fusion.103 = (f32[]{:T(128)}, f32[64,64]{1,0:T(8,128)S(1)}) fusion(pred[64]{0:T(512)(128)(4,1)S(1)} %get-tuple-element.489, pred[64]{0:T(512)(128)(4,1)S(1)} %get-tuple-element.490, f32[]{:T(128)} %get-tuple-element.540, bf16[64,1152]{1,0:T(8,128)(2,1)S(1)} %get-tuple-element.539, bf16[64,1152]{1,0:T(8,128)(2,1)S(1)} %collective-permute-done, ...), kind=kOutput, calls=%fused_computation.9.clone.1 | convolution fusion | flops 9498623 | bytes 311948 | tf_op jit(solution)/shard_map/while/body/eval_jaxpr/dot_general | solution.py:50
  49.7 1.3 %iota_compare_fusion.4 = (pred[64]{0:T(512)(128)(4,1)S(1)}, pred[64]{0:T(512)(128)(4,1)S(1)}) fusion(s32[]{:T(128)} %bitcast.135, s32[]{:T(128)} %get-tuple-element.534), kind=kLoop, calls=%fused_computation.14.clone.1 | loop fusion | flops 128 | bytes 136 | tf_op jit(solution)/shard_map/while/body/eval_jaxpr/lt | solution.py:59
  51.0 3.1 %collective-permute-done = bf16[64,1152]{1,0:T(8,128)(2,1)S(1)} collective-permute-done((bf16[64,1152]{1,0:T(8,128)(2,1)S(1)}, bf16[64,1152]{1,0:T(8,128)(2,1)S(1)}, u32[]{:S(2)}, u32[]{:S(2)}) %collective-permute-start) | collective-permute-done | bytes 147488 | tf_op jit(solution)/shard_map/while/body/eval_jaxpr/ppermute | solution.py:12
  54.1 1.5 %fusion.103 = (f32[]{:T(128)}, f32[64,64]{1,0:T(8,128)S(1)}) fusion(pred[64]{0:T(512)(128)(4,1)S(1)} %get-tuple-element.489, pred[64]{0:T(512)(128)(4,1)S(1)} %get-tuple-element.490, f32[]{:T(128)} %get-tuple-element.540, bf16[64,1152]{1,0:T(8,128)(2,1)S(1)} %get-tuple-element.539, bf16[64,1152]{1,0:T(8,128)(2,1)S(1)} %collective-permute-done, ...), kind=kOutput, calls=%fused_computation.9.clone.1 | convolution fusion | flops 9498623 | bytes 311948 | tf_op jit(solution)/shard_map/while/body/eval_jaxpr/dot_general | solution.py:50
  59.1 1.3 %iota_compare_fusion.4 = (pred[64]{0:T(512)(128)(4,1)S(1)}, pred[64]{0:T(512)(128)(4,1)S(1)}) fusion(s32[]{:T(128)} %bitcast.135, s32[]{:T(128)} %get-tuple-element.534), kind=kLoop, calls=%fused_computation.14.clone.1 | loop fusion | flops 128 | bytes 136 | tf_op jit(solution)/shard_map/while/body/eval_jaxpr/lt | solution.py:59
  60.4 3.1 %collective-permute-done = bf16[64,1152]{1,0:T(8,128)(2,1)S(1)} collective-permute-done((bf16[64,1152]{1,0:T(8,128)(2,1)S(1)}, bf16[64,1152]{1,0:T(8,128)(2,1)S(1)}, u32[]{:S(2)}, u32[]{:S(2)}) %collective-permute-start) | collective-permute-done | bytes 147488 | tf_op jit(solution)/shard_map/while/body/eval_jaxpr/ppermute | solution.py:12
  63.6 1.5 %fusion.103 = (f32[]{:T(128)}, f32[64,64]{1,0:T(8,128)S(1)}) fusion(pred[64]{0:T(512)(128)(4,1)S(1)} %get-tuple-element.489, pred[64]{0:T(512)(128)(4,1)S(1)} %get-tuple-element.490, f32[]{:T(128)} %get-tuple-element.540, bf16[64,1152]{1,0:T(8,128)(2,1)S(1)} %get-tuple-element.539, bf16[64,1152]{1,0:T(8,128)(2,1)S(1)} %collective-permute-done, ...), kind=kOutput, calls=%fused_computation.9.clone.1 | convolution fusion | flops 9498623 | bytes 311948 | tf_op jit(solution)/shard_map/while/body/eval_jaxpr/dot_general | solution.py:50
  69.9 3.1 %collective-permute-done = bf16[64,1152]{1,0:T(8,128)(2,1)S(1)} collective-permute-done((bf16[64,1152]{1,0:T(8,128)(2,1)S(1)}, bf16[64,1152]{1,0:T(8,128)(2,1)S(1)}, u32[]{:S(2)}, u32[]{:S(2)}) %collective-permute-start) | collective-permute-done | bytes 147488 | tf_op jit(solution)/shard_map/while/body/eval_jaxpr/ppermute | solution.py:12
  73.0 1.5 %fusion.103 = (f32[]{:T(128)}, f32[64,64]{1,0:T(8,128)S(1)}) fusion(pred[64]{0:T(512)(128)(4,1)S(1)} %get-tuple-element.489, pred[64]{0:T(512)(128)(4,1)S(1)} %get-tuple-element.490, f32[]{:T(128)} %get-tuple-element.540, bf16[64,1152]{1,0:T(8,128)(2,1)S(1)} %get-tuple-element.539, bf16[64,1152]{1,0:T(8,128)(2,1)S(1)} %collective-permute-done, ...), kind=kOutput, calls=%fused_computation.9.clone.1 | convolution fusion | flops 9498623 | bytes 311948 | tf_op jit(solution)/shard_map/while/body/eval_jaxpr/dot_general | solution.py:50
  79.1 5.0 %collective-permute-done.2 = f32[64,1152]{1,0:T(8,128)S(1)} collective-permute-done((f32[64,1152]{1,0:T(8,128)S(1)}, f32[64,1152]{1,0:T(8,128)S(1)}, u32[]{:S(2)}, u32[]{:S(2)}) %collective-permute-start.2) | collective-permute-done | bytes 294944 | tf_op jit(solution)/shard_map/ppermute | solution.py:12
  84.9 40.4 %all-reduce = (f32[2,1152]{1,0:T(2,128)}, f32[4]{0:T(128)S(1)}) all-reduce(f32[2,1152]{1,0:T(2,128)S(1)} %pad_maximum_fusion, f32[4]{0:T(128)S(1)} %compare_select_fusion.2), channel_id=1, replica_groups=mesh['blk'=8,'rep'=4] {'blk','rep'}, use_global_device_ids=true, to_apply=%region_19.20 | all-reduce | flops 2308 | bytes 18464 | tf_op jit(solution)/shard_map/psum | solution.py:181
  (112 shorter events, 24.5 us)
Async XLA Ops:
  0.6 8.1 %copy-start = (s32[1,512]{1,0:T(1,128)S(1)}, s32[1,512]{1,0:T(1,128)}, u32[]{:S(2)}) copy-start(s32[1,512]{1,0:T(1,128)} %param.18) | copy-start | bytes 6148
  0.6 1.2 copy-start.1
  0.7 1.3 %copy-start.2 = (bf16[1,64,1152]{2,1,0:T(8,128)(2,1)S(1)}, bf16[1,64,1152]{2,1,0:T(8,128)(2,1)}, u32[]{:S(2)}) copy-start(bf16[1,64,1152]{2,1,0:T(8,128)(2,1)} %param.12) | copy-start | bytes 442372
  2.4 0.7 copy-start.5
  3.0 3.2 %copy-start.4 = (f32[1152]{0:T(1024)S(1)}, f32[1152]{0:T(1024)}, u32[]{:S(2)}) copy-start(f32[1152]{0:T(1024)} %param.13) | copy-start | bytes 13828
  6.2 0.7 copy-start.3
  10.0 6.2 %collective-permute-start = (bf16[64,1152]{1,0:T(8,128)(2,1)S(1)}, bf16[64,1152]{1,0:T(8,128)(2,1)S(1)}, u32[]{:S(2)}, u32[]{:S(2)}) collective-permute-start(bf16[64,1152]{1,0:T(8,128)(2,1)S(1)} %get-tuple-element.514), channel_id=1, source_target_pairs={{0,4},{4,8},{8,12},{12,16},{16,20},{20,24},{24,28},{28,0},{1,5},{5... | collective-permute-start | bytes 442376 | tf_op jit(solution)/shard_map/while/body/eval_jaxpr/ppermute | solution.py:12
  10.6 8.8 %collective-permute-start.1 = (f32[64,1152]{1,0:T(8,128)S(1)}, f32[64,1152]{1,0:T(8,128)S(1)}, u32[]{:S(2)}, u32[]{:S(2)}) collective-permute-start(f32[64,1152]{1,0:T(8,128)S(1)} %broadcast_select_fusion.2), channel_id=1, source_target_pairs={{0,4},{4,8},{8,12},{12,16},{16,20},{20,24},{24,28},{28,0},{1,5},{5... | collective-permute-start | bytes 884744 | tf_op jit(solution)/shard_map/while/body/eval_jaxpr/ppermute | solution.py:12
  20.3 5.5 %collective-permute-start = (bf16[64,1152]{1,0:T(8,128)(2,1)S(1)}, bf16[64,1152]{1,0:T(8,128)(2,1)S(1)}, u32[]{:S(2)}, u32[]{:S(2)}) collective-permute-start(bf16[64,1152]{1,0:T(8,128)(2,1)S(1)} %get-tuple-element.514), channel_id=1, source_target_pairs={{0,4},{4,8},{8,12},{12,16},{16,20},{20,24},{24,28},{28,0},{1,5},{5... | collective-permute-start | bytes 442376 | tf_op jit(solution)/shard_map/while/body/eval_jaxpr/ppermute | solution.py:12
  20.3 8.6 %collective-permute-start.1 = (f32[64,1152]{1,0:T(8,128)S(1)}, f32[64,1152]{1,0:T(8,128)S(1)}, u32[]{:S(2)}, u32[]{:S(2)}) collective-permute-start(f32[64,1152]{1,0:T(8,128)S(1)} %broadcast_select_fusion.2), channel_id=1, source_target_pairs={{0,4},{4,8},{8,12},{12,16},{16,20},{20,24},{24,28},{28,0},{1,5},{5... | collective-permute-start | bytes 884744 | tf_op jit(solution)/shard_map/while/body/eval_jaxpr/ppermute | solution.py:12
  29.7 5.5 %collective-permute-start = (bf16[64,1152]{1,0:T(8,128)(2,1)S(1)}, bf16[64,1152]{1,0:T(8,128)(2,1)S(1)}, u32[]{:S(2)}, u32[]{:S(2)}) collective-permute-start(bf16[64,1152]{1,0:T(8,128)(2,1)S(1)} %get-tuple-element.514), channel_id=1, source_target_pairs={{0,4},{4,8},{8,12},{12,16},{16,20},{20,24},{24,28},{28,0},{1,5},{5... | collective-permute-start | bytes 442376 | tf_op jit(solution)/shard_map/while/body/eval_jaxpr/ppermute | solution.py:12
  29.8 8.6 %collective-permute-start.1 = (f32[64,1152]{1,0:T(8,128)S(1)}, f32[64,1152]{1,0:T(8,128)S(1)}, u32[]{:S(2)}, u32[]{:S(2)}) collective-permute-start(f32[64,1152]{1,0:T(8,128)S(1)} %broadcast_select_fusion.2), channel_id=1, source_target_pairs={{0,4},{4,8},{8,12},{12,16},{16,20},{20,24},{24,28},{28,0},{1,5},{5... | collective-permute-start | bytes 884744 | tf_op jit(solution)/shard_map/while/body/eval_jaxpr/ppermute | solution.py:12
  39.2 5.5 %collective-permute-start = (bf16[64,1152]{1,0:T(8,128)(2,1)S(1)}, bf16[64,1152]{1,0:T(8,128)(2,1)S(1)}, u32[]{:S(2)}, u32[]{:S(2)}) collective-permute-start(bf16[64,1152]{1,0:T(8,128)(2,1)S(1)} %get-tuple-element.514), channel_id=1, source_target_pairs={{0,4},{4,8},{8,12},{12,16},{16,20},{20,24},{24,28},{28,0},{1,5},{5... | collective-permute-start | bytes 442376 | tf_op jit(solution)/shard_map/while/body/eval_jaxpr/ppermute | solution.py:12
  39.2 8.6 %collective-permute-start.1 = (f32[64,1152]{1,0:T(8,128)S(1)}, f32[64,1152]{1,0:T(8,128)S(1)}, u32[]{:S(2)}, u32[]{:S(2)}) collective-permute-start(f32[64,1152]{1,0:T(8,128)S(1)} %broadcast_select_fusion.2), channel_id=1, source_target_pairs={{0,4},{4,8},{8,12},{12,16},{16,20},{20,24},{24,28},{28,0},{1,5},{5... | collective-permute-start | bytes 884744 | tf_op jit(solution)/shard_map/while/body/eval_jaxpr/ppermute | solution.py:12
  48.6 5.5 %collective-permute-start = (bf16[64,1152]{1,0:T(8,128)(2,1)S(1)}, bf16[64,1152]{1,0:T(8,128)(2,1)S(1)}, u32[]{:S(2)}, u32[]{:S(2)}) collective-permute-start(bf16[64,1152]{1,0:T(8,128)(2,1)S(1)} %get-tuple-element.514), channel_id=1, source_target_pairs={{0,4},{4,8},{8,12},{12,16},{16,20},{20,24},{24,28},{28,0},{1,5},{5... | collective-permute-start | bytes 442376 | tf_op jit(solution)/shard_map/while/body/eval_jaxpr/ppermute | solution.py:12
  48.7 8.6 %collective-permute-start.1 = (f32[64,1152]{1,0:T(8,128)S(1)}, f32[64,1152]{1,0:T(8,128)S(1)}, u32[]{:S(2)}, u32[]{:S(2)}) collective-permute-start(f32[64,1152]{1,0:T(8,128)S(1)} %broadcast_select_fusion.2), channel_id=1, source_target_pairs={{0,4},{4,8},{8,12},{12,16},{16,20},{20,24},{24,28},{28,0},{1,5},{5... | collective-permute-start | bytes 884744 | tf_op jit(solution)/shard_map/while/body/eval_jaxpr/ppermute | solution.py:12
  58.1 5.5 %collective-permute-start = (bf16[64,1152]{1,0:T(8,128)(2,1)S(1)}, bf16[64,1152]{1,0:T(8,128)(2,1)S(1)}, u32[]{:S(2)}, u32[]{:S(2)}) collective-permute-start(bf16[64,1152]{1,0:T(8,128)(2,1)S(1)} %get-tuple-element.514), channel_id=1, source_target_pairs={{0,4},{4,8},{8,12},{12,16},{16,20},{20,24},{24,28},{28,0},{1,5},{5... | collective-permute-start | bytes 442376 | tf_op jit(solution)/shard_map/while/body/eval_jaxpr/ppermute | solution.py:12
  58.1 8.6 %collective-permute-start.1 = (f32[64,1152]{1,0:T(8,128)S(1)}, f32[64,1152]{1,0:T(8,128)S(1)}, u32[]{:S(2)}, u32[]{:S(2)}) collective-permute-start(f32[64,1152]{1,0:T(8,128)S(1)} %broadcast_select_fusion.2), channel_id=1, source_target_pairs={{0,4},{4,8},{8,12},{12,16},{16,20},{20,24},{24,28},{28,0},{1,5},{5... | collective-permute-start | bytes 884744 | tf_op jit(solution)/shard_map/while/body/eval_jaxpr/ppermute | solution.py:12
  67.6 5.5 %collective-permute-start = (bf16[64,1152]{1,0:T(8,128)(2,1)S(1)}, bf16[64,1152]{1,0:T(8,128)(2,1)S(1)}, u32[]{:S(2)}, u32[]{:S(2)}) collective-permute-start(bf16[64,1152]{1,0:T(8,128)(2,1)S(1)} %get-tuple-element.514), channel_id=1, source_target_pairs={{0,4},{4,8},{8,12},{12,16},{16,20},{20,24},{24,28},{28,0},{1,5},{5... | collective-permute-start | bytes 442376 | tf_op jit(solution)/shard_map/while/body/eval_jaxpr/ppermute | solution.py:12
  67.6 8.6 %collective-permute-start.1 = (f32[64,1152]{1,0:T(8,128)S(1)}, f32[64,1152]{1,0:T(8,128)S(1)}, u32[]{:S(2)}, u32[]{:S(2)}) collective-permute-start(f32[64,1152]{1,0:T(8,128)S(1)} %broadcast_select_fusion.2), channel_id=1, source_target_pairs={{0,4},{4,8},{8,12},{12,16},{16,20},{20,24},{24,28},{28,0},{1,5},{5... | collective-permute-start | bytes 884744 | tf_op jit(solution)/shard_map/while/body/eval_jaxpr/ppermute | solution.py:12
  77.0 7.0 %collective-permute-start.2 = (f32[64,1152]{1,0:T(8,128)S(1)}, f32[64,1152]{1,0:T(8,128)S(1)}, u32[]{:S(2)}, u32[]{:S(2)}) collective-permute-start(f32[64,1152]{1,0:T(8,128)S(1)} %get-tuple-element.316), channel_id=1, source_target_pairs={{0,4},{4,8},{8,12},{12,16},{16,20},{20,24},{24,28},{28,0},{1,5},{5... | collective-permute-start | bytes 884744 | tf_op jit(solution)/shard_map/ppermute | solution.py:12
where the time goes:
time: 127 us
  blocking collectives  40.4 us (32%)
  waiting for transfers between devices  24.7 us (19%)
  matrix products  15.5 us (12%)
  other arithmetic  15.4 us (12%)
  loops' own time  13 us (10%)
  starting transfers between devices  6.93 us (5%)
  local copies, waits for them, and re-layouts  6.57 us (5%)
  between operations  4.08 us (3%)
    psum x1, blocking collectives, shards(): lax.psum((jnp.stack([image_part, text_part]), loss_vector), ('blk', 'rep'))  40.4 us
    ppermute x15, waiting for transfers between devices, from_behind(): return lax.ppermute(value, axis, pairs)  24.7 us
    another operation x1, loops' own time, shards(): lax.fori_loop(1, turns + 1, advance, (partial_value, image_total, caption...  13 us
    dot_general x8, matrix products, pair_tile(): lax.dot_general(image_side, text_side, (((1,), (1,)), ((), ())), preferre...  11.1 us
    lt x8, other arithmetic, pair_tile(): kept_pairs = (index_row < image_count) & (index_col < text_count)  9.72 us
    ppermute x15, starting transfers between devices, from_behind(): return lax.ppermute(value, axis, pairs)  6.93 us
    dynamic_slice x8, local copies, waits for them, and re-layouts, count_of(): return lax.dynamic_index_in_dim(block_counts, block, keepdims=False)  4.66 us
  transfers between devices with their start and end apart: 15, of which 15 were waited for; matrix products, arithmetic and copies ran while one was open for 21% of the time, Pallas kernels for 0%

commit v1 on v0

v1 whole, which is shorter than its diff:
```python
import jax
import jax.numpy as jnp
from jax import lax
from jax.sharding import PartitionSpec as P

epsilon = 1e-06


def embed_rows(pooled, gain):
    values = pooled.astype(jnp.float32)
    centred = values - jnp.mean(values, axis=-1, keepdims=True)
    inverse = lax.rsqrt(jnp.mean(centred * centred, axis=-1, keepdims=True) + epsilon)
    normed = centred * inverse
    scaled = normed * gain
    inv_length = lax.rsqrt(jnp.sum(scaled * scaled, axis=-1, keepdims=True) + epsilon)
    return (scaled * inv_length, normed, inverse, inv_length)


def embed_back(direction, unit_rows, normed, inverse, inv_length, gain):
    tangent = (
        direction - unit_rows * jnp.sum(unit_rows * direction, axis=-1, keepdims=True)
    ) * inv_length
    gain_part = jnp.sum(tangent * normed, axis=0)
    scaled = tangent * gain
    gradient = (
        scaled
        - jnp.mean(scaled, axis=-1, keepdims=True)
        - normed * jnp.mean(scaled * normed, axis=-1, keepdims=True)
    ) * inverse
    return (gradient, gain_part)


def pair_weights(scores, labels_pos, kept, score_sharpness_factor, score_shift_amount, grad_factor):
    score_similarity_table = score_sharpness_factor * scores + score_shift_amount
    labels = jnp.where(labels_pos, 1.0, -1.0).astype(jnp.float32)
    margin = -labels * score_similarity_table
    loss_sum = jnp.sum(jnp.where(kept, jax.nn.softplus(margin), 0.0))
    weights = jnp.where(kept, -labels * jax.nn.sigmoid(margin), 0.0) * grad_factor
    return loss_sum, weights.astype(jnp.bfloat16)


def shards(
    picture_averaged_features,
    caption_averaged_features,
    picture_rescale_factor,
    caption_rescale_factor,
    exponent_of_sharpness,
    score_shift_term,
    objective_multiplier,
    matching_caption_index,
    genuine_entry_counts,
):
    block_rows = picture_averaged_features.shape[1]
    members = lax.axis_size("blk")
    own_block = lax.axis_index("blk")
    group_rows = block_rows * members
    image_unit_rows, image_normalized, image_inverse_length, image_length = embed_rows(
        picture_averaged_features[0], picture_rescale_factor
    )
    text_unit_rows, text_normalized, text_inverse_length, text_length = embed_rows(
        caption_averaged_features[0], caption_rescale_factor
    )
    picture_feature_entries = image_unit_rows.astype(jnp.bfloat16)
    caption_feature_entries = text_unit_rows.astype(jnp.bfloat16)
    block_counts = genuine_entry_counts[0]
    partner = matching_caption_index[0]
    real_count = jnp.sum(block_counts).astype(jnp.float32)
    score_sharpness_factor = jnp.exp(exponent_of_sharpness[0])
    score_shift_amount = score_shift_term[0]
    grad_factor = objective_multiplier[0] / real_count

    both = jnp.stack([picture_feature_entries, caption_feature_entries])
    gathered = lax.all_gather(both, "blk", axis=1, tiled=True)
    image_all = gathered[0]
    text_all = gathered[1]

    rows = jnp.arange(group_rows, dtype=jnp.int32)
    real_all = (rows % block_rows) < block_counts[rows // block_rows]
    own_rows = jnp.arange(block_rows, dtype=jnp.int32)
    real_own = own_rows < lax.dynamic_index_in_dim(block_counts, own_block, keepdims=False)
    own_start = own_block * block_rows
    own_partner = lax.dynamic_slice_in_dim(partner, own_start, block_rows)

    row_scores = lax.dot_general(
        picture_feature_entries, text_all, (((1,), (1,)), ((), ())),
        preferred_element_type=jnp.float32,
    )
    row_pos = own_partner[:, None] == rows[None, :]
    row_kept = real_own[:, None] & real_all[None, :]
    loss_sum, row_weights = pair_weights(
        row_scores, row_pos, row_kept, score_sharpness_factor, score_shift_amount, grad_factor
    )
    image_direction = jnp.dot(row_weights, text_all, preferred_element_type=jnp.float32)

    col_scores = lax.dot_general(
        image_all, caption_feature_entries, (((1,), (1,)), ((), ())),
        preferred_element_type=jnp.float32,
    )
    col_pos = partner[:, None] == (own_start + own_rows)[None, :]
    col_kept = real_all[:, None] & real_own[None, :]
    unused, col_weights = pair_weights(
        col_scores, col_pos, col_kept, score_sharpness_factor, score_shift_amount, grad_factor
    )
    text_direction = lax.dot_general(
        col_weights, image_all, (((0,), (0,)), ((), ())),
        preferred_element_type=jnp.float32,
    )

    image_gradient, image_part = embed_back(
        score_sharpness_factor * image_direction,
        image_unit_rows,
        image_normalized,
        image_inverse_length,
        image_length,
        picture_rescale_factor,
    )
    text_gradient, text_part = embed_back(
        score_sharpness_factor * text_direction,
        text_unit_rows,
        text_normalized,
        text_inverse_length,
        text_length,
        caption_rescale_factor,
    )
    replicas = lax.axis_size("rep")
    group_index = lax.axis_index("rep")
    loss_vector = jnp.where(
        jnp.arange(replicas, dtype=jnp.int32) == group_index, loss_sum / real_count, 0.0
    )
    width = image_part.shape[0]
    flat = jnp.concatenate([image_part, text_part, loss_vector])
    total = lax.psum(flat, ("blk", "rep"))
    gain_grads = total[: 2 * width].reshape(2, width)
    group_loss = lax.dynamic_slice_in_dim(total[2 * width:], group_index, 1)
    return (
        image_gradient.astype(jnp.bfloat16)[None],
        text_gradient.astype(jnp.bfloat16)[None],
        gain_grads,
        group_loss,
    )


def solution(mesh):
    placed = (
        P("rep", "blk", None),
        P("rep", "blk", None),
        P(),
        P(),
        P(),
        P(),
        P(),
        P("rep", None),
        P("rep", None),
    )
    return jax.shard_map(
        shards,
        mesh=mesh,
        in_specs=placed,
        out_specs=(P("rep", "blk", None), P("rep", "blk", None), P(), P("rep")),
        check_vma=False,
    )
```

time: 127 us -> 105 us (0.83)
  between operations: 4.08 us -> 17.6 us
  loops' own time: 13 us -> 0 us
  matrix products: 15.5 us -> 5.8 us
  starting transfers between devices: 6.93 us -> 0.04 us
  local copies, waits for them, and re-layouts: 6.57 us -> 2.01 us
  waiting for transfers between devices: 24.7 us -> 21.6 us
  other arithmetic: 15.4 us -> 17.6 us
    ppermute x15 -> x0, waiting for transfers between devices: 24.7 us -> none  [from_behind(): return lax.ppermute(value, axis, pairs)]
    all_gather x0 -> x1, waiting for transfers between devices: none -> 21.6 us  [shards(): gathered = lax.all_gather(both, 'blk', axis=1, tiled=True)]
    another operation x1 -> x0, loops' own time: 13 us -> none  [shards(): lax.fori_loop(1, turns + 1, advance, (partial_value, image_total, caption...]
    dot_general x24 -> x3, matrix products: 15.5 us -> 5.8 us  [the longest x1 2.89 us: shards(): lax.dot_general(col_weights, image_all, (((0,), (0,)), ((), ())), preferr...]
    lt x8 -> x2, other arithmetic: 9.72 us -> 1.35 us  [the longest x1 0.7 us: shards(): real_all = rows % block_rows < block_counts[rows // block_rows]]
    ppermute x15 -> x0, starting transfers between devices: 6.93 us -> none  [from_behind(): return lax.ppermute(value, axis, pairs)]
    gather x0 -> x2, other arithmetic: none -> 4.67 us  [shards(): real_all = rows % block_rows < block_counts[rows // block_rows]]
    dynamic_slice x9 -> x2, local copies, waits for them, and re-layouts: 5.24 us -> 1.28 us  [the longest x1 0.7 us: shards(): lax.dynamic_index_in_dim(block_counts, own_block, keepdims=False)]
  transfers between devices with their start and end apart: 15 -> 1, of which waited for: 15 -> 1; matrix products, arithmetic and copies ran while one was open for 21% -> 7% of each run, Pallas kernels for 0% -> 0%
where the time goes in v1:
time: 105 us; the launch traced here: 104 us
  blocking collectives  39.5 us (38%)
  waiting for transfers between devices  21.6 us (21%)
  other arithmetic  17.6 us (17%)
  between operations  17.6 us (17%)
  matrix products  5.8 us (6%)
  local copies, waits for them, and re-layouts  2.01 us (2%)
    psum x1, blocking collectives, shards(): total = lax.psum(flat, ('blk', 'rep'))  39.5 us
    all_gather x1, waiting for transfers between devices, shards(): gathered = lax.all_gather(both, 'blk', axis=1, tiled=True)  21.6 us
    gather x2, other arithmetic, shards(): real_all = rows % block_rows < block_counts[rows // block_rows]  4.67 us
    dot_general x1, matrix products, shards(): lax.dot_general(col_weights, image_all, (((0,), (0,)), ((), ())), preferr...  2.89 us
    dot_general x1, matrix products, shards(): lax.dot_general(picture_feature_entries, text_all, (((1,), (1,)), ((), ()...  2.45 us
    reduce_sum x2, other arithmetic, embed_rows(): jnp.sum(scaled * scaled, axis=-1, keepdims=True) + epsilon  2.29 us
    reduce_sum x2, other arithmetic, embed_rows(): jnp.mean(centred * centred, axis=-1, keepdims=True) + epsilon  2.24 us
  transfers between devices with their start and end apart: 1, of which 1 were waited for; matrix products, arithmetic and copies ran while one was open for 7% of the time, Pallas kernels for 0%

profile of v1, /device:TPU:0, one launch (start us, length us, event | category | flops | bytes accessed | tf_op | source)
XLA Modules:
  0.0 104.2 jit_solution(15409728929251041915)
XLA Ops:
  7.3 1.1 %convert_reduce_fusion.1 = f32[64]{0:T(128)S(1)} fusion(bf16[1,64,1152]{2,1,0:T(8,128)(2,1)} %param.9), kind=kLoop, calls=%fused_computation.23 | loop fusion | flops 147392 | bytes 147712 | tf_op jit(solution)/shard_map/reduce_sum | solution.py:11
  8.3 1.1 %fusion.36 = f32[64]{0:T(128)S(1)} fusion(bf16[1,64,1152]{2,1,0:T(8,128)(2,1)} %param.9, f32[64]{0:T(128)S(1)} %broadcast_multiply_fusion.5), kind=kLoop, calls=%fused_computation.49 | loop fusion | flops 294848 | bytes 147968 | tf_op jit(solution)/shard_map/reduce_sum | solution.py:12
  9.5 1.1 %fusion.30 = f32[64]{0:T(128)S(1)} fusion(bf16[1,64,1152]{2,1,0:T(8,128)(2,1)} %param.9, f32[1152]{0:T(1024)} %param.11, f32[64]{0:T(128)S(1)} %add_rsqrt_fusion.3, f32[64]{0:T(128)S(1)} %broadcast_multiply_fusion.5), kind=kLoop, calls=%fused_computation.43 | loop fusion | flops 442304 | bytes 152832 | tf_op jit(solution)/shard_map/reduce_sum | solution.py:15
  10.6 1.0 convert_reduce_fusion
  11.7 1.1 %fusion.61 = f32[64]{0:T(128)S(1)} fusion(bf16[1,64,1152]{2,1,0:T(8,128)(2,1)} %param.10, f32[64]{0:T(128)S(1)} %broadcast_multiply_fusion.4), kind=kLoop, calls=%fused_computation.74 | loop fusion | flops 294848 | bytes 147968 | tf_op jit(solution)/shard_map/reduce_sum | solution.py:12
  12.8 1.1 %fusion.55 = f32[64]{0:T(128)S(1)} fusion(bf16[1,64,1152]{2,1,0:T(8,128)(2,1)} %param.10, f32[1152]{0:T(1024)} %param.12, f32[64]{0:T(128)S(1)} %add_rsqrt_fusion.1, f32[64]{0:T(128)S(1)} %broadcast_multiply_fusion.4), kind=kLoop, calls=%fused_computation.68 | loop fusion | flops 442304 | bytes 152832 | tf_op jit(solution)/shard_map/reduce_sum | solution.py:15
  14.0 1.3 %fusion.15 = (bf16[1,64,1152]{2,1,0:T(8,128)(2,1)S(1)}, bf16[1,64,1152]{2,1,0:T(8,128)(2,1)S(1)}) fusion(bf16[1,64,1152]{2,1,0:T(8,128)(2,1)} %param.9, f32[64]{0:T(128)S(1)} %add_rsqrt_fusion.2, f32[1152]{0:T(1024)} %param.11, f32[64]{0:T(128)S(1)} %add_rsqrt_fusion.3, f32[64]{0:T(128)S(1)} %broadcast_multiply_fusion.5, f32[64]{0:T(128)S(1)} %add_rsqrt_fusion, ...), kind=kLoop, calls=%fused_computation.28 | loop fusion | flops 884736 | bytes 600576 | tf_op jit(solution)/shard_map/convert_element_type | solution.py:63
  15.3 0.8 pad_maximum_fusion
  18.0 0.6 reduce_sum.150
  19.4 0.7 constant_dynamic-slice_fusion
  20.1 0.7 iota_compare_fusion.1
  20.8 4.6 %compare_select_fusion.2 = s32[512,1]{0,1:T(1,128)S(1)} fusion(s32[]{:T(128)} %bitcast.3, s32[]{:T(128)} %bitcast.4, s32[]{:T(128)} %bitcast.5, s32[]{:T(128)} %bitcast.6, s32[]{:T(128)} %bitcast.7, s32[]{:T(128)} %bitcast.9, s32[]{:T(128)} %bitcast.8), kind=kLoop, calls=%fused_computation.113 | loop fusion | flops 11776 | bytes 2076 | tf_op jit(solution)/shard_map/gather | solution.py:78
  25.5 0.7 fusion.92
  26.2 21.6 %all-gather.2.cloned.1.call-done = bf16[2,512,1152]{2,1,0:T(8,128)(2,1)} async-done(((bf16[2,64,1152]{2,1,0:T(8,128)(2,1)}), bf16[2,512,1152]{2,1,0:T(8,128)(2,1)}) %all-gather.2.cloned.1.call-update) | async-done | bytes 2359312 | tf_op jit(solution)/shard_map/all_gather | solution.py:73
  47.8 2.4 %fusion.73 = (f32[]{:T(128)}, f32[64,512]{1,0:T(8,128)S(1)}) fusion(pred[512]{0:T(512)(128)(4,1)S(1)} %fusion.92, pred[64]{0:T(512)(128)(4,1)S(1)} %iota_compare_fusion.1, f32[]{:T(128)} %bitcast.142, bf16[2,512,1152]{2,1,0:T(8,128)(2,1)} %all-gather.2.cloned.1.call-done, bf16[1,64,1152]{2,1,0:T(8,128)(2,1)S(1)} %get-tuple-element.27, f32[]{:T(128)} %bitcast, ...), kind=kOutput, calls=%fused_computation.90 | convolution fusion | flops 75988992 | bytes 1460036 | tf_op jit(solution)/shard_map/dot_general | solution.py:84
  51.0 2.9 %fusion.52 = (f32[64]{0:T(128)S(1)}, f32[64,1152]{1,0:T(8,128)S(1)}) fusion(bf16[1,64,1152]{2,1,0:T(8,128)(2,1)S(1)} %copy-done, f32[64]{0:T(128)S(1)} %add_rsqrt_fusion, f32[1152]{0:T(1024)S(1)} %copy-done.2, f32[64]{0:T(128)S(1)} %add_rsqrt_fusion.1, f32[64]{0:T(128)S(1)} %broadcast_multiply_fusion.4, ...), kind=kOutput, calls=%fused_computation.65 | convolution fusion | flops 152043456 | bytes 2959172 | tf_op jit(solution)/shard_map/dot_general | solution.py:104
  53.9 0.3 fusion.60
  54.2 0.5 fusion.27
  54.7 0.3 fusion.35
  55.0 39.5 %psum.7 = f32[2308]{0:T(1024)S(1)} all-reduce(f32[2308]{0:T(1024)S(1)} %pad_maximum_fusion.1), channel_id=1, replica_groups=mesh['blk'=8,'rep'=4] {'blk','rep'}, use_global_device_ids=true, to_apply=%region_16.17 | all-reduce | flops 2308 | bytes 18464 | tf_op jit(solution)/shard_map/psum | solution.py:132
  94.5 0.6 reshape.263
  95.1 0.6 dynamic_slice.12
  95.7 0.8 fusion.66
  96.5 0.8 fusion.67
  (32 shorter events, 0.3 us)
Async XLA Ops:
  7.2 43.8 %copy-start = (bf16[1,64,1152]{2,1,0:T(8,128)(2,1)S(1)}, bf16[1,64,1152]{2,1,0:T(8,128)(2,1)}, u32[]{:S(2)}) copy-start(bf16[1,64,1152]{2,1,0:T(8,128)(2,1)} %param.10) | copy-start | bytes 442372
  7.2 43.7 %copy-start.2 = (f32[1152]{0:T(1024)S(1)}, f32[1152]{0:T(1024)}, u32[]{:S(2)}) copy-start(f32[1152]{0:T(1024)} %param.12) | copy-start | bytes 13828
  7.2 10.8 %copy-start.4 = (s32[1,8]{1,0:T(1,128)S(1)}, s32[1,8]{1,0:T(1,128)}, u32[]{:S(2)}) copy-start(s32[1,8]{1,0:T(1,128)} %param.17) | copy-start | bytes 100
  7.2 13.6 %copy-start.6 = (s32[1,512]{1,0:T(1,128)S(1)}, s32[1,512]{1,0:T(1,128)}, u32[]{:S(2)}) copy-start(s32[1,512]{1,0:T(1,128)} %param.16) | copy-start | bytes 6148
  7.2 40.6 %all-gather.2.cloned.1.call-start = ((), (), s32[]{:S(2)}) async-start(), calls=%async_computation | async-start | bytes 2654208 | tf_op jit(solution)/shard_map/all_gather | solution.py:73
  50.9 3.3 %copy-start.1 = (bf16[1,64,1152]{2,1,0:T(8,128)(2,1)S(1)}, bf16[1,64,1152]{2,1,0:T(8,128)(2,1)}, u32[]{:S(2)}) copy-start(bf16[1,64,1152]{2,1,0:T(8,128)(2,1)} %param.9) | copy-start | bytes 442372
  50.9 3.3 %copy-start.3 = (f32[1152]{0:T(1024)S(1)}, f32[1152]{0:T(1024)}, u32[]{:S(2)}) copy-start(f32[1152]{0:T(1024)} %param.11) | copy-start | bytes 13828
  51.0 3.3 %copy-start.5 = (bf16[2,512,1152]{2,1,0:T(8,128)(2,1)S(1)}, bf16[2,512,1152]{2,1,0:T(8,128)(2,1)}, u32[]{:S(2)}) copy-start(bf16[2,512,1152]{2,1,0:T(8,128)(2,1)} %all-gather.2.cloned.1.call-done) | copy-start | bytes 7077892
Sparse Core Ops, SparseCore 0:
  16.2 31.5 all-gather.1

commit v2 on v1

--- a/solution.py
+++ b/solution.py
@@ -4,6 +4,54 @@
 from jax.sharding import PartitionSpec as P
 
 epsilon = 1e-06
+
+
+def xor_swap(value, axis, bit):
+    count = lax.axis_size(axis)
+    return lax.ppermute(value, axis, [(source, source ^ bit) for source in range(count)])
+
+
+def power_of_two(count):
+    return count > 1 and count & (count - 1) == 0
+
+
+def gather_blocks(both, axis):
+    count = lax.axis_size(axis)
+    rows = both.shape[1]
+    if not power_of_two(count) or count < 4 or rows % 2:
+        gathered = lax.all_gather(both, axis, axis=1, tiled=False)
+        return gathered, list(range(count)), [0] * count, True
+    chip_bits = [1 << b for b in range(1, count.bit_length() - 1)]
+    half = rows // 2
+    halves = [
+        [both[:, None, :half], [0], chip_bits],
+        [both[:, None, half:], [0], chip_bits[::-1]],
+    ]
+    for step in range(len(chip_bits)):
+        for held in halves:
+            bit = held[2][step]
+            held[0] = jnp.concatenate([held[0], xor_swap(held[0], axis, bit)], axis=1)
+            held[1] = held[1] + [mask ^ bit for mask in held[1]]
+    for held in halves:
+        held[0] = jnp.concatenate([held[0], xor_swap(held[0], axis, 1)], axis=1)
+        held[1] = held[1] + [mask ^ 1 for mask in held[1]]
+    gathered = jnp.concatenate([halves[0][0], halves[1][0]], axis=1)
+    masks = halves[0][1] + halves[1][1]
+    offsets = [0] * count + [half] * count
+    return gathered, masks, offsets, False
+
+
+def all_sum(value, axes):
+    for axis in axes:
+        count = lax.axis_size(axis)
+        if not power_of_two(count):
+            value = lax.psum(value, axis)
+            continue
+        bit = 1
+        while bit < count:
+            value = value + xor_swap(value, axis, bit)
+            bit *= 2
+    return value
 
 
 def embed_rows(pooled, gain):
@@ -51,9 +99,7 @@
     genuine_entry_counts,
 ):
     block_rows = picture_averaged_features.shape[1]
-    members = lax.axis_size("blk")
     own_block = lax.axis_index("blk")
-    group_rows = block_rows * members
     image_unit_rows, image_normalized, image_inverse_length, image_length = embed_rows(
         picture_averaged_features[0], picture_rescale_factor
     )
@@ -70,16 +116,23 @@
     grad_factor = objective_multiplier[0] / real_count
 
     both = jnp.stack([picture_feature_entries, caption_feature_entries])
-    gathered = lax.all_gather(both, "blk", axis=1, tiled=True)
-    image_all = gathered[0]
-    text_all = gathered[1]
-
-    rows = jnp.arange(group_rows, dtype=jnp.int32)
-    real_all = (rows % block_rows) < block_counts[rows // block_rows]
+    gathered, masks, offsets, natural = gather_blocks(both, "blk")
+    positions = gathered.shape[1]
+    piece = gathered.shape[2]
+    image_all = gathered[0].reshape(positions * piece, -1)
+    text_all = gathered[1].reshape(positions * piece, -1)
+    if natural:
+        held_block = jnp.arange(positions, dtype=jnp.int32)
+    else:
+        held_block = own_block ^ jnp.asarray(masks, jnp.int32)
+    first_row = jnp.asarray(offsets, jnp.int32)[:, None] + jnp.arange(piece, dtype=jnp.int32)[None, :]
+    rows = (held_block[:, None] * block_rows + first_row).reshape(-1)
+    real_all = (first_row < block_counts[held_block][:, None]).reshape(-1)
     own_rows = jnp.arange(block_rows, dtype=jnp.int32)
     real_own = own_rows < lax.dynamic_index_in_dim(block_counts, own_block, keepdims=False)
     own_start = own_block * block_rows
     own_partner = lax.dynamic_slice_in_dim(partner, own_start, block_rows)
+    held_partner = partner[rows]
 
     row_scores = lax.dot_general(
         picture_feature_entries, text_all, (((1,), (1,)), ((), ())),
@@ -96,7 +149,7 @@
         image_all, caption_feature_entries, (((1,), (1,)), ((), ())),
         preferred_element_type=jnp.float32,
     )
-    col_pos = partner[:, None] == (own_start + own_rows)[None, :]
+    col_pos = held_partner[:, None] == (own_start + own_rows)[None, :]
     col_kept = real_all[:, None] & real_own[None, :]
     unused, col_weights = pair_weights(
         col_scores, col_pos, col_kept, score_sharpness_factor, score_shift_amount, grad_factor
@@ -129,7 +182,7 @@
     )
     width = image_part.shape[0]
     flat = jnp.concatenate([image_part, text_part, loss_vector])
-    total = lax.psum(flat, ("blk", "rep"))
+    total = all_sum(flat, ("blk", "rep"))
     gain_grads = total[: 2 * width].reshape(2, width)
     group_loss = lax.dynamic_slice_in_dim(total[2 * width:], group_index, 1)
     return (

time: 105 us -> 76.6 us (0.73)
  blocking collectives: 39.5 us -> 0 us
  starting transfers between devices: 0.04 us -> 15.6 us
  between operations: 17.6 us -> 4.24 us
  waiting for transfers between devices: 21.6 us -> 29.6 us
  local copies, waits for them, and re-layouts: 2.01 us -> 9.86 us
  other arithmetic: 17.6 us -> 14.2 us
  matrix products: 5.8 us -> 2.73 us
    psum x1 -> x0, blocking collectives: 39.5 us -> none  [shards(): total = lax.psum(flat, ('blk', 'rep'))]
    ppermute x0 -> x11, waiting for transfers between devices: none -> 29.6 us  [xor_swap(): lax.ppermute(value, axis, [(source, source ^ bit) for source in range(cou...]
    all_gather x1 -> x0, waiting for transfers between devices: 21.6 us -> none  [shards(): gathered = lax.all_gather(both, 'blk', axis=1, tiled=True)]
    ppermute x0 -> x11, starting transfers between devices: none -> 15.6 us  [xor_swap(): lax.ppermute(value, axis, [(source, source ^ bit) for source in range(cou...]
    gather x2 -> x1, other arithmetic: 4.67 us -> 0.01 us  [shards(): held_partner = partner[rows]]
    gather x0 -> x2, local copies, waits for them, and re-layouts: none -> 4.15 us  [the longest x1 3.49 us: shards(): held_partner = partner[rows]]
    concatenate x0 -> x4, other arithmetic: none -> 2.53 us  [gather_blocks(): held[0] = jnp.concatenate([held[0], xor_swap(held[0], axis, bit)], axis=1)]
    dot_general x1, matrix products: 2.89 us -> 1.1 us  [shards(): lax.dot_general(col_weights, image_all, (((0,), (0,)), ((), ())), preferr...]
  transfers between devices with their start and end apart: 1 -> 11, of which waited for: 1 -> 10; matrix products, arithmetic and copies ran while one was open for 7% -> 11% of each run, Pallas kernels for 0% -> 0%
where the time goes in v2:
time: 76.6 us; the launch traced here: 76.2 us
  waiting for transfers between devices  29.6 us (39%)
  starting transfers between devices  15.6 us (20%)
  other arithmetic  14.2 us (19%)
  local copies, waits for them, and re-layouts  9.86 us (13%)
  between operations  4.24 us (6%)
  matrix products  2.73 us (4%)
    ppermute x11, waiting for transfers between devices, xor_swap(): lax.ppermute(value, axis, [(source, source ^ bit) for source in range(cou...  29.6 us
    ppermute x11, starting transfers between devices, xor_swap(): lax.ppermute(value, axis, [(source, source ^ bit) for source in range(cou...  15.6 us
    gather x1, local copies, waits for them, and re-layouts, shards(): held_partner = partner[rows]  3.49 us
    concatenate x4, other arithmetic, gather_blocks(): held[0] = jnp.concatenate([held[0], xor_swap(held[0], axis, bit)], axis=1)  2.53 us
    reduce_sum x2, other arithmetic, embed_rows(): jnp.sum(scaled * scaled, axis=-1, keepdims=True) + epsilon  2.29 us
    reduce_sum x2, other arithmetic, embed_rows(): jnp.mean(centred * centred, axis=-1, keepdims=True) + epsilon  2.24 us
    reduce_sum x2, other arithmetic, embed_rows(): centred = values - jnp.mean(values, axis=-1, keepdims=True)  2.08 us
  transfers between devices with their start and end apart: 11, of which 10 were waited for; matrix products, arithmetic and copies ran while one was open for 11% of the time, Pallas kernels for 0%

profile of v2, /device:TPU:0, one launch (start us, length us, event | category | flops | bytes accessed | tf_op | source)
XLA Modules:
  0.0 76.2 jit_solution(7466453607137542335)
XLA Ops:
  2.9 1.1 %fusion.30 = f32[64]{0:T(128)S(1)} fusion(bf16[1,64,1152]{2,1,0:T(8,128)(2,1)} %param.11, f32[1152]{0:T(1024)} %param.13, f32[64]{0:T(128)S(1)} %add_rsqrt_fusion.3, f32[64]{0:T(128)S(1)} %broadcast_multiply_fusion.5), kind=kLoop, calls=%fused_computation.45 | loop fusion | flops 442304 | bytes 152832 | tf_op jit(solution)/shard_map/reduce_sum | solution.py:63
  6.2 1.1 %fusion.55 = f32[64]{0:T(128)S(1)} fusion(bf16[1,64,1152]{2,1,0:T(8,128)(2,1)} %param.12, f32[1152]{0:T(1024)} %param.14, f32[64]{0:T(128)S(1)} %add_rsqrt_fusion.1, f32[64]{0:T(128)S(1)} %broadcast_multiply_fusion.4), kind=kLoop, calls=%fused_computation.70 | loop fusion | flops 442304 | bytes 152832 | tf_op jit(solution)/shard_map/reduce_sum | solution.py:63
  7.4 1.3 %fusion.15 = (bf16[1,64,1152]{2,1,0:T(8,128)(2,1)S(1)}, bf16[1,64,1152]{2,1,0:T(8,128)(2,1)S(1)}) fusion(bf16[1,64,1152]{2,1,0:T(8,128)(2,1)} %param.11, f32[64]{0:T(128)S(1)} %add_rsqrt_fusion.2, f32[1152]{0:T(1024)} %param.13, f32[64]{0:T(128)S(1)} %add_rsqrt_fusion.3, f32[64]{0:T(128)S(1)} %broadcast_multiply_fusion.5, f32[64]{0:T(128)S(1)} %add_rsqrt_fusion, ...), kind=kLoop, calls=%fused_computation.30 | loop fusion | flops 884736 | bytes 600576 | tf_op jit(solution)/shard_map/convert_element_type | solution.py:109
  8.7 3.0 %collective-permute-start = (bf16[2,1,32,1152]{3,2,0,1:T(8,128)(2,1)S(1)}, bf16[2,1,32,1152]{3,2,0,1:T(8,128)(2,1)S(1)}, u32[]{:S(2)}, u32[]{:S(2)}) collective-permute-start(bf16[2,1,32,1152]{3,2,0,1:T(8,128)(2,1)S(1)} %get-tuple-element.15), channel_id=1, source_target_pairs={{0,8},{4,12},{8,0},{12,4},{16,24},{20,28},{24,16},{28,20},{1,9},{5... | collective-permute-start | bytes 442376 | tf_op jit(solution)/shard_map/ppermute | solution.py:11
  11.7 3.8 %collective-permute-done = bf16[2,1,32,1152]{3,2,0,1:T(8,128)(2,1)S(1)} collective-permute-done((bf16[2,1,32,1152]{3,2,0,1:T(8,128)(2,1)S(1)}, bf16[2,1,32,1152]{3,2,0,1:T(8,128)(2,1)S(1)}, u32[]{:S(2)}, u32[]{:S(2)}) %collective-permute-start) | collective-permute-done | bytes 147488 | tf_op jit(solution)/shard_map/ppermute | solution.py:11
  16.3 1.8 %collective-permute-start.1 = (bf16[2,2,32,1152]{3,2,0,1:T(8,128)(2,1)}, bf16[2,2,32,1152]{3,2,0,1:T(8,128)(2,1)S(1)}, u32[]{:S(2)}, u32[]{:S(2)}) collective-permute-start(bf16[2,2,32,1152]{3,2,0,1:T(8,128)(2,1)} %pad_maximum_fusion.2), channel_id=1, source_target_pairs={{0,16},{4,20},{8,24},{12,28},{16,0},{20,4},{24,8},{28,12},{1,17},{... | collective-permute-start | bytes 884744 | tf_op jit(solution)/shard_map/ppermute | solution.py:11
  18.1 6.6 %collective-permute-done.1 = bf16[2,2,32,1152]{3,2,0,1:T(8,128)(2,1)S(1)} collective-permute-done((bf16[2,2,32,1152]{3,2,0,1:T(8,128)(2,1)}, bf16[2,2,32,1152]{3,2,0,1:T(8,128)(2,1)S(1)}, u32[]{:S(2)}, u32[]{:S(2)}) %collective-permute-start.1) | collective-permute-done | bytes 294944 | tf_op jit(solution)/shard_map/ppermute | solution.py:11
  25.8 2.1 %collective-permute-done.2 = bf16[2,4,32,1152]{3,2,0,1:T(8,128)(2,1)} collective-permute-done((bf16[2,4,32,1152]{3,2,0,1:T(8,128)(2,1)}, bf16[2,4,32,1152]{3,2,0,1:T(8,128)(2,1)}, u32[]{:S(2)}, u32[]{:S(2)}) %collective-permute-start.2) | collective-permute-done | bytes 589856 | tf_op jit(solution)/shard_map/ppermute | solution.py:11
  29.1 1.6 %collective-permute-start.3 = (bf16[2,1,32,1152]{3,2,0,1:T(8,128)(2,1)S(1)}, bf16[2,1,32,1152]{3,2,0,1:T(8,128)(2,1)S(1)}, u32[]{:S(2)}, u32[]{:S(2)}) collective-permute-start(bf16[2,1,32,1152]{3,2,0,1:T(8,128)(2,1)S(1)} %get-tuple-element.13), channel_id=1, source_target_pairs={{0,16},{4,20},{8,24},{12,28},{16,0},{20,4},{24,8},{28,12},{1,17},{... | collective-permute-start | bytes 442376 | tf_op jit(solution)/shard_map/ppermute | solution.py:11
  31.9 3.1 %collective-permute-done.3 = bf16[2,1,32,1152]{3,2,0,1:T(8,128)(2,1)S(1)} collective-permute-done((bf16[2,1,32,1152]{3,2,0,1:T(8,128)(2,1)S(1)}, bf16[2,1,32,1152]{3,2,0,1:T(8,128)(2,1)S(1)}, u32[]{:S(2)}, u32[]{:S(2)}) %collective-permute-start.3) | collective-permute-done | bytes 147488 | tf_op jit(solution)/shard_map/ppermute | solution.py:11
  35.1 1.5 %collective-permute-start.4 = (bf16[2,2,32,1152]{3,2,0,1:T(8,128)(2,1)S(1)}, bf16[2,2,32,1152]{3,2,0,1:T(8,128)(2,1)S(1)}, u32[]{:S(2)}, u32[]{:S(2)}) collective-permute-start(bf16[2,2,32,1152]{3,2,0,1:T(8,128)(2,1)S(1)} %pad_maximum_fusion.3), channel_id=1, source_target_pairs={{0,8},{4,12},{8,0},{12,4},{16,24},{20,28},{24,16},{28,20},{1,9},{5... | collective-permute-start | bytes 884744 | tf_op jit(solution)/shard_map/ppermute | solution.py:11
  37.3 6.0 %collective-permute-done.4 = bf16[2,2,32,1152]{3,2,0,1:T(8,128)(2,1)S(1)} collective-permute-done((bf16[2,2,32,1152]{3,2,0,1:T(8,128)(2,1)S(1)}, bf16[2,2,32,1152]{3,2,0,1:T(8,128)(2,1)S(1)}, u32[]{:S(2)}, u32[]{:S(2)}) %collective-permute-start.4) | collective-permute-done | bytes 294944 | tf_op jit(solution)/shard_map/ppermute | solution.py:11
  47.7 3.5 %gather_fusion.1 = s32[512]{0:T(512)S(1)} fusion(s32[512]{0:T(512)S(1)} %bitcast.134, s32[1024]{0:T(1024)S(1)} %get-tuple-element.28), kind=kCustom, calls=%fused_computation.1 | custom fusion | bytes 6144 | tf_op jit(solution)/shard_map/gather | solution.py:135
  51.4 1.1 %constant_dynamic-update-slice_fusion = bf16[2,16,32,1152]{3,2,0,1:T(8,128)(2,1)S(1)} fusion(bf16[2,16,32,1152]{3,2,0,1:T(8,128)(2,1)S(1)} %constant_dynamic-update-slice_fusion.1, bf16[2,4,32,1152]{3,2,0,1:T(8,128)(2,1)} %collective-permute-done.5), kind=kLoop, calls=%fused_computation.119 | loop fusion | bytes 1179648 | tf_op jit(solution)/shard_map/concatenate | solution.py:38
  52.5 1.2 %fusion.108 = (bf16[1,16,32,1152]{3,2,0,1:T(8,128)(2,1)}, bf16[1,16,32,1152]{3,2,0,1:T(8,128)(2,1)S(1)}) fusion(bf16[2,16,32,1152]{3,2,0,1:T(8,128)(2,1)S(1)} %constant_dynamic-update-slice_fusion), kind=kLoop, calls=%fused_computation.157 | loop fusion | bytes 4718592 | tf_op jit(solution)/shard_map/slice | solution.py:122
  53.7 1.2 %fusion.76 = (f32[]{:T(128)}, f32[64,512]{1,0:T(8,128)S(1)}) fusion(pred[512]{0:T(512)(128)(4,1)S(1)} %lt.65, pred[64]{0:T(512)(128)(4,1)S(1)} %iota_compare_fusion, f32[]{:T(128)} %bitcast.131, bf16[512,1152]{1,0:T(8,128)(2,1)S(1)} %bitcast.137, bf16[1,64,1152]{2,1,0:T(8,128)(2,1)S(1)} %get-tuple-element.26, f32[]{:T(128)} %bitcast, s32[512]{0:T(512)S(1)} %add.172, ...), kind=kOutput, calls=%fused_computation.99 | convolution fusion | flops 75988992 | bytes 1461068 | tf_op jit(solution)/shard_map/dot_general | solution.py:137
  59.2 1.5 %collective-permute-start.7 = (f32[2308]{0:T(1024)S(1)}, f32[2308]{0:T(1024)S(1)}, u32[]{:S(2)}, u32[]{:S(2)}) collective-permute-start(f32[2308]{0:T(1024)S(1)} %fusion.115), channel_id=1, source_target_pairs={{0,8},{4,12},{8,0},{12,4},{16,24},{20,28},{24,16},{28,20},{1,9},{5... | collective-permute-start | bytes 27704 | tf_op jit(solution)/shard_map/ppermute | solution.py:11
  61.6 1.4 %collective-permute-done.7 = f32[2308]{0:T(1024)S(1)} collective-permute-done((f32[2308]{0:T(1024)S(1)}, f32[2308]{0:T(1024)S(1)}, u32[]{:S(2)}, u32[]{:S(2)}) %collective-permute-start.7) | collective-permute-done | bytes 9264 | tf_op jit(solution)/shard_map/ppermute | solution.py:11
  63.0 1.5 %collective-permute-start.8 = (f32[2308]{0:T(1024)S(1)}, f32[2308]{0:T(1024)S(1)}, u32[]{:S(2)}, u32[]{:S(2)}) collective-permute-start(f32[2308]{0:T(1024)S(1)} %add.190), channel_id=1, source_target_pairs={{0,16},{4,20},{8,24},{12,28},{16,0},{20,4},{24,8},{28,12},{1,17},{... | collective-permute-start | bytes 27704 | tf_op jit(solution)/shard_map/ppermute | solution.py:11
  64.5 2.2 %collective-permute-done.8 = f32[2308]{0:T(1024)S(1)} collective-permute-done((f32[2308]{0:T(1024)S(1)}, f32[2308]{0:T(1024)S(1)}, u32[]{:S(2)}, u32[]{:S(2)}) %collective-permute-start.8) | collective-permute-done | bytes 9264 | tf_op jit(solution)/shard_map/ppermute | solution.py:11
  66.7 1.5 %collective-permute-start.9 = (f32[2308]{0:T(1024)S(1)}, f32[2308]{0:T(1024)S(1)}, u32[]{:S(2)}, u32[]{:S(2)}) collective-permute-start(f32[2308]{0:T(1024)S(1)} %add.191), channel_id=1, source_target_pairs={{0,1},{1,0},{2,3},{3,2},{4,5},{5,4},{6,7},{7,6},{8,9},{9,8},{10,11... | collective-permute-start | bytes 27704 | tf_op jit(solution)/shard_map/ppermute | solution.py:11
  68.3 2.1 %collective-permute-done.9 = f32[2308]{0:T(1024)S(1)} collective-permute-done((f32[2308]{0:T(1024)S(1)}, f32[2308]{0:T(1024)S(1)}, u32[]{:S(2)}, u32[]{:S(2)}) %collective-permute-start.9) | collective-permute-done | bytes 9264 | tf_op jit(solution)/shard_map/ppermute | solution.py:11
  70.4 2.6 %collective-permute-start.10 = (f32[2308]{0:T(1024)S(1)}, f32[2308]{0:T(1024)S(1)}, u32[]{:S(2)}, u32[]{:S(2)}) collective-permute-start(f32[2308]{0:T(1024)S(1)} %add.192), channel_id=1, source_target_pairs={{0,2},{1,3},{2,0},{3,1},{4,6},{5,7},{6,4},{7,5},{8,10},{9,11},{10,... | collective-permute-start | bytes 27704 | tf_op jit(solution)/shard_map/ppermute | solution.py:11
  73.8 1.2 %collective-permute-done.10 = f32[2308]{0:T(1024)S(1)} collective-permute-done((f32[2308]{0:T(1024)S(1)}, f32[2308]{0:T(1024)S(1)}, u32[]{:S(2)}, u32[]{:S(2)}) %collective-permute-start.10) | collective-permute-done | bytes 9264 | tf_op jit(solution)/shard_map/ppermute | solution.py:11
  (78 shorter events, 17.7 us)
Async XLA Ops:
  0.6 47.1 %copy-start = (s32[1,512]{1,0:T(1,128)S(1)}, s32[1,512]{1,0:T(1,128)}, u32[]{:S(2)}) copy-start(s32[1,512]{1,0:T(1,128)} %param.18) | copy-start | bytes 6148
  0.6 17.4 %copy-start.8 = (s32[16]{0:T(128)S(1)}, s32[16]{0:T(128)}, u32[]{:S(2)}) copy-start(s32[16]{0:T(128)} %constant.55.clone) | copy-start | bytes 196
  0.7 24.9 %copy-start.7 = (s32[16]{0:T(128)S(1)}, s32[16]{0:T(128)}, u32[]{:S(2)}) copy-start(s32[16]{0:T(128)} %constant.56.clone) | copy-start | bytes 196
  8.7 22.0 %copy-start.1 = (s32[1,8]{1,0:T(1,128)S(1)}, s32[1,8]{1,0:T(1,128)}, u32[]{:S(2)}) copy-start(s32[1,8]{1,0:T(1,128)} %param.19) | copy-start | bytes 100
  8.7 6.9 %collective-permute-start = (bf16[2,1,32,1152]{3,2,0,1:T(8,128)(2,1)S(1)}, bf16[2,1,32,1152]{3,2,0,1:T(8,128)(2,1)S(1)}, u32[]{:S(2)}, u32[]{:S(2)}) collective-permute-start(bf16[2,1,32,1152]{3,2,0,1:T(8,128)(2,1)S(1)} %get-tuple-element.15), channel_id=1, source_target_pairs={{0,8},{4,12},{8,0},{12,4},{16,24},{20,28},{24,16},{28,20},{1,9},{5... | collective-permute-start | bytes 442376 | tf_op jit(solution)/shard_map/ppermute | solution.py:11
  16.3 8.4 %collective-permute-start.1 = (bf16[2,2,32,1152]{3,2,0,1:T(8,128)(2,1)}, bf16[2,2,32,1152]{3,2,0,1:T(8,128)(2,1)S(1)}, u32[]{:S(2)}, u32[]{:S(2)}) collective-permute-start(bf16[2,2,32,1152]{3,2,0,1:T(8,128)(2,1)} %pad_maximum_fusion.2), channel_id=1, source_target_pairs={{0,16},{4,20},{8,24},{12,28},{16,0},{20,4},{24,8},{28,12},{1,17},{... | collective-permute-start | bytes 884744 | tf_op jit(solution)/shard_map/ppermute | solution.py:11
  25.6 2.3 %collective-permute-start.2 = (bf16[2,4,32,1152]{3,2,0,1:T(8,128)(2,1)}, bf16[2,4,32,1152]{3,2,0,1:T(8,128)(2,1)}, u32[]{:S(2)}, u32[]{:S(2)}) collective-permute-start(bf16[2,4,32,1152]{3,2,0,1:T(8,128)(2,1)} %pad_maximum_fusion), channel_id=1, source_target_pairs={{0,4},{4,0},{8,12},{12,8},{16,20},{20,16},{24,28},{28,24},{1,5},{5... | collective-permute-start | bytes 1769480 | tf_op jit(solution)/shard_map/ppermute | solution.py:11
  29.1 6.0 %collective-permute-start.3 = (bf16[2,1,32,1152]{3,2,0,1:T(8,128)(2,1)S(1)}, bf16[2,1,32,1152]{3,2,0,1:T(8,128)(2,1)S(1)}, u32[]{:S(2)}, u32[]{:S(2)}) collective-permute-start(bf16[2,1,32,1152]{3,2,0,1:T(8,128)(2,1)S(1)} %get-tuple-element.13), channel_id=1, source_target_pairs={{0,16},{4,20},{8,24},{12,28},{16,0},{20,4},{24,8},{28,12},{1,17},{... | collective-permute-start | bytes 442376 | tf_op jit(solution)/shard_map/ppermute | solution.py:11
  35.1 8.3 %collective-permute-start.4 = (bf16[2,2,32,1152]{3,2,0,1:T(8,128)(2,1)S(1)}, bf16[2,2,32,1152]{3,2,0,1:T(8,128)(2,1)S(1)}, u32[]{:S(2)}, u32[]{:S(2)}) collective-permute-start(bf16[2,2,32,1152]{3,2,0,1:T(8,128)(2,1)S(1)} %pad_maximum_fusion.3), channel_id=1, source_target_pairs={{0,8},{4,12},{8,0},{12,4},{16,24},{20,28},{24,16},{28,20},{1,9},{5... | collective-permute-start | bytes 884744 | tf_op jit(solution)/shard_map/ppermute | solution.py:11
  44.2 7.1 %collective-permute-start.5 = (bf16[2,4,32,1152]{3,2,0,1:T(8,128)(2,1)}, bf16[2,4,32,1152]{3,2,0,1:T(8,128)(2,1)}, u32[]{:S(2)}, u32[]{:S(2)}) collective-permute-start(bf16[2,4,32,1152]{3,2,0,1:T(8,128)(2,1)} %pad_maximum_fusion.1), channel_id=1, source_target_pairs={{0,4},{4,0},{8,12},{12,8},{16,20},{20,16},{24,28},{28,24},{1,5},{5... | collective-permute-start | bytes 1769480 | tf_op jit(solution)/shard_map/ppermute | solution.py:11
  52.5 2.4 %copy-start.2 = (bf16[1,64,1152]{2,1,0:T(8,128)(2,1)S(1)}, bf16[1,64,1152]{2,1,0:T(8,128)(2,1)}, u32[]{:S(2)}) copy-start(bf16[1,64,1152]{2,1,0:T(8,128)(2,1)} %param.11) | copy-start | bytes 442372
  52.5 2.4 %copy-start.5 = (f32[1152]{0:T(1024)S(1)}, f32[1152]{0:T(1024)}, u32[]{:S(2)}) copy-start(f32[1152]{0:T(1024)} %param.13) | copy-start | bytes 13828
  53.7 2.6 %copy-start.3 = (bf16[1,64,1152]{2,1,0:T(8,128)(2,1)S(1)}, bf16[1,64,1152]{2,1,0:T(8,128)(2,1)}, u32[]{:S(2)}) copy-start(bf16[1,64,1152]{2,1,0:T(8,128)(2,1)} %param.12) | copy-start | bytes 442372
  53.7 2.7 %copy-start.4 = (bf16[1,16,32,1152]{3,2,0,1:T(8,128)(2,1)S(1)}, bf16[1,16,32,1152]{3,2,0,1:T(8,128)(2,1)}, u32[]{:S(2)}) copy-start(bf16[1,16,32,1152]{3,2,0,1:T(8,128)(2,1)} %get-tuple-element.16) | copy-start | bytes 3538948
  53.7 2.7 %copy-start.6 = (f32[1152]{0:T(1024)S(1)}, f32[1152]{0:T(1024)}, u32[]{:S(2)}) copy-start(f32[1152]{0:T(1024)} %param.14) | copy-start | bytes 13828
  57.8 1.4 %collective-permute-start.6 = (f32[2308]{0:T(1024)S(1)}, f32[2308]{0:T(1024)S(1)}, u32[]{:S(2)}, u32[]{:S(2)}) collective-permute-start(f32[2308]{0:T(1024)S(1)} %pad_maximum_fusion.5), channel_id=1, source_target_pairs={{0,4},{4,0},{8,12},{12,8},{16,20},{20,16},{24,28},{28,24},{1,5},{5... | collective-permute-start | bytes 27704 | tf_op jit(solution)/shard_map/ppermute | solution.py:11
  59.2 3.8 %collective-permute-start.7 = (f32[2308]{0:T(1024)S(1)}, f32[2308]{0:T(1024)S(1)}, u32[]{:S(2)}, u32[]{:S(2)}) collective-permute-start(f32[2308]{0:T(1024)S(1)} %fusion.115), channel_id=1, source_target_pairs={{0,8},{4,12},{8,0},{12,4},{16,24},{20,28},{24,16},{28,20},{1,9},{5... | collective-permute-start | bytes 27704 | tf_op jit(solution)/shard_map/ppermute | solution.py:11
  63.0 3.7 %collective-permute-start.8 = (f32[2308]{0:T(1024)S(1)}, f32[2308]{0:T(1024)S(1)}, u32[]{:S(2)}, u32[]{:S(2)}) collective-permute-start(f32[2308]{0:T(1024)S(1)} %add.190), channel_id=1, source_target_pairs={{0,16},{4,20},{8,24},{12,28},{16,0},{20,4},{24,8},{28,12},{1,17},{... | collective-permute-start | bytes 27704 | tf_op jit(solution)/shard_map/ppermute | solution.py:11
  66.7 3.7 %collective-permute-start.9 = (f32[2308]{0:T(1024)S(1)}, f32[2308]{0:T(1024)S(1)}, u32[]{:S(2)}, u32[]{:S(2)}) collective-permute-start(f32[2308]{0:T(1024)S(1)} %add.191), channel_id=1, source_target_pairs={{0,1},{1,0},{2,3},{3,2},{4,5},{5,4},{6,7},{7,6},{8,9},{9,8},{10,11... | collective-permute-start | bytes 27704 | tf_op jit(solution)/shard_map/ppermute | solution.py:11
  70.4 4.6 %collective-permute-start.10 = (f32[2308]{0:T(1024)S(1)}, f32[2308]{0:T(1024)S(1)}, u32[]{:S(2)}, u32[]{:S(2)}) collective-permute-start(f32[2308]{0:T(1024)S(1)} %add.192), channel_id=1, source_target_pairs={{0,2},{1,3},{2,0},{3,1},{4,6},{5,7},{6,4},{7,5},{8,10},{9,11},{10,... | collective-permute-start | bytes 27704 | tf_op jit(solution)/shard_map/ppermute | solution.py:11

commit v3 on v2

--- a/solution.py
+++ b/solution.py
@@ -23,20 +23,17 @@
         return gathered, list(range(count)), [0] * count, True
     chip_bits = [1 << b for b in range(1, count.bit_length() - 1)]
     half = rows // 2
-    halves = [
-        [both[:, None, :half], [0], chip_bits],
-        [both[:, None, half:], [0], chip_bits[::-1]],
-    ]
-    for step in range(len(chip_bits)):
-        for held in halves:
-            bit = held[2][step]
-            held[0] = jnp.concatenate([held[0], xor_swap(held[0], axis, bit)], axis=1)
-            held[1] = held[1] + [mask ^ bit for mask in held[1]]
-    for held in halves:
-        held[0] = jnp.concatenate([held[0], xor_swap(held[0], axis, 1)], axis=1)
-        held[1] = held[1] + [mask ^ 1 for mask in held[1]]
-    gathered = jnp.concatenate([halves[0][0], halves[1][0]], axis=1)
-    masks = halves[0][1] + halves[1][1]
+    orders = (chip_bits + [1], chip_bits[::-1] + [1])
+    pieces = ([both[:, :half]], [both[:, half:]])
+    held = ([0], [0])
+    for step in range(len(chip_bits) + 1):
+        sent = [xor_swap(tuple(pieces[h]), axis, orders[h][step]) for h in range(2)]
+        for h in range(2):
+            bit = orders[h][step]
+            pieces[h].extend(sent[h])
+            held[h].extend([mask ^ bit for mask in held[h]])
+    gathered = jnp.stack(pieces[0] + pieces[1], axis=1)
+    masks = held[0] + held[1]
     offsets = [0] * count + [half] * count
     return gathered, masks, offsets, False
 

time: 76.6 us -> 67.6 us (0.88)
  waiting for transfers between devices: 29.6 us -> 23.1 us
  local copies, waits for them, and re-layouts: 9.86 us -> 7.8 us
  matrix products: 2.73 us -> 4.02 us
  other arithmetic: 14.2 us -> 13 us
    ppermute x11 -> x19, waiting for transfers between devices: 29.6 us -> 23.1 us  [xor_swap(): lax.ppermute(value, axis, [(source, source ^ bit) for source in range(cou...]
    concatenate x4 -> x0, other arithmetic: 2.53 us -> none  [gather_blocks(): held[0] = jnp.concatenate([held[0], xor_swap(held[0], axis, bit)], axis=1)]
    dot_general x1, matrix products: 0.46 us -> 1.74 us  [shards(): jnp.dot(row_weights, text_all, preferred_element_type=jnp.float32)]
    concatenate x1 -> x0, local copies, waits for them, and re-layouts: 1.13 us -> none  [gather_blocks(): gathered = jnp.concatenate([halves[0][0], halves[1][0]], axis=1)]
    unnamed x23 -> x31, local copies, waits for them, and re-layouts: 1.28 us -> 0.29 us
    ppermute x11 -> x19, starting transfers between devices: 15.6 us -> 14.9 us  [xor_swap(): lax.ppermute(value, axis, [(source, source ^ bit) for source in range(cou...]
  transfers between devices with their start and end apart: 11 -> 19, of which waited for: 10 -> 10; matrix products, arithmetic and copies ran while one was open for 11% -> 14% of each run, Pallas kernels for 0% -> 0%
where the time goes in v3:
time: 67.6 us; the launch traced here: 67.2 us
  waiting for transfers between devices  23.1 us (34%)
  starting transfers between devices  14.9 us (22%)
  other arithmetic  13 us (19%)
  local copies, waits for them, and re-layouts  7.8 us (12%)
  between operations  4.34 us (6%)
  matrix products  4.02 us (6%)
    ppermute x19, waiting for transfers between devices, xor_swap(): lax.ppermute(value, axis, [(source, source ^ bit) for source in range(cou...  23.1 us
    ppermute x19, starting transfers between devices, xor_swap(): lax.ppermute(value, axis, [(source, source ^ bit) for source in range(cou...  14.9 us
    gather x1, local copies, waits for them, and re-layouts, shards(): held_partner = partner[rows]  3.51 us
    reduce_sum x2, other arithmetic, embed_rows(): jnp.sum(scaled * scaled, axis=-1, keepdims=True) + epsilon  2.29 us
    reduce_sum x2, other arithmetic, embed_rows(): jnp.mean(centred * centred, axis=-1, keepdims=True) + epsilon  2.24 us
    reduce_sum x2, other arithmetic, embed_rows(): centred = values - jnp.mean(values, axis=-1, keepdims=True)  2.08 us
    dot_general x1, matrix products, shards(): jnp.dot(row_weights, text_all, preferred_element_type=jnp.float32)  1.74 us
  transfers between devices with their start and end apart: 19, of which 10 were waited for; matrix products, arithmetic and copies ran while one was open for 14% of the time, Pallas kernels for 0%

profile of v3, /device:TPU:0, one launch (start us, length us, event | category | flops | bytes accessed | tf_op | source)
XLA Modules:
  0.0 67.2 jit_solution(8562545840522709060)
XLA Ops:
  1.7 1.1 %fusion.61 = f32[64]{0:T(128)S(1)} fusion(bf16[1,64,1152]{2,1,0:T(8,128)(2,1)} %param.12, f32[64]{0:T(128)S(1)} %broadcast_multiply_fusion.4), kind=kLoop, calls=%fused_computation.74 | loop fusion | flops 294848 | bytes 147968 | tf_op jit(solution)/shard_map/reduce_sum | solution.py:57
  2.9 1.1 %fusion.55 = f32[64]{0:T(128)S(1)} fusion(bf16[1,64,1152]{2,1,0:T(8,128)(2,1)} %param.12, f32[1152]{0:T(1024)} %param.14, f32[64]{0:T(128)S(1)} %add_rsqrt_fusion.1, f32[64]{0:T(128)S(1)} %broadcast_multiply_fusion.4), kind=kLoop, calls=%fused_computation.68 | loop fusion | flops 442304 | bytes 152832 | tf_op jit(solution)/shard_map/reduce_sum | solution.py:60
  5.1 1.1 %fusion.36 = f32[64]{0:T(128)S(1)} fusion(bf16[1,64,1152]{2,1,0:T(8,128)(2,1)} %param.11, f32[64]{0:T(128)S(1)} %broadcast_multiply_fusion.5), kind=kLoop, calls=%fused_computation.49 | loop fusion | flops 294848 | bytes 147968 | tf_op jit(solution)/shard_map/reduce_sum | solution.py:57
  6.2 1.1 %fusion.30 = f32[64]{0:T(128)S(1)} fusion(bf16[1,64,1152]{2,1,0:T(8,128)(2,1)} %param.11, f32[1152]{0:T(1024)} %param.13, f32[64]{0:T(128)S(1)} %add_rsqrt_fusion.3, f32[64]{0:T(128)S(1)} %broadcast_multiply_fusion.5), kind=kLoop, calls=%fused_computation.43 | loop fusion | flops 442304 | bytes 152832 | tf_op jit(solution)/shard_map/reduce_sum | solution.py:60
  7.4 1.3 %fusion.15 = (bf16[1,64,1152]{2,1,0:T(8,128)(2,1)S(1)}, bf16[1,64,1152]{2,1,0:T(8,128)(2,1)S(1)}) fusion(bf16[1,64,1152]{2,1,0:T(8,128)(2,1)} %param.11, f32[64]{0:T(128)S(1)} %add_rsqrt_fusion.2, f32[1152]{0:T(1024)} %param.13, f32[64]{0:T(128)S(1)} %add_rsqrt_fusion.3, f32[64]{0:T(128)S(1)} %broadcast_multiply_fusion.5, f32[64]{0:T(128)S(1)} %add_rsqrt_fusion, ...), kind=kLoop, calls=%fused_computation.28 | loop fusion | flops 884736 | bytes 600576 | tf_op jit(solution)/shard_map/convert_element_type | solution.py:106
  8.7 3.0 %collective-permute-start = (bf16[2,32,1152]{2,1,0:T(8,128)(2,1)S(1)}, bf16[2,32,1152]{2,1,0:T(8,128)(2,1)S(1)}, u32[]{:S(2)}, u32[]{:S(2)}) collective-permute-start(bf16[2,32,1152]{2,1,0:T(8,128)(2,1)S(1)} %get-tuple-element.15), channel_id=1, source_target_pairs={{0,8},{4,12},{8,0},{12,4},{16,24},{20,28},{24,16},{28,20},{1,9},{5... | collective-permute-start | bytes 442376 | tf_op jit(solution)/shard_map/ppermute | solution.py:11
  11.7 1.5 %collective-permute-start.1 = (bf16[2,32,1152]{2,1,0:T(8,128)(2,1)S(1)}, bf16[2,32,1152]{2,1,0:T(8,128)(2,1)S(1)}, u32[]{:S(2)}, u32[]{:S(2)}) collective-permute-start(bf16[2,32,1152]{2,1,0:T(8,128)(2,1)S(1)} %get-tuple-element.15), channel_id=1, source_target_pairs={{0,16},{4,20},{8,24},{12,28},{16,0},{20,4},{24,8},{28,12},{1,17},{... | collective-permute-start | bytes 442376 | tf_op jit(solution)/shard_map/ppermute | solution.py:11
  18.0 5.1 %collective-permute-done.2 = bf16[2,32,1152]{2,1,0:T(8,128)(2,1)S(1)} collective-permute-done((bf16[2,32,1152]{2,1,0:T(8,128)(2,1)S(1)}, bf16[2,32,1152]{2,1,0:T(8,128)(2,1)S(1)}, u32[]{:S(2)}, u32[]{:S(2)}) %collective-permute-start.2) | collective-permute-done | bytes 147488 | tf_op jit(solution)/shard_map/ppermute | solution.py:11
  23.2 1.2 %collective-permute-done.6 = bf16[2,32,1152]{2,1,0:T(8,128)(2,1)S(1)} collective-permute-done((bf16[2,32,1152]{2,1,0:T(8,128)(2,1)S(1)}, bf16[2,32,1152]{2,1,0:T(8,128)(2,1)S(1)}, u32[]{:S(2)}, u32[]{:S(2)}) %collective-permute-start.6) | collective-permute-done | bytes 147488 | tf_op jit(solution)/shard_map/ppermute | solution.py:11
  28.5 3.5 %gather_fusion.1 = s32[512]{0:T(512)S(1)} fusion(s32[512]{0:T(512)S(1)} %bitcast.160, s32[1024]{0:T(1024)S(1)} %get-tuple-element.28), kind=kCustom, calls=%fused_computation.1 | custom fusion | bytes 6144 | tf_op jit(solution)/shard_map/gather | solution.py:132
  32.6 1.6 %collective-permute-start.9 = (bf16[2,32,1152]{2,1,0:T(8,128)(2,1)S(1)}, bf16[2,32,1152]{2,1,0:T(8,128)(2,1)S(1)}, u32[]{:S(2)}, u32[]{:S(2)}) collective-permute-start(bf16[2,32,1152]{2,1,0:T(8,128)(2,1)S(1)} %collective-permute-done.7), channel_id=1, source_target_pairs={{0,8},{4,12},{8,0},{12,4},{16,24},{20,28},{24,16},{28,20},{1,9},{5... | collective-permute-start | bytes 442376 | tf_op jit(solution)/shard_map/ppermute | solution.py:11
  34.4 4.4 %collective-permute-done.8 = bf16[2,32,1152]{2,1,0:T(8,128)(2,1)S(1)} collective-permute-done((bf16[2,32,1152]{2,1,0:T(8,128)(2,1)S(1)}, bf16[2,32,1152]{2,1,0:T(8,128)(2,1)S(1)}, u32[]{:S(2)}, u32[]{:S(2)}) %collective-permute-start.8) | collective-permute-done | bytes 147488 | tf_op jit(solution)/shard_map/ppermute | solution.py:11
  38.9 2.0 %collective-permute-done.9 = bf16[2,32,1152]{2,1,0:T(8,128)(2,1)S(1)} collective-permute-done((bf16[2,32,1152]{2,1,0:T(8,128)(2,1)S(1)}, bf16[2,32,1152]{2,1,0:T(8,128)(2,1)S(1)}, u32[]{:S(2)}, u32[]{:S(2)}) %collective-permute-start.9) | collective-permute-done | bytes 147488 | tf_op jit(solution)/shard_map/ppermute | solution.py:11
  41.1 1.2 %collective-permute-done.13 = bf16[2,32,1152]{2,1,0:T(8,128)(2,1)S(1)} collective-permute-done((bf16[2,32,1152]{2,1,0:T(8,128)(2,1)S(1)}, bf16[2,32,1152]{2,1,0:T(8,128)(2,1)S(1)}, u32[]{:S(2)}, u32[]{:S(2)}) %collective-permute-start.13) | collective-permute-done | bytes 147488 | tf_op jit(solution)/shard_map/ppermute | solution.py:11
  42.3 1.2 %fusion.105 = (bf16[1,16,32,1152]{3,2,0,1:T(8,128)(2,1)}, bf16[1,16,32,1152]{3,2,0,1:T(8,128)(2,1)S(1)}) fusion(bf16[2,16,32,1152]{3,2,0,1:T(8,128)(2,1)S(1)} %bitcast_dynamic-update-slice_fusion), kind=kLoop, calls=%fused_computation.159 | loop fusion | bytes 4718592 | tf_op jit(solution)/shard_map/slice | solution.py:119
  43.6 1.2 %fusion.74 = (f32[]{:T(128)}, f32[64,512]{1,0:T(8,128)S(1)}) fusion(pred[512]{0:T(512)(128)(4,1)S(1)} %lt.65, pred[64]{0:T(512)(128)(4,1)S(1)} %iota_compare_fusion, f32[]{:T(128)} %bitcast.157, bf16[512,1152]{1,0:T(8,128)(2,1)S(1)} %bitcast.163, bf16[1,64,1152]{2,1,0:T(8,128)(2,1)S(1)} %get-tuple-element.26, f32[]{:T(128)} %bitcast, s32[512]{0:T(512)S(1)} %add.172, ...), kind=kOutput, calls=%fused_computation.109 | convolution fusion | flops 75988992 | bytes 1461068 | tf_op jit(solution)/shard_map/dot_general | solution.py:134
  45.4 1.7 %fusion.27 = (f32[64]{0:T(128)S(1)}, f32[64,1152]{1,0:T(8,128)S(1)}) fusion(bf16[1,64,1152]{2,1,0:T(8,128)(2,1)S(1)} %copy-done.3, f32[64]{0:T(128)S(1)} %add_rsqrt_fusion.2, f32[1152]{0:T(1024)S(1)} %copy-done.7, f32[64]{0:T(128)S(1)} %add_rsqrt_fusion.3, f32[64]{0:T(128)S(1)} %broadcast_multiply_fusion.5, bf16[512,1152]{1,0:T(8,128)(2,1)} %bitcast.164, ...), kind=kOutput, calls=%fused_computation.40 | convolution fusion | flops 76447680 | bytes 1761608 | tf_op jit(solution)/shard_map/dot_general | solution.py:143
  51.5 2.5 %collective-permute-done.15 = f32[2308]{0:T(1024)S(1)} collective-permute-done((f32[2308]{0:T(1024)S(1)}, f32[2308]{0:T(1024)S(1)}, u32[]{:S(2)}, u32[]{:S(2)}) %collective-permute-start.15) | collective-permute-done | bytes 9264 | tf_op jit(solution)/shard_map/ppermute | solution.py:11
  54.0 1.5 %collective-permute-start.16 = (f32[2308]{0:T(1024)S(1)}, f32[2308]{0:T(1024)S(1)}, u32[]{:S(2)}, u32[]{:S(2)}) collective-permute-start(f32[2308]{0:T(1024)S(1)} %add.190), channel_id=1, source_target_pairs={{0,16},{4,20},{8,24},{12,28},{16,0},{20,4},{24,8},{28,12},{1,17},{... | collective-permute-start | bytes 27704 | tf_op jit(solution)/shard_map/ppermute | solution.py:11
  55.5 2.2 %collective-permute-done.16 = f32[2308]{0:T(1024)S(1)} collective-permute-done((f32[2308]{0:T(1024)S(1)}, f32[2308]{0:T(1024)S(1)}, u32[]{:S(2)}, u32[]{:S(2)}) %collective-permute-start.16) | collective-permute-done | bytes 9264 | tf_op jit(solution)/shard_map/ppermute | solution.py:11
  57.7 1.6 %collective-permute-start.17 = (f32[2308]{0:T(1024)S(1)}, f32[2308]{0:T(1024)S(1)}, u32[]{:S(2)}, u32[]{:S(2)}) collective-permute-start(f32[2308]{0:T(1024)S(1)} %add.191), channel_id=1, source_target_pairs={{0,1},{1,0},{2,3},{3,2},{4,5},{5,4},{6,7},{7,6},{8,9},{9,8},{10,11... | collective-permute-start | bytes 27704 | tf_op jit(solution)/shard_map/ppermute | solution.py:11
  59.3 2.1 %collective-permute-done.17 = f32[2308]{0:T(1024)S(1)} collective-permute-done((f32[2308]{0:T(1024)S(1)}, f32[2308]{0:T(1024)S(1)}, u32[]{:S(2)}, u32[]{:S(2)}) %collective-permute-start.17) | collective-permute-done | bytes 9264 | tf_op jit(solution)/shard_map/ppermute | solution.py:11
  61.4 2.6 %collective-permute-start.18 = (f32[2308]{0:T(1024)S(1)}, f32[2308]{0:T(1024)S(1)}, u32[]{:S(2)}, u32[]{:S(2)}) collective-permute-start(f32[2308]{0:T(1024)S(1)} %add.192), channel_id=1, source_target_pairs={{0,2},{1,3},{2,0},{3,1},{4,6},{5,7},{6,4},{7,5},{8,10},{9,11},{10,... | collective-permute-start | bytes 27704 | tf_op jit(solution)/shard_map/ppermute | solution.py:11
  64.8 1.2 %collective-permute-done.18 = f32[2308]{0:T(1024)S(1)} collective-permute-done((f32[2308]{0:T(1024)S(1)}, f32[2308]{0:T(1024)S(1)}, u32[]{:S(2)}, u32[]{:S(2)}) %collective-permute-start.18) | collective-permute-done | bytes 9264 | tf_op jit(solution)/shard_map/ppermute | solution.py:11
  (98 shorter events, 15.5 us)
Async XLA Ops:
  0.6 27.9 %copy-start = (s32[1,512]{1,0:T(1,128)S(1)}, s32[1,512]{1,0:T(1,128)}, u32[]{:S(2)}) copy-start(s32[1,512]{1,0:T(1,128)} %param.18) | copy-start | bytes 6148
  0.6 14.7 %copy-start.8 = (s32[16]{0:T(128)S(1)}, s32[16]{0:T(128)}, u32[]{:S(2)}) copy-start(s32[16]{0:T(128)} %constant.56.clone) | copy-start | bytes 196
  0.7 14.1 %copy-start.1 = (s32[1,8]{1,0:T(1,128)S(1)}, s32[1,8]{1,0:T(1,128)}, u32[]{:S(2)}) copy-start(s32[1,8]{1,0:T(1,128)} %param.19) | copy-start | bytes 100
  8.7 8.0 %collective-permute-start = (bf16[2,32,1152]{2,1,0:T(8,128)(2,1)S(1)}, bf16[2,32,1152]{2,1,0:T(8,128)(2,1)S(1)}, u32[]{:S(2)}, u32[]{:S(2)}) collective-permute-start(bf16[2,32,1152]{2,1,0:T(8,128)(2,1)S(1)} %get-tuple-element.15), channel_id=1, source_target_pairs={{0,8},{4,12},{8,0},{12,4},{16,24},{20,28},{24,16},{28,20},{1,9},{5... | collective-permute-start | bytes 442376 | tf_op jit(solution)/shard_map/ppermute | solution.py:11
  11.7 5.8 %collective-permute-start.1 = (bf16[2,32,1152]{2,1,0:T(8,128)(2,1)S(1)}, bf16[2,32,1152]{2,1,0:T(8,128)(2,1)S(1)}, u32[]{:S(2)}, u32[]{:S(2)}) collective-permute-start(bf16[2,32,1152]{2,1,0:T(8,128)(2,1)S(1)} %get-tuple-element.15), channel_id=1, source_target_pairs={{0,16},{4,20},{8,24},{12,28},{16,0},{20,4},{24,8},{28,12},{1,17},{... | collective-permute-start | bytes 442376 | tf_op jit(solution)/shard_map/ppermute | solution.py:11
  13.2 9.8 %collective-permute-start.3 = (bf16[2,32,1152]{2,1,0:T(8,128)(2,1)S(1)}, bf16[2,32,1152]{2,1,0:T(8,128)(2,1)S(1)}, u32[]{:S(2)}, u32[]{:S(2)}) collective-permute-start(bf16[2,32,1152]{2,1,0:T(8,128)(2,1)S(1)} %get-tuple-element.15), channel_id=1, source_target_pairs={{0,4},{4,0},{8,12},{12,8},{16,20},{20,16},{24,28},{28,24},{1,5},{5... | collective-permute-start | bytes 442376 | tf_op jit(solution)/shard_map/ppermute | solution.py:11
  16.7 6.3 %collective-permute-start.2 = (bf16[2,32,1152]{2,1,0:T(8,128)(2,1)S(1)}, bf16[2,32,1152]{2,1,0:T(8,128)(2,1)S(1)}, u32[]{:S(2)}, u32[]{:S(2)}) collective-permute-start(bf16[2,32,1152]{2,1,0:T(8,128)(2,1)S(1)} %collective-permute-done), channel_id=1, source_target_pairs={{0,16},{4,20},{8,24},{12,28},{16,0},{20,4},{24,8},{28,12},{1,17},{... | collective-permute-start | bytes 442376 | tf_op jit(solution)/shard_map/ppermute | solution.py:11
  17.3 5.8 %collective-permute-start.4 = (bf16[2,32,1152]{2,1,0:T(8,128)(2,1)S(1)}, bf16[2,32,1152]{2,1,0:T(8,128)(2,1)S(1)}, u32[]{:S(2)}, u32[]{:S(2)}) collective-permute-start(bf16[2,32,1152]{2,1,0:T(8,128)(2,1)S(1)} %collective-permute-done), channel_id=1, source_target_pairs={{0,4},{4,0},{8,12},{12,8},{16,20},{20,16},{24,28},{28,24},{1,5},{5... | collective-permute-start | bytes 442376 | tf_op jit(solution)/shard_map/ppermute | solution.py:11
  17.6 5.6 %collective-permute-start.5 = (bf16[2,32,1152]{2,1,0:T(8,128)(2,1)S(1)}, bf16[2,32,1152]{2,1,0:T(8,128)(2,1)S(1)}, u32[]{:S(2)}, u32[]{:S(2)}) collective-permute-start(bf16[2,32,1152]{2,1,0:T(8,128)(2,1)S(1)} %collective-permute-done.1), channel_id=1, source_target_pairs={{0,4},{4,0},{8,12},{12,8},{16,20},{20,16},{24,28},{28,24},{1,5},{5... | collective-permute-start | bytes 442376 | tf_op jit(solution)/shard_map/ppermute | solution.py:11
  23.1 1.4 %collective-permute-start.6 = (bf16[2,32,1152]{2,1,0:T(8,128)(2,1)S(1)}, bf16[2,32,1152]{2,1,0:T(8,128)(2,1)S(1)}, u32[]{:S(2)}, u32[]{:S(2)}) collective-permute-start(bf16[2,32,1152]{2,1,0:T(8,128)(2,1)S(1)} %collective-permute-done.2), channel_id=1, source_target_pairs={{0,4},{4,0},{8,12},{12,8},{16,20},{20,16},{24,28},{28,24},{1,5},{5... | collective-permute-start | bytes 442376 | tf_op jit(solution)/shard_map/ppermute | solution.py:11
  24.5 8.1 %collective-permute-start.7 = (bf16[2,32,1152]{2,1,0:T(8,128)(2,1)S(1)}, bf16[2,32,1152]{2,1,0:T(8,128)(2,1)S(1)}, u32[]{:S(2)}, u32[]{:S(2)}) collective-permute-start(bf16[2,32,1152]{2,1,0:T(8,128)(2,1)S(1)} %get-tuple-element.13), channel_id=1, source_target_pairs={{0,16},{4,20},{8,24},{12,28},{16,0},{20,4},{24,8},{28,12},{1,17},{... | collective-permute-start | bytes 442376 | tf_op jit(solution)/shard_map/ppermute | solution.py:11
  32.1 6.7 %collective-permute-start.8 = (bf16[2,32,1152]{2,1,0:T(8,128)(2,1)S(1)}, bf16[2,32,1152]{2,1,0:T(8,128)(2,1)S(1)}, u32[]{:S(2)}, u32[]{:S(2)}) collective-permute-start(bf16[2,32,1152]{2,1,0:T(8,128)(2,1)S(1)} %get-tuple-element.13), channel_id=1, source_target_pairs={{0,8},{4,12},{8,0},{12,4},{16,24},{20,28},{24,16},{28,20},{1,9},{5... | collective-permute-start | bytes 442376 | tf_op jit(solution)/shard_map/ppermute | solution.py:11
  32.6 8.4 %collective-permute-start.10 = (bf16[2,32,1152]{2,1,0:T(8,128)(2,1)S(1)}, bf16[2,32,1152]{2,1,0:T(8,128)(2,1)S(1)}, u32[]{:S(2)}, u32[]{:S(2)}) collective-permute-start(bf16[2,32,1152]{2,1,0:T(8,128)(2,1)S(1)} %get-tuple-element.13), channel_id=1, source_target_pairs={{0,4},{4,0},{8,12},{12,8},{16,20},{20,16},{24,28},{28,24},{1,5},{5... | collective-permute-start | bytes 442376 | tf_op jit(solution)/shard_map/ppermute | solution.py:11
  32.6 8.4 %collective-permute-start.9 = (bf16[2,32,1152]{2,1,0:T(8,128)(2,1)S(1)}, bf16[2,32,1152]{2,1,0:T(8,128)(2,1)S(1)}, u32[]{:S(2)}, u32[]{:S(2)}) collective-permute-start(bf16[2,32,1152]{2,1,0:T(8,128)(2,1)S(1)} %collective-permute-done.7), channel_id=1, source_target_pairs={{0,8},{4,12},{8,0},{12,4},{16,24},{20,28},{24,16},{28,20},{1,9},{5... | collective-permute-start | bytes 442376 | tf_op jit(solution)/shard_map/ppermute | solution.py:11
  34.2 6.8 %collective-permute-start.11 = (bf16[2,32,1152]{2,1,0:T(8,128)(2,1)S(1)}, bf16[2,32,1152]{2,1,0:T(8,128)(2,1)S(1)}, u32[]{:S(2)}, u32[]{:S(2)}) collective-permute-start(bf16[2,32,1152]{2,1,0:T(8,128)(2,1)S(1)} %collective-permute-done.7), channel_id=1, source_target_pairs={{0,4},{4,0},{8,12},{12,8},{16,20},{20,16},{24,28},{28,24},{1,5},{5... | collective-permute-start | bytes 442376 | tf_op jit(solution)/shard_map/ppermute | solution.py:11
  38.9 2.2 %collective-permute-start.12 = (bf16[2,32,1152]{2,1,0:T(8,128)(2,1)S(1)}, bf16[2,32,1152]{2,1,0:T(8,128)(2,1)S(1)}, u32[]{:S(2)}, u32[]{:S(2)}) collective-permute-start(bf16[2,32,1152]{2,1,0:T(8,128)(2,1)S(1)} %collective-permute-done.8), channel_id=1, source_target_pairs={{0,4},{4,0},{8,12},{12,8},{16,20},{20,16},{24,28},{28,24},{1,5},{5... | collective-permute-start | bytes 442376 | tf_op jit(solution)/shard_map/ppermute | solution.py:11
  40.9 1.4 %collective-permute-start.13 = (bf16[2,32,1152]{2,1,0:T(8,128)(2,1)S(1)}, bf16[2,32,1152]{2,1,0:T(8,128)(2,1)S(1)}, u32[]{:S(2)}, u32[]{:S(2)}) collective-permute-start(bf16[2,32,1152]{2,1,0:T(8,128)(2,1)S(1)} %collective-permute-done.9), channel_id=1, source_target_pairs={{0,4},{4,0},{8,12},{12,8},{16,20},{20,16},{24,28},{28,24},{1,5},{5... | collective-permute-start | bytes 442376 | tf_op jit(solution)/shard_map/ppermute | solution.py:11
  43.6 3.6 %copy-start.4 = (bf16[1,16,32,1152]{3,2,0,1:T(8,128)(2,1)S(1)}, bf16[1,16,32,1152]{3,2,0,1:T(8,128)(2,1)}, u32[]{:S(2)}) copy-start(bf16[1,16,32,1152]{3,2,0,1:T(8,128)(2,1)} %get-tuple-element.16) | copy-start | bytes 3538948
  43.6 3.6 %copy-start.6 = (f32[1152]{0:T(1024)S(1)}, f32[1152]{0:T(1024)}, u32[]{:S(2)}) copy-start(f32[1152]{0:T(1024)} %param.14) | copy-start | bytes 13828
  49.0 1.2 %collective-permute-start.14 = (f32[2308]{0:T(1024)S(1)}, f32[2308]{0:T(1024)S(1)}, u32[]{:S(2)}, u32[]{:S(2)}) collective-permute-start(f32[2308]{0:T(1024)S(1)} %pad_maximum_fusion.1), channel_id=1, source_target_pairs={{0,4},{4,0},{8,12},{12,8},{16,20},{20,16},{24,28},{28,24},{1,5},{5... | collective-permute-start | bytes 27704 | tf_op jit(solution)/shard_map/ppermute | solution.py:11
  50.2 3.8 %collective-permute-start.15 = (f32[2308]{0:T(1024)S(1)}, f32[2308]{0:T(1024)S(1)}, u32[]{:S(2)}, u32[]{:S(2)}) collective-permute-start(f32[2308]{0:T(1024)S(1)} %fusion.112), channel_id=1, source_target_pairs={{0,8},{4,12},{8,0},{12,4},{16,24},{20,28},{24,16},{28,20},{1,9},{5... | collective-permute-start | bytes 27704 | tf_op jit(solution)/shard_map/ppermute | solution.py:11
  54.0 3.7 %collective-permute-start.16 = (f32[2308]{0:T(1024)S(1)}, f32[2308]{0:T(1024)S(1)}, u32[]{:S(2)}, u32[]{:S(2)}) collective-permute-start(f32[2308]{0:T(1024)S(1)} %add.190), channel_id=1, source_target_pairs={{0,16},{4,20},{8,24},{12,28},{16,0},{20,4},{24,8},{28,12},{1,17},{... | collective-permute-start | bytes 27704 | tf_op jit(solution)/shard_map/ppermute | solution.py:11
  57.7 3.7 %collective-permute-start.17 = (f32[2308]{0:T(1024)S(1)}, f32[2308]{0:T(1024)S(1)}, u32[]{:S(2)}, u32[]{:S(2)}) collective-permute-start(f32[2308]{0:T(1024)S(1)} %add.191), channel_id=1, source_target_pairs={{0,1},{1,0},{2,3},{3,2},{4,5},{5,4},{6,7},{7,6},{8,9},{9,8},{10,11... | collective-permute-start | bytes 27704 | tf_op jit(solution)/shard_map/ppermute | solution.py:11
  61.4 4.6 %collective-permute-start.18 = (f32[2308]{0:T(1024)S(1)}, f32[2308]{0:T(1024)S(1)}, u32[]{:S(2)}, u32[]{:S(2)}) collective-permute-start(f32[2308]{0:T(1024)S(1)} %add.192), channel_id=1, source_target_pairs={{0,2},{1,3},{2,0},{3,1},{4,6},{5,7},{6,4},{7,5},{8,10},{9,11},{10,... | collective-permute-start | bytes 27704 | tf_op jit(solution)/shard_map/ppermute | solution.py:11
  (4 other events, 11.0 us)

commit v4 on v3

--- a/solution.py
+++ b/solution.py
@@ -23,17 +23,28 @@
         return gathered, list(range(count)), [0] * count, True
     chip_bits = [1 << b for b in range(1, count.bit_length() - 1)]
     half = rows // 2
-    orders = (chip_bits + [1], chip_bits[::-1] + [1])
-    pieces = ([both[:, :half]], [both[:, half:]])
-    held = ([0], [0])
+    orders = (chip_bits, chip_bits[::-1])
+    routed = ([both[:, :half]], [both[:, half:]])
+    routed_masks = ([0], [0])
+    fresh = ([0], [0])
+    shared = ([], [])
+    shared_masks = ([], [])
     for step in range(len(chip_bits) + 1):
-        sent = [xor_swap(tuple(pieces[h]), axis, orders[h][step]) for h in range(2)]
+        last = step == len(chip_bits)
+        sent = [None, None]
+        if not last:
+            sent = [xor_swap(tuple(routed[h]), axis, orders[h][step]) for h in range(2)]
+        across = [xor_swap(tuple(routed[h][i] for i in fresh[h]), axis, 1) for h in range(2)]
         for h in range(2):
-            bit = orders[h][step]
-            pieces[h].extend(sent[h])
-            held[h].extend([mask ^ bit for mask in held[h]])
-    gathered = jnp.stack(pieces[0] + pieces[1], axis=1)
-    masks = held[0] + held[1]
+            shared[h].extend(across[h])
+            shared_masks[h].extend([routed_masks[h][i] ^ 1 for i in fresh[h]])
+            if not last:
+                bit = orders[h][step]
+                fresh[h][:] = list(range(len(routed[h]), 2 * len(routed[h])))
+                routed[h].extend(sent[h])
+                routed_masks[h].extend([mask ^ bit for mask in routed_masks[h]])
+    gathered = jnp.stack(routed[0] + shared[0] + routed[1] + shared[1], axis=1)
+    masks = routed_masks[0] + shared_masks[0] + routed_masks[1] + shared_masks[1]
     offsets = [0] * count + [half] * count
     return gathered, masks, offsets, False
 
@@ -129,7 +140,11 @@
     real_own = own_rows < lax.dynamic_index_in_dim(block_counts, own_block, keepdims=False)
     own_start = own_block * block_rows
     own_partner = lax.dynamic_slice_in_dim(partner, own_start, block_rows)
-    held_partner = partner[rows]
+    own_texts = own_start + own_rows
+    matched_image = jnp.sum(
+        jnp.where(partner[:, None] == own_texts[None, :], jnp.arange(partner.shape[0], dtype=jnp.int32)[:, None], 0),
+        axis=0,
+    )
 
     row_scores = lax.dot_general(
         picture_feature_entries, text_all, (((1,), (1,)), ((), ())),
@@ -146,7 +161,7 @@
         image_all, caption_feature_entries, (((1,), (1,)), ((), ())),
         preferred_element_type=jnp.float32,
     )
-    col_pos = held_partner[:, None] == (own_start + own_rows)[None, :]
+    col_pos = rows[:, None] == matched_image[None, :]
     col_kept = real_all[:, None] & real_own[None, :]
     unused, col_weights = pair_weights(
         col_scores, col_pos, col_kept, score_sharpness_factor, score_shift_amount, grad_factor

time: 67.6 us -> 63.9 us (0.945)
  local copies, waits for them, and re-layouts: 7.8 us -> 4.19 us
  waiting for transfers between devices: 23.1 us -> 24 us
  starting transfers between devices: 14.9 us -> 14.1 us
    gather x1 -> x0, local copies, waits for them, and re-layouts: 3.51 us -> none  [shards(): held_partner = partner[rows]]
    ppermute x19, waiting for transfers between devices: 23.1 us -> 24 us  [xor_swap(): lax.ppermute(value, axis, [(source, source ^ bit) for source in range(cou...]
    ppermute x19, starting transfers between devices: 14.9 us -> 14.1 us  [xor_swap(): lax.ppermute(value, axis, [(source, source ^ bit) for source in range(cou...]
  transfers between devices with their start and end apart: 19 -> 19, of which waited for: 10 -> 11; matrix products, arithmetic and copies ran while one was open for 14% -> 10% of each run, Pallas kernels for 0% -> 0%
where the time goes in v4:
time: 63.9 us; the launch traced here: 63.6 us
  waiting for transfers between devices  24 us (38%)
  starting transfers between devices  14.1 us (22%)
  other arithmetic  13.2 us (21%)
  between operations  4.32 us (7%)
  local copies, waits for them, and re-layouts  4.19 us (7%)
  matrix products  3.79 us (6%)
    ppermute x19, waiting for transfers between devices, xor_swap(): lax.ppermute(value, axis, [(source, source ^ bit) for source in range(cou...  24 us
    ppermute x19, starting transfers between devices, xor_swap(): lax.ppermute(value, axis, [(source, source ^ bit) for source in range(cou...  14.1 us
    reduce_sum x2, other arithmetic, embed_rows(): jnp.sum(scaled * scaled, axis=-1, keepdims=True) + epsilon  2.29 us
    reduce_sum x2, other arithmetic, embed_rows(): jnp.mean(centred * centred, axis=-1, keepdims=True) + epsilon  2.24 us
    reduce_sum x2, other arithmetic, embed_rows(): centred = values - jnp.mean(values, axis=-1, keepdims=True)  2.08 us
    dot_general x1, matrix products, shards(): jnp.dot(row_weights, text_all, preferred_element_type=jnp.float32)  1.74 us
  transfers between devices with their start and end apart: 19, of which 11 were waited for; matrix products, arithmetic and copies ran while one was open for 10% of the time, Pallas kernels for 0%

profile of v4, /device:TPU:0, one launch (start us, length us, event | category | flops | bytes accessed | tf_op | source)
XLA Modules:
  0.0 63.6 jit_solution(12052127641738024706)
XLA Ops:
  0.7 1.0 %convert_reduce_fusion = f32[64]{0:T(128)S(1)} fusion(bf16[1,64,1152]{2,1,0:T(8,128)(2,1)} %param.12), kind=kLoop, calls=%fused_computation.19 | loop fusion | flops 147392 | bytes 147712 | tf_op jit(solution)/shard_map/reduce_sum | solution.py:67
  1.7 1.1 %fusion.61 = f32[64]{0:T(128)S(1)} fusion(bf16[1,64,1152]{2,1,0:T(8,128)(2,1)} %param.12, f32[64]{0:T(128)S(1)} %broadcast_multiply_fusion.4), kind=kLoop, calls=%fused_computation.73 | loop fusion | flops 294848 | bytes 147968 | tf_op jit(solution)/shard_map/reduce_sum | solution.py:68
  2.8 1.1 %fusion.55 = f32[64]{0:T(128)S(1)} fusion(bf16[1,64,1152]{2,1,0:T(8,128)(2,1)} %param.12, f32[1152]{0:T(1024)} %param.14, f32[64]{0:T(128)S(1)} %add_rsqrt_fusion.1, f32[64]{0:T(128)S(1)} %broadcast_multiply_fusion.4), kind=kLoop, calls=%fused_computation.67 | loop fusion | flops 442304 | bytes 152832 | tf_op jit(solution)/shard_map/reduce_sum | solution.py:71
  5.1 1.1 %fusion.36 = f32[64]{0:T(128)S(1)} fusion(bf16[1,64,1152]{2,1,0:T(8,128)(2,1)} %param.11, f32[64]{0:T(128)S(1)} %broadcast_multiply_fusion.5), kind=kLoop, calls=%fused_computation.48 | loop fusion | flops 294848 | bytes 147968 | tf_op jit(solution)/shard_map/reduce_sum | solution.py:68
  6.2 1.1 %fusion.30 = f32[64]{0:T(128)S(1)} fusion(bf16[1,64,1152]{2,1,0:T(8,128)(2,1)} %param.11, f32[1152]{0:T(1024)} %param.13, f32[64]{0:T(128)S(1)} %add_rsqrt_fusion.3, f32[64]{0:T(128)S(1)} %broadcast_multiply_fusion.5), kind=kLoop, calls=%fused_computation.42 | loop fusion | flops 442304 | bytes 152832 | tf_op jit(solution)/shard_map/reduce_sum | solution.py:71
  7.4 1.3 %fusion.15 = (bf16[1,64,1152]{2,1,0:T(8,128)(2,1)S(1)}, bf16[1,64,1152]{2,1,0:T(8,128)(2,1)S(1)}) fusion(bf16[1,64,1152]{2,1,0:T(8,128)(2,1)} %param.11, f32[64]{0:T(128)S(1)} %add_rsqrt_fusion.2, f32[1152]{0:T(1024)} %param.13, f32[64]{0:T(128)S(1)} %add_rsqrt_fusion.3, f32[64]{0:T(128)S(1)} %broadcast_multiply_fusion.5, f32[64]{0:T(128)S(1)} %add_rsqrt_fusion, ...), kind=kLoop, calls=%fused_computation.27 | loop fusion | flops 884736 | bytes 600576 | tf_op jit(solution)/shard_map/convert_element_type | solution.py:117
  8.7 3.0 %collective-permute-start = (bf16[2,32,1152]{2,1,0:T(8,128)(2,1)S(1)}, bf16[2,32,1152]{2,1,0:T(8,128)(2,1)S(1)}, u32[]{:S(2)}, u32[]{:S(2)}) collective-permute-start(bf16[2,32,1152]{2,1,0:T(8,128)(2,1)S(1)} %get-tuple-element.15), channel_id=1, source_target_pairs={{0,8},{4,12},{8,0},{12,4},{16,24},{20,28},{24,16},{28,20},{1,9},{5... | collective-permute-start | bytes 442376 | tf_op jit(solution)/shard_map/ppermute | solution.py:11
  11.7 1.5 %collective-permute-start.1 = (bf16[2,32,1152]{2,1,0:T(8,128)(2,1)S(1)}, bf16[2,32,1152]{2,1,0:T(8,128)(2,1)S(1)}, u32[]{:S(2)}, u32[]{:S(2)}) collective-permute-start(bf16[2,32,1152]{2,1,0:T(8,128)(2,1)S(1)} %get-tuple-element.15), channel_id=1, source_target_pairs={{0,16},{4,20},{8,24},{12,28},{16,0},{20,4},{24,8},{28,12},{1,17},{... | collective-permute-start | bytes 442376 | tf_op jit(solution)/shard_map/ppermute | solution.py:11
  18.0 5.0 %collective-permute-done.2 = bf16[2,32,1152]{2,1,0:T(8,128)(2,1)S(1)} collective-permute-done((bf16[2,32,1152]{2,1,0:T(8,128)(2,1)S(1)}, bf16[2,32,1152]{2,1,0:T(8,128)(2,1)S(1)}, u32[]{:S(2)}, u32[]{:S(2)}) %collective-permute-start.2) | collective-permute-done | bytes 147488 | tf_op jit(solution)/shard_map/ppermute | solution.py:11
  23.1 1.2 %collective-permute-done.6 = bf16[2,32,1152]{2,1,0:T(8,128)(2,1)S(1)} collective-permute-done((bf16[2,32,1152]{2,1,0:T(8,128)(2,1)S(1)}, bf16[2,32,1152]{2,1,0:T(8,128)(2,1)S(1)}, u32[]{:S(2)}, u32[]{:S(2)}) %collective-permute-start.6) | collective-permute-done | bytes 147488 | tf_op jit(solution)/shard_map/ppermute | solution.py:11
  29.3 1.1 %collective-permute-done.7 = bf16[2,32,1152]{2,1,0:T(8,128)(2,1)S(1)} collective-permute-done((bf16[2,32,1152]{2,1,0:T(8,128)(2,1)S(1)}, bf16[2,32,1152]{2,1,0:T(8,128)(2,1)S(1)}, u32[]{:S(2)}, u32[]{:S(2)}) %collective-permute-start.7) | collective-permute-done | bytes 147488 | tf_op jit(solution)/shard_map/ppermute | solution.py:11
  31.0 4.4 %collective-permute-done.8 = bf16[2,32,1152]{2,1,0:T(8,128)(2,1)S(1)} collective-permute-done((bf16[2,32,1152]{2,1,0:T(8,128)(2,1)S(1)}, bf16[2,32,1152]{2,1,0:T(8,128)(2,1)S(1)}, u32[]{:S(2)}, u32[]{:S(2)}) %collective-permute-start.8) | collective-permute-done | bytes 147488 | tf_op jit(solution)/shard_map/ppermute | solution.py:11
  35.5 2.0 %collective-permute-done.9 = bf16[2,32,1152]{2,1,0:T(8,128)(2,1)S(1)} collective-permute-done((bf16[2,32,1152]{2,1,0:T(8,128)(2,1)S(1)}, bf16[2,32,1152]{2,1,0:T(8,128)(2,1)S(1)}, u32[]{:S(2)}, u32[]{:S(2)}) %collective-permute-start.9) | collective-permute-done | bytes 147488 | tf_op jit(solution)/shard_map/ppermute | solution.py:11
  37.7 1.2 %collective-permute-done.13 = bf16[2,32,1152]{2,1,0:T(8,128)(2,1)S(1)} collective-permute-done((bf16[2,32,1152]{2,1,0:T(8,128)(2,1)S(1)}, bf16[2,32,1152]{2,1,0:T(8,128)(2,1)S(1)}, u32[]{:S(2)}, u32[]{:S(2)}) %collective-permute-start.13) | collective-permute-done | bytes 147488 | tf_op jit(solution)/shard_map/ppermute | solution.py:11
  38.9 1.2 %fusion.105 = (bf16[1,16,32,1152]{3,2,0,1:T(8,128)(2,1)}, bf16[1,16,32,1152]{3,2,0,1:T(8,128)(2,1)S(1)}) fusion(bf16[2,16,32,1152]{3,2,0,1:T(8,128)(2,1)S(1)} %bitcast_dynamic-update-slice_fusion), kind=kLoop, calls=%fused_computation.157 | loop fusion | bytes 4718592 | tf_op jit(solution)/shard_map/slice | solution.py:130
  40.2 1.2 %fusion.70 = (f32[]{:T(128)}, f32[64,512]{1,0:T(8,128)S(1)}) fusion(pred[512]{0:T(512)(128)(4,1)S(1)} %lt.52, pred[64]{0:T(512)(128)(4,1)S(1)} %iota_compare_fusion, f32[]{:T(128)} %bitcast.156, bf16[512,1152]{1,0:T(8,128)(2,1)S(1)} %bitcast.161, bf16[1,64,1152]{2,1,0:T(8,128)(2,1)S(1)} %get-tuple-element.26, f32[]{:T(128)} %bitcast, s32[512]{0:T(512)S(1)} %add.147, ...), kind=kOutput, calls=%fused_computation.104 | convolution fusion | flops 75988992 | bytes 1461068 | tf_op jit(solution)/shard_map/dot_general | solution.py:149
  42.0 1.7 %fusion.27 = (f32[64]{0:T(128)S(1)}, f32[64,1152]{1,0:T(8,128)S(1)}) fusion(bf16[1,64,1152]{2,1,0:T(8,128)(2,1)S(1)} %copy-done.2, f32[64]{0:T(128)S(1)} %add_rsqrt_fusion.2, f32[1152]{0:T(1024)S(1)} %copy-done.6, f32[64]{0:T(128)S(1)} %add_rsqrt_fusion.3, f32[64]{0:T(128)S(1)} %broadcast_multiply_fusion.5, bf16[512,1152]{1,0:T(8,128)(2,1)} %bitcast.162, ...), kind=kOutput, calls=%fused_computation.39 | convolution fusion | flops 76447680 | bytes 1761608 | tf_op jit(solution)/shard_map/dot_general | solution.py:158
  48.0 2.4 %collective-permute-done.15 = f32[2308]{0:T(1024)S(1)} collective-permute-done((f32[2308]{0:T(1024)S(1)}, f32[2308]{0:T(1024)S(1)}, u32[]{:S(2)}, u32[]{:S(2)}) %collective-permute-start.15) | collective-permute-done | bytes 9264 | tf_op jit(solution)/shard_map/ppermute | solution.py:11
  50.4 1.5 %collective-permute-start.16 = (f32[2308]{0:T(1024)S(1)}, f32[2308]{0:T(1024)S(1)}, u32[]{:S(2)}, u32[]{:S(2)}) collective-permute-start(f32[2308]{0:T(1024)S(1)} %add.162), channel_id=1, source_target_pairs={{0,16},{4,20},{8,24},{12,28},{16,0},{20,4},{24,8},{28,12},{1,17},{... | collective-permute-start | bytes 27704 | tf_op jit(solution)/shard_map/ppermute | solution.py:11
  51.9 2.2 %collective-permute-done.16 = f32[2308]{0:T(1024)S(1)} collective-permute-done((f32[2308]{0:T(1024)S(1)}, f32[2308]{0:T(1024)S(1)}, u32[]{:S(2)}, u32[]{:S(2)}) %collective-permute-start.16) | collective-permute-done | bytes 9264 | tf_op jit(solution)/shard_map/ppermute | solution.py:11
  54.1 1.6 %collective-permute-start.17 = (f32[2308]{0:T(1024)S(1)}, f32[2308]{0:T(1024)S(1)}, u32[]{:S(2)}, u32[]{:S(2)}) collective-permute-start(f32[2308]{0:T(1024)S(1)} %add.163), channel_id=1, source_target_pairs={{0,1},{1,0},{2,3},{3,2},{4,5},{5,4},{6,7},{7,6},{8,9},{9,8},{10,11... | collective-permute-start | bytes 27704 | tf_op jit(solution)/shard_map/ppermute | solution.py:11
  55.6 2.1 %collective-permute-done.17 = f32[2308]{0:T(1024)S(1)} collective-permute-done((f32[2308]{0:T(1024)S(1)}, f32[2308]{0:T(1024)S(1)}, u32[]{:S(2)}, u32[]{:S(2)}) %collective-permute-start.17) | collective-permute-done | bytes 9264 | tf_op jit(solution)/shard_map/ppermute | solution.py:11
  57.8 2.6 %collective-permute-start.18 = (f32[2308]{0:T(1024)S(1)}, f32[2308]{0:T(1024)S(1)}, u32[]{:S(2)}, u32[]{:S(2)}) collective-permute-start(f32[2308]{0:T(1024)S(1)} %add.164), channel_id=1, source_target_pairs={{0,2},{1,3},{2,0},{3,1},{4,6},{5,7},{6,4},{7,5},{8,10},{9,11},{10,... | collective-permute-start | bytes 27704 | tf_op jit(solution)/shard_map/ppermute | solution.py:11
  61.2 1.2 %collective-permute-done.18 = f32[2308]{0:T(1024)S(1)} collective-permute-done((f32[2308]{0:T(1024)S(1)}, f32[2308]{0:T(1024)S(1)}, u32[]{:S(2)}, u32[]{:S(2)}) %collective-permute-start.18) | collective-permute-done | bytes 9264 | tf_op jit(solution)/shard_map/ppermute | solution.py:11
  (96 shorter events, 15.1 us)
Async XLA Ops:
  0.6 14.7 %copy-start.8 = (s32[16]{0:T(128)S(1)}, s32[16]{0:T(128)}, u32[]{:S(2)}) copy-start(s32[16]{0:T(128)} %constant.54.clone) | copy-start | bytes 196
  0.6 14.0 %copy-start = (s32[1,8]{1,0:T(1,128)S(1)}, s32[1,8]{1,0:T(1,128)}, u32[]{:S(2)}) copy-start(s32[1,8]{1,0:T(1,128)} %param.19) | copy-start | bytes 100
  5.1 19.9 %copy-start.7 = (s32[1,512]{1,0:T(1,128)S(1)}, s32[1,512]{1,0:T(1,128)}, u32[]{:S(2)}) copy-start(s32[1,512]{1,0:T(1,128)} %param.18) | copy-start | bytes 6148
  8.7 7.9 %collective-permute-start = (bf16[2,32,1152]{2,1,0:T(8,128)(2,1)S(1)}, bf16[2,32,1152]{2,1,0:T(8,128)(2,1)S(1)}, u32[]{:S(2)}, u32[]{:S(2)}) collective-permute-start(bf16[2,32,1152]{2,1,0:T(8,128)(2,1)S(1)} %get-tuple-element.15), channel_id=1, source_target_pairs={{0,8},{4,12},{8,0},{12,4},{16,24},{20,28},{24,16},{28,20},{1,9},{5... | collective-permute-start | bytes 442376 | tf_op jit(solution)/shard_map/ppermute | solution.py:11
  11.7 5.7 %collective-permute-start.1 = (bf16[2,32,1152]{2,1,0:T(8,128)(2,1)S(1)}, bf16[2,32,1152]{2,1,0:T(8,128)(2,1)S(1)}, u32[]{:S(2)}, u32[]{:S(2)}) collective-permute-start(bf16[2,32,1152]{2,1,0:T(8,128)(2,1)S(1)} %get-tuple-element.15), channel_id=1, source_target_pairs={{0,16},{4,20},{8,24},{12,28},{16,0},{20,4},{24,8},{28,12},{1,17},{... | collective-permute-start | bytes 442376 | tf_op jit(solution)/shard_map/ppermute | solution.py:11
  13.2 9.8 %collective-permute-start.3 = (bf16[2,32,1152]{2,1,0:T(8,128)(2,1)S(1)}, bf16[2,32,1152]{2,1,0:T(8,128)(2,1)S(1)}, u32[]{:S(2)}, u32[]{:S(2)}) collective-permute-start(bf16[2,32,1152]{2,1,0:T(8,128)(2,1)S(1)} %get-tuple-element.15), channel_id=1, source_target_pairs={{0,4},{4,0},{8,12},{12,8},{16,20},{20,16},{24,28},{28,24},{1,5},{5... | collective-permute-start | bytes 442376 | tf_op jit(solution)/shard_map/ppermute | solution.py:11
  16.6 6.3 %collective-permute-start.2 = (bf16[2,32,1152]{2,1,0:T(8,128)(2,1)S(1)}, bf16[2,32,1152]{2,1,0:T(8,128)(2,1)S(1)}, u32[]{:S(2)}, u32[]{:S(2)}) collective-permute-start(bf16[2,32,1152]{2,1,0:T(8,128)(2,1)S(1)} %collective-permute-done), channel_id=1, source_target_pairs={{0,16},{4,20},{8,24},{12,28},{16,0},{20,4},{24,8},{28,12},{1,17},{... | collective-permute-start | bytes 442376 | tf_op jit(solution)/shard_map/ppermute | solution.py:11
  17.3 5.7 %collective-permute-start.4 = (bf16[2,32,1152]{2,1,0:T(8,128)(2,1)S(1)}, bf16[2,32,1152]{2,1,0:T(8,128)(2,1)S(1)}, u32[]{:S(2)}, u32[]{:S(2)}) collective-permute-start(bf16[2,32,1152]{2,1,0:T(8,128)(2,1)S(1)} %collective-permute-done), channel_id=1, source_target_pairs={{0,4},{4,0},{8,12},{12,8},{16,20},{20,16},{24,28},{28,24},{1,5},{5... | collective-permute-start | bytes 442376 | tf_op jit(solution)/shard_map/ppermute | solution.py:11
  17.5 5.6 %collective-permute-start.5 = (bf16[2,32,1152]{2,1,0:T(8,128)(2,1)S(1)}, bf16[2,32,1152]{2,1,0:T(8,128)(2,1)S(1)}, u32[]{:S(2)}, u32[]{:S(2)}) collective-permute-start(bf16[2,32,1152]{2,1,0:T(8,128)(2,1)S(1)} %collective-permute-done.1), channel_id=1, source_target_pairs={{0,4},{4,0},{8,12},{12,8},{16,20},{20,16},{24,28},{28,24},{1,5},{5... | collective-permute-start | bytes 442376 | tf_op jit(solution)/shard_map/ppermute | solution.py:11
  23.0 1.4 %collective-permute-start.6 = (bf16[2,32,1152]{2,1,0:T(8,128)(2,1)S(1)}, bf16[2,32,1152]{2,1,0:T(8,128)(2,1)S(1)}, u32[]{:S(2)}, u32[]{:S(2)}) collective-permute-start(bf16[2,32,1152]{2,1,0:T(8,128)(2,1)S(1)} %collective-permute-done.2), channel_id=1, source_target_pairs={{0,4},{4,0},{8,12},{12,8},{16,20},{20,16},{24,28},{28,24},{1,5},{5... | collective-permute-start | bytes 442376 | tf_op jit(solution)/shard_map/ppermute | solution.py:11
  24.4 6.0 %collective-permute-start.7 = (bf16[2,32,1152]{2,1,0:T(8,128)(2,1)S(1)}, bf16[2,32,1152]{2,1,0:T(8,128)(2,1)S(1)}, u32[]{:S(2)}, u32[]{:S(2)}) collective-permute-start(bf16[2,32,1152]{2,1,0:T(8,128)(2,1)S(1)} %get-tuple-element.13), channel_id=1, source_target_pairs={{0,16},{4,20},{8,24},{12,28},{16,0},{20,4},{24,8},{28,12},{1,17},{... | collective-permute-start | bytes 442376 | tf_op jit(solution)/shard_map/ppermute | solution.py:11
  28.7 6.8 %collective-permute-start.8 = (bf16[2,32,1152]{2,1,0:T(8,128)(2,1)S(1)}, bf16[2,32,1152]{2,1,0:T(8,128)(2,1)S(1)}, u32[]{:S(2)}, u32[]{:S(2)}) collective-permute-start(bf16[2,32,1152]{2,1,0:T(8,128)(2,1)S(1)} %get-tuple-element.13), channel_id=1, source_target_pairs={{0,8},{4,12},{8,0},{12,4},{16,24},{20,28},{24,16},{28,20},{1,9},{5... | collective-permute-start | bytes 442376 | tf_op jit(solution)/shard_map/ppermute | solution.py:11
  29.3 8.3 %collective-permute-start.10 = (bf16[2,32,1152]{2,1,0:T(8,128)(2,1)S(1)}, bf16[2,32,1152]{2,1,0:T(8,128)(2,1)S(1)}, u32[]{:S(2)}, u32[]{:S(2)}) collective-permute-start(bf16[2,32,1152]{2,1,0:T(8,128)(2,1)S(1)} %get-tuple-element.13), channel_id=1, source_target_pairs={{0,4},{4,0},{8,12},{12,8},{16,20},{20,16},{24,28},{28,24},{1,5},{5... | collective-permute-start | bytes 442376 | tf_op jit(solution)/shard_map/ppermute | solution.py:11
  30.4 7.2 %collective-permute-start.9 = (bf16[2,32,1152]{2,1,0:T(8,128)(2,1)S(1)}, bf16[2,32,1152]{2,1,0:T(8,128)(2,1)S(1)}, u32[]{:S(2)}, u32[]{:S(2)}) collective-permute-start(bf16[2,32,1152]{2,1,0:T(8,128)(2,1)S(1)} %collective-permute-done.7), channel_id=1, source_target_pairs={{0,8},{4,12},{8,0},{12,4},{16,24},{20,28},{24,16},{28,20},{1,9},{5... | collective-permute-start | bytes 442376 | tf_op jit(solution)/shard_map/ppermute | solution.py:11
  30.9 6.7 %collective-permute-start.11 = (bf16[2,32,1152]{2,1,0:T(8,128)(2,1)S(1)}, bf16[2,32,1152]{2,1,0:T(8,128)(2,1)S(1)}, u32[]{:S(2)}, u32[]{:S(2)}) collective-permute-start(bf16[2,32,1152]{2,1,0:T(8,128)(2,1)S(1)} %collective-permute-done.7), channel_id=1, source_target_pairs={{0,4},{4,0},{8,12},{12,8},{16,20},{20,16},{24,28},{28,24},{1,5},{5... | collective-permute-start | bytes 442376 | tf_op jit(solution)/shard_map/ppermute | solution.py:11
  35.5 2.2 %collective-permute-start.12 = (bf16[2,32,1152]{2,1,0:T(8,128)(2,1)S(1)}, bf16[2,32,1152]{2,1,0:T(8,128)(2,1)S(1)}, u32[]{:S(2)}, u32[]{:S(2)}) collective-permute-start(bf16[2,32,1152]{2,1,0:T(8,128)(2,1)S(1)} %collective-permute-done.8), channel_id=1, source_target_pairs={{0,4},{4,0},{8,12},{12,8},{16,20},{20,16},{24,28},{28,24},{1,5},{5... | collective-permute-start | bytes 442376 | tf_op jit(solution)/shard_map/ppermute | solution.py:11
  37.5 1.4 %collective-permute-start.13 = (bf16[2,32,1152]{2,1,0:T(8,128)(2,1)S(1)}, bf16[2,32,1152]{2,1,0:T(8,128)(2,1)S(1)}, u32[]{:S(2)}, u32[]{:S(2)}) collective-permute-start(bf16[2,32,1152]{2,1,0:T(8,128)(2,1)S(1)} %collective-permute-done.9), channel_id=1, source_target_pairs={{0,4},{4,0},{8,12},{12,8},{16,20},{20,16},{24,28},{28,24},{1,5},{5... | collective-permute-start | bytes 442376 | tf_op jit(solution)/shard_map/ppermute | solution.py:11
  40.2 3.6 %copy-start.3 = (bf16[1,16,32,1152]{3,2,0,1:T(8,128)(2,1)S(1)}, bf16[1,16,32,1152]{3,2,0,1:T(8,128)(2,1)}, u32[]{:S(2)}) copy-start(bf16[1,16,32,1152]{3,2,0,1:T(8,128)(2,1)} %get-tuple-element.16) | copy-start | bytes 3538948
  40.2 3.6 %copy-start.5 = (f32[1152]{0:T(1024)S(1)}, f32[1152]{0:T(1024)}, u32[]{:S(2)}) copy-start(f32[1152]{0:T(1024)} %param.14) | copy-start | bytes 13828
  45.3 1.2 %collective-permute-start.14 = (f32[2308]{0:T(1024)S(1)}, f32[2308]{0:T(1024)S(1)}, u32[]{:S(2)}, u32[]{:S(2)}) collective-permute-start(f32[2308]{0:T(1024)S(1)} %pad_maximum_fusion.1), channel_id=1, source_target_pairs={{0,4},{4,0},{8,12},{12,8},{16,20},{20,16},{24,28},{28,24},{1,5},{5... | collective-permute-start | bytes 27704 | tf_op jit(solution)/shard_map/ppermute | solution.py:11
  46.6 3.8 %collective-permute-start.15 = (f32[2308]{0:T(1024)S(1)}, f32[2308]{0:T(1024)S(1)}, u32[]{:S(2)}, u32[]{:S(2)}) collective-permute-start(f32[2308]{0:T(1024)S(1)} %fusion.112), channel_id=1, source_target_pairs={{0,8},{4,12},{8,0},{12,4},{16,24},{20,28},{24,16},{28,20},{1,9},{5... | collective-permute-start | bytes 27704 | tf_op jit(solution)/shard_map/ppermute | solution.py:11
  50.4 3.7 %collective-permute-start.16 = (f32[2308]{0:T(1024)S(1)}, f32[2308]{0:T(1024)S(1)}, u32[]{:S(2)}, u32[]{:S(2)}) collective-permute-start(f32[2308]{0:T(1024)S(1)} %add.162), channel_id=1, source_target_pairs={{0,16},{4,20},{8,24},{12,28},{16,0},{20,4},{24,8},{28,12},{1,17},{... | collective-permute-start | bytes 27704 | tf_op jit(solution)/shard_map/ppermute | solution.py:11
  54.1 3.7 %collective-permute-start.17 = (f32[2308]{0:T(1024)S(1)}, f32[2308]{0:T(1024)S(1)}, u32[]{:S(2)}, u32[]{:S(2)}) collective-permute-start(f32[2308]{0:T(1024)S(1)} %add.163), channel_id=1, source_target_pairs={{0,1},{1,0},{2,3},{3,2},{4,5},{5,4},{6,7},{7,6},{8,9},{9,8},{10,11... | collective-permute-start | bytes 27704 | tf_op jit(solution)/shard_map/ppermute | solution.py:11
  57.8 4.6 %collective-permute-start.18 = (f32[2308]{0:T(1024)S(1)}, f32[2308]{0:T(1024)S(1)}, u32[]{:S(2)}, u32[]{:S(2)}) collective-permute-start(f32[2308]{0:T(1024)S(1)} %add.164), channel_id=1, source_target_pairs={{0,2},{1,3},{2,0},{3,1},{4,6},{5,7},{6,4},{7,5},{8,10},{9,11},{10,... | collective-permute-start | bytes 27704 | tf_op jit(solution)/shard_map/ppermute | solution.py:11
  (4 other events, 11.0 us)

commit v5 on v4

--- a/solution.py
+++ b/solution.py
@@ -2,6 +2,8 @@
 import jax.numpy as jnp
 from jax import lax
 from jax.sharding import PartitionSpec as P
+from jax.experimental import pallas as pl
+from jax.experimental.pallas import tpu as pltpu
 
 epsilon = 1e-06
 
@@ -62,6 +64,28 @@
     return value
 
 
+def embed_kernel(picture_ref, caption_ref, picture_gain_ref, caption_gain_ref, out_ref):
+    towers = ((picture_ref, picture_gain_ref), (caption_ref, caption_gain_ref))
+    for tower, (pooled_ref, gain_ref) in enumerate(towers):
+        values = pooled_ref[...].astype(jnp.float32)
+        centred = values - jnp.mean(values, axis=-1, keepdims=True)
+        inverse = lax.rsqrt(jnp.mean(centred * centred, axis=-1, keepdims=True) + epsilon)
+        scaled = centred * inverse * gain_ref[...]
+        inv_length = lax.rsqrt(jnp.sum(scaled * scaled, axis=-1, keepdims=True) + epsilon)
+        out_ref[tower] = (scaled * inv_length).astype(out_ref.dtype)
+
+
+def embed_both(picture, caption, picture_gain, caption_gain):
+    rows, width = picture.shape
+    vmem = pltpu.MemorySpace.VMEM
+    return pl.pallas_call(
+        embed_kernel,
+        out_shape=jax.ShapeDtypeStruct((2, rows, width), jnp.bfloat16),
+        in_specs=[pl.BlockSpec(memory_space=vmem)] * 4,
+        out_specs=pl.BlockSpec(memory_space=vmem),
+    )(picture, caption, picture_gain.reshape(1, width), caption_gain.reshape(1, width))
+
+
 def embed_rows(pooled, gain):
     values = pooled.astype(jnp.float32)
     centred = values - jnp.mean(values, axis=-1, keepdims=True)
@@ -114,8 +138,14 @@
     text_unit_rows, text_normalized, text_inverse_length, text_length = embed_rows(
         caption_averaged_features[0], caption_rescale_factor
     )
-    picture_feature_entries = image_unit_rows.astype(jnp.bfloat16)
-    caption_feature_entries = text_unit_rows.astype(jnp.bfloat16)
+    both = embed_both(
+        picture_averaged_features[0],
+        caption_averaged_features[0],
+        picture_rescale_factor,
+        caption_rescale_factor,
+    )
+    picture_feature_entries = both[0]
+    caption_feature_entries = both[1]
     block_counts = genuine_entry_counts[0]
     partner = matching_caption_index[0]
     real_count = jnp.sum(block_counts).astype(jnp.float32)
@@ -123,7 +153,6 @@
     score_shift_amount = score_shift_term[0]
     grad_factor = objective_multiplier[0] / real_count
 
-    both = jnp.stack([picture_feature_entries, caption_feature_entries])
     gathered, masks, offsets, natural = gather_blocks(both, "blk")
     positions = gathered.shape[1]
     piece = gathered.shape[2]

time: 63.9 us -> 75.9 us (1.19)
  local copies, waits for them, and re-layouts: 4.19 us -> 14.9 us
  waiting for transfers between devices: 24 us -> 16 us
  starting transfers between devices: 14.1 us -> 18.5 us
  other arithmetic: 13.2 us -> 15.3 us
  Pallas kernels: 0 us -> 2.07 us
    ppermute x19, waiting for transfers between devices: 24 us -> 16 us  [xor_swap(): lax.ppermute(value, axis, [(source, source ^ bit) for source in range(cou...]
    ppermute x19, starting transfers between devices: 14.1 us -> 18.5 us  [xor_swap(): lax.ppermute(value, axis, [(source, source ^ bit) for source in range(cou...]
    reshape x0 -> x2, local copies, waits for them, and re-layouts: none -> 2.63 us  [the longest x1 1.33 us: embed_both(): picture_gain.reshape(1, width)]
    unnamed x31 -> x57, local copies, waits for them, and re-layouts: 0.29 us -> 2.9 us
    pallas_call x0 -> x1, Pallas kernels: none -> 2.07 us  [embed_both(): pl.pallas_call(embed_kernel, out_shape=jax.ShapeDtypeStruct((2, rows, wid...]
    slice x0 -> x1, local copies, waits for them, and re-layouts: none -> 1.76 us  [gather_blocks(): routed = ([both[:, :half]], [both[:, half:]])]
    dot_general x1, matrix products: 0.88 us -> 2.51 us  [shards(): lax.dot_general(col_weights, image_all, (((0,), (0,)), ((), ())), preferr...]
    dot_general x1, matrix products: 1.74 us -> 0.46 us  [shards(): jnp.dot(row_weights, text_all, preferred_element_type=jnp.float32)]
  transfers between devices with their start and end apart: 19 -> 19, of which waited for: 11 -> 8; matrix products, arithmetic and copies ran while one was open for 10% -> 28% of each run, Pallas kernels for 0% -> 0%
where the time goes in v5:
time: 75.9 us; the launch traced here: 75.4 us
  starting transfers between devices  18.5 us (24%)
  waiting for transfers between devices  16 us (21%)
  other arithmetic  15.3 us (20%)
  local copies, waits for them, and re-layouts  14.9 us (20%)
  between operations  4.46 us (6%)
  matrix products  4.15 us (5%)
  Pallas kernels  2.07 us (3%)
    ppermute x19, starting transfers between devices, xor_swap(): lax.ppermute(value, axis, [(source, source ^ bit) for source in range(cou...  18.5 us
    ppermute x19, waiting for transfers between devices, xor_swap(): lax.ppermute(value, axis, [(source, source ^ bit) for source in range(cou...  16 us
    unnamed x57, local copies, waits for them, and re-layouts  2.9 us
    reduce_sum x2, other arithmetic, embed_rows(): centred = values - jnp.mean(values, axis=-1, keepdims=True)  2.58 us
    dot_general x1, matrix products, shards(): lax.dot_general(col_weights, image_all, (((0,), (0,)), ((), ())), preferr...  2.51 us
    pallas_call x1, Pallas kernels, embed_both(): pl.pallas_call(embed_kernel, out_shape=jax.ShapeDtypeStruct((2, rows, wid...  2.07 us
    slice x1, local copies, waits for them, and re-layouts, gather_blocks(): routed = ([both[:, :half]], [both[:, half:]])  1.76 us
  transfers between devices with their start and end apart: 19, of which 8 were waited for; matrix products, arithmetic and copies ran while one was open for 28% of the time, Pallas kernels for 0%

profile of v5, /device:TPU:0, one launch (start us, length us, event | category | flops | bytes accessed | tf_op | source)
XLA Modules:
  0.0 75.4 jit_solution(17725550944552298840)
XLA Ops:
  0.7 1.3 %reshape.174.picture_gain_ref = f32[1,1152]{1,0:T(1,128)} reshape(f32[1152]{0:T(1024)} %param.13) | data formatting | bytes 9216 | tf_op jit(solution)/shard_map/reshape | solution.py:86
  2.0 1.3 %reshape.175.caption_gain_ref = f32[1,1152]{1,0:T(1,128)} reshape(f32[1152]{0:T(1024)} %param.14) | data formatting | bytes 9216 | tf_op jit(solution)/shard_map/reshape | solution.py:86
  3.3 2.1 %shard_map.138 = bf16[2,64,1152]{2,1,0:T(8,128)(2,1)} custom-call(bf16[64,1152]{1,0:T(8,128)(2,1)} %bitcast.87, bf16[64,1152]{1,0:T(8,128)(2,1)} %bitcast.86, f32[1,1152]{1,0:T(1,128)} %reshape.174.picture_gain_ref, f32[1,1152]{1,0:T(1,128)} %reshape.175.caption_gain_ref), custom_call_target="tpu_custom_call" | custom-call | tf_op jit(solution)/shard_map/pallas_call | solution.py:81
  5.4 1.8 %fusion.91 = (bf16[2,32,1152]{2,1,0:T(8,128)(2,1)}, bf16[2,32,1152]{2,1,0:T(8,128)(2,1)}) fusion(bf16[2,64,1152]{2,1,0:T(8,128)(2,1)} %shard_map.138), kind=kLoop, calls=%fused_computation.142 | loop fusion | bytes 589824 | tf_op jit(solution)/shard_map/slice | solution.py:29
  7.1 3.0 %collective-permute-start = (bf16[2,32,1152]{2,1,0:T(8,128)(2,1)}, bf16[2,32,1152]{2,1,0:T(8,128)(2,1)S(1)}, u32[]{:S(2)}, u32[]{:S(2)}) collective-permute-start(bf16[2,32,1152]{2,1,0:T(8,128)(2,1)} %get-tuple-element.15), channel_id=1, source_target_pairs={{0,8},{4,12},{8,0},{12,4},{16,24},{20,28},{24,16},{28,20},{1,9},{5... | collective-permute-start | bytes 442376 | tf_op jit(solution)/shard_map/ppermute | solution.py:13
  10.1 1.5 %collective-permute-start.1 = (bf16[2,32,1152]{2,1,0:T(8,128)(2,1)}, bf16[2,32,1152]{2,1,0:T(8,128)(2,1)S(1)}, u32[]{:S(2)}, u32[]{:S(2)}) collective-permute-start(bf16[2,32,1152]{2,1,0:T(8,128)(2,1)} %get-tuple-element.15), channel_id=1, source_target_pairs={{0,16},{4,20},{8,24},{12,28},{16,0},{20,4},{24,8},{28,12},{1,17},{... | collective-permute-start | bytes 442376 | tf_op jit(solution)/shard_map/ppermute | solution.py:13
  14.6 1.6 %convert_reduce_fusion.1 = f32[64]{0:T(128)} fusion(bf16[1,64,1152]{2,1,0:T(8,128)(2,1)} %param.11), kind=kLoop, calls=%fused_computation.21 | loop fusion | flops 147392 | bytes 147712 | tf_op jit(solution)/shard_map/reduce_sum | solution.py:91
  16.2 1.2 %constant_dynamic-slice_fusion = s32[1,1]{1,0:T(1,128)} fusion(s32[1,8]{1,0:T(1,128)} %param.19, s32[]{:T(128)S(6)} %select_n.44), kind=kLoop, calls=%fused_computation.127 | loop fusion | bytes 12 | tf_op jit(solution)/shard_map/jit(dynamic_index_in_dim)/dynamic_slice | solution.py:169
  17.4 1.2 %iota_compare_fusion = pred[64]{0:T(512)(128)(4,1)} fusion(s32[]{:T(128)} %bitcast.1), kind=kLoop, calls=%fused_computation.128 | loop fusion | flops 64 | bytes 68 | tf_op jit(solution)/shard_map/lt | solution.py:169
  22.2 1.3 %fusion.80 = s32[16,32]{1,0:T(8,128)} fusion(s32[16]{0:T(128)S(1)} %get-tuple-element.17, s32[16]{0:T(128)} %constant.54.clone), kind=kLoop, calls=%fused_computation.115 | loop fusion | flops 1024 | bytes 2176 | tf_op jit(solution)/shard_map/add | solution.py:166
  23.5 1.2 %gather_fusion = s32[16]{0:T(128)} fusion(s32[8]{0:T(128)S(1)} %bitcast.85, s32[1024]{0:T(1024)S(1)} %pad_clamp_fusion), kind=kCustom, calls=%fused_computation | custom fusion | bytes 192 | tf_op jit(solution)/shard_map/gather | solution.py:167
  27.7 1.3 %dynamic-slice_bitcast_fusion = s32[64]{0:T(128)} fusion(s32[1,512]{1,0:T(1,128)} %param.18, s32[]{:T(128)S(6)} %select_n.46), kind=kLoop, calls=%fused_computation.126 | loop fusion | bytes 516 | tf_op jit(solution)/shard_map/eq | solution.py:182
  34.9 1.9 %collective-permute-start.2 = (bf16[2,32,1152]{2,1,0:T(8,128)(2,1)S(1)}, bf16[2,32,1152]{2,1,0:T(8,128)(2,1)S(1)}, u32[]{:S(2)}, u32[]{:S(2)}) collective-permute-start(bf16[2,32,1152]{2,1,0:T(8,128)(2,1)S(1)} %collective-permute-done), channel_id=1, source_target_pairs={{0,16},{4,20},{8,24},{12,28},{16,0},{20,4},{24,8},{28,12},{1,17},{... | collective-permute-start | bytes 442376 | tf_op jit(solution)/shard_map/ppermute | solution.py:13
  36.8 4.5 %collective-permute-done.2 = bf16[2,32,1152]{2,1,0:T(8,128)(2,1)S(1)} collective-permute-done((bf16[2,32,1152]{2,1,0:T(8,128)(2,1)S(1)}, bf16[2,32,1152]{2,1,0:T(8,128)(2,1)S(1)}, u32[]{:S(2)}, u32[]{:S(2)}) %collective-permute-start.2) | collective-permute-done | bytes 147488 | tf_op jit(solution)/shard_map/ppermute | solution.py:13
  41.9 1.7 %collective-permute-start.9 = (bf16[2,32,1152]{2,1,0:T(8,128)(2,1)S(1)}, bf16[2,32,1152]{2,1,0:T(8,128)(2,1)S(1)}, u32[]{:S(2)}, u32[]{:S(2)}) collective-permute-start(bf16[2,32,1152]{2,1,0:T(8,128)(2,1)S(1)} %collective-permute-done.7), channel_id=1, source_target_pairs={{0,8},{4,12},{8,0},{12,4},{16,24},{20,28},{24,16},{28,20},{1,9},{5... | collective-permute-start | bytes 442376 | tf_op jit(solution)/shard_map/ppermute | solution.py:13
  44.4 3.3 %collective-permute-done.9 = bf16[2,32,1152]{2,1,0:T(8,128)(2,1)S(1)} collective-permute-done((bf16[2,32,1152]{2,1,0:T(8,128)(2,1)S(1)}, bf16[2,32,1152]{2,1,0:T(8,128)(2,1)S(1)}, u32[]{:S(2)}, u32[]{:S(2)}) %collective-permute-start.9) | collective-permute-done | bytes 147488 | tf_op jit(solution)/shard_map/ppermute | solution.py:13
  49.2 1.2 %fusion.90 = (bf16[1,16,32,1152]{3,2,0,1:T(8,128)(2,1)}, bf16[1,16,32,1152]{3,2,0,1:T(8,128)(2,1)S(1)}) fusion(bf16[2,16,32,1152]{3,2,0,1:T(8,128)(2,1)S(1)} %bitcast_dynamic-update-slice_fusion), kind=kLoop, calls=%fused_computation.141 | loop fusion | bytes 4718592 | tf_op jit(solution)/shard_map/slice | solution.py:159
  53.5 2.5 %fusion.32 = (f32[64]{0:T(128)S(1)}, f32[64,1152]{1,0:T(8,128)S(1)}) fusion(f32[64]{0:T(128)S(1)} %copy-done.17, f32[1152]{0:T(1024)S(1)} %copy-done.6, f32[64]{0:T(128)S(1)} %copy-done.15, f32[64]{0:T(128)S(1)} %copy-done.11, bf16[1,64,1152]{2,1,0:T(8,128)(2,1)S(1)} %copy-done.1, bf16[512,1152]{1,0:T(8,128)(2,1)} %bitcast.90, ...), kind=kOutput, calls=%fused_computation.42 | convolution fusion | flops 152043456 | bytes 2964228 | tf_op jit(solution)/shard_map/dot_general | solution.py:198
  58.4 1.8 %collective-permute-start.15 = (f32[2308]{0:T(1024)S(1)}, f32[2308]{0:T(1024)S(1)}, u32[]{:S(2)}, u32[]{:S(2)}) collective-permute-start(f32[2308]{0:T(1024)S(1)} %fusion.96), channel_id=1, source_target_pairs={{0,8},{4,12},{8,0},{12,4},{16,24},{20,28},{24,16},{28,20},{1,9},{5... | collective-permute-start | bytes 27704 | tf_op jit(solution)/shard_map/ppermute | solution.py:13
  60.2 2.0 %collective-permute-done.15 = f32[2308]{0:T(1024)S(1)} collective-permute-done((f32[2308]{0:T(1024)S(1)}, f32[2308]{0:T(1024)S(1)}, u32[]{:S(2)}, u32[]{:S(2)}) %collective-permute-start.15) | collective-permute-done | bytes 9264 | tf_op jit(solution)/shard_map/ppermute | solution.py:13
  62.2 1.7 %collective-permute-start.16 = (f32[2308]{0:T(1024)S(1)}, f32[2308]{0:T(1024)S(1)}, u32[]{:S(2)}, u32[]{:S(2)}) collective-permute-start(f32[2308]{0:T(1024)S(1)} %add.162), channel_id=1, source_target_pairs={{0,16},{4,20},{8,24},{12,28},{16,0},{20,4},{24,8},{28,12},{1,17},{... | collective-permute-start | bytes 27704 | tf_op jit(solution)/shard_map/ppermute | solution.py:13
  65.9 1.8 %collective-permute-start.17 = (f32[2308]{0:T(1024)S(1)}, f32[2308]{0:T(1024)S(1)}, u32[]{:S(2)}, u32[]{:S(2)}) collective-permute-start(f32[2308]{0:T(1024)S(1)} %add.163), channel_id=1, source_target_pairs={{0,1},{1,0},{2,3},{3,2},{4,5},{5,4},{6,7},{7,6},{8,9},{9,8},{10,11... | collective-permute-start | bytes 27704 | tf_op jit(solution)/shard_map/ppermute | solution.py:13
  67.7 1.9 %collective-permute-done.17 = f32[2308]{0:T(1024)S(1)} collective-permute-done((f32[2308]{0:T(1024)S(1)}, f32[2308]{0:T(1024)S(1)}, u32[]{:S(2)}, u32[]{:S(2)}) %collective-permute-start.17) | collective-permute-done | bytes 9264 | tf_op jit(solution)/shard_map/ppermute | solution.py:13
  69.6 2.8 %collective-permute-start.18 = (f32[2308]{0:T(1024)S(1)}, f32[2308]{0:T(1024)S(1)}, u32[]{:S(2)}, u32[]{:S(2)}) collective-permute-start(f32[2308]{0:T(1024)S(1)} %add.164), channel_id=1, source_target_pairs={{0,2},{1,3},{2,0},{3,1},{4,6},{5,7},{6,4},{7,5},{8,10},{9,11},{10,... | collective-permute-start | bytes 27704 | tf_op jit(solution)/shard_map/ppermute | solution.py:13
  (121 shorter events, 24.9 us)
Async XLA Ops:
  0.6 26.0 %copy-start.7 = (f32[1152]{0:T(1024)S(1)}, f32[1152]{0:T(1024)}, u32[]{:S(2)}) copy-start(f32[1152]{0:T(1024)} %param.13) | copy-start | bytes 13828
  0.6 25.5 %copy-start.2 = (bf16[1,64,1152]{2,1,0:T(8,128)(2,1)S(1)}, bf16[1,64,1152]{2,1,0:T(8,128)(2,1)}, u32[]{:S(2)}) copy-start(bf16[1,64,1152]{2,1,0:T(8,128)(2,1)} %param.11) | copy-start | bytes 442372
  0.7 22.8 %copy-start = (s32[1,8]{1,0:T(1,128)S(1)}, s32[1,8]{1,0:T(1,128)}, u32[]{:S(2)}) copy-start(s32[1,8]{1,0:T(1,128)} %param.19) | copy-start | bytes 100
  5.4 42.4 %copy-start.3 = (bf16[2,64,1152]{2,1,0:T(8,128)(2,1)S(1)}, bf16[2,64,1152]{2,1,0:T(8,128)(2,1)}, u32[]{:S(2)}) copy-start(bf16[2,64,1152]{2,1,0:T(8,128)(2,1)} %shard_map.138) | copy-start | bytes 884740
  7.1 27.5 %collective-permute-start = (bf16[2,32,1152]{2,1,0:T(8,128)(2,1)}, bf16[2,32,1152]{2,1,0:T(8,128)(2,1)S(1)}, u32[]{:S(2)}, u32[]{:S(2)}) collective-permute-start(bf16[2,32,1152]{2,1,0:T(8,128)(2,1)} %get-tuple-element.15), channel_id=1, source_target_pairs={{0,8},{4,12},{8,0},{12,4},{16,24},{20,28},{24,16},{28,20},{1,9},{5... | collective-permute-start | bytes 442376 | tf_op jit(solution)/shard_map/ppermute | solution.py:13
  10.1 24.8 %collective-permute-start.1 = (bf16[2,32,1152]{2,1,0:T(8,128)(2,1)}, bf16[2,32,1152]{2,1,0:T(8,128)(2,1)S(1)}, u32[]{:S(2)}, u32[]{:S(2)}) collective-permute-start(bf16[2,32,1152]{2,1,0:T(8,128)(2,1)} %get-tuple-element.15), channel_id=1, source_target_pairs={{0,16},{4,20},{8,24},{12,28},{16,0},{20,4},{24,8},{28,12},{1,17},{... | collective-permute-start | bytes 442376 | tf_op jit(solution)/shard_map/ppermute | solution.py:13
  11.6 29.7 %collective-permute-start.3 = (bf16[2,32,1152]{2,1,0:T(8,128)(2,1)}, bf16[2,32,1152]{2,1,0:T(8,128)(2,1)S(1)}, u32[]{:S(2)}, u32[]{:S(2)}) collective-permute-start(bf16[2,32,1152]{2,1,0:T(8,128)(2,1)} %get-tuple-element.15), channel_id=1, source_target_pairs={{0,4},{4,0},{8,12},{12,8},{16,20},{20,16},{24,28},{28,24},{1,5},{5... | collective-permute-start | bytes 442376 | tf_op jit(solution)/shard_map/ppermute | solution.py:13
  11.6 30.3 %collective-permute-start.7 = (bf16[2,32,1152]{2,1,0:T(8,128)(2,1)}, bf16[2,32,1152]{2,1,0:T(8,128)(2,1)S(1)}, u32[]{:S(2)}, u32[]{:S(2)}) collective-permute-start(bf16[2,32,1152]{2,1,0:T(8,128)(2,1)} %get-tuple-element.14), channel_id=1, source_target_pairs={{0,16},{4,20},{8,24},{12,28},{16,0},{20,4},{24,8},{28,12},{1,17},{... | collective-permute-start | bytes 442376 | tf_op jit(solution)/shard_map/ppermute | solution.py:13
  12.1 31.5 %collective-permute-start.8 = (bf16[2,32,1152]{2,1,0:T(8,128)(2,1)}, bf16[2,32,1152]{2,1,0:T(8,128)(2,1)S(1)}, u32[]{:S(2)}, u32[]{:S(2)}) collective-permute-start(bf16[2,32,1152]{2,1,0:T(8,128)(2,1)} %get-tuple-element.14), channel_id=1, source_target_pairs={{0,8},{4,12},{8,0},{12,4},{16,24},{20,28},{24,16},{28,20},{1,9},{5... | collective-permute-start | bytes 442376 | tf_op jit(solution)/shard_map/ppermute | solution.py:13
  34.6 13.3 %collective-permute-start.10 = (bf16[2,32,1152]{2,1,0:T(8,128)(2,1)}, bf16[2,32,1152]{2,1,0:T(8,128)(2,1)S(1)}, u32[]{:S(2)}, u32[]{:S(2)}) collective-permute-start(bf16[2,32,1152]{2,1,0:T(8,128)(2,1)} %get-tuple-element.14), channel_id=1, source_target_pairs={{0,4},{4,0},{8,12},{12,8},{16,20},{20,16},{24,28},{28,24},{1,5},{5... | collective-permute-start | bytes 442376 | tf_op jit(solution)/shard_map/ppermute | solution.py:13
  34.9 6.4 %collective-permute-start.2 = (bf16[2,32,1152]{2,1,0:T(8,128)(2,1)S(1)}, bf16[2,32,1152]{2,1,0:T(8,128)(2,1)S(1)}, u32[]{:S(2)}, u32[]{:S(2)}) collective-permute-start(bf16[2,32,1152]{2,1,0:T(8,128)(2,1)S(1)} %collective-permute-done), channel_id=1, source_target_pairs={{0,16},{4,20},{8,24},{12,28},{16,0},{20,4},{24,8},{28,12},{1,17},{... | collective-permute-start | bytes 442376 | tf_op jit(solution)/shard_map/ppermute | solution.py:13
  41.3 2.4 %collective-permute-start.4 = (bf16[2,32,1152]{2,1,0:T(8,128)(2,1)S(1)}, bf16[2,32,1152]{2,1,0:T(8,128)(2,1)S(1)}, u32[]{:S(2)}, u32[]{:S(2)}) collective-permute-start(bf16[2,32,1152]{2,1,0:T(8,128)(2,1)S(1)} %collective-permute-done), channel_id=1, source_target_pairs={{0,4},{4,0},{8,12},{12,8},{16,20},{20,16},{24,28},{28,24},{1,5},{5... | collective-permute-start | bytes 442376 | tf_op jit(solution)/shard_map/ppermute | solution.py:13
  41.3 2.9 %collective-permute-start.5 = (bf16[2,32,1152]{2,1,0:T(8,128)(2,1)S(1)}, bf16[2,32,1152]{2,1,0:T(8,128)(2,1)S(1)}, u32[]{:S(2)}, u32[]{:S(2)}) collective-permute-start(bf16[2,32,1152]{2,1,0:T(8,128)(2,1)S(1)} %collective-permute-done.1), channel_id=1, source_target_pairs={{0,4},{4,0},{8,12},{12,8},{16,20},{20,16},{24,28},{28,24},{1,5},{5... | collective-permute-start | bytes 442376 | tf_op jit(solution)/shard_map/ppermute | solution.py:13
  41.9 5.8 %collective-permute-start.9 = (bf16[2,32,1152]{2,1,0:T(8,128)(2,1)S(1)}, bf16[2,32,1152]{2,1,0:T(8,128)(2,1)S(1)}, u32[]{:S(2)}, u32[]{:S(2)}) collective-permute-start(bf16[2,32,1152]{2,1,0:T(8,128)(2,1)S(1)} %collective-permute-done.7), channel_id=1, source_target_pairs={{0,8},{4,12},{8,0},{12,4},{16,24},{20,28},{24,16},{28,20},{1,9},{5... | collective-permute-start | bytes 442376 | tf_op jit(solution)/shard_map/ppermute | solution.py:13
  43.6 4.3 %collective-permute-start.11 = (bf16[2,32,1152]{2,1,0:T(8,128)(2,1)S(1)}, bf16[2,32,1152]{2,1,0:T(8,128)(2,1)S(1)}, u32[]{:S(2)}, u32[]{:S(2)}) collective-permute-start(bf16[2,32,1152]{2,1,0:T(8,128)(2,1)S(1)} %collective-permute-done.7), channel_id=1, source_target_pairs={{0,4},{4,0},{8,12},{12,8},{16,20},{20,16},{24,28},{28,24},{1,5},{5... | collective-permute-start | bytes 442376 | tf_op jit(solution)/shard_map/ppermute | solution.py:13
  43.7 4.2 %collective-permute-start.12 = (bf16[2,32,1152]{2,1,0:T(8,128)(2,1)S(1)}, bf16[2,32,1152]{2,1,0:T(8,128)(2,1)S(1)}, u32[]{:S(2)}, u32[]{:S(2)}) collective-permute-start(bf16[2,32,1152]{2,1,0:T(8,128)(2,1)S(1)} %collective-permute-done.8), channel_id=1, source_target_pairs={{0,4},{4,0},{8,12},{12,8},{16,20},{20,16},{24,28},{28,24},{1,5},{5... | collective-permute-start | bytes 442376 | tf_op jit(solution)/shard_map/ppermute | solution.py:13
  44.2 3.5 %collective-permute-start.6 = (bf16[2,32,1152]{2,1,0:T(8,128)(2,1)S(1)}, bf16[2,32,1152]{2,1,0:T(8,128)(2,1)S(1)}, u32[]{:S(2)}, u32[]{:S(2)}) collective-permute-start(bf16[2,32,1152]{2,1,0:T(8,128)(2,1)S(1)} %collective-permute-done.2), channel_id=1, source_target_pairs={{0,4},{4,0},{8,12},{12,8},{16,20},{20,16},{24,28},{28,24},{1,5},{5... | collective-permute-start | bytes 442376 | tf_op jit(solution)/shard_map/ppermute | solution.py:13
  47.7 1.4 %collective-permute-start.13 = (bf16[2,32,1152]{2,1,0:T(8,128)(2,1)S(1)}, bf16[2,32,1152]{2,1,0:T(8,128)(2,1)S(1)}, u32[]{:S(2)}, u32[]{:S(2)}) collective-permute-start(bf16[2,32,1152]{2,1,0:T(8,128)(2,1)S(1)} %collective-permute-done.9), channel_id=1, source_target_pairs={{0,4},{4,0},{8,12},{12,8},{16,20},{20,16},{24,28},{28,24},{1,5},{5... | collective-permute-start | bytes 442376 | tf_op jit(solution)/shard_map/ppermute | solution.py:13
  49.1 4.3 %copy-start.1 = (bf16[1,64,1152]{2,1,0:T(8,128)(2,1)S(1)}, bf16[1,64,1152]{2,1,0:T(8,128)(2,1)}, u32[]{:S(2)}) copy-start(bf16[1,64,1152]{2,1,0:T(8,128)(2,1)} %param.12) | copy-start | bytes 442372
  57.1 1.2 %collective-permute-start.14 = (f32[2308]{0:T(1024)S(1)}, f32[2308]{0:T(1024)S(1)}, u32[]{:S(2)}, u32[]{:S(2)}) collective-permute-start(f32[2308]{0:T(1024)S(1)} %pad_maximum_fusion), channel_id=1, source_target_pairs={{0,4},{4,0},{8,12},{12,8},{16,20},{20,16},{24,28},{28,24},{1,5},{5... | collective-permute-start | bytes 27704 | tf_op jit(solution)/shard_map/ppermute | solution.py:13
  58.4 3.8 %collective-permute-start.15 = (f32[2308]{0:T(1024)S(1)}, f32[2308]{0:T(1024)S(1)}, u32[]{:S(2)}, u32[]{:S(2)}) collective-permute-start(f32[2308]{0:T(1024)S(1)} %fusion.96), channel_id=1, source_target_pairs={{0,8},{4,12},{8,0},{12,4},{16,24},{20,28},{24,16},{28,20},{1,9},{5... | collective-permute-start | bytes 27704 | tf_op jit(solution)/shard_map/ppermute | solution.py:13
  62.2 3.7 %collective-permute-start.16 = (f32[2308]{0:T(1024)S(1)}, f32[2308]{0:T(1024)S(1)}, u32[]{:S(2)}, u32[]{:S(2)}) collective-permute-start(f32[2308]{0:T(1024)S(1)} %add.162), channel_id=1, source_target_pairs={{0,16},{4,20},{8,24},{12,28},{16,0},{20,4},{24,8},{28,12},{1,17},{... | collective-permute-start | bytes 27704 | tf_op jit(solution)/shard_map/ppermute | solution.py:13
  65.9 3.7 %collective-permute-start.17 = (f32[2308]{0:T(1024)S(1)}, f32[2308]{0:T(1024)S(1)}, u32[]{:S(2)}, u32[]{:S(2)}) collective-permute-start(f32[2308]{0:T(1024)S(1)} %add.163), channel_id=1, source_target_pairs={{0,1},{1,0},{2,3},{3,2},{4,5},{5,4},{6,7},{7,6},{8,9},{9,8},{10,11... | collective-permute-start | bytes 27704 | tf_op jit(solution)/shard_map/ppermute | solution.py:13
  69.6 4.6 %collective-permute-start.18 = (f32[2308]{0:T(1024)S(1)}, f32[2308]{0:T(1024)S(1)}, u32[]{:S(2)}, u32[]{:S(2)}) collective-permute-start(f32[2308]{0:T(1024)S(1)} %add.164), channel_id=1, source_target_pairs={{0,2},{1,3},{2,0},{3,1},{4,6},{5,7},{6,4},{7,5},{8,10},{9,11},{10,... | collective-permute-start | bytes 27704 | tf_op jit(solution)/shard_map/ppermute | solution.py:13
  (16 other events, 44.3 us)

commit v6 on v4

v6 whole, which is shorter than its diff:
```python
import jax
import jax.numpy as jnp
from jax import lax
from jax.sharding import PartitionSpec as P
from jax.experimental import pallas as pl
from jax.experimental.pallas import tpu as pltpu

epsilon = 1e-06


def xor_swap(value, axis, bit):
    count = lax.axis_size(axis)
    return lax.ppermute(value, axis, [(source, source ^ bit) for source in range(count)])


def power_of_two(count):
    return count > 1 and count & (count - 1) == 0


def gather_blocks(both, axis):
    count = lax.axis_size(axis)
    rows = both.shape[1]
    if not power_of_two(count) or count < 4 or rows % 2:
        gathered = lax.all_gather(both, axis, axis=1, tiled=False)
        return gathered, list(range(count)), [0] * count, True
    chip_bits = [1 << b for b in range(1, count.bit_length() - 1)]
    half = rows // 2
    orders = (chip_bits, chip_bits[::-1])
    routed = ([both[:, :half]], [both[:, half:]])
    routed_masks = ([0], [0])
    fresh = ([0], [0])
    shared = ([], [])
    shared_masks = ([], [])
    for step in range(len(chip_bits) + 1):
        last = step == len(chip_bits)
        sent = [None, None]
        if not last:
            sent = [xor_swap(tuple(routed[h]), axis, orders[h][step]) for h in range(2)]
        across = [xor_swap(tuple(routed[h][i] for i in fresh[h]), axis, 1) for h in range(2)]
        for h in range(2):
            shared[h].extend(across[h])
            shared_masks[h].extend([routed_masks[h][i] ^ 1 for i in fresh[h]])
            if not last:
                bit = orders[h][step]
                fresh[h][:] = list(range(len(routed[h]), 2 * len(routed[h])))
                routed[h].extend(sent[h])
                routed_masks[h].extend([mask ^ bit for mask in routed_masks[h]])
    gathered = routed[0] + shared[0] + routed[1] + shared[1]
    masks = routed_masks[0] + shared_masks[0] + routed_masks[1] + shared_masks[1]
    offsets = [0] * count + [half] * count
    return gathered, masks, offsets, False


def all_sum(value, axes):
    for axis in axes:
        count = lax.axis_size(axis)
        if not power_of_two(count):
            value = lax.psum(value, axis)
            continue
        bit = 1
        while bit < count:
            value = value + xor_swap(value, axis, bit)
            bit *= 2
    return value


def embed_kernel(pooled_ref, gain_ref, out_ref):
    for tower in range(2):
        values = pooled_ref[tower].astype(jnp.float32)
        centred = values - jnp.mean(values, axis=-1, keepdims=True)
        inverse = lax.rsqrt(jnp.mean(centred * centred, axis=-1, keepdims=True) + epsilon)
        scaled = centred * inverse * gain_ref[tower : tower + 1, :]
        inv_length = lax.rsqrt(jnp.sum(scaled * scaled, axis=-1, keepdims=True) + epsilon)
        out_ref[tower] = (scaled * inv_length).astype(out_ref.dtype)


def embed_both(pooled, gains):
    vmem = pltpu.MemorySpace.VMEM
    return pl.pallas_call(
        embed_kernel,
        out_shape=jax.ShapeDtypeStruct(pooled.shape, jnp.bfloat16),
        in_specs=[pl.BlockSpec(memory_space=vmem)] * 2,
        out_specs=pl.BlockSpec(memory_space=vmem),
    )(pooled, gains)


def embed_rows(pooled, gain):
    values = pooled.astype(jnp.float32)
    centred = values - jnp.mean(values, axis=-1, keepdims=True)
    inverse = lax.rsqrt(jnp.mean(centred * centred, axis=-1, keepdims=True) + epsilon)
    normed = centred * inverse
    scaled = normed * gain
    inv_length = lax.rsqrt(jnp.sum(scaled * scaled, axis=-1, keepdims=True) + epsilon)
    return (scaled * inv_length, normed, inverse, inv_length)


def embed_back(direction, unit_rows, normed, inverse, inv_length, gain):
    tangent = (
        direction - unit_rows * jnp.sum(unit_rows * direction, axis=-1, keepdims=True)
    ) * inv_length
    gain_part = jnp.sum(tangent * normed, axis=0)
    scaled = tangent * gain
    gradient = (
        scaled
        - jnp.mean(scaled, axis=-1, keepdims=True)
        - normed * jnp.mean(scaled * normed, axis=-1, keepdims=True)
    ) * inverse
    return (gradient, gain_part)


def pair_weights(scores, labels_pos, kept, score_sharpness_factor, score_shift_amount, grad_factor):
    score_similarity_table = score_sharpness_factor * scores + score_shift_amount
    labels = jnp.where(labels_pos, 1.0, -1.0).astype(jnp.float32)
    margin = -labels * score_similarity_table
    loss_sum = jnp.sum(jnp.where(kept, jax.nn.softplus(margin), 0.0))
    weights = jnp.where(kept, -labels * jax.nn.sigmoid(margin), 0.0) * grad_factor
    return loss_sum, weights.astype(jnp.bfloat16)


def grad_kernel(
    scalars_ref, counts_ref, pooled_ref, gain_ref, own_ref, gathered_ref, partner_ref, grads_ref, sums_ref
):
    blocks = counts_ref.shape[0] - 2
    own_block = counts_ref[blocks]
    group_index = counts_ref[blocks + 1]
    block_rows = own_ref.shape[1]
    group_rows = gathered_ref.shape[1]
    width = own_ref.shape[2]
    own_start = own_block * block_rows
    total = counts_ref[0]
    for block in range(1, blocks):
        total = total + counts_ref[block]
    real_count = jnp.full((1, 1), total, jnp.int32).astype(jnp.float32)
    score_sharpness_factor = jnp.exp(jnp.full((1, 1), scalars_ref[0], jnp.float32))
    score_shift_amount = jnp.full((1, 1), scalars_ref[1], jnp.float32)
    grad_factor = jnp.full((1, 1), scalars_ref[2], jnp.float32) / real_count

    lane = lax.broadcasted_iota(jnp.int32, (1, group_rows), 1)
    lane_limit = jnp.zeros((1, group_rows), jnp.int32)
    for block in range(blocks):
        lane_limit = jnp.where(lane // block_rows == block, counts_ref[block], lane_limit)
    real_group = (lane % block_rows) < lane_limit
    sub = lax.broadcasted_iota(jnp.int32, (block_rows, 1), 0)
    real_own = sub < counts_ref[own_block]
    kept = real_own & real_group

    partner_row = partner_ref[...]
    columns = lax.broadcasted_iota(jnp.int32, (block_rows, group_rows), 1)
    own_index = own_start + lax.broadcasted_iota(jnp.int32, (block_rows, group_rows), 0)
    own_partner = jnp.sum(
        jnp.where(columns == own_index, partner_row.astype(jnp.float32), 0.0), axis=1, keepdims=True
    ).astype(jnp.int32)
    positives = (
        own_partner == columns,
        partner_row == own_index,
    )

    loss_rows = []
    for tower in range(2):
        values = pooled_ref[tower].astype(jnp.float32)
        gain = gain_ref[tower : tower + 1, :]
        centred = values - jnp.mean(values, axis=-1, keepdims=True)
        inverse = lax.rsqrt(jnp.mean(centred * centred, axis=-1, keepdims=True) + epsilon)
        normed = centred * inverse
        scaled = normed * gain
        inv_length = lax.rsqrt(jnp.sum(scaled * scaled, axis=-1, keepdims=True) + epsilon)
        unit_rows = scaled * inv_length

        other = gathered_ref[1 - tower]
        scores = lax.dot_general(
            own_ref[tower], other, (((1,), (1,)), ((), ())), preferred_element_type=jnp.float32
        )
        score_similarity_table = score_sharpness_factor * scores + score_shift_amount
        labels = jnp.where(positives[tower], 1.0, -1.0)
        margin = -labels * score_similarity_table
        if tower == 0:
            softplus = jnp.maximum(margin, 0.0) + jnp.log1p(jnp.exp(-jnp.abs(margin)))
            loss_rows.append(jnp.sum(jnp.where(kept, softplus, 0.0), axis=(0, 1), keepdims=True))
        weights = jnp.where(kept, -labels * jax.nn.sigmoid(margin), 0.0) * grad_factor
        direction = score_sharpness_factor * jnp.dot(
            weights.astype(jnp.bfloat16), other, preferred_element_type=jnp.float32
        )
        tangent = (
            direction - unit_rows * jnp.sum(unit_rows * direction, axis=-1, keepdims=True)
        ) * inv_length
        sums_ref[tower : tower + 1, :] = jnp.sum(tangent * normed, axis=0, keepdims=True)
        scaled_back = tangent * gain
        gradient = (
            scaled_back
            - jnp.mean(scaled_back, axis=-1, keepdims=True)
            - normed * jnp.mean(scaled_back * normed, axis=-1, keepdims=True)
        ) * inverse
        grads_ref[tower] = gradient.astype(grads_ref.dtype)
    group_lane = lax.broadcasted_iota(jnp.int32, (1, width), 1)
    sums_ref[2:3, :] = jnp.where(group_lane == group_index, loss_rows[0] / real_count, 0.0)


def shards(
    picture_averaged_features,
    caption_averaged_features,
    picture_rescale_factor,
    caption_rescale_factor,
    exponent_of_sharpness,
    score_shift_term,
    objective_multiplier,
    matching_caption_index,
    genuine_entry_counts,
):
    block_rows = picture_averaged_features.shape[1]
    width = picture_averaged_features.shape[2]
    members = lax.axis_size("blk")
    own_block = lax.axis_index("blk")
    group_index = lax.axis_index("rep")
    pooled = jnp.concatenate([picture_averaged_features, caption_averaged_features])
    gains = jnp.stack([picture_rescale_factor, caption_rescale_factor])
    both = embed_both(pooled, gains)

    pieces, masks, offsets, natural = gather_blocks(both, "blk")
    if natural:
        gathered = pieces.reshape(2, members * block_rows, width)
    else:
        gathered = jnp.zeros((2, members, block_rows, width), both.dtype)
        for piece, mask, offset in zip(pieces, masks, offsets):
            gathered = lax.dynamic_update_slice(
                gathered, piece[:, None], (0, own_block ^ mask, offset, 0)
            )
        gathered = gathered.reshape(2, members * block_rows, width)

    scalars = jnp.concatenate([exponent_of_sharpness, score_shift_term, objective_multiplier])
    counts = jnp.concatenate(
        [genuine_entry_counts[0], jnp.stack([own_block, group_index]).astype(jnp.int32)]
    )
    smem = pltpu.MemorySpace.SMEM
    vmem = pltpu.MemorySpace.VMEM
    grads, sums = pl.pallas_call(
        grad_kernel,
        out_shape=(
            jax.ShapeDtypeStruct((2, block_rows, width), jnp.bfloat16),
            jax.ShapeDtypeStruct((3, width), jnp.float32),
        ),
        in_specs=[pl.BlockSpec(memory_space=smem)] * 2 + [pl.BlockSpec(memory_space=vmem)] * 5,
        out_specs=(pl.BlockSpec(memory_space=vmem), pl.BlockSpec(memory_space=vmem)),
    )(scalars, counts, pooled, gains, both, gathered, matching_caption_index)

    total = all_sum(sums, ("blk", "rep"))
    gain_grads = total[:2]
    group_loss = lax.dynamic_slice_in_dim(total[2], group_index, 1)
    return (grads[0:1], grads[1:2], gain_grads, group_loss)


def solution(mesh):
    placed = (
        P("rep", "blk", None),
        P("rep", "blk", None),
        P(),
        P(),
        P(),
        P(),
        P(),
        P("rep", None),
        P("rep", None),
    )
    return jax.shard_map(
        shards,
        mesh=mesh,
        in_specs=placed,
        out_specs=(P("rep", "blk", None), P("rep", "blk", None), P(), P("rep")),
        check_vma=False,
    )
```

time: 63.9 us -> 57 us (0.89)
  other arithmetic: 13.2 us -> 2.6 us
  waiting for transfers between devices: 24 us -> 16.2 us
  Pallas kernels: 0 us -> 6.44 us
  local copies, waits for them, and re-layouts: 4.19 us -> 10 us
  starting transfers between devices: 14.1 us -> 18.5 us
  matrix products: 3.79 us -> 0 us
  between operations: 4.32 us -> 2.79 us
    reduce_sum x10 -> x0, other arithmetic: 8.05 us -> none  [the longest x2 2.29 us: embed_rows(): jnp.sum(scaled * scaled, axis=-1, keepdims=True) + epsilon]
    ppermute x19, waiting for transfers between devices: 24 us -> 16.2 us  [xor_swap(): lax.ppermute(value, axis, [(source, source ^ bit) for source in range(cou...]
    pallas_call x0 -> x2, Pallas kernels: none -> 6.44 us  [the longest x1 4.37 us: shards(): pl.pallas_call(grad_kernel, out_shape=(jax.ShapeDtypeStruct((2, block_row...]
    ppermute x19, starting transfers between devices: 14.1 us -> 18.5 us  [xor_swap(): lax.ppermute(value, axis, [(source, source ^ bit) for source in range(cou...]
    dot_general x3 -> x0, matrix products: 3.79 us -> none  [the longest x1 1.74 us: shards(): jnp.dot(row_weights, text_all, preferred_element_type=jnp.float32)]
    slice x2 -> x4, local copies, waits for them, and re-layouts: 1.22 us -> 4.03 us  [the longest x1 1.71 us: shards(): return (grads[0:1], grads[1:2], gain_grads, group_loss)]
    unnamed x31 -> x9, local copies, waits for them, and re-layouts: 0.29 us -> 2.42 us
    broadcast_in_dim x2 -> x0, other arithmetic: 1.62 us -> none  [the longest x1 0.81 us: shards(): image_gradient.astype(jnp.bfloat16)[None]]
  transfers between devices with their start and end apart: 19 -> 19, of which waited for: 11 -> 9; matrix products, arithmetic and copies ran while one was open for 10% -> 6% of each run, Pallas kernels for 0% -> 0%
where the time goes in v6:
time: 57 us; the launch traced here: 56.5 us
  starting transfers between devices  18.5 us (32%)
  waiting for transfers between devices  16.2 us (28%)
  local copies, waits for them, and re-layouts  10 us (18%)
  Pallas kernels  6.44 us (11%)
  between operations  2.79 us (5%)
  other arithmetic  2.6 us (5%)
    ppermute x19, starting transfers between devices, xor_swap(): lax.ppermute(value, axis, [(source, source ^ bit) for source in range(cou...  18.5 us
    ppermute x19, waiting for transfers between devices, xor_swap(): lax.ppermute(value, axis, [(source, source ^ bit) for source in range(cou...  16.2 us
    pallas_call x1, Pallas kernels, shards(): pl.pallas_call(grad_kernel, out_shape=(jax.ShapeDtypeStruct((2, block_row...  4.37 us
    unnamed x9, local copies, waits for them, and re-layouts  2.42 us
    pallas_call x1, Pallas kernels, embed_both(): pl.pallas_call(embed_kernel, out_shape=jax.ShapeDtypeStruct(pooled.shape,...  2.08 us
    slice x1, local copies, waits for them, and re-layouts, shards(): return (grads[0:1], grads[1:2], gain_grads, group_loss)  1.71 us
    slice x1, local copies, waits for them, and re-layouts, gather_blocks(): routed = ([both[:, :half]], [both[:, half:]])  1.71 us
    another operation x2, local copies, waits for them, and re-layouts, shards(): gains = jnp.stack([picture_rescale_factor, caption_rescale_factor])  1.4 us
  transfers between devices with their start and end apart: 19, of which 9 were waited for; matrix products, arithmetic and copies ran while one was open for 6% of the time, Pallas kernels for 0%

profile of v6, /device:TPU:0, one launch (start us, length us, event | category | flops | bytes accessed | tf_op | source)
XLA Modules:
  0.0 56.5 jit_solution(8325618049580799981)
XLA Ops:
  0.6 0.9 %constant_dynamic-update-slice_fusion.1 = bf16[2,64,1152]{2,1,0:T(8,128)(2,1)S(1)} fusion(bf16[1,64,1152]{2,1,0:T(8,128)(2,1)} %param.9), kind=kLoop, calls=%fused_computation.18 | loop fusion | bytes 294912
  1.6 0.7 %stack.17 = f32[1,1152]{1,0:T(1,128)S(1)} reshape(f32[1152]{0:T(1024)} %param.11) | data formatting | bytes 9216 | tf_op jit(solution)/shard_map/stack | solution.py:215
  3.0 0.9 %constant_dynamic-update-slice_fusion.pooled_ref = bf16[2,64,1152]{2,1,0:T(8,128)(2,1)S(1)} fusion(bf16[2,64,1152]{2,1,0:T(8,128)(2,1)S(1)} %constant_dynamic-update-slice_fusion.1, bf16[1,64,1152]{2,1,0:T(8,128)(2,1)} %param.10), kind=kLoop, calls=%fused_computation.17 | loop fusion | bytes 294912 | tf_op jit(solution)/shard_map/concatenate | solution.py:214
  4.6 2.1 %shard_map.120.own_ref = bf16[2,64,1152]{2,1,0:T(8,128)(2,1)} custom-call(bf16[2,64,1152]{2,1,0:T(8,128)(2,1)} %copy-done.2, f32[2,1152]{1,0:T(2,128)} %pad_maximum_fusion.gain_ref), custom_call_target="tpu_custom_call" | custom-call | tf_op jit(solution)/shard_map/pallas_call | solution.py:79
  6.7 1.7 %fusion.1 = (bf16[2,32,1152]{2,1,0:T(8,128)(2,1)S(1)}, bf16[2,32,1152]{2,1,0:T(8,128)(2,1)}) fusion(bf16[2,64,1152]{2,1,0:T(8,128)(2,1)} %shard_map.120.own_ref), kind=kLoop, calls=%fused_computation.23 | loop fusion | bytes 589824 | tf_op jit(solution)/shard_map/slice | solution.py:29
  8.4 3.0 %collective-permute-start = (bf16[2,32,1152]{2,1,0:T(8,128)(2,1)}, bf16[2,32,1152]{2,1,0:T(8,128)(2,1)S(1)}, u32[]{:S(2)}, u32[]{:S(2)}) collective-permute-start(bf16[2,32,1152]{2,1,0:T(8,128)(2,1)} %get-tuple-element.11), channel_id=1, source_target_pairs={{0,8},{4,12},{8,0},{12,4},{16,24},{20,28},{24,16},{28,20},{1,9},{5... | collective-permute-start | bytes 442376 | tf_op jit(solution)/shard_map/ppermute | solution.py:13
  11.4 1.5 %collective-permute-start.1 = (bf16[2,32,1152]{2,1,0:T(8,128)(2,1)}, bf16[2,32,1152]{2,1,0:T(8,128)(2,1)S(1)}, u32[]{:S(2)}, u32[]{:S(2)}) collective-permute-start(bf16[2,32,1152]{2,1,0:T(8,128)(2,1)} %get-tuple-element.11), channel_id=1, source_target_pairs={{0,16},{4,20},{8,24},{12,28},{16,0},{20,4},{24,8},{28,12},{1,17},{... | collective-permute-start | bytes 442376 | tf_op jit(solution)/shard_map/ppermute | solution.py:13
  17.8 2.0 %collective-permute-start.2 = (bf16[2,32,1152]{2,1,0:T(8,128)(2,1)S(1)}, bf16[2,32,1152]{2,1,0:T(8,128)(2,1)S(1)}, u32[]{:S(2)}, u32[]{:S(2)}) collective-permute-start(bf16[2,32,1152]{2,1,0:T(8,128)(2,1)S(1)} %collective-permute-done), channel_id=1, source_target_pairs={{0,16},{4,20},{8,24},{12,28},{16,0},{20,4},{24,8},{28,12},{1,17},{... | collective-permute-start | bytes 442376 | tf_op jit(solution)/shard_map/ppermute | solution.py:13
  19.9 3.7 %collective-permute-done.2 = bf16[2,32,1152]{2,1,0:T(8,128)(2,1)S(1)} collective-permute-done((bf16[2,32,1152]{2,1,0:T(8,128)(2,1)S(1)}, bf16[2,32,1152]{2,1,0:T(8,128)(2,1)S(1)}, u32[]{:S(2)}, u32[]{:S(2)}) %collective-permute-start.2) | collective-permute-done | bytes 147488 | tf_op jit(solution)/shard_map/ppermute | solution.py:13
  24.2 1.7 %collective-permute-start.9 = (bf16[2,32,1152]{2,1,0:T(8,128)(2,1)S(1)}, bf16[2,32,1152]{2,1,0:T(8,128)(2,1)S(1)}, u32[]{:S(2)}, u32[]{:S(2)}) collective-permute-start(bf16[2,32,1152]{2,1,0:T(8,128)(2,1)S(1)} %collective-permute-done.7), channel_id=1, source_target_pairs={{0,8},{4,12},{8,0},{12,4},{16,24},{20,28},{24,16},{28,20},{1,9},{5... | collective-permute-start | bytes 442376 | tf_op jit(solution)/shard_map/ppermute | solution.py:13
  26.7 3.3 %collective-permute-done.9 = bf16[2,32,1152]{2,1,0:T(8,128)(2,1)S(1)} collective-permute-done((bf16[2,32,1152]{2,1,0:T(8,128)(2,1)S(1)}, bf16[2,32,1152]{2,1,0:T(8,128)(2,1)S(1)}, u32[]{:S(2)}, u32[]{:S(2)}) %collective-permute-start.9) | collective-permute-done | bytes 147488 | tf_op jit(solution)/shard_map/ppermute | solution.py:13
  30.4 1.1 %collective-permute-done.13 = bf16[2,32,1152]{2,1,0:T(8,128)(2,1)S(1)} collective-permute-done((bf16[2,32,1152]{2,1,0:T(8,128)(2,1)S(1)}, bf16[2,32,1152]{2,1,0:T(8,128)(2,1)S(1)}, u32[]{:S(2)}, u32[]{:S(2)}) %collective-permute-start.13) | collective-permute-done | bytes 147488 | tf_op jit(solution)/shard_map/ppermute | solution.py:13
  31.5 1.4 %copy-done = bf16[2,8,64,1152]{3,2,1,0:T(8,128)(2,1)} copy-done((bf16[2,8,64,1152]{3,2,1,0:T(8,128)(2,1)}, bf16[2,8,64,1152]{3,2,1,0:T(8,128)(2,1)S(1)}, u32[]{:S(2)}) %copy-start) | copy-done | bytes 2359320
  32.9 4.4 %shard_map.121 = (bf16[2,64,1152]{2,1,0:T(8,128)(2,1)}, f32[3,1152]{1,0:T(4,128)}) custom-call(f32[3]{0:T(128)} %pad_maximum_fusion.1.scalars_ref, s32[10]{0:T(128)} %pad_add_fusion.counts_ref, bf16[2,64,1152]{2,1,0:T(8,128)(2,1)} %copy-done.2, f32[2,1152]{1,0:T(2,128)} %pad_maximum_fusion.gain_ref, bf16[2,64,1152]{2,1,0:T(8,128)(2,1)} %shard_map.120.own_ref, ...), custom_call_target="tpu_custom_call" | custom-call | tf_op jit(solution)/shard_map/pallas_call | solution.py:235
  37.4 1.2 %collective-permute-done.14 = f32[3,1152]{1,0:T(4,128)S(1)} collective-permute-done((f32[3,1152]{1,0:T(4,128)}, f32[3,1152]{1,0:T(4,128)S(1)}, u32[]{:S(2)}, u32[]{:S(2)}) %collective-permute-start.14) | collective-permute-done | bytes 13856 | tf_op jit(solution)/shard_map/ppermute | solution.py:13
  38.6 0.7 %add.58 = f32[3,1152]{1,0:T(4,128)S(1)} add(f32[3,1152]{1,0:T(4,128)} %get-tuple-element.7, f32[3,1152]{1,0:T(4,128)S(1)} %collective-permute-done.14) | non-fusion elementwise | flops 3456 | bytes 41472 | tf_op jit(solution)/shard_map/add | solution.py:62
  39.4 1.7 %collective-permute-start.15 = (f32[3,1152]{1,0:T(4,128)S(1)}, f32[3,1152]{1,0:T(4,128)S(1)}, u32[]{:S(2)}, u32[]{:S(2)}) collective-permute-start(f32[3,1152]{1,0:T(4,128)S(1)} %add.58), channel_id=1, source_target_pairs={{0,8},{4,12},{8,0},{12,4},{16,24},{20,28},{24,16},{28,20},{1,9},{5... | collective-permute-start | bytes 41480 | tf_op jit(solution)/shard_map/ppermute | solution.py:13
  41.1 2.0 %collective-permute-done.15 = f32[3,1152]{1,0:T(4,128)S(1)} collective-permute-done((f32[3,1152]{1,0:T(4,128)S(1)}, f32[3,1152]{1,0:T(4,128)S(1)}, u32[]{:S(2)}, u32[]{:S(2)}) %collective-permute-start.15) | collective-permute-done | bytes 13856 | tf_op jit(solution)/shard_map/ppermute | solution.py:13
  43.1 1.7 %collective-permute-start.16 = (f32[3,1152]{1,0:T(4,128)S(1)}, f32[3,1152]{1,0:T(4,128)S(1)}, u32[]{:S(2)}, u32[]{:S(2)}) collective-permute-start(f32[3,1152]{1,0:T(4,128)S(1)} %add.59), channel_id=1, source_target_pairs={{0,16},{4,20},{8,24},{12,28},{16,0},{20,4},{24,8},{28,12},{1,17},{... | collective-permute-start | bytes 41480 | tf_op jit(solution)/shard_map/ppermute | solution.py:13
  44.9 2.0 %collective-permute-done.16 = f32[3,1152]{1,0:T(4,128)S(1)} collective-permute-done((f32[3,1152]{1,0:T(4,128)S(1)}, f32[3,1152]{1,0:T(4,128)S(1)}, u32[]{:S(2)}, u32[]{:S(2)}) %collective-permute-start.16) | collective-permute-done | bytes 13856 | tf_op jit(solution)/shard_map/ppermute | solution.py:13
  46.9 1.8 %collective-permute-start.17 = (f32[3,1152]{1,0:T(4,128)S(1)}, f32[3,1152]{1,0:T(4,128)S(1)}, u32[]{:S(2)}, u32[]{:S(2)}) collective-permute-start(f32[3,1152]{1,0:T(4,128)S(1)} %add.60), channel_id=1, source_target_pairs={{0,1},{1,0},{2,3},{3,2},{4,5},{5,4},{6,7},{7,6},{8,9},{9,8},{10,11... | collective-permute-start | bytes 41480 | tf_op jit(solution)/shard_map/ppermute | solution.py:13
  48.7 2.0 %collective-permute-done.17 = f32[3,1152]{1,0:T(4,128)S(1)} collective-permute-done((f32[3,1152]{1,0:T(4,128)S(1)}, f32[3,1152]{1,0:T(4,128)S(1)}, u32[]{:S(2)}, u32[]{:S(2)}) %collective-permute-start.17) | collective-permute-done | bytes 13856 | tf_op jit(solution)/shard_map/ppermute | solution.py:13
  50.7 2.8 %collective-permute-start.18 = (f32[3,1152]{1,0:T(4,128)S(1)}, f32[3,1152]{1,0:T(4,128)S(1)}, u32[]{:S(2)}, u32[]{:S(2)}) collective-permute-start(f32[3,1152]{1,0:T(4,128)S(1)} %add.61), channel_id=1, source_target_pairs={{0,2},{1,3},{2,0},{3,1},{4,6},{5,7},{6,4},{7,5},{8,10},{9,11},{10,... | collective-permute-start | bytes 41480 | tf_op jit(solution)/shard_map/ppermute | solution.py:13
  53.5 1.7 %fusion = (bf16[1,64,1152]{2,1,0:T(8,128)(2,1)}, bf16[1,64,1152]{2,1,0:T(8,128)(2,1)}) fusion(bf16[2,64,1152]{2,1,0:T(8,128)(2,1)} %get-tuple-element.6), kind=kLoop, calls=%fused_computation.22 | loop fusion | bytes 589824 | tf_op jit(solution)/shard_map/slice | solution.py:248
  (58 shorter events, 7.5 us)
Async XLA Ops:
  0.6 13.2 %copy-start.3 = (s32[1,8]{1,0:T(1,128)S(1)}, s32[1,8]{1,0:T(1,128)}, u32[]{:S(2)}) copy-start(s32[1,8]{1,0:T(1,128)} %param.17) | copy-start | bytes 100
  3.9 0.7 %copy-start.2 = (bf16[2,64,1152]{2,1,0:T(8,128)(2,1)}, bf16[2,64,1152]{2,1,0:T(8,128)(2,1)S(1)}, u32[]{:S(2)}) copy-start(bf16[2,64,1152]{2,1,0:T(8,128)(2,1)S(1)} %constant_dynamic-update-slice_fusion.pooled_ref) | copy-start | bytes 884740
  6.7 7.1 %copy-start.1 = (bf16[2,64,1152]{2,1,0:T(8,128)(2,1)S(1)}, bf16[2,64,1152]{2,1,0:T(8,128)(2,1)}, u32[]{:S(2)}) copy-start(bf16[2,64,1152]{2,1,0:T(8,128)(2,1)} %shard_map.120.own_ref) | copy-start | bytes 884740
  8.4 8.5 %collective-permute-start = (bf16[2,32,1152]{2,1,0:T(8,128)(2,1)}, bf16[2,32,1152]{2,1,0:T(8,128)(2,1)S(1)}, u32[]{:S(2)}, u32[]{:S(2)}) collective-permute-start(bf16[2,32,1152]{2,1,0:T(8,128)(2,1)} %get-tuple-element.11), channel_id=1, source_target_pairs={{0,8},{4,12},{8,0},{12,4},{16,24},{20,28},{24,16},{28,20},{1,9},{5... | collective-permute-start | bytes 442376 | tf_op jit(solution)/shard_map/ppermute | solution.py:13
  11.4 6.4 %collective-permute-start.1 = (bf16[2,32,1152]{2,1,0:T(8,128)(2,1)}, bf16[2,32,1152]{2,1,0:T(8,128)(2,1)S(1)}, u32[]{:S(2)}, u32[]{:S(2)}) collective-permute-start(bf16[2,32,1152]{2,1,0:T(8,128)(2,1)} %get-tuple-element.11), channel_id=1, source_target_pairs={{0,16},{4,20},{8,24},{12,28},{16,0},{20,4},{24,8},{28,12},{1,17},{... | collective-permute-start | bytes 442376 | tf_op jit(solution)/shard_map/ppermute | solution.py:13
  12.9 10.7 %collective-permute-start.3 = (bf16[2,32,1152]{2,1,0:T(8,128)(2,1)}, bf16[2,32,1152]{2,1,0:T(8,128)(2,1)S(1)}, u32[]{:S(2)}, u32[]{:S(2)}) collective-permute-start(bf16[2,32,1152]{2,1,0:T(8,128)(2,1)} %get-tuple-element.11), channel_id=1, source_target_pairs={{0,4},{4,0},{8,12},{12,8},{16,20},{20,16},{24,28},{28,24},{1,5},{5... | collective-permute-start | bytes 442376 | tf_op jit(solution)/shard_map/ppermute | solution.py:13
  12.9 11.3 %collective-permute-start.7 = (bf16[2,32,1152]{2,1,0:T(8,128)(2,1)S(1)}, bf16[2,32,1152]{2,1,0:T(8,128)(2,1)S(1)}, u32[]{:S(2)}, u32[]{:S(2)}) collective-permute-start(bf16[2,32,1152]{2,1,0:T(8,128)(2,1)S(1)} %get-tuple-element.10), channel_id=1, source_target_pairs={{0,16},{4,20},{8,24},{12,28},{16,0},{20,4},{24,8},{28,12},{1,17},{... | collective-permute-start | bytes 442376 | tf_op jit(solution)/shard_map/ppermute | solution.py:13
  13.4 12.5 %collective-permute-start.8 = (bf16[2,32,1152]{2,1,0:T(8,128)(2,1)S(1)}, bf16[2,32,1152]{2,1,0:T(8,128)(2,1)S(1)}, u32[]{:S(2)}, u32[]{:S(2)}) collective-permute-start(bf16[2,32,1152]{2,1,0:T(8,128)(2,1)S(1)} %get-tuple-element.10), channel_id=1, source_target_pairs={{0,8},{4,12},{8,0},{12,4},{16,24},{20,28},{24,16},{28,20},{1,9},{5... | collective-permute-start | bytes 442376 | tf_op jit(solution)/shard_map/ppermute | solution.py:13
  17.0 13.3 %collective-permute-start.10 = (bf16[2,32,1152]{2,1,0:T(8,128)(2,1)S(1)}, bf16[2,32,1152]{2,1,0:T(8,128)(2,1)S(1)}, u32[]{:S(2)}, u32[]{:S(2)}) collective-permute-start(bf16[2,32,1152]{2,1,0:T(8,128)(2,1)S(1)} %get-tuple-element.10), channel_id=1, source_target_pairs={{0,4},{4,0},{8,12},{12,8},{16,20},{20,16},{24,28},{28,24},{1,5},{5... | collective-permute-start | bytes 442376 | tf_op jit(solution)/shard_map/ppermute | solution.py:13
  17.8 5.8 %collective-permute-start.2 = (bf16[2,32,1152]{2,1,0:T(8,128)(2,1)S(1)}, bf16[2,32,1152]{2,1,0:T(8,128)(2,1)S(1)}, u32[]{:S(2)}, u32[]{:S(2)}) collective-permute-start(bf16[2,32,1152]{2,1,0:T(8,128)(2,1)S(1)} %collective-permute-done), channel_id=1, source_target_pairs={{0,16},{4,20},{8,24},{12,28},{16,0},{20,4},{24,8},{28,12},{1,17},{... | collective-permute-start | bytes 442376 | tf_op jit(solution)/shard_map/ppermute | solution.py:13
  23.6 2.4 %collective-permute-start.4 = (bf16[2,32,1152]{2,1,0:T(8,128)(2,1)S(1)}, bf16[2,32,1152]{2,1,0:T(8,128)(2,1)S(1)}, u32[]{:S(2)}, u32[]{:S(2)}) collective-permute-start(bf16[2,32,1152]{2,1,0:T(8,128)(2,1)S(1)} %collective-permute-done), channel_id=1, source_target_pairs={{0,4},{4,0},{8,12},{12,8},{16,20},{20,16},{24,28},{28,24},{1,5},{5... | collective-permute-start | bytes 442376 | tf_op jit(solution)/shard_map/ppermute | solution.py:13
  23.6 2.9 %collective-permute-start.5 = (bf16[2,32,1152]{2,1,0:T(8,128)(2,1)S(1)}, bf16[2,32,1152]{2,1,0:T(8,128)(2,1)S(1)}, u32[]{:S(2)}, u32[]{:S(2)}) collective-permute-start(bf16[2,32,1152]{2,1,0:T(8,128)(2,1)S(1)} %collective-permute-done.1), channel_id=1, source_target_pairs={{0,4},{4,0},{8,12},{12,8},{16,20},{20,16},{24,28},{28,24},{1,5},{5... | collective-permute-start | bytes 442376 | tf_op jit(solution)/shard_map/ppermute | solution.py:13
  24.2 5.8 %collective-permute-start.9 = (bf16[2,32,1152]{2,1,0:T(8,128)(2,1)S(1)}, bf16[2,32,1152]{2,1,0:T(8,128)(2,1)S(1)}, u32[]{:S(2)}, u32[]{:S(2)}) collective-permute-start(bf16[2,32,1152]{2,1,0:T(8,128)(2,1)S(1)} %collective-permute-done.7), channel_id=1, source_target_pairs={{0,8},{4,12},{8,0},{12,4},{16,24},{20,28},{24,16},{28,20},{1,9},{5... | collective-permute-start | bytes 442376 | tf_op jit(solution)/shard_map/ppermute | solution.py:13
  26.0 4.3 %collective-permute-start.11 = (bf16[2,32,1152]{2,1,0:T(8,128)(2,1)S(1)}, bf16[2,32,1152]{2,1,0:T(8,128)(2,1)S(1)}, u32[]{:S(2)}, u32[]{:S(2)}) collective-permute-start(bf16[2,32,1152]{2,1,0:T(8,128)(2,1)S(1)} %collective-permute-done.7), channel_id=1, source_target_pairs={{0,4},{4,0},{8,12},{12,8},{16,20},{20,16},{24,28},{28,24},{1,5},{5... | collective-permute-start | bytes 442376 | tf_op jit(solution)/shard_map/ppermute | solution.py:13
  26.0 4.3 %collective-permute-start.12 = (bf16[2,32,1152]{2,1,0:T(8,128)(2,1)S(1)}, bf16[2,32,1152]{2,1,0:T(8,128)(2,1)S(1)}, u32[]{:S(2)}, u32[]{:S(2)}) collective-permute-start(bf16[2,32,1152]{2,1,0:T(8,128)(2,1)S(1)} %collective-permute-done.8), channel_id=1, source_target_pairs={{0,4},{4,0},{8,12},{12,8},{16,20},{20,16},{24,28},{28,24},{1,5},{5... | collective-permute-start | bytes 442376 | tf_op jit(solution)/shard_map/ppermute | solution.py:13
  26.6 3.5 %collective-permute-start.6 = (bf16[2,32,1152]{2,1,0:T(8,128)(2,1)S(1)}, bf16[2,32,1152]{2,1,0:T(8,128)(2,1)S(1)}, u32[]{:S(2)}, u32[]{:S(2)}) collective-permute-start(bf16[2,32,1152]{2,1,0:T(8,128)(2,1)S(1)} %collective-permute-done.2), channel_id=1, source_target_pairs={{0,4},{4,0},{8,12},{12,8},{16,20},{20,16},{24,28},{28,24},{1,5},{5... | collective-permute-start | bytes 442376 | tf_op jit(solution)/shard_map/ppermute | solution.py:13
  30.0 1.4 %collective-permute-start.13 = (bf16[2,32,1152]{2,1,0:T(8,128)(2,1)S(1)}, bf16[2,32,1152]{2,1,0:T(8,128)(2,1)S(1)}, u32[]{:S(2)}, u32[]{:S(2)}) collective-permute-start(bf16[2,32,1152]{2,1,0:T(8,128)(2,1)S(1)} %collective-permute-done.9), channel_id=1, source_target_pairs={{0,4},{4,0},{8,12},{12,8},{16,20},{20,16},{24,28},{28,24},{1,5},{5... | collective-permute-start | bytes 442376 | tf_op jit(solution)/shard_map/ppermute | solution.py:13
  31.4 1.4 %copy-start = (bf16[2,8,64,1152]{3,2,1,0:T(8,128)(2,1)}, bf16[2,8,64,1152]{3,2,1,0:T(8,128)(2,1)S(1)}, u32[]{:S(2)}) copy-start(bf16[2,8,64,1152]{3,2,1,0:T(8,128)(2,1)S(1)} %bitcast_dynamic-update-slice_fusion) | copy-start | bytes 7077892
  37.2 1.4 %collective-permute-start.14 = (f32[3,1152]{1,0:T(4,128)}, f32[3,1152]{1,0:T(4,128)S(1)}, u32[]{:S(2)}, u32[]{:S(2)}) collective-permute-start(f32[3,1152]{1,0:T(4,128)} %get-tuple-element.7), channel_id=1, source_target_pairs={{0,4},{4,0},{8,12},{12,8},{16,20},{20,16},{24,28},{28,24},{1,5},{5... | collective-permute-start | bytes 41480 | tf_op jit(solution)/shard_map/ppermute | solution.py:13
  39.4 3.8 %collective-permute-start.15 = (f32[3,1152]{1,0:T(4,128)S(1)}, f32[3,1152]{1,0:T(4,128)S(1)}, u32[]{:S(2)}, u32[]{:S(2)}) collective-permute-start(f32[3,1152]{1,0:T(4,128)S(1)} %add.58), channel_id=1, source_target_pairs={{0,8},{4,12},{8,0},{12,4},{16,24},{20,28},{24,16},{28,20},{1,9},{5... | collective-permute-start | bytes 41480 | tf_op jit(solution)/shard_map/ppermute | solution.py:13
  43.1 3.8 %collective-permute-start.16 = (f32[3,1152]{1,0:T(4,128)S(1)}, f32[3,1152]{1,0:T(4,128)S(1)}, u32[]{:S(2)}, u32[]{:S(2)}) collective-permute-start(f32[3,1152]{1,0:T(4,128)S(1)} %add.59), channel_id=1, source_target_pairs={{0,16},{4,20},{8,24},{12,28},{16,0},{20,4},{24,8},{28,12},{1,17},{... | collective-permute-start | bytes 41480 | tf_op jit(solution)/shard_map/ppermute | solution.py:13
  46.9 3.8 %collective-permute-start.17 = (f32[3,1152]{1,0:T(4,128)S(1)}, f32[3,1152]{1,0:T(4,128)S(1)}, u32[]{:S(2)}, u32[]{:S(2)}) collective-permute-start(f32[3,1152]{1,0:T(4,128)S(1)} %add.60), channel_id=1, source_target_pairs={{0,1},{1,0},{2,3},{3,2},{4,5},{5,4},{6,7},{7,6},{8,9},{9,8},{10,11... | collective-permute-start | bytes 41480 | tf_op jit(solution)/shard_map/ppermute | solution.py:13
  50.7 4.7 %collective-permute-start.18 = (f32[3,1152]{1,0:T(4,128)S(1)}, f32[3,1152]{1,0:T(4,128)S(1)}, u32[]{:S(2)}, u32[]{:S(2)}) collective-permute-start(f32[3,1152]{1,0:T(4,128)S(1)} %add.61), channel_id=1, source_target_pairs={{0,2},{1,3},{2,0},{3,1},{4,6},{5,7},{6,4},{7,5},{8,10},{9,11},{10,... | collective-permute-start | bytes 41480 | tf_op jit(solution)/shard_map/ppermute | solution.py:13

commit v7 on v6

v7 whole, which is shorter than its diff:
```python
import functools

import jax
import jax.numpy as jnp
from jax import lax
from jax.sharding import PartitionSpec as P
from jax.experimental import pallas as pl
from jax.experimental.pallas import tpu as pltpu

epsilon = 1e-06


def xor_swap(value, axis, bit):
    count = lax.axis_size(axis)
    return lax.ppermute(value, axis, [(source, source ^ bit) for source in range(count)])


def power_of_two(count):
    return count > 1 and count & (count - 1) == 0


def gather_blocks(first, second, axis):
    count = lax.axis_size(axis)
    half = first.shape[1]
    if not power_of_two(count) or count < 4:
        own = lax.axis_index(axis)
        pieces = [lax.all_gather(part, axis, axis=1, tiled=False) for part in (first, second)]
        pieces = [
            lax.dynamic_index_in_dim(part, own ^ mask, axis=1, keepdims=False)
            for part in pieces
            for mask in range(count)
        ]
        return pieces, list(range(count)) * 2, [0] * count + [half] * count
    chip_bits = [1 << b for b in range(1, count.bit_length() - 1)]
    orders = (chip_bits, chip_bits[::-1])
    routed = ([first], [second])
    routed_masks = ([0], [0])
    fresh = ([0], [0])
    shared = ([], [])
    shared_masks = ([], [])
    for step in range(len(chip_bits) + 1):
        last = step == len(chip_bits)
        sent = [None, None]
        if not last:
            sent = [xor_swap(tuple(routed[h]), axis, orders[h][step]) for h in range(2)]
        across = [xor_swap(tuple(routed[h][i] for i in fresh[h]), axis, 1) for h in range(2)]
        for h in range(2):
            shared[h].extend(across[h])
            shared_masks[h].extend([routed_masks[h][i] ^ 1 for i in fresh[h]])
            if not last:
                bit = orders[h][step]
                fresh[h][:] = list(range(len(routed[h]), 2 * len(routed[h])))
                routed[h].extend(sent[h])
                routed_masks[h].extend([mask ^ bit for mask in routed_masks[h]])
    gathered = routed[0] + shared[0] + routed[1] + shared[1]
    masks = routed_masks[0] + shared_masks[0] + routed_masks[1] + shared_masks[1]
    offsets = [0] * count + [half] * count
    return gathered, masks, offsets


def all_sum(value, axes):
    for axis in axes:
        count = lax.axis_size(axis)
        if not power_of_two(count):
            value = lax.psum(value, axis)
            continue
        bit = 1
        while bit < count:
            value = value + xor_swap(value, axis, bit)
            bit *= 2
    return value


def embed_kernel(picture_ref, caption_ref, picture_gain_ref, caption_gain_ref, first_ref, second_ref):
    half = first_ref.shape[1]
    towers = ((picture_ref, picture_gain_ref), (caption_ref, caption_gain_ref))
    for tower, (pooled_ref, gain_ref) in enumerate(towers):
        values = pooled_ref[0].astype(jnp.float32)
        centred = values - jnp.mean(values, axis=-1, keepdims=True)
        inverse = lax.rsqrt(jnp.mean(centred * centred, axis=-1, keepdims=True) + epsilon)
        scaled = centred * inverse * gain_ref[...][None, :]
        inv_length = lax.rsqrt(jnp.sum(scaled * scaled, axis=-1, keepdims=True) + epsilon)
        unit_rows = (scaled * inv_length).astype(first_ref.dtype)
        first_ref[tower] = unit_rows[:half]
        second_ref[tower] = unit_rows[half:]


def embed_both(picture, caption, picture_gain, caption_gain):
    rows, width = picture.shape[1:]
    vmem = pltpu.MemorySpace.VMEM
    half = jax.ShapeDtypeStruct((2, rows // 2, width), jnp.bfloat16)
    return pl.pallas_call(
        embed_kernel,
        out_shape=(half, half),
        in_specs=[pl.BlockSpec(memory_space=vmem)] * 4,
        out_specs=(pl.BlockSpec(memory_space=vmem), pl.BlockSpec(memory_space=vmem)),
    )(picture, caption, picture_gain, caption_gain)


def grad_kernel(masks, offsets, *refs):
    (sharpness_ref, shift_ref, multiplier_ref, counts_ref, picture_ref, caption_ref, picture_gain_ref,
     caption_gain_ref, gathered_ref, partner_ref, image_grad_ref, text_grad_ref, sums_ref) = refs
    blocks = counts_ref.shape[1]
    own_block = lax.axis_index("blk")
    group_index = lax.axis_index("rep")
    block_rows = picture_ref.shape[1]
    width = picture_ref.shape[2]
    piece = gathered_ref.shape[1] // len(masks)
    group_rows = gathered_ref.shape[1]
    own_start = own_block * block_rows
    total = counts_ref[0, 0]
    for block in range(1, blocks):
        total = total + counts_ref[0, block]
    real_count = jnp.full((1, 1), total, jnp.int32).astype(jnp.float32)
    score_sharpness_factor = jnp.exp(jnp.full((1, 1), sharpness_ref[0], jnp.float32))
    score_shift_amount = jnp.full((1, 1), shift_ref[0], jnp.float32)
    grad_factor = jnp.full((1, 1), multiplier_ref[0], jnp.float32) / real_count

    lane = lax.broadcasted_iota(jnp.int32, (1, group_rows), 1)
    held_row = jnp.zeros((1, group_rows), jnp.int32)
    limit = jnp.zeros((1, group_rows), jnp.int32)
    for position, (mask, offset) in enumerate(zip(masks, offsets)):
        block = own_block ^ mask
        here = lane // piece == position
        held_row = jnp.where(here, block * block_rows + offset + lane % piece, held_row)
        limit = jnp.where(here, counts_ref[0, block], limit)
    real_group = (held_row % block_rows) < limit
    sub = lax.broadcasted_iota(jnp.int32, (block_rows, 1), 0)
    real_own = sub < counts_ref[0, own_block]
    kept = real_own & real_group

    natural = lax.broadcasted_iota(jnp.int32, (block_rows, group_rows), 1)
    own_index = own_start + lax.broadcasted_iota(jnp.int32, (block_rows, group_rows), 0)
    partner_row = partner_ref[...]
    own_partner = jnp.sum(
        jnp.where(natural == own_index, partner_row.astype(jnp.float32), 0.0), axis=1, keepdims=True
    ).astype(jnp.int32)
    matched_image = jnp.sum(
        jnp.where(partner_row == own_index, natural.astype(jnp.float32), 0.0), axis=1, keepdims=True
    ).astype(jnp.int32)
    positives = (own_partner == held_row, matched_image == held_row)

    start_b = len(masks) // 2 * piece
    loss_rows = []
    towers = ((picture_ref, picture_gain_ref, image_grad_ref), (caption_ref, caption_gain_ref, text_grad_ref))
    for tower, (pooled_ref, gain_ref, grad_ref) in enumerate(towers):
        values = pooled_ref[0].astype(jnp.float32)
        gain = gain_ref[...][None, :]
        centred = values - jnp.mean(values, axis=-1, keepdims=True)
        inverse = lax.rsqrt(jnp.mean(centred * centred, axis=-1, keepdims=True) + epsilon)
        normed = centred * inverse
        scaled = normed * gain
        inv_length = lax.rsqrt(jnp.sum(scaled * scaled, axis=-1, keepdims=True) + epsilon)
        unit_rows = scaled * inv_length

        own = jnp.concatenate(
            [gathered_ref[tower, 0:piece, :], gathered_ref[tower, start_b : start_b + piece, :]], axis=0
        )
        other = gathered_ref[1 - tower]
        scores = lax.dot_general(own, other, (((1,), (1,)), ((), ())), preferred_element_type=jnp.float32)
        score_similarity_table = score_sharpness_factor * scores + score_shift_amount
        labels = jnp.where(positives[tower], 1.0, -1.0)
        margin = -labels * score_similarity_table
        if tower == 0:
            softplus = jnp.maximum(margin, 0.0) + jnp.log1p(jnp.exp(-jnp.abs(margin)))
            loss_rows.append(jnp.sum(jnp.where(kept, softplus, 0.0), axis=(0, 1), keepdims=True))
        weights = jnp.where(kept, -labels * jax.nn.sigmoid(margin), 0.0) * grad_factor
        direction = score_sharpness_factor * jnp.dot(
            weights.astype(jnp.bfloat16), other, preferred_element_type=jnp.float32
        )
        tangent = (
            direction - unit_rows * jnp.sum(unit_rows * direction, axis=-1, keepdims=True)
        ) * inv_length
        sums_ref[tower : tower + 1, :] = jnp.sum(tangent * normed, axis=0, keepdims=True)
        scaled_back = tangent * gain
        gradient = (
            scaled_back
            - jnp.mean(scaled_back, axis=-1, keepdims=True)
            - normed * jnp.mean(scaled_back * normed, axis=-1, keepdims=True)
        ) * inverse
        grad_ref[0] = gradient.astype(grad_ref.dtype)
    group_lane = lax.broadcasted_iota(jnp.int32, (1, width), 1)
    sums_ref[2:3, :] = jnp.where(group_lane == group_index, loss_rows[0] / real_count, 0.0)


def shards(
    picture_averaged_features,
    caption_averaged_features,
    picture_rescale_factor,
    caption_rescale_factor,
    exponent_of_sharpness,
    score_shift_term,
    objective_multiplier,
    matching_caption_index,
    genuine_entry_counts,
):
    width = picture_averaged_features.shape[2]
    first, second = embed_both(
        picture_averaged_features, caption_averaged_features, picture_rescale_factor, caption_rescale_factor
    )
    pieces, masks, offsets = gather_blocks(first, second, "blk")
    gathered = jnp.concatenate(pieces, axis=1)

    smem = pltpu.MemorySpace.SMEM
    vmem = pltpu.MemorySpace.VMEM
    grad_shape = jax.ShapeDtypeStruct(picture_averaged_features.shape, jnp.bfloat16)
    image_grad, text_grad, sums = pl.pallas_call(
        functools.partial(grad_kernel, tuple(masks), tuple(offsets)),
        out_shape=(grad_shape, grad_shape, jax.ShapeDtypeStruct((3, width), jnp.float32)),
        in_specs=[pl.BlockSpec(memory_space=smem)] * 4 + [pl.BlockSpec(memory_space=vmem)] * 6,
        out_specs=(pl.BlockSpec(memory_space=vmem),) * 3,
    )(
        exponent_of_sharpness,
        score_shift_term,
        objective_multiplier,
        genuine_entry_counts,
        picture_averaged_features,
        caption_averaged_features,
        picture_rescale_factor,
        caption_rescale_factor,
        gathered,
        matching_caption_index,
    )

    total = all_sum(sums, ("blk", "rep"))
    gain_grads = total[:2]
    group_loss = lax.dynamic_slice_in_dim(total[2], lax.axis_index("rep"), 1)
    return (image_grad, text_grad, gain_grads, group_loss)


def solution(mesh):
    placed = (
        P("rep", "blk", None),
        P("rep", "blk", None),
        P(),
        P(),
        P(),
        P(),
        P(),
        P("rep", None),
        P("rep", None),
    )
    return jax.shard_map(
        shards,
        mesh=mesh,
        in_specs=placed,
        out_specs=(P("rep", "blk", None), P("rep", "blk", None), P(), P("rep")),
        check_vma=False,
    )
```

time: 57 us -> 50.9 us (0.89)
  local copies, waits for them, and re-layouts: 10 us -> 3.84 us
  waiting for transfers between devices: 16.2 us -> 18.6 us
  other arithmetic: 2.6 us -> 0.75 us
    slice x3 -> x1, local copies, waits for them, and re-layouts: 3.43 us -> 0.01 us  [shards(): group_loss = lax.dynamic_slice_in_dim(total[2], lax.axis_index('rep'), 1)]
    ppermute x19, waiting for transfers between devices: 16.2 us -> 18.6 us  [xor_swap(): lax.ppermute(value, axis, [(source, source ^ bit) for source in range(cou...]
    another operation x2 -> x0, local copies, waits for them, and re-layouts: 1.4 us -> none  [shards(): gains = jnp.stack([picture_rescale_factor, caption_rescale_factor])]
    concatenate x2 -> x0, other arithmetic: 1.18 us -> none  [the longest x1 0.59 us: shards(): jnp.concatenate([genuine_entry_counts[0], jnp.stack([own_block, group_ind...]
    concatenate x1, local copies, waits for them, and re-layouts: 0.93 us -> 0.02 us  [shards(): gathered = jnp.concatenate(pieces, axis=1)]
    another operation x1 -> x0, other arithmetic: 0.67 us -> none  [shards(): gains = jnp.stack([picture_rescale_factor, caption_rescale_factor])]
    unnamed x9 -> x19, local copies, waits for them, and re-layouts: 2.42 us -> 2.63 us
  transfers between devices with their start and end apart: 19 -> 19, of which waited for: 9 -> 9; matrix products, arithmetic and copies ran while one was open for 6% -> 2% of each run, Pallas kernels for 0% -> 0%
where the time goes in v7:
time: 50.9 us; the launch traced here: 50.6 us
  waiting for transfers between devices  18.6 us (37%)
  starting transfers between devices  18 us (35%)
  Pallas kernels  6.56 us (13%)
  local copies, waits for them, and re-layouts  3.84 us (8%)
  between operations  2.75 us (5%)
  other arithmetic  0.75 us (1%)
    ppermute x19, waiting for transfers between devices, xor_swap(): lax.ppermute(value, axis, [(source, source ^ bit) for source in range(cou...  18.6 us
    ppermute x19, starting transfers between devices, xor_swap(): lax.ppermute(value, axis, [(source, source ^ bit) for source in range(cou...  18 us
    pallas_call x1, Pallas kernels, shards(): pl.pallas_call(functools.partial(grad_kernel, tuple(masks), tuple(offsets...  4.5 us
    unnamed x19, local copies, waits for them, and re-layouts  2.63 us
    pallas_call x1, Pallas kernels, embed_both(): pl.pallas_call(embed_kernel, out_shape=(half, half), in_specs=[pl.BlockSp...  2.06 us
  transfers between devices with their start and end apart: 19, of which 9 were waited for; matrix products, arithmetic and copies ran while one was open for 2% of the time, Pallas kernels for 0%

profile of v7, /device:TPU:0, one launch (start us, length us, event | category | flops | bytes accessed | tf_op | source)
XLA Modules:
  0.0 50.6 jit_solution(14888044438603215323)
XLA Ops:
  0.6 2.1 %shard_map.120 = (bf16[2,32,1152]{2,1,0:T(8,128)(2,1)}, bf16[2,32,1152]{2,1,0:T(8,128)(2,1)}) custom-call(bf16[1,64,1152]{2,1,0:T(8,128)(2,1)} %refs_4_.1, bf16[1,64,1152]{2,1,0:T(8,128)(2,1)} %refs_5_.1, f32[1152]{0:T(1024)} %refs_6_.1, f32[1152]{0:T(1024)} %refs_7_.1), custom_call_target="tpu_custom_call" | custom-call | tf_op jit(solution)/shard_map/pallas_call | solution.py:92
  2.7 3.0 %collective-permute-start = (bf16[2,32,1152]{2,1,0:T(8,128)(2,1)}, bf16[2,32,1152]{2,1,0:T(8,128)(2,1)S(1)}, u32[]{:S(2)}, u32[]{:S(2)}) collective-permute-start(bf16[2,32,1152]{2,1,0:T(8,128)(2,1)} %get-tuple-element.9), channel_id=1, source_target_pairs={{0,8},{4,12},{8,0},{12,4},{16,24},{20,28},{24,16},{28,20},{1,9},{5... | collective-permute-start | bytes 442376 | tf_op jit(solution)/shard_map/ppermute | solution.py:15
  5.7 1.5 %collective-permute-start.1 = (bf16[2,32,1152]{2,1,0:T(8,128)(2,1)}, bf16[2,32,1152]{2,1,0:T(8,128)(2,1)S(1)}, u32[]{:S(2)}, u32[]{:S(2)}) collective-permute-start(bf16[2,32,1152]{2,1,0:T(8,128)(2,1)} %get-tuple-element.9), channel_id=1, source_target_pairs={{0,16},{4,20},{8,24},{12,28},{16,0},{20,4},{24,8},{28,12},{1,17},{... | collective-permute-start | bytes 442376 | tf_op jit(solution)/shard_map/ppermute | solution.py:15
  9.7 0.9 %constant_dynamic-update-slice_fusion.15 = bf16[2,512,1152]{2,1,0:T(8,128)(2,1)S(1)} fusion(bf16[2,32,1152]{2,1,0:T(8,128)(2,1)} %get-tuple-element.9), kind=kLoop, calls=%fused_computation.15 | loop fusion | bytes 294912
  10.9 0.9 %collective-permute-done.1 = bf16[2,32,1152]{2,1,0:T(8,128)(2,1)S(1)} collective-permute-done((bf16[2,32,1152]{2,1,0:T(8,128)(2,1)}, bf16[2,32,1152]{2,1,0:T(8,128)(2,1)S(1)}, u32[]{:S(2)}, u32[]{:S(2)}) %collective-permute-start.1) | collective-permute-done | bytes 147488 | tf_op jit(solution)/shard_map/ppermute | solution.py:15
  11.9 2.2 %collective-permute-start.2 = (bf16[2,32,1152]{2,1,0:T(8,128)(2,1)S(1)}, bf16[2,32,1152]{2,1,0:T(8,128)(2,1)S(1)}, u32[]{:S(2)}, u32[]{:S(2)}) collective-permute-start(bf16[2,32,1152]{2,1,0:T(8,128)(2,1)S(1)} %collective-permute-done), channel_id=1, source_target_pairs={{0,16},{4,20},{8,24},{12,28},{16,0},{20,4},{24,8},{28,12},{1,17},{... | collective-permute-start | bytes 442376 | tf_op jit(solution)/shard_map/ppermute | solution.py:15
  14.1 3.4 %collective-permute-done.2 = bf16[2,32,1152]{2,1,0:T(8,128)(2,1)S(1)} collective-permute-done((bf16[2,32,1152]{2,1,0:T(8,128)(2,1)S(1)}, bf16[2,32,1152]{2,1,0:T(8,128)(2,1)S(1)}, u32[]{:S(2)}, u32[]{:S(2)}) %collective-permute-start.2) | collective-permute-done | bytes 147488 | tf_op jit(solution)/shard_map/ppermute | solution.py:15
  18.1 1.5 %collective-permute-start.9 = (bf16[2,32,1152]{2,1,0:T(8,128)(2,1)S(1)}, bf16[2,32,1152]{2,1,0:T(8,128)(2,1)S(1)}, u32[]{:S(2)}, u32[]{:S(2)}) collective-permute-start(bf16[2,32,1152]{2,1,0:T(8,128)(2,1)S(1)} %collective-permute-done.7), channel_id=1, source_target_pairs={{0,8},{4,12},{8,0},{12,4},{16,24},{20,28},{24,16},{28,20},{1,9},{5... | collective-permute-start | bytes 442376 | tf_op jit(solution)/shard_map/ppermute | solution.py:15
  20.4 3.5 %collective-permute-done.9 = bf16[2,32,1152]{2,1,0:T(8,128)(2,1)S(1)} collective-permute-done((bf16[2,32,1152]{2,1,0:T(8,128)(2,1)S(1)}, bf16[2,32,1152]{2,1,0:T(8,128)(2,1)S(1)}, u32[]{:S(2)}, u32[]{:S(2)}) %collective-permute-start.9) | collective-permute-done | bytes 147488 | tf_op jit(solution)/shard_map/ppermute | solution.py:15
  24.2 1.1 %collective-permute-done.13 = bf16[2,32,1152]{2,1,0:T(8,128)(2,1)S(1)} collective-permute-done((bf16[2,32,1152]{2,1,0:T(8,128)(2,1)S(1)}, bf16[2,32,1152]{2,1,0:T(8,128)(2,1)S(1)}, u32[]{:S(2)}, u32[]{:S(2)}) %collective-permute-start.13) | collective-permute-done | bytes 147488 | tf_op jit(solution)/shard_map/ppermute | solution.py:15
  25.3 1.4 %copy-done = bf16[2,512,1152]{2,1,0:T(8,128)(2,1)} copy-done((bf16[2,512,1152]{2,1,0:T(8,128)(2,1)}, bf16[2,512,1152]{2,1,0:T(8,128)(2,1)S(1)}, u32[]{:S(2)}) %copy-start) | copy-done | bytes 2359320
  26.8 4.5 %shard_map.121 = (bf16[1,64,1152]{2,1,0:T(8,128)(2,1)}, bf16[1,64,1152]{2,1,0:T(8,128)(2,1)}, f32[3,1152]{1,0:T(4,128)}) custom-call(f32[1]{0:T(128)S(6)} %copy.28.refs_0_, f32[1]{0:T(128)S(6)} %copy.29.refs_1_, f32[1]{0:T(128)S(6)} %copy.30.refs_2_, s32[1,8]{1,0:T(1,128)} %refs_3_.1, bf16[1,64,1152]{2,1,0:T(8,128)(2,1)} %refs_4_.1, ...), custom_call_target="tpu_custom_call" | custom-call | tf_op jit(solution)/shard_map/pallas_call | solution.py:207
  31.4 1.3 %collective-permute-done.14 = f32[3,1152]{1,0:T(4,128)S(1)} collective-permute-done((f32[3,1152]{1,0:T(4,128)}, f32[3,1152]{1,0:T(4,128)S(1)}, u32[]{:S(2)}, u32[]{:S(2)}) %collective-permute-start.14) | collective-permute-done | bytes 13856 | tf_op jit(solution)/shard_map/ppermute | solution.py:15
  32.7 0.7 %add.18 = f32[3,1152]{1,0:T(4,128)S(1)} add(f32[3,1152]{1,0:T(4,128)} %get-tuple-element.13, f32[3,1152]{1,0:T(4,128)S(1)} %collective-permute-done.14) | non-fusion elementwise | flops 3456 | bytes 41472 | tf_op jit(solution)/shard_map/add | solution.py:69
  33.4 1.5 %collective-permute-start.15 = (f32[3,1152]{1,0:T(4,128)S(1)}, f32[3,1152]{1,0:T(4,128)S(1)}, u32[]{:S(2)}, u32[]{:S(2)}) collective-permute-start(f32[3,1152]{1,0:T(4,128)S(1)} %add.18), channel_id=1, source_target_pairs={{0,8},{4,12},{8,0},{12,4},{16,24},{20,28},{24,16},{28,20},{1,9},{5... | collective-permute-start | bytes 41480 | tf_op jit(solution)/shard_map/ppermute | solution.py:15
  34.9 2.2 %collective-permute-done.15 = f32[3,1152]{1,0:T(4,128)S(1)} collective-permute-done((f32[3,1152]{1,0:T(4,128)S(1)}, f32[3,1152]{1,0:T(4,128)S(1)}, u32[]{:S(2)}, u32[]{:S(2)}) %collective-permute-start.15) | collective-permute-done | bytes 13856 | tf_op jit(solution)/shard_map/ppermute | solution.py:15
  37.2 1.8 %collective-permute-start.16 = (f32[3,1152]{1,0:T(4,128)S(1)}, f32[3,1152]{1,0:T(4,128)S(1)}, u32[]{:S(2)}, u32[]{:S(2)}) collective-permute-start(f32[3,1152]{1,0:T(4,128)S(1)} %add.19), channel_id=1, source_target_pairs={{0,16},{4,20},{8,24},{12,28},{16,0},{20,4},{24,8},{28,12},{1,17},{... | collective-permute-start | bytes 41480 | tf_op jit(solution)/shard_map/ppermute | solution.py:15
  38.9 2.0 %collective-permute-done.16 = f32[3,1152]{1,0:T(4,128)S(1)} collective-permute-done((f32[3,1152]{1,0:T(4,128)S(1)}, f32[3,1152]{1,0:T(4,128)S(1)}, u32[]{:S(2)}, u32[]{:S(2)}) %collective-permute-start.16) | collective-permute-done | bytes 13856 | tf_op jit(solution)/shard_map/ppermute | solution.py:15
  40.9 1.6 %collective-permute-start.17 = (f32[3,1152]{1,0:T(4,128)S(1)}, f32[3,1152]{1,0:T(4,128)S(1)}, u32[]{:S(2)}, u32[]{:S(2)}) collective-permute-start(f32[3,1152]{1,0:T(4,128)S(1)} %add.20), channel_id=1, source_target_pairs={{0,1},{1,0},{2,3},{3,2},{4,5},{5,4},{6,7},{7,6},{8,9},{9,8},{10,11... | collective-permute-start | bytes 41480 | tf_op jit(solution)/shard_map/ppermute | solution.py:15
  42.6 2.1 %collective-permute-done.17 = f32[3,1152]{1,0:T(4,128)S(1)} collective-permute-done((f32[3,1152]{1,0:T(4,128)S(1)}, f32[3,1152]{1,0:T(4,128)S(1)}, u32[]{:S(2)}, u32[]{:S(2)}) %collective-permute-start.17) | collective-permute-done | bytes 13856 | tf_op jit(solution)/shard_map/ppermute | solution.py:15
  44.7 2.6 %collective-permute-start.18 = (f32[3,1152]{1,0:T(4,128)S(1)}, f32[3,1152]{1,0:T(4,128)S(1)}, u32[]{:S(2)}, u32[]{:S(2)}) collective-permute-start(f32[3,1152]{1,0:T(4,128)S(1)} %add.21), channel_id=1, source_target_pairs={{0,2},{1,3},{2,0},{3,1},{4,6},{5,7},{6,4},{7,5},{8,10},{9,11},{10,... | collective-permute-start | bytes 41480 | tf_op jit(solution)/shard_map/ppermute | solution.py:15
  47.3 2.0 %collective-permute-done.18 = f32[3,1152]{1,0:T(4,128)S(1)} collective-permute-done((f32[3,1152]{1,0:T(4,128)S(1)}, f32[3,1152]{1,0:T(4,128)S(1)}, u32[]{:S(2)}, u32[]{:S(2)}) %collective-permute-start.18) | collective-permute-done | bytes 13856 | tf_op jit(solution)/shard_map/ppermute | solution.py:15
  49.4 0.6 %slice.8 = f32[2,1152]{1,0:T(2,128)} slice(f32[3,1152]{1,0:T(4,128)S(1)} %add.22), slice={[0:2], [0:1152]} | slice | bytes 18432 | tf_op jit(solution)/shard_map/slice | solution.py:226
  50.0 0.6 %constant_dynamic-slice_fusion = f32[1,1]{1,0:T(1,128)} fusion(f32[1,1152]{1,0:T(1,128)S(1)} %slice.9, s32[]{:T(128)S(6)} %select_n.3), kind=kLoop, calls=%fused_computation.16 | loop fusion | bytes 12 | tf_op jit(solution)/shard_map/dynamic_slice | solution.py:227
  (44 shorter events, 2.6 us)
Async XLA Ops:
  2.7 21.3 %copy-start.1 = (bf16[2,32,1152]{2,1,0:T(8,128)(2,1)S(1)}, bf16[2,32,1152]{2,1,0:T(8,128)(2,1)}, u32[]{:S(2)}) copy-start(bf16[2,32,1152]{2,1,0:T(8,128)(2,1)} %get-tuple-element.10) | copy-start | bytes 442372
  2.7 7.9 %collective-permute-start = (bf16[2,32,1152]{2,1,0:T(8,128)(2,1)}, bf16[2,32,1152]{2,1,0:T(8,128)(2,1)S(1)}, u32[]{:S(2)}, u32[]{:S(2)}) collective-permute-start(bf16[2,32,1152]{2,1,0:T(8,128)(2,1)} %get-tuple-element.9), channel_id=1, source_target_pairs={{0,8},{4,12},{8,0},{12,4},{16,24},{20,28},{24,16},{28,20},{1,9},{5... | collective-permute-start | bytes 442376 | tf_op jit(solution)/shard_map/ppermute | solution.py:15
  5.7 6.2 %collective-permute-start.1 = (bf16[2,32,1152]{2,1,0:T(8,128)(2,1)}, bf16[2,32,1152]{2,1,0:T(8,128)(2,1)S(1)}, u32[]{:S(2)}, u32[]{:S(2)}) collective-permute-start(bf16[2,32,1152]{2,1,0:T(8,128)(2,1)} %get-tuple-element.9), channel_id=1, source_target_pairs={{0,16},{4,20},{8,24},{12,28},{16,0},{20,4},{24,8},{28,12},{1,17},{... | collective-permute-start | bytes 442376 | tf_op jit(solution)/shard_map/ppermute | solution.py:15
  7.2 10.3 %collective-permute-start.3 = (bf16[2,32,1152]{2,1,0:T(8,128)(2,1)}, bf16[2,32,1152]{2,1,0:T(8,128)(2,1)S(1)}, u32[]{:S(2)}, u32[]{:S(2)}) collective-permute-start(bf16[2,32,1152]{2,1,0:T(8,128)(2,1)} %get-tuple-element.9), channel_id=1, source_target_pairs={{0,4},{4,0},{8,12},{12,8},{16,20},{20,16},{24,28},{28,24},{1,5},{5... | collective-permute-start | bytes 442376 | tf_op jit(solution)/shard_map/ppermute | solution.py:15
  7.2 10.9 %collective-permute-start.7 = (bf16[2,32,1152]{2,1,0:T(8,128)(2,1)}, bf16[2,32,1152]{2,1,0:T(8,128)(2,1)S(1)}, u32[]{:S(2)}, u32[]{:S(2)}) collective-permute-start(bf16[2,32,1152]{2,1,0:T(8,128)(2,1)} %get-tuple-element.10), channel_id=1, source_target_pairs={{0,16},{4,20},{8,24},{12,28},{16,0},{20,4},{24,8},{28,12},{1,17},{... | collective-permute-start | bytes 442376 | tf_op jit(solution)/shard_map/ppermute | solution.py:15
  7.7 12.0 %collective-permute-start.8 = (bf16[2,32,1152]{2,1,0:T(8,128)(2,1)}, bf16[2,32,1152]{2,1,0:T(8,128)(2,1)S(1)}, u32[]{:S(2)}, u32[]{:S(2)}) collective-permute-start(bf16[2,32,1152]{2,1,0:T(8,128)(2,1)} %get-tuple-element.10), channel_id=1, source_target_pairs={{0,8},{4,12},{8,0},{12,4},{16,24},{20,28},{24,16},{28,20},{1,9},{5... | collective-permute-start | bytes 442376 | tf_op jit(solution)/shard_map/ppermute | solution.py:15
  10.6 13.5 %collective-permute-start.10 = (bf16[2,32,1152]{2,1,0:T(8,128)(2,1)}, bf16[2,32,1152]{2,1,0:T(8,128)(2,1)S(1)}, u32[]{:S(2)}, u32[]{:S(2)}) collective-permute-start(bf16[2,32,1152]{2,1,0:T(8,128)(2,1)} %get-tuple-element.10), channel_id=1, source_target_pairs={{0,4},{4,0},{8,12},{12,8},{16,20},{20,16},{24,28},{28,24},{1,5},{5... | collective-permute-start | bytes 442376 | tf_op jit(solution)/shard_map/ppermute | solution.py:15
  11.9 5.6 %collective-permute-start.2 = (bf16[2,32,1152]{2,1,0:T(8,128)(2,1)S(1)}, bf16[2,32,1152]{2,1,0:T(8,128)(2,1)S(1)}, u32[]{:S(2)}, u32[]{:S(2)}) collective-permute-start(bf16[2,32,1152]{2,1,0:T(8,128)(2,1)S(1)} %collective-permute-done), channel_id=1, source_target_pairs={{0,16},{4,20},{8,24},{12,28},{16,0},{20,4},{24,8},{28,12},{1,17},{... | collective-permute-start | bytes 442376 | tf_op jit(solution)/shard_map/ppermute | solution.py:15
  17.5 2.2 %collective-permute-start.4 = (bf16[2,32,1152]{2,1,0:T(8,128)(2,1)S(1)}, bf16[2,32,1152]{2,1,0:T(8,128)(2,1)S(1)}, u32[]{:S(2)}, u32[]{:S(2)}) collective-permute-start(bf16[2,32,1152]{2,1,0:T(8,128)(2,1)S(1)} %collective-permute-done), channel_id=1, source_target_pairs={{0,4},{4,0},{8,12},{12,8},{16,20},{20,16},{24,28},{28,24},{1,5},{5... | collective-permute-start | bytes 442376 | tf_op jit(solution)/shard_map/ppermute | solution.py:15
  17.5 2.7 %collective-permute-start.5 = (bf16[2,32,1152]{2,1,0:T(8,128)(2,1)S(1)}, bf16[2,32,1152]{2,1,0:T(8,128)(2,1)S(1)}, u32[]{:S(2)}, u32[]{:S(2)}) collective-permute-start(bf16[2,32,1152]{2,1,0:T(8,128)(2,1)S(1)} %collective-permute-done.1), channel_id=1, source_target_pairs={{0,4},{4,0},{8,12},{12,8},{16,20},{20,16},{24,28},{28,24},{1,5},{5... | collective-permute-start | bytes 442376 | tf_op jit(solution)/shard_map/ppermute | solution.py:15
  18.1 5.8 %collective-permute-start.9 = (bf16[2,32,1152]{2,1,0:T(8,128)(2,1)S(1)}, bf16[2,32,1152]{2,1,0:T(8,128)(2,1)S(1)}, u32[]{:S(2)}, u32[]{:S(2)}) collective-permute-start(bf16[2,32,1152]{2,1,0:T(8,128)(2,1)S(1)} %collective-permute-done.7), channel_id=1, source_target_pairs={{0,8},{4,12},{8,0},{12,4},{16,24},{20,28},{24,16},{28,20},{1,9},{5... | collective-permute-start | bytes 442376 | tf_op jit(solution)/shard_map/ppermute | solution.py:15
  19.7 4.5 %collective-permute-start.11 = (bf16[2,32,1152]{2,1,0:T(8,128)(2,1)S(1)}, bf16[2,32,1152]{2,1,0:T(8,128)(2,1)S(1)}, u32[]{:S(2)}, u32[]{:S(2)}) collective-permute-start(bf16[2,32,1152]{2,1,0:T(8,128)(2,1)S(1)} %collective-permute-done.7), channel_id=1, source_target_pairs={{0,4},{4,0},{8,12},{12,8},{16,20},{20,16},{24,28},{28,24},{1,5},{5... | collective-permute-start | bytes 442376 | tf_op jit(solution)/shard_map/ppermute | solution.py:15
  19.7 4.4 %collective-permute-start.12 = (bf16[2,32,1152]{2,1,0:T(8,128)(2,1)S(1)}, bf16[2,32,1152]{2,1,0:T(8,128)(2,1)S(1)}, u32[]{:S(2)}, u32[]{:S(2)}) collective-permute-start(bf16[2,32,1152]{2,1,0:T(8,128)(2,1)S(1)} %collective-permute-done.8), channel_id=1, source_target_pairs={{0,4},{4,0},{8,12},{12,8},{16,20},{20,16},{24,28},{28,24},{1,5},{5... | collective-permute-start | bytes 442376 | tf_op jit(solution)/shard_map/ppermute | solution.py:15
  20.3 3.7 %collective-permute-start.6 = (bf16[2,32,1152]{2,1,0:T(8,128)(2,1)S(1)}, bf16[2,32,1152]{2,1,0:T(8,128)(2,1)S(1)}, u32[]{:S(2)}, u32[]{:S(2)}) collective-permute-start(bf16[2,32,1152]{2,1,0:T(8,128)(2,1)S(1)} %collective-permute-done.2), channel_id=1, source_target_pairs={{0,4},{4,0},{8,12},{12,8},{16,20},{20,16},{24,28},{28,24},{1,5},{5... | collective-permute-start | bytes 442376 | tf_op jit(solution)/shard_map/ppermute | solution.py:15
  23.9 1.4 %collective-permute-start.13 = (bf16[2,32,1152]{2,1,0:T(8,128)(2,1)S(1)}, bf16[2,32,1152]{2,1,0:T(8,128)(2,1)S(1)}, u32[]{:S(2)}, u32[]{:S(2)}) collective-permute-start(bf16[2,32,1152]{2,1,0:T(8,128)(2,1)S(1)} %collective-permute-done.9), channel_id=1, source_target_pairs={{0,4},{4,0},{8,12},{12,8},{16,20},{20,16},{24,28},{28,24},{1,5},{5... | collective-permute-start | bytes 442376 | tf_op jit(solution)/shard_map/ppermute | solution.py:15
  25.3 1.4 %copy-start = (bf16[2,512,1152]{2,1,0:T(8,128)(2,1)}, bf16[2,512,1152]{2,1,0:T(8,128)(2,1)S(1)}, u32[]{:S(2)}) copy-start(bf16[2,512,1152]{2,1,0:T(8,128)(2,1)S(1)} %constant_dynamic-update-slice_fusion.refs_8_) | copy-start | bytes 7077892
  31.3 1.4 %collective-permute-start.14 = (f32[3,1152]{1,0:T(4,128)}, f32[3,1152]{1,0:T(4,128)S(1)}, u32[]{:S(2)}, u32[]{:S(2)}) collective-permute-start(f32[3,1152]{1,0:T(4,128)} %get-tuple-element.13), channel_id=1, source_target_pairs={{0,4},{4,0},{8,12},{12,8},{16,20},{20,16},{24,28},{28,24},{1,5},{5... | collective-permute-start | bytes 41480 | tf_op jit(solution)/shard_map/ppermute | solution.py:15
  33.4 3.8 %collective-permute-start.15 = (f32[3,1152]{1,0:T(4,128)S(1)}, f32[3,1152]{1,0:T(4,128)S(1)}, u32[]{:S(2)}, u32[]{:S(2)}) collective-permute-start(f32[3,1152]{1,0:T(4,128)S(1)} %add.18), channel_id=1, source_target_pairs={{0,8},{4,12},{8,0},{12,4},{16,24},{20,28},{24,16},{28,20},{1,9},{5... | collective-permute-start | bytes 41480 | tf_op jit(solution)/shard_map/ppermute | solution.py:15
  37.2 3.8 %collective-permute-start.16 = (f32[3,1152]{1,0:T(4,128)S(1)}, f32[3,1152]{1,0:T(4,128)S(1)}, u32[]{:S(2)}, u32[]{:S(2)}) collective-permute-start(f32[3,1152]{1,0:T(4,128)S(1)} %add.19), channel_id=1, source_target_pairs={{0,16},{4,20},{8,24},{12,28},{16,0},{20,4},{24,8},{28,12},{1,17},{... | collective-permute-start | bytes 41480 | tf_op jit(solution)/shard_map/ppermute | solution.py:15
  40.9 3.8 %collective-permute-start.17 = (f32[3,1152]{1,0:T(4,128)S(1)}, f32[3,1152]{1,0:T(4,128)S(1)}, u32[]{:S(2)}, u32[]{:S(2)}) collective-permute-start(f32[3,1152]{1,0:T(4,128)S(1)} %add.20), channel_id=1, source_target_pairs={{0,1},{1,0},{2,3},{3,2},{4,5},{5,4},{6,7},{7,6},{8,9},{9,8},{10,11... | collective-permute-start | bytes 41480 | tf_op jit(solution)/shard_map/ppermute | solution.py:15
  44.7 4.7 %collective-permute-start.18 = (f32[3,1152]{1,0:T(4,128)S(1)}, f32[3,1152]{1,0:T(4,128)S(1)}, u32[]{:S(2)}, u32[]{:S(2)}) collective-permute-start(f32[3,1152]{1,0:T(4,128)S(1)} %add.21), channel_id=1, source_target_pairs={{0,2},{1,3},{2,0},{3,1},{4,6},{5,7},{6,4},{7,5},{8,10},{9,11},{10,... | collective-permute-start | bytes 41480 | tf_op jit(solution)/shard_map/ppermute | solution.py:15

commit v8 on v7

--- a/solution.py
+++ b/solution.py
@@ -58,16 +58,18 @@
     return gathered, masks, offsets
 
 
-def all_sum(value, axes):
-    for axis in axes:
-        count = lax.axis_size(axis)
-        if not power_of_two(count):
-            value = lax.psum(value, axis)
-            continue
-        bit = 1
-        while bit < count:
+def all_sum(value, axis, keep=None):
+    keep = value.shape[0] if keep is None else keep
+    count = lax.axis_size(axis)
+    if not power_of_two(count):
+        return lax.psum(value, axis)[:keep]
+    bit = 1
+    while bit < count:
+        if bit * 2 < count:
             value = value + xor_swap(value, axis, bit)
-            bit *= 2
+        else:
+            value = value[:keep] + xor_swap(value, axis, bit)[:keep]
+        bit *= 2
     return value
 
 
@@ -99,13 +101,22 @@
 
 def grad_kernel(masks, offsets, *refs):
     (sharpness_ref, shift_ref, multiplier_ref, counts_ref, picture_ref, caption_ref, picture_gain_ref,
-     caption_gain_ref, gathered_ref, partner_ref, image_grad_ref, text_grad_ref, sums_ref) = refs
+     caption_gain_ref, partner_ref) = refs[:9]
+    pieces = refs[9 : 9 + len(masks)]
+    image_grad_ref, text_grad_ref, sums_ref, gathered_ref, copy_sems = refs[9 + len(masks) :]
+    piece = pieces[0].shape[1]
+    arrivals = [
+        pltpu.make_async_copy(
+            source, gathered_ref.at[:, position * piece : (position + 1) * piece, :], copy_sems.at[position]
+        )
+        for position, source in enumerate(pieces)
+    ]
+    for arrival in arrivals:
+        arrival.start()
     blocks = counts_ref.shape[1]
     own_block = lax.axis_index("blk")
-    group_index = lax.axis_index("rep")
     block_rows = picture_ref.shape[1]
     width = picture_ref.shape[2]
-    piece = gathered_ref.shape[1] // len(masks)
     group_rows = gathered_ref.shape[1]
     own_start = own_block * block_rows
     total = counts_ref[0, 0]
@@ -141,6 +152,8 @@
     positives = (own_partner == held_row, matched_image == held_row)
 
     start_b = len(masks) // 2 * piece
+    for arrival in arrivals:
+        arrival.wait()
     loss_rows = []
     towers = ((picture_ref, picture_gain_ref, image_grad_ref), (caption_ref, caption_gain_ref, text_grad_ref))
     for tower, (pooled_ref, gain_ref, grad_ref) in enumerate(towers):
@@ -179,8 +192,8 @@
             - normed * jnp.mean(scaled_back * normed, axis=-1, keepdims=True)
         ) * inverse
         grad_ref[0] = gradient.astype(grad_ref.dtype)
-    group_lane = lax.broadcasted_iota(jnp.int32, (1, width), 1)
-    sums_ref[2:3, :] = jnp.where(group_lane == group_index, loss_rows[0] / real_count, 0.0)
+    first_lane = lax.broadcasted_iota(jnp.int32, (1, width), 1) == 0
+    sums_ref[2:3, :] = jnp.where(first_lane, loss_rows[0] / real_count, 0.0)
 
 
 def shards(
@@ -199,7 +212,6 @@
         picture_averaged_features, caption_averaged_features, picture_rescale_factor, caption_rescale_factor
     )
     pieces, masks, offsets = gather_blocks(first, second, "blk")
-    gathered = jnp.concatenate(pieces, axis=1)
 
     smem = pltpu.MemorySpace.SMEM
     vmem = pltpu.MemorySpace.VMEM
@@ -207,8 +219,14 @@
     image_grad, text_grad, sums = pl.pallas_call(
         functools.partial(grad_kernel, tuple(masks), tuple(offsets)),
         out_shape=(grad_shape, grad_shape, jax.ShapeDtypeStruct((3, width), jnp.float32)),
-        in_specs=[pl.BlockSpec(memory_space=smem)] * 4 + [pl.BlockSpec(memory_space=vmem)] * 6,
+        in_specs=[pl.BlockSpec(memory_space=smem)] * 4
+        + [pl.BlockSpec(memory_space=vmem)] * 5
+        + [pl.BlockSpec(memory_space=pl.ANY)] * len(pieces),
         out_specs=(pl.BlockSpec(memory_space=vmem),) * 3,
+        scratch_shapes=[
+            pltpu.VMEM((2, len(pieces) * pieces[0].shape[1], width), pieces[0].dtype),
+            pltpu.SemaphoreType.DMA((len(pieces),)),
+        ],
     )(
         exponent_of_sharpness,
         score_shift_term,
@@ -218,13 +236,13 @@
         caption_averaged_features,
         picture_rescale_factor,
         caption_rescale_factor,
-        gathered,
         matching_caption_index,
-    )
-
-    total = all_sum(sums, ("blk", "rep"))
-    gain_grads = total[:2]
-    group_loss = lax.dynamic_slice_in_dim(total[2], lax.axis_index("rep"), 1)
+        *pieces,
+    )
+
+    group_sums = all_sum(sums, "blk")
+    group_loss = group_sums[2, 0:1]
+    gain_grads = all_sum(group_sums, "rep", keep=2)
     return (image_grad, text_grad, gain_grads, group_loss)
 
 

time: 50.9 us -> 47.1 us (0.925)
  local copies, waits for them, and re-layouts: 3.84 us -> 1.89 us
  starting transfers between devices: 18 us -> 16.3 us
  waiting for transfers between devices: 18.6 us -> 17 us
  Pallas kernels: 6.56 us -> 7.49 us
  other arithmetic: 0.75 us -> 1.35 us
    ppermute x19, starting transfers between devices: 18 us -> 16.3 us  [xor_swap(): lax.ppermute(value, axis, [(source, source ^ bit) for source in range(cou...]
    ppermute x19, waiting for transfers between devices: 18.6 us -> 17 us  [xor_swap(): lax.ppermute(value, axis, [(source, source ^ bit) for source in range(cou...]
    unnamed x19 -> x28, local copies, waits for them, and re-layouts: 2.63 us -> 1.38 us
    pallas_call x1, Pallas kernels: 4.5 us -> 5.44 us  [shards(): pl.pallas_call(functools.partial(grad_kernel, tuple(masks), tuple(offsets...]
    add x0 -> x2, other arithmetic: none -> 0.61 us  [all_sum(): value = value[:keep] + xor_swap(value, axis, bit)[:keep]]
    dynamic_slice x1 -> x0, local copies, waits for them, and re-layouts: 0.58 us -> none  [shards(): group_loss = lax.dynamic_slice_in_dim(total[2], lax.axis_index('rep'), 1)]
  transfers between devices with their start and end apart: 19 -> 19, of which waited for: 9 -> 10; matrix products, arithmetic and copies ran while one was open for 2% -> 1% of each run, Pallas kernels for 0% -> 0%
where the time goes in v8:
time: 47.1 us; the launch traced here: 46.8 us
  waiting for transfers between devices  17 us (36%)
  starting transfers between devices  16.3 us (35%)
  Pallas kernels  7.49 us (16%)
  between operations  2.78 us (6%)
  local copies, waits for them, and re-layouts  1.89 us (4%)
  other arithmetic  1.35 us (3%)
    ppermute x19, waiting for transfers between devices, xor_swap(): lax.ppermute(value, axis, [(source, source ^ bit) for source in range(cou...  17 us
    ppermute x19, starting transfers between devices, xor_swap(): lax.ppermute(value, axis, [(source, source ^ bit) for source in range(cou...  16.3 us
    pallas_call x1, Pallas kernels, shards(): pl.pallas_call(functools.partial(grad_kernel, tuple(masks), tuple(offsets...  5.44 us
    pallas_call x1, Pallas kernels, embed_both(): pl.pallas_call(embed_kernel, out_shape=(half, half), in_specs=[pl.BlockSp...  2.05 us
    unnamed x28, local copies, waits for them, and re-layouts  1.38 us
  transfers between devices with their start and end apart: 19, of which 10 were waited for; matrix products, arithmetic and copies ran while one was open for 1% of the time, Pallas kernels for 0%

profile of v8, /device:TPU:0, one launch (start us, length us, event | category | flops | bytes accessed | tf_op | source)
XLA Modules:
  0.0 46.8 jit_solution(7171121220669924729)
XLA Ops:
  0.6 2.1 %shard_map.120 = (bf16[2,32,1152]{2,1,0:T(8,128)(2,1)}, bf16[2,32,1152]{2,1,0:T(8,128)(2,1)}) custom-call(bf16[1,64,1152]{2,1,0:T(8,128)(2,1)} %refs_4_.1, bf16[1,64,1152]{2,1,0:T(8,128)(2,1)} %refs_5_.1, f32[1152]{0:T(1024)} %refs_6_.1, f32[1152]{0:T(1024)} %refs_7_.1), custom_call_target="tpu_custom_call" | custom-call | tf_op jit(solution)/shard_map/pallas_call | solution.py:94
  3.2 2.5 %collective-permute-start.1 = (bf16[2,32,1152]{2,1,0:T(8,128)(2,1)}, bf16[2,32,1152]{2,1,0:T(8,128)(2,1)S(1)}, u32[]{:S(2)}, u32[]{:S(2)}) collective-permute-start(bf16[2,32,1152]{2,1,0:T(8,128)(2,1)} %get-tuple-element.9.refs_9_), channel_id=1, source_target_pairs={{0,16},{4,20},{8,24},{12,28},{16,0},{20,4},{24,8},{28,12},{1,17},{... | collective-permute-start | bytes 442376 | tf_op jit(solution)/shard_map/ppermute | solution.py:15
  5.7 1.5 %collective-permute-start = (bf16[2,32,1152]{2,1,0:T(8,128)(2,1)}, bf16[2,32,1152]{2,1,0:T(8,128)(2,1)S(1)}, u32[]{:S(2)}, u32[]{:S(2)}) collective-permute-start(bf16[2,32,1152]{2,1,0:T(8,128)(2,1)} %get-tuple-element.9.refs_9_), channel_id=1, source_target_pairs={{0,8},{4,12},{8,0},{12,4},{16,24},{20,28},{24,16},{28,20},{1,9},{5... | collective-permute-start | bytes 442376 | tf_op jit(solution)/shard_map/ppermute | solution.py:15
  7.9 2.7 %collective-permute-done.1.refs_11_ = bf16[2,32,1152]{2,1,0:T(8,128)(2,1)S(1)} collective-permute-done((bf16[2,32,1152]{2,1,0:T(8,128)(2,1)}, bf16[2,32,1152]{2,1,0:T(8,128)(2,1)S(1)}, u32[]{:S(2)}, u32[]{:S(2)}) %collective-permute-start.1) | collective-permute-done | bytes 147488 | tf_op jit(solution)/shard_map/ppermute | solution.py:15
  10.6 2.0 %collective-permute-done.refs_10_ = bf16[2,32,1152]{2,1,0:T(8,128)(2,1)S(1)} collective-permute-done((bf16[2,32,1152]{2,1,0:T(8,128)(2,1)}, bf16[2,32,1152]{2,1,0:T(8,128)(2,1)S(1)}, u32[]{:S(2)}, u32[]{:S(2)}) %collective-permute-start) | collective-permute-done | bytes 147488 | tf_op jit(solution)/shard_map/ppermute | solution.py:15
  12.7 0.9 %collective-permute-done.7.refs_18_ = bf16[2,32,1152]{2,1,0:T(8,128)(2,1)S(1)} collective-permute-done((bf16[2,32,1152]{2,1,0:T(8,128)(2,1)}, bf16[2,32,1152]{2,1,0:T(8,128)(2,1)S(1)}, u32[]{:S(2)}, u32[]{:S(2)}) %collective-permute-start.7) | collective-permute-done | bytes 147488 | tf_op jit(solution)/shard_map/ppermute | solution.py:15
  13.6 1.7 %collective-permute-start.9 = (bf16[2,32,1152]{2,1,0:T(8,128)(2,1)S(1)}, bf16[2,32,1152]{2,1,0:T(8,128)(2,1)S(1)}, u32[]{:S(2)}, u32[]{:S(2)}) collective-permute-start(bf16[2,32,1152]{2,1,0:T(8,128)(2,1)S(1)} %collective-permute-done.7.refs_18_), channel_id=1, source_target_pairs={{0,8},{4,12},{8,0},{12,4},{16,24},{20,28},{24,16},{28,20},{1,9},{5... | collective-permute-start | bytes 442376 | tf_op jit(solution)/shard_map/ppermute | solution.py:15
  15.9 1.9 %collective-permute-done.2.refs_12_ = bf16[2,32,1152]{2,1,0:T(8,128)(2,1)S(1)} collective-permute-done((bf16[2,32,1152]{2,1,0:T(8,128)(2,1)S(1)}, bf16[2,32,1152]{2,1,0:T(8,128)(2,1)S(1)}, u32[]{:S(2)}, u32[]{:S(2)}) %collective-permute-start.2) | collective-permute-done | bytes 147488 | tf_op jit(solution)/shard_map/ppermute | solution.py:15
  17.8 1.2 %collective-permute-done.9.refs_20_ = bf16[2,32,1152]{2,1,0:T(8,128)(2,1)S(1)} collective-permute-done((bf16[2,32,1152]{2,1,0:T(8,128)(2,1)S(1)}, bf16[2,32,1152]{2,1,0:T(8,128)(2,1)S(1)}, u32[]{:S(2)}, u32[]{:S(2)}) %collective-permute-start.9) | collective-permute-done | bytes 147488 | tf_op jit(solution)/shard_map/ppermute | solution.py:15
  21.8 0.7 %copy-done.13 = bf16[2,32,1152]{2,1,0:T(8,128)(2,1)} copy-done((bf16[2,32,1152]{2,1,0:T(8,128)(2,1)}, bf16[2,32,1152]{2,1,0:T(8,128)(2,1)S(1)}, u32[]{:S(2)}) %copy-start.13) | copy-done | bytes 147480
  22.4 5.4 %shard_map.121 = (bf16[1,64,1152]{2,1,0:T(8,128)(2,1)}, bf16[1,64,1152]{2,1,0:T(8,128)(2,1)}, f32[3,1152]{1,0:T(4,128)}) custom-call(f32[1]{0:T(128)S(6)} %copy.13.refs_0_, f32[1]{0:T(128)S(6)} %copy.14.refs_1_, f32[1]{0:T(128)S(6)} %copy.15.refs_2_, s32[1,8]{1,0:T(1,128)} %refs_3_.1, bf16[1,64,1152]{2,1,0:T(8,128)(2,1)} %refs_4_.1, ...), custom_call_target="tpu_custom_call" | custom-call | tf_op jit(solution)/shard_map/pallas_call | solution.py:219
  27.9 0.6 %collective-permute-start.14 = (f32[3,1152]{1,0:T(4,128)}, f32[3,1152]{1,0:T(4,128)S(1)}, u32[]{:S(2)}, u32[]{:S(2)}) collective-permute-start(f32[3,1152]{1,0:T(4,128)} %get-tuple-element.13), channel_id=1, source_target_pairs={{0,4},{4,0},{8,12},{12,8},{16,20},{20,16},{24,28},{28,24},{1,5},{5... | collective-permute-start | bytes 41480 | tf_op jit(solution)/shard_map/ppermute | solution.py:15
  28.4 1.1 %collective-permute-done.14 = f32[3,1152]{1,0:T(4,128)S(1)} collective-permute-done((f32[3,1152]{1,0:T(4,128)}, f32[3,1152]{1,0:T(4,128)S(1)}, u32[]{:S(2)}, u32[]{:S(2)}) %collective-permute-start.14) | collective-permute-done | bytes 13856 | tf_op jit(solution)/shard_map/ppermute | solution.py:15
  29.5 0.7 %add.15 = f32[3,1152]{1,0:T(4,128)S(1)} add(f32[3,1152]{1,0:T(4,128)} %get-tuple-element.13, f32[3,1152]{1,0:T(4,128)S(1)} %collective-permute-done.14) | non-fusion elementwise | flops 3456 | bytes 41472 | tf_op jit(solution)/shard_map/add | solution.py:69
  30.2 1.7 %collective-permute-start.15 = (f32[3,1152]{1,0:T(4,128)S(1)}, f32[3,1152]{1,0:T(4,128)S(1)}, u32[]{:S(2)}, u32[]{:S(2)}) collective-permute-start(f32[3,1152]{1,0:T(4,128)S(1)} %add.15), channel_id=1, source_target_pairs={{0,8},{4,12},{8,0},{12,4},{16,24},{20,28},{24,16},{28,20},{1,9},{5... | collective-permute-start | bytes 41480 | tf_op jit(solution)/shard_map/ppermute | solution.py:15
  32.0 2.0 %collective-permute-done.15 = f32[3,1152]{1,0:T(4,128)S(1)} collective-permute-done((f32[3,1152]{1,0:T(4,128)S(1)}, f32[3,1152]{1,0:T(4,128)S(1)}, u32[]{:S(2)}, u32[]{:S(2)}) %collective-permute-start.15) | collective-permute-done | bytes 13856 | tf_op jit(solution)/shard_map/ppermute | solution.py:15
  34.0 1.8 %collective-permute-start.16 = (f32[3,1152]{1,0:T(4,128)S(1)}, f32[3,1152]{1,0:T(4,128)S(1)}, u32[]{:S(2)}, u32[]{:S(2)}) collective-permute-start(f32[3,1152]{1,0:T(4,128)S(1)} %add.16), channel_id=1, source_target_pairs={{0,16},{4,20},{8,24},{12,28},{16,0},{20,4},{24,8},{28,12},{1,17},{... | collective-permute-start | bytes 41480 | tf_op jit(solution)/shard_map/ppermute | solution.py:15
  35.8 2.0 %collective-permute-done.16 = f32[3,1152]{1,0:T(4,128)S(1)} collective-permute-done((f32[3,1152]{1,0:T(4,128)S(1)}, f32[3,1152]{1,0:T(4,128)S(1)}, u32[]{:S(2)}, u32[]{:S(2)}) %collective-permute-start.16) | collective-permute-done | bytes 13856 | tf_op jit(solution)/shard_map/ppermute | solution.py:15
  37.8 1.8 %collective-permute-start.17 = (f32[3,1152]{1,0:T(4,128)S(1)}, f32[3,1152]{1,0:T(4,128)S(1)}, u32[]{:S(2)}, u32[]{:S(2)}) collective-permute-start(f32[3,1152]{1,0:T(4,128)S(1)} %add.17), channel_id=1, source_target_pairs={{0,1},{1,0},{2,3},{3,2},{4,5},{5,4},{6,7},{7,6},{8,9},{9,8},{10,11... | collective-permute-start | bytes 41480 | tf_op jit(solution)/shard_map/ppermute | solution.py:15
  39.6 1.9 %collective-permute-done.17 = f32[3,1152]{1,0:T(4,128)S(1)} collective-permute-done((f32[3,1152]{1,0:T(4,128)S(1)}, f32[3,1152]{1,0:T(4,128)S(1)}, u32[]{:S(2)}, u32[]{:S(2)}) %collective-permute-start.17) | collective-permute-done | bytes 13856 | tf_op jit(solution)/shard_map/ppermute | solution.py:15
  41.5 2.8 %collective-permute-start.18 = (f32[3,1152]{1,0:T(4,128)S(1)}, f32[3,1152]{1,0:T(4,128)S(1)}, u32[]{:S(2)}, u32[]{:S(2)}) collective-permute-start(f32[3,1152]{1,0:T(4,128)S(1)} %add.18), channel_id=1, source_target_pairs={{0,2},{1,3},{2,0},{3,1},{4,6},{5,7},{6,4},{7,5},{8,10},{9,11},{10,... | collective-permute-start | bytes 41480 | tf_op jit(solution)/shard_map/ppermute | solution.py:15
  44.4 0.5 %slice.14 = f32[1,1]{1,0:T(1,128)} slice(f32[3,1152]{1,0:T(4,128)S(1)} %add.17), slice={[2:3], [0:1]} | slice | bytes 8 | tf_op jit(solution)/shard_map/slice | solution.py:244
  44.9 1.3 %collective-permute-done.18 = f32[3,1152]{1,0:T(4,128)S(1)} collective-permute-done((f32[3,1152]{1,0:T(4,128)S(1)}, f32[3,1152]{1,0:T(4,128)S(1)}, u32[]{:S(2)}, u32[]{:S(2)}) %collective-permute-start.18) | collective-permute-done | bytes 13856 | tf_op jit(solution)/shard_map/ppermute | solution.py:15
  46.2 0.6 %slice_add_fusion = f32[2,1152]{1,0:T(2,128)} fusion(f32[3,1152]{1,0:T(4,128)S(1)} %collective-permute-done.18, f32[3,1152]{1,0:T(4,128)S(1)} %add.18), kind=kLoop, calls=%fused_computation | loop fusion | flops 2304 | bytes 27648 | tf_op jit(solution)/shard_map/add | solution.py:71
  (50 shorter events, 2.6 us)
Async XLA Ops:
  2.7 5.0 %collective-permute-start.3 = (bf16[2,32,1152]{2,1,0:T(8,128)(2,1)}, bf16[2,32,1152]{2,1,0:T(8,128)(2,1)S(1)}, u32[]{:S(2)}, u32[]{:S(2)}) collective-permute-start(bf16[2,32,1152]{2,1,0:T(8,128)(2,1)} %get-tuple-element.9.refs_9_), channel_id=1, source_target_pairs={{0,4},{4,0},{8,12},{12,8},{16,20},{20,16},{24,28},{28,24},{1,5},{5... | collective-permute-start | bytes 442376 | tf_op jit(solution)/shard_map/ppermute | solution.py:15
  3.2 7.4 %collective-permute-start.1 = (bf16[2,32,1152]{2,1,0:T(8,128)(2,1)}, bf16[2,32,1152]{2,1,0:T(8,128)(2,1)S(1)}, u32[]{:S(2)}, u32[]{:S(2)}) collective-permute-start(bf16[2,32,1152]{2,1,0:T(8,128)(2,1)} %get-tuple-element.9.refs_9_), channel_id=1, source_target_pairs={{0,16},{4,20},{8,24},{12,28},{16,0},{20,4},{24,8},{28,12},{1,17},{... | collective-permute-start | bytes 442376 | tf_op jit(solution)/shard_map/ppermute | solution.py:15
  5.7 6.9 %collective-permute-start = (bf16[2,32,1152]{2,1,0:T(8,128)(2,1)}, bf16[2,32,1152]{2,1,0:T(8,128)(2,1)S(1)}, u32[]{:S(2)}, u32[]{:S(2)}) collective-permute-start(bf16[2,32,1152]{2,1,0:T(8,128)(2,1)} %get-tuple-element.9.refs_9_), channel_id=1, source_target_pairs={{0,8},{4,12},{8,0},{12,4},{16,24},{20,28},{24,16},{28,20},{1,9},{5... | collective-permute-start | bytes 442376 | tf_op jit(solution)/shard_map/ppermute | solution.py:15
  7.2 6.4 %collective-permute-start.7 = (bf16[2,32,1152]{2,1,0:T(8,128)(2,1)}, bf16[2,32,1152]{2,1,0:T(8,128)(2,1)S(1)}, u32[]{:S(2)}, u32[]{:S(2)}) collective-permute-start(bf16[2,32,1152]{2,1,0:T(8,128)(2,1)} %get-tuple-element.10.refs_17_), channel_id=1, source_target_pairs={{0,16},{4,20},{8,24},{12,28},{16,0},{20,4},{24,8},{28,12},{1,17},{... | collective-permute-start | bytes 442376 | tf_op jit(solution)/shard_map/ppermute | solution.py:15
  7.7 7.6 %collective-permute-start.10 = (bf16[2,32,1152]{2,1,0:T(8,128)(2,1)}, bf16[2,32,1152]{2,1,0:T(8,128)(2,1)S(1)}, u32[]{:S(2)}, u32[]{:S(2)}) collective-permute-start(bf16[2,32,1152]{2,1,0:T(8,128)(2,1)} %get-tuple-element.10.refs_17_), channel_id=1, source_target_pairs={{0,4},{4,0},{8,12},{12,8},{16,20},{20,16},{24,28},{28,24},{1,5},{5... | collective-permute-start | bytes 442376 | tf_op jit(solution)/shard_map/ppermute | solution.py:15
  7.7 13.3 %copy-start = (bf16[2,32,1152]{2,1,0:T(8,128)(2,1)}, bf16[2,32,1152]{2,1,0:T(8,128)(2,1)S(1)}, u32[]{:S(2)}) copy-start(bf16[2,32,1152]{2,1,0:T(8,128)(2,1)S(1)} %collective-permute-done.3.refs_13_) | copy-start | bytes 442372
  7.7 7.6 %collective-permute-start.8 = (bf16[2,32,1152]{2,1,0:T(8,128)(2,1)}, bf16[2,32,1152]{2,1,0:T(8,128)(2,1)S(1)}, u32[]{:S(2)}, u32[]{:S(2)}) collective-permute-start(bf16[2,32,1152]{2,1,0:T(8,128)(2,1)} %get-tuple-element.10.refs_17_), channel_id=1, source_target_pairs={{0,8},{4,12},{8,0},{12,4},{16,24},{20,28},{24,16},{28,20},{1,9},{5... | collective-permute-start | bytes 442376 | tf_op jit(solution)/shard_map/ppermute | solution.py:15
  10.6 10.4 %copy-start.1 = (bf16[2,32,1152]{2,1,0:T(8,128)(2,1)}, bf16[2,32,1152]{2,1,0:T(8,128)(2,1)S(1)}, u32[]{:S(2)}) copy-start(bf16[2,32,1152]{2,1,0:T(8,128)(2,1)S(1)} %collective-permute-done.1.refs_11_) | copy-start | bytes 442372
  10.6 5.2 %collective-permute-start.5 = (bf16[2,32,1152]{2,1,0:T(8,128)(2,1)S(1)}, bf16[2,32,1152]{2,1,0:T(8,128)(2,1)S(1)}, u32[]{:S(2)}, u32[]{:S(2)}) collective-permute-start(bf16[2,32,1152]{2,1,0:T(8,128)(2,1)S(1)} %collective-permute-done.1.refs_11_), channel_id=1, source_target_pairs={{0,4},{4,0},{8,12},{12,8},{16,20},{20,16},{24,28},{28,24},{1,5},{5... | collective-permute-start | bytes 442376 | tf_op jit(solution)/shard_map/ppermute | solution.py:15
  12.6 8.4 %copy-start.2 = (bf16[2,32,1152]{2,1,0:T(8,128)(2,1)}, bf16[2,32,1152]{2,1,0:T(8,128)(2,1)S(1)}, u32[]{:S(2)}) copy-start(bf16[2,32,1152]{2,1,0:T(8,128)(2,1)S(1)} %collective-permute-done.refs_10_) | copy-start | bytes 442372
  12.6 5.1 %collective-permute-start.2 = (bf16[2,32,1152]{2,1,0:T(8,128)(2,1)S(1)}, bf16[2,32,1152]{2,1,0:T(8,128)(2,1)S(1)}, u32[]{:S(2)}, u32[]{:S(2)}) collective-permute-start(bf16[2,32,1152]{2,1,0:T(8,128)(2,1)S(1)} %collective-permute-done.refs_10_), channel_id=1, source_target_pairs={{0,16},{4,20},{8,24},{12,28},{16,0},{20,4},{24,8},{28,12},{1,17},{... | collective-permute-start | bytes 442376 | tf_op jit(solution)/shard_map/ppermute | solution.py:15
  13.6 7.5 %copy-start.3 = (bf16[2,32,1152]{2,1,0:T(8,128)(2,1)}, bf16[2,32,1152]{2,1,0:T(8,128)(2,1)S(1)}, u32[]{:S(2)}) copy-start(bf16[2,32,1152]{2,1,0:T(8,128)(2,1)S(1)} %collective-permute-done.7.refs_18_) | copy-start | bytes 442372
  13.6 5.4 %collective-permute-start.9 = (bf16[2,32,1152]{2,1,0:T(8,128)(2,1)S(1)}, bf16[2,32,1152]{2,1,0:T(8,128)(2,1)S(1)}, u32[]{:S(2)}, u32[]{:S(2)}) collective-permute-start(bf16[2,32,1152]{2,1,0:T(8,128)(2,1)S(1)} %collective-permute-done.7.refs_18_), channel_id=1, source_target_pairs={{0,8},{4,12},{8,0},{12,4},{16,24},{20,28},{24,16},{28,20},{1,9},{5... | collective-permute-start | bytes 442376 | tf_op jit(solution)/shard_map/ppermute | solution.py:15
  15.3 5.7 %copy-start.4 = (bf16[2,32,1152]{2,1,0:T(8,128)(2,1)}, bf16[2,32,1152]{2,1,0:T(8,128)(2,1)S(1)}, u32[]{:S(2)}) copy-start(bf16[2,32,1152]{2,1,0:T(8,128)(2,1)S(1)} %collective-permute-done.10.refs_21_) | copy-start | bytes 442372
  15.3 5.6 %collective-permute-start.4 = (bf16[2,32,1152]{2,1,0:T(8,128)(2,1)S(1)}, bf16[2,32,1152]{2,1,0:T(8,128)(2,1)S(1)}, u32[]{:S(2)}, u32[]{:S(2)}) collective-permute-start(bf16[2,32,1152]{2,1,0:T(8,128)(2,1)S(1)} %collective-permute-done.refs_10_), channel_id=1, source_target_pairs={{0,4},{4,0},{8,12},{12,8},{16,20},{20,16},{24,28},{28,24},{1,5},{5... | collective-permute-start | bytes 442376 | tf_op jit(solution)/shard_map/ppermute | solution.py:15
  15.3 5.6 %collective-permute-start.11 = (bf16[2,32,1152]{2,1,0:T(8,128)(2,1)S(1)}, bf16[2,32,1152]{2,1,0:T(8,128)(2,1)S(1)}, u32[]{:S(2)}, u32[]{:S(2)}) collective-permute-start(bf16[2,32,1152]{2,1,0:T(8,128)(2,1)S(1)} %collective-permute-done.7.refs_18_), channel_id=1, source_target_pairs={{0,4},{4,0},{8,12},{12,8},{16,20},{20,16},{24,28},{28,24},{1,5},{5... | collective-permute-start | bytes 442376 | tf_op jit(solution)/shard_map/ppermute | solution.py:15
  15.8 5.1 %collective-permute-start.12 = (bf16[2,32,1152]{2,1,0:T(8,128)(2,1)S(1)}, bf16[2,32,1152]{2,1,0:T(8,128)(2,1)S(1)}, u32[]{:S(2)}, u32[]{:S(2)}) collective-permute-start(bf16[2,32,1152]{2,1,0:T(8,128)(2,1)S(1)} %collective-permute-done.8.refs_19_), channel_id=1, source_target_pairs={{0,4},{4,0},{8,12},{12,8},{16,20},{20,16},{24,28},{28,24},{1,5},{5... | collective-permute-start | bytes 442376 | tf_op jit(solution)/shard_map/ppermute | solution.py:15
  17.8 3.2 %collective-permute-start.6 = (bf16[2,32,1152]{2,1,0:T(8,128)(2,1)S(1)}, bf16[2,32,1152]{2,1,0:T(8,128)(2,1)S(1)}, u32[]{:S(2)}, u32[]{:S(2)}) collective-permute-start(bf16[2,32,1152]{2,1,0:T(8,128)(2,1)S(1)} %collective-permute-done.2.refs_12_), channel_id=1, source_target_pairs={{0,4},{4,0},{8,12},{12,8},{16,20},{20,16},{24,28},{28,24},{1,5},{5... | collective-permute-start | bytes 442376 | tf_op jit(solution)/shard_map/ppermute | solution.py:15
  18.9 2.0 %collective-permute-start.13 = (bf16[2,32,1152]{2,1,0:T(8,128)(2,1)S(1)}, bf16[2,32,1152]{2,1,0:T(8,128)(2,1)S(1)}, u32[]{:S(2)}, u32[]{:S(2)}) collective-permute-start(bf16[2,32,1152]{2,1,0:T(8,128)(2,1)S(1)} %collective-permute-done.9.refs_20_), channel_id=1, source_target_pairs={{0,4},{4,0},{8,12},{12,8},{16,20},{20,16},{24,28},{28,24},{1,5},{5... | collective-permute-start | bytes 442376 | tf_op jit(solution)/shard_map/ppermute | solution.py:15
  27.9 1.6 %collective-permute-start.14 = (f32[3,1152]{1,0:T(4,128)}, f32[3,1152]{1,0:T(4,128)S(1)}, u32[]{:S(2)}, u32[]{:S(2)}) collective-permute-start(f32[3,1152]{1,0:T(4,128)} %get-tuple-element.13), channel_id=1, source_target_pairs={{0,4},{4,0},{8,12},{12,8},{16,20},{20,16},{24,28},{28,24},{1,5},{5... | collective-permute-start | bytes 41480 | tf_op jit(solution)/shard_map/ppermute | solution.py:15
  30.2 3.8 %collective-permute-start.15 = (f32[3,1152]{1,0:T(4,128)S(1)}, f32[3,1152]{1,0:T(4,128)S(1)}, u32[]{:S(2)}, u32[]{:S(2)}) collective-permute-start(f32[3,1152]{1,0:T(4,128)S(1)} %add.15), channel_id=1, source_target_pairs={{0,8},{4,12},{8,0},{12,4},{16,24},{20,28},{24,16},{28,20},{1,9},{5... | collective-permute-start | bytes 41480 | tf_op jit(solution)/shard_map/ppermute | solution.py:15
  34.0 3.8 %collective-permute-start.16 = (f32[3,1152]{1,0:T(4,128)S(1)}, f32[3,1152]{1,0:T(4,128)S(1)}, u32[]{:S(2)}, u32[]{:S(2)}) collective-permute-start(f32[3,1152]{1,0:T(4,128)S(1)} %add.16), channel_id=1, source_target_pairs={{0,16},{4,20},{8,24},{12,28},{16,0},{20,4},{24,8},{28,12},{1,17},{... | collective-permute-start | bytes 41480 | tf_op jit(solution)/shard_map/ppermute | solution.py:15
  37.8 3.8 %collective-permute-start.17 = (f32[3,1152]{1,0:T(4,128)S(1)}, f32[3,1152]{1,0:T(4,128)S(1)}, u32[]{:S(2)}, u32[]{:S(2)}) collective-permute-start(f32[3,1152]{1,0:T(4,128)S(1)} %add.17), channel_id=1, source_target_pairs={{0,1},{1,0},{2,3},{3,2},{4,5},{5,4},{6,7},{7,6},{8,9},{9,8},{10,11... | collective-permute-start | bytes 41480 | tf_op jit(solution)/shard_map/ppermute | solution.py:15
  41.5 4.7 %collective-permute-start.18 = (f32[3,1152]{1,0:T(4,128)S(1)}, f32[3,1152]{1,0:T(4,128)S(1)}, u32[]{:S(2)}, u32[]{:S(2)}) collective-permute-start(f32[3,1152]{1,0:T(4,128)S(1)} %add.18), channel_id=1, source_target_pairs={{0,2},{1,3},{2,0},{3,1},{4,6},{5,7},{6,4},{7,5},{8,10},{9,11},{10,... | collective-permute-start | bytes 41480 | tf_op jit(solution)/shard_map/ppermute | solution.py:15
  (9 other events, 19.9 us)

commit v9 on v8

--- a/solution.py
+++ b/solution.py
@@ -196,6 +196,168 @@
     sums_ref[2:3, :] = jnp.where(first_lane, loss_rows[0] / real_count, 0.0)
 
 
+def group_kernel(image_masks, text_masks, *refs):
+    (sharpness_ref, shift_ref, multiplier_ref, counts_ref, picture_gain_ref, caption_gain_ref,
+     partner_ref) = refs[:7]
+    count = len(image_masks)
+    pieces = refs[7 : 7 + 2 * count]
+    (image_grad_ref, text_grad_ref, sums_ref, raw_ref, unit_ref, short_ref, normed_ref, inverse_ref,
+     length_ref, weights_ref, flipped_ref, copy_sems) = refs[7 + 2 * count :]
+    block_rows = pieces[0].shape[1]
+    group_rows = raw_ref.shape[1]
+    width = raw_ref.shape[2]
+    arrivals = []
+    for position, source in enumerate(pieces):
+        tower, slot = divmod(position, count)
+        rows = pl.ds(slot * block_rows, block_rows)
+        arrival = pltpu.make_async_copy(source.at[0], raw_ref.at[tower, rows, :], copy_sems.at[position])
+        arrival.start()
+        arrivals.append(arrival)
+
+    own_block = lax.axis_index("blk")
+    blocks = counts_ref.shape[1]
+    total = counts_ref[0, 0]
+    for block in range(1, blocks):
+        total = total + counts_ref[0, block]
+    real_count = jnp.full((1, 1), total, jnp.int32).astype(jnp.float32)
+    score_sharpness_factor = jnp.exp(jnp.full((1, 1), sharpness_ref[0], jnp.float32))
+    score_shift_amount = jnp.full((1, 1), shift_ref[0], jnp.float32)
+    grad_factor = jnp.full((1, 1), multiplier_ref[0], jnp.float32) / real_count
+
+    def held(masks, shape, dim):
+        place = lax.broadcasted_iota(jnp.int32, shape, dim)
+        row = jnp.zeros(shape, jnp.int32)
+        limit = jnp.zeros(shape, jnp.int32)
+        for slot, mask in enumerate(masks):
+            block = own_block ^ mask
+            here = place // block_rows == slot
+            row = jnp.where(here, block * block_rows + place % block_rows, row)
+            limit = jnp.where(here, counts_ref[0, block], limit)
+        return row, (row % block_rows) < limit
+
+    image_row, image_real = held(image_masks, (group_rows, 1), 0)
+    text_row, text_real = held(text_masks, (1, group_rows), 1)
+    natural = lax.broadcasted_iota(jnp.int32, (group_rows, group_rows), 1)
+    partner_of_image = jnp.sum(
+        jnp.where(natural == image_row, partner_ref[...].astype(jnp.float32), 0.0), axis=1, keepdims=True
+    ).astype(jnp.int32)
+
+    for arrival in arrivals:
+        arrival.wait()
+    gains = (picture_gain_ref[...][None, :], caption_gain_ref[...][None, :])
+    chunk = min(128, group_rows)
+    for tower in range(2):
+        for first in range(0, group_rows, chunk):
+            rows = pl.ds(first, chunk)
+            values = raw_ref[tower, rows, :].astype(jnp.float32)
+            centred = values - jnp.mean(values, axis=-1, keepdims=True)
+            inverse = lax.rsqrt(jnp.mean(centred * centred, axis=-1, keepdims=True) + epsilon)
+            normed = centred * inverse
+            scaled = normed * gains[tower]
+            inv_length = lax.rsqrt(jnp.sum(scaled * scaled, axis=-1, keepdims=True) + epsilon)
+            unit_rows = scaled * inv_length
+            unit_ref[tower, rows, :] = unit_rows
+            short_ref[tower, rows, :] = unit_rows.astype(short_ref.dtype)
+            normed_ref[tower, rows, :] = normed
+            inverse_ref[tower, rows, :] = inverse
+            length_ref[tower, rows, :] = inv_length
+
+    loss = jnp.zeros((1, 1), jnp.float32)
+    for first in range(0, group_rows, chunk):
+        rows = pl.ds(first, chunk)
+        scores = lax.dot_general(
+            short_ref[0, rows, :], short_ref[1], (((1,), (1,)), ((), ())), preferred_element_type=jnp.float32
+        )
+        score_similarity_table = score_sharpness_factor * scores + score_shift_amount
+        labels = jnp.where(partner_of_image[first : first + chunk] == text_row, 1.0, -1.0)
+        kept = image_real[first : first + chunk] & text_real
+        margin = -labels * score_similarity_table
+        softplus = jnp.maximum(margin, 0.0) + jnp.log1p(jnp.exp(-jnp.abs(margin)))
+        loss = loss + jnp.sum(jnp.where(kept, softplus, 0.0), axis=(0, 1), keepdims=True)
+        weights = jnp.where(kept, -labels * jax.nn.sigmoid(margin), 0.0) * grad_factor
+        weights_ref[rows, :] = weights.astype(weights_ref.dtype)
+        flipped_ref[:, rows] = weights.T.astype(flipped_ref.dtype)
+
+    for tower, (pair_ref, grad_ref) in enumerate(((weights_ref, image_grad_ref), (flipped_ref, text_grad_ref))):
+        gain_sum = jnp.zeros((1, width), jnp.float32)
+        for first in range(0, group_rows, chunk):
+            rows = pl.ds(first, chunk)
+            direction = score_sharpness_factor * jnp.dot(
+                pair_ref[rows, :], short_ref[1 - tower], preferred_element_type=jnp.float32
+            )
+            unit_rows = unit_ref[tower, rows, :]
+            normed = normed_ref[tower, rows, :]
+            tangent = (
+                direction - unit_rows * jnp.sum(unit_rows * direction, axis=-1, keepdims=True)
+            ) * length_ref[tower, rows, :]
+            gain_sum = gain_sum + jnp.sum(tangent * normed, axis=0, keepdims=True)
+            if first == 0:
+                own = slice(0, block_rows)
+                scaled_back = tangent[own] * gains[tower]
+                gradient = (
+                    scaled_back
+                    - jnp.mean(scaled_back, axis=-1, keepdims=True)
+                    - normed[own] * jnp.mean(scaled_back * normed[own], axis=-1, keepdims=True)
+                ) * inverse_ref[tower, 0:block_rows, :]
+                grad_ref[0] = gradient.astype(grad_ref.dtype)
+        sums_ref[tower : tower + 1, :] = gain_sum
+    first_lane = lax.broadcasted_iota(jnp.int32, (1, width), 1) == 0
+    sums_ref[2:3, :] = jnp.where(first_lane, loss / real_count, 0.0)
+
+
+def whole_group(
+    picture_averaged_features,
+    caption_averaged_features,
+    picture_rescale_factor,
+    caption_rescale_factor,
+    exponent_of_sharpness,
+    score_shift_term,
+    objective_multiplier,
+    matching_caption_index,
+    genuine_entry_counts,
+):
+    count = lax.axis_size("blk")
+    block_rows, width = picture_averaged_features.shape[1:]
+    group_rows = count * block_rows
+    pieces, masks, unused = gather_blocks(picture_averaged_features, caption_averaged_features, "blk")
+    smem = pltpu.MemorySpace.SMEM
+    vmem = pltpu.MemorySpace.VMEM
+    grad_shape = jax.ShapeDtypeStruct(picture_averaged_features.shape, jnp.bfloat16)
+    full = (2, group_rows, width)
+    column = (2, group_rows, 1)
+    image_grad, text_grad, sums = pl.pallas_call(
+        functools.partial(group_kernel, tuple(masks[:count]), tuple(masks[count:])),
+        out_shape=(grad_shape, grad_shape, jax.ShapeDtypeStruct((3, width), jnp.float32)),
+        in_specs=[pl.BlockSpec(memory_space=smem)] * 4
+        + [pl.BlockSpec(memory_space=vmem)] * 3
+        + [pl.BlockSpec(memory_space=pl.ANY)] * len(pieces),
+        out_specs=(pl.BlockSpec(memory_space=vmem),) * 3,
+        scratch_shapes=[
+            pltpu.VMEM(full, jnp.bfloat16),
+            pltpu.VMEM(full, jnp.float32),
+            pltpu.VMEM(full, jnp.bfloat16),
+            pltpu.VMEM(full, jnp.float32),
+            pltpu.VMEM(column, jnp.float32),
+            pltpu.VMEM(column, jnp.float32),
+            pltpu.VMEM((group_rows, group_rows), jnp.bfloat16),
+            pltpu.VMEM((group_rows, group_rows), jnp.bfloat16),
+            pltpu.SemaphoreType.DMA((len(pieces),)),
+        ],
+    )(
+        exponent_of_sharpness,
+        score_shift_term,
+        objective_multiplier,
+        genuine_entry_counts,
+        picture_rescale_factor,
+        caption_rescale_factor,
+        matching_caption_index,
+        *pieces,
+    )
+    group_loss = sums[2, 0:1]
+    gain_grads = all_sum(sums, "rep", keep=2)
+    return (image_grad, text_grad, gain_grads, group_loss)
+
+
 def shards(
     picture_averaged_features,
     caption_averaged_features,
@@ -246,6 +408,11 @@
     return (image_grad, text_grad, gain_grads, group_loss)
 
 
+def body(*args):
+    group_rows = args[0].shape[1] * lax.axis_size("blk")
+    return (whole_group if group_rows <= 512 else shards)(*args)
+
+
 def solution(mesh):
     placed = (
         P("rep", "blk", None),
@@ -259,7 +426,7 @@
         P("rep", None),
     )
     return jax.shard_map(
-        shards,
+        body,
         mesh=mesh,
         in_specs=placed,
         out_specs=(P("rep", "blk", None), P("rep", "blk", None), P(), P("rep")),

time: 47.1 us -> 40.3 us (0.86)
  waiting for transfers between devices: 17 us -> 12.2 us
  starting transfers between devices: 16.3 us -> 11.7 us
  Pallas kernels: 7.49 us -> 9.38 us
  local copies, waits for them, and re-layouts: 1.89 us -> 2.59 us
    ppermute x19 -> x16, waiting for transfers between devices: 17 us -> 12.2 us  [xor_swap(): lax.ppermute(value, axis, [(source, source ^ bit) for source in range(cou...]
    ppermute x19 -> x16, starting transfers between devices: 16.3 us -> 11.7 us  [xor_swap(): lax.ppermute(value, axis, [(source, source ^ bit) for source in range(cou...]
    pallas_call x2 -> x1, Pallas kernels: 7.49 us -> 9.38 us  [whole_group(): pl.pallas_call(functools.partial(group_kernel, tuple(masks[:count]), tupl...]
    slice x1, local copies, waits for them, and re-layouts: 0.51 us -> 1.18 us  [whole_group(): group_loss = sums[2, 0:1]]
  transfers between devices with their start and end apart: 19 -> 16, of which waited for: 10 -> 7; matrix products, arithmetic and copies ran while one was open for 1% -> 3% of each run, Pallas kernels for 0% -> 0%
where the time goes in v9:
time: 40.3 us; the launch traced here: 40 us
  waiting for transfers between devices  12.2 us (30%)
  starting transfers between devices  11.7 us (29%)
  Pallas kernels  9.38 us (23%)
  between operations  2.77 us (7%)
  local copies, waits for them, and re-layouts  2.59 us (6%)
  other arithmetic  1.33 us (3%)
    ppermute x16, waiting for transfers between devices, xor_swap(): lax.ppermute(value, axis, [(source, source ^ bit) for source in range(cou...  12.2 us
    ppermute x16, starting transfers between devices, xor_swap(): lax.ppermute(value, axis, [(source, source ^ bit) for source in range(cou...  11.7 us
    pallas_call x1, Pallas kernels, whole_group(): pl.pallas_call(functools.partial(group_kernel, tuple(masks[:count]), tupl...  9.38 us
    unnamed x28, local copies, waits for them, and re-layouts  1.41 us
    slice x1, local copies, waits for them, and re-layouts, whole_group(): group_loss = sums[2, 0:1]  1.18 us
  transfers between devices with their start and end apart: 16, of which 7 were waited for; matrix products, arithmetic and copies ran while one was open for 3% of the time, Pallas kernels for 0%

profile of v9, /device:TPU:0, one launch (start us, length us, event | category | flops | bytes accessed | tf_op | source)
XLA Modules:
  0.0 40.0 jit_solution(18245235250476374642)
XLA Ops:
  0.6 3.1 %collective-permute-start.1 = (bf16[1,64,1152]{2,1,0:T(8,128)(2,1)}, bf16[1,64,1152]{2,1,0:T(8,128)(2,1)S(1)}, u32[]{:S(2)}, u32[]{:S(2)}) collective-permute-start(bf16[1,64,1152]{2,1,0:T(8,128)(2,1)} %refs_7_.1), channel_id=1, source_target_pairs={{0,16},{4,20},{8,24},{12,28},{16,0},{20,4},{24,8},{28,12},{1,17},{... | collective-permute-start | bytes 442376 | tf_op jit(solution)/shard_map/ppermute | solution.py:15
  3.7 1.5 %collective-permute-start = (bf16[1,64,1152]{2,1,0:T(8,128)(2,1)}, bf16[1,64,1152]{2,1,0:T(8,128)(2,1)S(1)}, u32[]{:S(2)}, u32[]{:S(2)}) collective-permute-start(bf16[1,64,1152]{2,1,0:T(8,128)(2,1)} %refs_7_.1), channel_id=1, source_target_pairs={{0,8},{4,12},{8,0},{12,4},{16,24},{20,28},{24,16},{28,20},{1,9},{5... | collective-permute-start | bytes 442376 | tf_op jit(solution)/shard_map/ppermute | solution.py:15
  5.2 0.5 %collective-permute-start.7 = (bf16[1,64,1152]{2,1,0:T(8,128)(2,1)}, bf16[1,64,1152]{2,1,0:T(8,128)(2,1)S(1)}, u32[]{:S(2)}, u32[]{:S(2)}) collective-permute-start(bf16[1,64,1152]{2,1,0:T(8,128)(2,1)} %refs_15_.1), channel_id=1, source_target_pairs={{0,16},{4,20},{8,24},{12,28},{16,0},{20,4},{24,8},{28,12},{1,17},{... | collective-permute-start | bytes 442376 | tf_op jit(solution)/shard_map/ppermute | solution.py:15
  5.7 0.1 collective-permute-start.8
  5.8 1.9 %collective-permute-done.1.refs_9_ = bf16[1,64,1152]{2,1,0:T(8,128)(2,1)S(1)} collective-permute-done((bf16[1,64,1152]{2,1,0:T(8,128)(2,1)}, bf16[1,64,1152]{2,1,0:T(8,128)(2,1)S(1)}, u32[]{:S(2)}, u32[]{:S(2)}) %collective-permute-start.1) | collective-permute-done | bytes 147488 | tf_op jit(solution)/shard_map/ppermute | solution.py:15
  7.8 2.0 %collective-permute-done.refs_8_ = bf16[1,64,1152]{2,1,0:T(8,128)(2,1)S(1)} collective-permute-done((bf16[1,64,1152]{2,1,0:T(8,128)(2,1)}, bf16[1,64,1152]{2,1,0:T(8,128)(2,1)S(1)}, u32[]{:S(2)}, u32[]{:S(2)}) %collective-permute-start) | collective-permute-done | bytes 147488 | tf_op jit(solution)/shard_map/ppermute | solution.py:15
  9.8 0.7 %collective-permute-start.2 = (bf16[1,64,1152]{2,1,0:T(8,128)(2,1)S(1)}, bf16[1,64,1152]{2,1,0:T(8,128)(2,1)S(1)}, u32[]{:S(2)}, u32[]{:S(2)}) collective-permute-start(bf16[1,64,1152]{2,1,0:T(8,128)(2,1)S(1)} %collective-permute-done.refs_8_), channel_id=1, source_target_pairs={{0,16},{4,20},{8,24},{12,28},{16,0},{20,4},{24,8},{28,12},{1,17},{... | collective-permute-start | bytes 442376 | tf_op jit(solution)/shard_map/ppermute | solution.py:15
  10.5 1.2 %collective-permute-done.7.refs_16_ = bf16[1,64,1152]{2,1,0:T(8,128)(2,1)S(1)} collective-permute-done((bf16[1,64,1152]{2,1,0:T(8,128)(2,1)}, bf16[1,64,1152]{2,1,0:T(8,128)(2,1)S(1)}, u32[]{:S(2)}, u32[]{:S(2)}) %collective-permute-start.7) | collective-permute-done | bytes 147488 | tf_op jit(solution)/shard_map/ppermute | solution.py:15
  11.7 1.0 %collective-permute-start.9 = (bf16[1,64,1152]{2,1,0:T(8,128)(2,1)S(1)}, bf16[1,64,1152]{2,1,0:T(8,128)(2,1)S(1)}, u32[]{:S(2)}, u32[]{:S(2)}) collective-permute-start(bf16[1,64,1152]{2,1,0:T(8,128)(2,1)S(1)} %collective-permute-done.7.refs_16_), channel_id=1, source_target_pairs={{0,8},{4,12},{8,0},{12,4},{16,24},{20,28},{24,16},{28,20},{1,9},{5... | collective-permute-start | bytes 442376 | tf_op jit(solution)/shard_map/ppermute | solution.py:15
  12.7 0.5 %collective-permute-start.11 = (bf16[1,64,1152]{2,1,0:T(8,128)(2,1)S(1)}, bf16[1,64,1152]{2,1,0:T(8,128)(2,1)S(1)}, u32[]{:S(2)}, u32[]{:S(2)}) collective-permute-start(bf16[1,64,1152]{2,1,0:T(8,128)(2,1)S(1)} %collective-permute-done.7.refs_16_), channel_id=1, source_target_pairs={{0,4},{4,0},{8,12},{12,8},{16,20},{20,16},{24,28},{28,24},{1,5},{5... | collective-permute-start | bytes 442376 | tf_op jit(solution)/shard_map/ppermute | solution.py:15
  13.2 0.1 collective-permute-start.12
  13.3 2.8 %collective-permute-done.2.refs_10_ = bf16[1,64,1152]{2,1,0:T(8,128)(2,1)S(1)} collective-permute-done((bf16[1,64,1152]{2,1,0:T(8,128)(2,1)S(1)}, bf16[1,64,1152]{2,1,0:T(8,128)(2,1)S(1)}, u32[]{:S(2)}, u32[]{:S(2)}) %collective-permute-start.2) | collective-permute-done | bytes 147488 | tf_op jit(solution)/shard_map/ppermute | solution.py:15
  16.0 1.0 %collective-permute-done.9.refs_18_ = bf16[1,64,1152]{2,1,0:T(8,128)(2,1)S(1)} collective-permute-done((bf16[1,64,1152]{2,1,0:T(8,128)(2,1)S(1)}, bf16[1,64,1152]{2,1,0:T(8,128)(2,1)S(1)}, u32[]{:S(2)}, u32[]{:S(2)}) %collective-permute-start.9) | collective-permute-done | bytes 147488 | tf_op jit(solution)/shard_map/ppermute | solution.py:15
  19.2 0.5 %copy-done.9 = bf16[1,64,1152]{2,1,0:T(8,128)(2,1)} copy-done((bf16[1,64,1152]{2,1,0:T(8,128)(2,1)}, bf16[1,64,1152]{2,1,0:T(8,128)(2,1)S(1)}, u32[]{:S(2)}) %copy-start.9) | copy-done | bytes 147480
  19.8 0.1 copy-done.12
  19.9 0.7 %copy-done.13 = bf16[1,64,1152]{2,1,0:T(8,128)(2,1)} copy-done((bf16[1,64,1152]{2,1,0:T(8,128)(2,1)}, bf16[1,64,1152]{2,1,0:T(8,128)(2,1)S(1)}, u32[]{:S(2)}) %copy-start.13) | copy-done | bytes 147480
  20.6 9.4 %shard_map.120 = (bf16[1,64,1152]{2,1,0:T(8,128)(2,1)}, bf16[1,64,1152]{2,1,0:T(8,128)(2,1)}, f32[3,1152]{1,0:T(4,128)}) custom-call(f32[1]{0:T(128)S(6)} %copy.13.refs_0_, f32[1]{0:T(128)S(6)} %copy.14.refs_1_, f32[1]{0:T(128)S(6)} %copy.15.refs_2_, s32[1,8]{1,0:T(1,128)} %refs_3_.1, f32[1152]{0:T(1024)} %refs_4_.1, f32[1152]{0:T(1024)} %refs_5_.1, ...), custom_call_target="tpu_custom_call" | custom-call | tf_op jit(solution)/shard_map/pallas_call | solution.py:328
  30.0 1.6 %collective-permute-start.14 = (f32[3,1152]{1,0:T(4,128)}, f32[3,1152]{1,0:T(4,128)S(1)}, u32[]{:S(2)}, u32[]{:S(2)}) collective-permute-start(f32[3,1152]{1,0:T(4,128)} %get-tuple-element.9), channel_id=1, source_target_pairs={{0,1},{1,0},{2,3},{3,2},{4,5},{5,4},{6,7},{7,6},{8,9},{9,8},{10,11... | collective-permute-start | bytes 41480 | tf_op jit(solution)/shard_map/ppermute | solution.py:15
  31.6 2.4 %collective-permute-done.14 = f32[3,1152]{1,0:T(4,128)S(1)} collective-permute-done((f32[3,1152]{1,0:T(4,128)}, f32[3,1152]{1,0:T(4,128)S(1)}, u32[]{:S(2)}, u32[]{:S(2)}) %collective-permute-start.14) | collective-permute-done | bytes 13856 | tf_op jit(solution)/shard_map/ppermute | solution.py:15
  34.0 0.7 %add.6 = f32[3,1152]{1,0:T(4,128)S(1)} add(f32[3,1152]{1,0:T(4,128)} %get-tuple-element.9, f32[3,1152]{1,0:T(4,128)S(1)} %collective-permute-done.14) | non-fusion elementwise | flops 3456 | bytes 41472 | tf_op jit(solution)/shard_map/add | solution.py:69
  34.7 2.6 %collective-permute-start.15 = (f32[3,1152]{1,0:T(4,128)S(1)}, f32[3,1152]{1,0:T(4,128)S(1)}, u32[]{:S(2)}, u32[]{:S(2)}) collective-permute-start(f32[3,1152]{1,0:T(4,128)S(1)} %add.6), channel_id=1, source_target_pairs={{0,2},{1,3},{2,0},{3,1},{4,6},{5,7},{6,4},{7,5},{8,10},{9,11},{10,... | collective-permute-start | bytes 41480 | tf_op jit(solution)/shard_map/ppermute | solution.py:15
  37.3 1.2 %slice.11 = f32[1,1]{1,0:T(1,128)} slice(f32[3,1152]{1,0:T(4,128)} %get-tuple-element.9), slice={[2:3], [0:1]} | slice | bytes 8 | tf_op jit(solution)/shard_map/slice | solution.py:356
  38.5 0.9 %collective-permute-done.15 = f32[3,1152]{1,0:T(4,128)S(1)} collective-permute-done((f32[3,1152]{1,0:T(4,128)S(1)}, f32[3,1152]{1,0:T(4,128)S(1)}, u32[]{:S(2)}, u32[]{:S(2)}) %collective-permute-start.15) | collective-permute-done | bytes 13856 | tf_op jit(solution)/shard_map/ppermute | solution.py:15
  39.4 0.6 %slice_add_fusion = f32[2,1152]{1,0:T(2,128)} fusion(f32[3,1152]{1,0:T(4,128)S(1)} %collective-permute-done.15, f32[3,1152]{1,0:T(4,128)S(1)} %add.6), kind=kLoop, calls=%fused_computation | loop fusion | flops 2304 | bytes 27648 | tf_op jit(solution)/shard_map/add | solution.py:71
  (40 shorter events, 0.2 us)
Async XLA Ops:
  0.6 7.1 %collective-permute-start.1 = (bf16[1,64,1152]{2,1,0:T(8,128)(2,1)}, bf16[1,64,1152]{2,1,0:T(8,128)(2,1)S(1)}, u32[]{:S(2)}, u32[]{:S(2)}) collective-permute-start(bf16[1,64,1152]{2,1,0:T(8,128)(2,1)} %refs_7_.1), channel_id=1, source_target_pairs={{0,16},{4,20},{8,24},{12,28},{16,0},{20,4},{24,8},{28,12},{1,17},{... | collective-permute-start | bytes 442376 | tf_op jit(solution)/shard_map/ppermute | solution.py:15
  3.7 6.0 %collective-permute-start = (bf16[1,64,1152]{2,1,0:T(8,128)(2,1)}, bf16[1,64,1152]{2,1,0:T(8,128)(2,1)S(1)}, u32[]{:S(2)}, u32[]{:S(2)}) collective-permute-start(bf16[1,64,1152]{2,1,0:T(8,128)(2,1)} %refs_7_.1), channel_id=1, source_target_pairs={{0,8},{4,12},{8,0},{12,4},{16,24},{20,28},{24,16},{28,20},{1,9},{5... | collective-permute-start | bytes 442376 | tf_op jit(solution)/shard_map/ppermute | solution.py:15
  5.2 4.6 %collective-permute-start.3 = (bf16[1,64,1152]{2,1,0:T(8,128)(2,1)}, bf16[1,64,1152]{2,1,0:T(8,128)(2,1)S(1)}, u32[]{:S(2)}, u32[]{:S(2)}) collective-permute-start(bf16[1,64,1152]{2,1,0:T(8,128)(2,1)} %refs_7_.1), channel_id=1, source_target_pairs={{0,4},{4,0},{8,12},{12,8},{16,20},{20,16},{24,28},{28,24},{1,5},{5... | collective-permute-start | bytes 442376 | tf_op jit(solution)/shard_map/ppermute | solution.py:15
  5.2 6.5 %collective-permute-start.7 = (bf16[1,64,1152]{2,1,0:T(8,128)(2,1)}, bf16[1,64,1152]{2,1,0:T(8,128)(2,1)S(1)}, u32[]{:S(2)}, u32[]{:S(2)}) collective-permute-start(bf16[1,64,1152]{2,1,0:T(8,128)(2,1)} %refs_15_.1), channel_id=1, source_target_pairs={{0,16},{4,20},{8,24},{12,28},{16,0},{20,4},{24,8},{28,12},{1,17},{... | collective-permute-start | bytes 442376 | tf_op jit(solution)/shard_map/ppermute | solution.py:15
  5.7 7.0 %collective-permute-start.8 = (bf16[1,64,1152]{2,1,0:T(8,128)(2,1)}, bf16[1,64,1152]{2,1,0:T(8,128)(2,1)S(1)}, u32[]{:S(2)}, u32[]{:S(2)}) collective-permute-start(bf16[1,64,1152]{2,1,0:T(8,128)(2,1)} %refs_15_.1), channel_id=1, source_target_pairs={{0,8},{4,12},{8,0},{12,4},{16,24},{20,28},{24,16},{28,20},{1,9},{5... | collective-permute-start | bytes 442376 | tf_op jit(solution)/shard_map/ppermute | solution.py:15
  7.8 11.4 %copy-start = (bf16[1,64,1152]{2,1,0:T(8,128)(2,1)}, bf16[1,64,1152]{2,1,0:T(8,128)(2,1)S(1)}, u32[]{:S(2)}) copy-start(bf16[1,64,1152]{2,1,0:T(8,128)(2,1)S(1)} %collective-permute-done.1.refs_9_) | copy-start | bytes 442372
  7.8 4.9 %collective-permute-start.10 = (bf16[1,64,1152]{2,1,0:T(8,128)(2,1)}, bf16[1,64,1152]{2,1,0:T(8,128)(2,1)S(1)}, u32[]{:S(2)}, u32[]{:S(2)}) collective-permute-start(bf16[1,64,1152]{2,1,0:T(8,128)(2,1)} %refs_15_.1), channel_id=1, source_target_pairs={{0,4},{4,0},{8,12},{12,8},{16,20},{20,16},{24,28},{28,24},{1,5},{5... | collective-permute-start | bytes 442376 | tf_op jit(solution)/shard_map/ppermute | solution.py:15
  9.7 9.4 %copy-start.1 = (bf16[1,64,1152]{2,1,0:T(8,128)(2,1)}, bf16[1,64,1152]{2,1,0:T(8,128)(2,1)S(1)}, u32[]{:S(2)}) copy-start(bf16[1,64,1152]{2,1,0:T(8,128)(2,1)S(1)} %collective-permute-done.refs_8_) | copy-start | bytes 442372
  9.7 3.4 %collective-permute-start.5 = (bf16[1,64,1152]{2,1,0:T(8,128)(2,1)S(1)}, bf16[1,64,1152]{2,1,0:T(8,128)(2,1)S(1)}, u32[]{:S(2)}, u32[]{:S(2)}) collective-permute-start(bf16[1,64,1152]{2,1,0:T(8,128)(2,1)S(1)} %collective-permute-done.1.refs_9_), channel_id=1, source_target_pairs={{0,4},{4,0},{8,12},{12,8},{16,20},{20,16},{24,28},{28,24},{1,5},{5... | collective-permute-start | bytes 442376 | tf_op jit(solution)/shard_map/ppermute | solution.py:15
  9.7 9.4 %copy-start.2 = (bf16[1,64,1152]{2,1,0:T(8,128)(2,1)}, bf16[1,64,1152]{2,1,0:T(8,128)(2,1)S(1)}, u32[]{:S(2)}) copy-start(bf16[1,64,1152]{2,1,0:T(8,128)(2,1)S(1)} %collective-permute-done.3.refs_11_) | copy-start | bytes 442372
  9.8 6.3 %collective-permute-start.2 = (bf16[1,64,1152]{2,1,0:T(8,128)(2,1)S(1)}, bf16[1,64,1152]{2,1,0:T(8,128)(2,1)S(1)}, u32[]{:S(2)}, u32[]{:S(2)}) collective-permute-start(bf16[1,64,1152]{2,1,0:T(8,128)(2,1)S(1)} %collective-permute-done.refs_8_), channel_id=1, source_target_pairs={{0,16},{4,20},{8,24},{12,28},{16,0},{20,4},{24,8},{28,12},{1,17},{... | collective-permute-start | bytes 442376 | tf_op jit(solution)/shard_map/ppermute | solution.py:15
  11.7 7.5 %copy-start.3 = (bf16[1,64,1152]{2,1,0:T(8,128)(2,1)}, bf16[1,64,1152]{2,1,0:T(8,128)(2,1)S(1)}, u32[]{:S(2)}) copy-start(bf16[1,64,1152]{2,1,0:T(8,128)(2,1)S(1)} %collective-permute-done.7.refs_16_) | copy-start | bytes 442372
  11.7 5.4 %collective-permute-start.9 = (bf16[1,64,1152]{2,1,0:T(8,128)(2,1)S(1)}, bf16[1,64,1152]{2,1,0:T(8,128)(2,1)S(1)}, u32[]{:S(2)}, u32[]{:S(2)}) collective-permute-start(bf16[1,64,1152]{2,1,0:T(8,128)(2,1)S(1)} %collective-permute-done.7.refs_16_), channel_id=1, source_target_pairs={{0,8},{4,12},{8,0},{12,4},{16,24},{20,28},{24,16},{28,20},{1,9},{5... | collective-permute-start | bytes 442376 | tf_op jit(solution)/shard_map/ppermute | solution.py:15
  12.6 6.5 %copy-start.4 = (bf16[1,64,1152]{2,1,0:T(8,128)(2,1)}, bf16[1,64,1152]{2,1,0:T(8,128)(2,1)S(1)}, u32[]{:S(2)}) copy-start(bf16[1,64,1152]{2,1,0:T(8,128)(2,1)S(1)} %collective-permute-done.8.refs_17_) | copy-start | bytes 442372
  12.7 6.4 %collective-permute-start.4 = (bf16[1,64,1152]{2,1,0:T(8,128)(2,1)S(1)}, bf16[1,64,1152]{2,1,0:T(8,128)(2,1)S(1)}, u32[]{:S(2)}, u32[]{:S(2)}) collective-permute-start(bf16[1,64,1152]{2,1,0:T(8,128)(2,1)S(1)} %collective-permute-done.refs_8_), channel_id=1, source_target_pairs={{0,4},{4,0},{8,12},{12,8},{16,20},{20,16},{24,28},{28,24},{1,5},{5... | collective-permute-start | bytes 442376 | tf_op jit(solution)/shard_map/ppermute | solution.py:15
  12.7 6.5 %copy-start.5 = (bf16[1,64,1152]{2,1,0:T(8,128)(2,1)}, bf16[1,64,1152]{2,1,0:T(8,128)(2,1)S(1)}, u32[]{:S(2)}) copy-start(bf16[1,64,1152]{2,1,0:T(8,128)(2,1)S(1)} %collective-permute-done.10.refs_19_) | copy-start | bytes 442372
  12.7 6.4 %collective-permute-start.11 = (bf16[1,64,1152]{2,1,0:T(8,128)(2,1)S(1)}, bf16[1,64,1152]{2,1,0:T(8,128)(2,1)S(1)}, u32[]{:S(2)}, u32[]{:S(2)}) collective-permute-start(bf16[1,64,1152]{2,1,0:T(8,128)(2,1)S(1)} %collective-permute-done.7.refs_16_), channel_id=1, source_target_pairs={{0,4},{4,0},{8,12},{12,8},{16,20},{20,16},{24,28},{28,24},{1,5},{5... | collective-permute-start | bytes 442376 | tf_op jit(solution)/shard_map/ppermute | solution.py:15
  13.2 6.0 %copy-start.6 = (bf16[1,64,1152]{2,1,0:T(8,128)(2,1)}, bf16[1,64,1152]{2,1,0:T(8,128)(2,1)S(1)}, u32[]{:S(2)}) copy-start(bf16[1,64,1152]{2,1,0:T(8,128)(2,1)S(1)} %collective-permute-done.5.refs_13_) | copy-start | bytes 442372
  13.2 5.9 %collective-permute-start.12 = (bf16[1,64,1152]{2,1,0:T(8,128)(2,1)S(1)}, bf16[1,64,1152]{2,1,0:T(8,128)(2,1)S(1)}, u32[]{:S(2)}, u32[]{:S(2)}) collective-permute-start(bf16[1,64,1152]{2,1,0:T(8,128)(2,1)S(1)} %collective-permute-done.8.refs_17_), channel_id=1, source_target_pairs={{0,4},{4,0},{8,12},{12,8},{16,20},{20,16},{24,28},{28,24},{1,5},{5... | collective-permute-start | bytes 442376 | tf_op jit(solution)/shard_map/ppermute | solution.py:15
  16.0 3.2 %copy-start.7 = (bf16[1,64,1152]{2,1,0:T(8,128)(2,1)}, bf16[1,64,1152]{2,1,0:T(8,128)(2,1)S(1)}, u32[]{:S(2)}) copy-start(bf16[1,64,1152]{2,1,0:T(8,128)(2,1)S(1)} %collective-permute-done.2.refs_10_) | copy-start | bytes 442372
  16.0 3.1 %collective-permute-start.6 = (bf16[1,64,1152]{2,1,0:T(8,128)(2,1)S(1)}, bf16[1,64,1152]{2,1,0:T(8,128)(2,1)S(1)}, u32[]{:S(2)}, u32[]{:S(2)}) collective-permute-start(bf16[1,64,1152]{2,1,0:T(8,128)(2,1)S(1)} %collective-permute-done.2.refs_10_), channel_id=1, source_target_pairs={{0,4},{4,0},{8,12},{12,8},{16,20},{20,16},{24,28},{28,24},{1,5},{5... | collective-permute-start | bytes 442376 | tf_op jit(solution)/shard_map/ppermute | solution.py:15
  17.1 2.0 %collective-permute-start.13 = (bf16[1,64,1152]{2,1,0:T(8,128)(2,1)S(1)}, bf16[1,64,1152]{2,1,0:T(8,128)(2,1)S(1)}, u32[]{:S(2)}, u32[]{:S(2)}) collective-permute-start(bf16[1,64,1152]{2,1,0:T(8,128)(2,1)S(1)} %collective-permute-done.9.refs_18_), channel_id=1, source_target_pairs={{0,4},{4,0},{8,12},{12,8},{16,20},{20,16},{24,28},{28,24},{1,5},{5... | collective-permute-start | bytes 442376 | tf_op jit(solution)/shard_map/ppermute | solution.py:15
  30.0 4.0 %collective-permute-start.14 = (f32[3,1152]{1,0:T(4,128)}, f32[3,1152]{1,0:T(4,128)S(1)}, u32[]{:S(2)}, u32[]{:S(2)}) collective-permute-start(f32[3,1152]{1,0:T(4,128)} %get-tuple-element.9), channel_id=1, source_target_pairs={{0,1},{1,0},{2,3},{3,2},{4,5},{5,4},{6,7},{7,6},{8,9},{9,8},{10,11... | collective-permute-start | bytes 41480 | tf_op jit(solution)/shard_map/ppermute | solution.py:15
  34.7 4.7 %collective-permute-start.15 = (f32[3,1152]{1,0:T(4,128)S(1)}, f32[3,1152]{1,0:T(4,128)S(1)}, u32[]{:S(2)}, u32[]{:S(2)}) collective-permute-start(f32[3,1152]{1,0:T(4,128)S(1)} %add.6), channel_id=1, source_target_pairs={{0,2},{1,3},{2,0},{3,1},{4,6},{5,7},{6,4},{7,5},{8,10},{9,11},{10,... | collective-permute-start | bytes 41480 | tf_op jit(solution)/shard_map/ppermute | solution.py:15
  (6 other events, 5.7 us)

commit v10 on v9

--- a/solution.py
+++ b/solution.py
@@ -202,7 +202,7 @@
     count = len(image_masks)
     pieces = refs[7 : 7 + 2 * count]
     (image_grad_ref, text_grad_ref, sums_ref, raw_ref, unit_ref, short_ref, normed_ref, inverse_ref,
-     length_ref, weights_ref, flipped_ref, copy_sems) = refs[7 + 2 * count :]
+     length_ref, weights_ref, copy_sems) = refs[7 + 2 * count :]
     block_rows = pieces[0].shape[1]
     group_rows = raw_ref.shape[1]
     width = raw_ref.shape[2]
@@ -272,18 +272,25 @@
         labels = jnp.where(partner_of_image[first : first + chunk] == text_row, 1.0, -1.0)
         kept = image_real[first : first + chunk] & text_real
         margin = -labels * score_similarity_table
-        softplus = jnp.maximum(margin, 0.0) + jnp.log1p(jnp.exp(-jnp.abs(margin)))
+        decay = jnp.exp(-jnp.abs(margin))
+        softplus = jnp.maximum(margin, 0.0) + jnp.log1p(decay)
         loss = loss + jnp.sum(jnp.where(kept, softplus, 0.0), axis=(0, 1), keepdims=True)
-        weights = jnp.where(kept, -labels * jax.nn.sigmoid(margin), 0.0) * grad_factor
+        sigmoid = jnp.where(margin >= 0.0, 1.0, decay) / (1.0 + decay)
+        weights = jnp.where(kept, -labels * sigmoid, 0.0) * grad_factor
         weights_ref[rows, :] = weights.astype(weights_ref.dtype)
-        flipped_ref[:, rows] = weights.T.astype(flipped_ref.dtype)
-
-    for tower, (pair_ref, grad_ref) in enumerate(((weights_ref, image_grad_ref), (flipped_ref, text_grad_ref))):
+
+    for tower, grad_ref in enumerate((image_grad_ref, text_grad_ref)):
         gain_sum = jnp.zeros((1, width), jnp.float32)
         for first in range(0, group_rows, chunk):
             rows = pl.ds(first, chunk)
-            direction = score_sharpness_factor * jnp.dot(
-                pair_ref[rows, :], short_ref[1 - tower], preferred_element_type=jnp.float32
+            if tower == 0:
+                pairs = weights_ref[rows, :]
+                contract = (((1,), (0,)), ((), ()))
+            else:
+                pairs = weights_ref[:, rows]
+                contract = (((0,), (0,)), ((), ()))
+            direction = score_sharpness_factor * lax.dot_general(
+                pairs, short_ref[1 - tower], contract, preferred_element_type=jnp.float32
             )
             unit_rows = unit_ref[tower, rows, :]
             normed = normed_ref[tower, rows, :]
@@ -340,7 +347,6 @@
             pltpu.VMEM(column, jnp.float32),
             pltpu.VMEM(column, jnp.float32),
             pltpu.VMEM((group_rows, group_rows), jnp.bfloat16),
-            pltpu.VMEM((group_rows, group_rows), jnp.bfloat16),
             pltpu.SemaphoreType.DMA((len(pieces),)),
         ],
     )(

time: 40.3 us -> 40.3 us (level)
  no operation moved by 1% of the time
where the time goes in v10:
time: 40.3 us; the launch traced here: 40 us
  waiting for transfers between devices  12.2 us (30%)
  starting transfers between devices  11.7 us (29%)
  Pallas kernels  9.42 us (23%)
  between operations  2.77 us (7%)
  local copies, waits for them, and re-layouts  2.59 us (6%)
  other arithmetic  1.33 us (3%)
    ppermute x16, waiting for transfers between devices, xor_swap(): lax.ppermute(value, axis, [(source, source ^ bit) for source in range(cou...  12.2 us
    ppermute x16, starting transfers between devices, xor_swap(): lax.ppermute(value, axis, [(source, source ^ bit) for source in range(cou...  11.7 us
    pallas_call x1, Pallas kernels, whole_group(): pl.pallas_call(functools.partial(group_kernel, tuple(masks[:count]), tupl...  9.42 us
    unnamed x28, local copies, waits for them, and re-layouts  1.41 us
    slice x1, local copies, waits for them, and re-layouts, whole_group(): group_loss = sums[2, 0:1]  1.18 us
  transfers between devices with their start and end apart: 16, of which 7 were waited for; matrix products, arithmetic and copies ran while one was open for 3% of the time, Pallas kernels for 0%

profile of v10, /device:TPU:0, one launch (start us, length us, event | category | flops | bytes accessed | tf_op | source)
XLA Modules:
  0.0 40.0 jit_solution(8540337018210855631)
XLA Ops:
  0.6 3.1 %collective-permute-start.1 = (bf16[1,64,1152]{2,1,0:T(8,128)(2,1)}, bf16[1,64,1152]{2,1,0:T(8,128)(2,1)S(1)}, u32[]{:S(2)}, u32[]{:S(2)}) collective-permute-start(bf16[1,64,1152]{2,1,0:T(8,128)(2,1)} %refs_7_.1), channel_id=1, source_target_pairs={{0,16},{4,20},{8,24},{12,28},{16,0},{20,4},{24,8},{28,12},{1,17},{... | collective-permute-start | bytes 442376 | tf_op jit(solution)/shard_map/ppermute | solution.py:15
  3.7 1.5 %collective-permute-start = (bf16[1,64,1152]{2,1,0:T(8,128)(2,1)}, bf16[1,64,1152]{2,1,0:T(8,128)(2,1)S(1)}, u32[]{:S(2)}, u32[]{:S(2)}) collective-permute-start(bf16[1,64,1152]{2,1,0:T(8,128)(2,1)} %refs_7_.1), channel_id=1, source_target_pairs={{0,8},{4,12},{8,0},{12,4},{16,24},{20,28},{24,16},{28,20},{1,9},{5... | collective-permute-start | bytes 442376 | tf_op jit(solution)/shard_map/ppermute | solution.py:15
  5.2 0.5 %collective-permute-start.7 = (bf16[1,64,1152]{2,1,0:T(8,128)(2,1)}, bf16[1,64,1152]{2,1,0:T(8,128)(2,1)S(1)}, u32[]{:S(2)}, u32[]{:S(2)}) collective-permute-start(bf16[1,64,1152]{2,1,0:T(8,128)(2,1)} %refs_15_.1), channel_id=1, source_target_pairs={{0,16},{4,20},{8,24},{12,28},{16,0},{20,4},{24,8},{28,12},{1,17},{... | collective-permute-start | bytes 442376 | tf_op jit(solution)/shard_map/ppermute | solution.py:15
  5.7 0.1 collective-permute-start.8
  5.8 1.9 %collective-permute-done.1.refs_9_ = bf16[1,64,1152]{2,1,0:T(8,128)(2,1)S(1)} collective-permute-done((bf16[1,64,1152]{2,1,0:T(8,128)(2,1)}, bf16[1,64,1152]{2,1,0:T(8,128)(2,1)S(1)}, u32[]{:S(2)}, u32[]{:S(2)}) %collective-permute-start.1) | collective-permute-done | bytes 147488 | tf_op jit(solution)/shard_map/ppermute | solution.py:15
  7.8 2.0 %collective-permute-done.refs_8_ = bf16[1,64,1152]{2,1,0:T(8,128)(2,1)S(1)} collective-permute-done((bf16[1,64,1152]{2,1,0:T(8,128)(2,1)}, bf16[1,64,1152]{2,1,0:T(8,128)(2,1)S(1)}, u32[]{:S(2)}, u32[]{:S(2)}) %collective-permute-start) | collective-permute-done | bytes 147488 | tf_op jit(solution)/shard_map/ppermute | solution.py:15
  9.8 0.7 %collective-permute-start.2 = (bf16[1,64,1152]{2,1,0:T(8,128)(2,1)S(1)}, bf16[1,64,1152]{2,1,0:T(8,128)(2,1)S(1)}, u32[]{:S(2)}, u32[]{:S(2)}) collective-permute-start(bf16[1,64,1152]{2,1,0:T(8,128)(2,1)S(1)} %collective-permute-done.refs_8_), channel_id=1, source_target_pairs={{0,16},{4,20},{8,24},{12,28},{16,0},{20,4},{24,8},{28,12},{1,17},{... | collective-permute-start | bytes 442376 | tf_op jit(solution)/shard_map/ppermute | solution.py:15
  10.5 1.2 %collective-permute-done.7.refs_16_ = bf16[1,64,1152]{2,1,0:T(8,128)(2,1)S(1)} collective-permute-done((bf16[1,64,1152]{2,1,0:T(8,128)(2,1)}, bf16[1,64,1152]{2,1,0:T(8,128)(2,1)S(1)}, u32[]{:S(2)}, u32[]{:S(2)}) %collective-permute-start.7) | collective-permute-done | bytes 147488 | tf_op jit(solution)/shard_map/ppermute | solution.py:15
  11.7 1.0 %collective-permute-start.9 = (bf16[1,64,1152]{2,1,0:T(8,128)(2,1)S(1)}, bf16[1,64,1152]{2,1,0:T(8,128)(2,1)S(1)}, u32[]{:S(2)}, u32[]{:S(2)}) collective-permute-start(bf16[1,64,1152]{2,1,0:T(8,128)(2,1)S(1)} %collective-permute-done.7.refs_16_), channel_id=1, source_target_pairs={{0,8},{4,12},{8,0},{12,4},{16,24},{20,28},{24,16},{28,20},{1,9},{5... | collective-permute-start | bytes 442376 | tf_op jit(solution)/shard_map/ppermute | solution.py:15
  12.7 0.5 %collective-permute-start.11 = (bf16[1,64,1152]{2,1,0:T(8,128)(2,1)S(1)}, bf16[1,64,1152]{2,1,0:T(8,128)(2,1)S(1)}, u32[]{:S(2)}, u32[]{:S(2)}) collective-permute-start(bf16[1,64,1152]{2,1,0:T(8,128)(2,1)S(1)} %collective-permute-done.7.refs_16_), channel_id=1, source_target_pairs={{0,4},{4,0},{8,12},{12,8},{16,20},{20,16},{24,28},{28,24},{1,5},{5... | collective-permute-start | bytes 442376 | tf_op jit(solution)/shard_map/ppermute | solution.py:15
  13.2 0.1 collective-permute-start.12
  13.3 2.8 %collective-permute-done.2.refs_10_ = bf16[1,64,1152]{2,1,0:T(8,128)(2,1)S(1)} collective-permute-done((bf16[1,64,1152]{2,1,0:T(8,128)(2,1)S(1)}, bf16[1,64,1152]{2,1,0:T(8,128)(2,1)S(1)}, u32[]{:S(2)}, u32[]{:S(2)}) %collective-permute-start.2) | collective-permute-done | bytes 147488 | tf_op jit(solution)/shard_map/ppermute | solution.py:15
  16.0 1.0 %collective-permute-done.9.refs_18_ = bf16[1,64,1152]{2,1,0:T(8,128)(2,1)S(1)} collective-permute-done((bf16[1,64,1152]{2,1,0:T(8,128)(2,1)S(1)}, bf16[1,64,1152]{2,1,0:T(8,128)(2,1)S(1)}, u32[]{:S(2)}, u32[]{:S(2)}) %collective-permute-start.9) | collective-permute-done | bytes 147488 | tf_op jit(solution)/shard_map/ppermute | solution.py:15
  19.2 0.5 %copy-done.9 = bf16[1,64,1152]{2,1,0:T(8,128)(2,1)} copy-done((bf16[1,64,1152]{2,1,0:T(8,128)(2,1)}, bf16[1,64,1152]{2,1,0:T(8,128)(2,1)S(1)}, u32[]{:S(2)}) %copy-start.9) | copy-done | bytes 147480
  19.8 0.1 copy-done.12
  19.9 0.7 %copy-done.13 = bf16[1,64,1152]{2,1,0:T(8,128)(2,1)} copy-done((bf16[1,64,1152]{2,1,0:T(8,128)(2,1)}, bf16[1,64,1152]{2,1,0:T(8,128)(2,1)S(1)}, u32[]{:S(2)}) %copy-start.13) | copy-done | bytes 147480
  20.6 9.4 %shard_map.120 = (bf16[1,64,1152]{2,1,0:T(8,128)(2,1)}, bf16[1,64,1152]{2,1,0:T(8,128)(2,1)}, f32[3,1152]{1,0:T(4,128)}) custom-call(f32[1]{0:T(128)S(6)} %copy.13.refs_0_, f32[1]{0:T(128)S(6)} %copy.14.refs_1_, f32[1]{0:T(128)S(6)} %copy.15.refs_2_, s32[1,8]{1,0:T(1,128)} %refs_3_.1, f32[1152]{0:T(1024)} %refs_4_.1, f32[1152]{0:T(1024)} %refs_5_.1, ...), custom_call_target="tpu_custom_call" | custom-call | tf_op jit(solution)/shard_map/pallas_call | solution.py:335
  30.0 1.6 %collective-permute-start.14 = (f32[3,1152]{1,0:T(4,128)}, f32[3,1152]{1,0:T(4,128)S(1)}, u32[]{:S(2)}, u32[]{:S(2)}) collective-permute-start(f32[3,1152]{1,0:T(4,128)} %get-tuple-element.9), channel_id=1, source_target_pairs={{0,1},{1,0},{2,3},{3,2},{4,5},{5,4},{6,7},{7,6},{8,9},{9,8},{10,11... | collective-permute-start | bytes 41480 | tf_op jit(solution)/shard_map/ppermute | solution.py:15
  31.6 2.4 %collective-permute-done.14 = f32[3,1152]{1,0:T(4,128)S(1)} collective-permute-done((f32[3,1152]{1,0:T(4,128)}, f32[3,1152]{1,0:T(4,128)S(1)}, u32[]{:S(2)}, u32[]{:S(2)}) %collective-permute-start.14) | collective-permute-done | bytes 13856 | tf_op jit(solution)/shard_map/ppermute | solution.py:15
  34.0 0.7 %add.6 = f32[3,1152]{1,0:T(4,128)S(1)} add(f32[3,1152]{1,0:T(4,128)} %get-tuple-element.9, f32[3,1152]{1,0:T(4,128)S(1)} %collective-permute-done.14) | non-fusion elementwise | flops 3456 | bytes 41472 | tf_op jit(solution)/shard_map/add | solution.py:69
  34.8 2.6 %collective-permute-start.15 = (f32[3,1152]{1,0:T(4,128)S(1)}, f32[3,1152]{1,0:T(4,128)S(1)}, u32[]{:S(2)}, u32[]{:S(2)}) collective-permute-start(f32[3,1152]{1,0:T(4,128)S(1)} %add.6), channel_id=1, source_target_pairs={{0,2},{1,3},{2,0},{3,1},{4,6},{5,7},{6,4},{7,5},{8,10},{9,11},{10,... | collective-permute-start | bytes 41480 | tf_op jit(solution)/shard_map/ppermute | solution.py:15
  37.4 1.2 %slice.11 = f32[1,1]{1,0:T(1,128)} slice(f32[3,1152]{1,0:T(4,128)} %get-tuple-element.9), slice={[2:3], [0:1]} | slice | bytes 8 | tf_op jit(solution)/shard_map/slice | solution.py:362
  38.5 0.9 %collective-permute-done.15 = f32[3,1152]{1,0:T(4,128)S(1)} collective-permute-done((f32[3,1152]{1,0:T(4,128)S(1)}, f32[3,1152]{1,0:T(4,128)S(1)}, u32[]{:S(2)}, u32[]{:S(2)}) %collective-permute-start.15) | collective-permute-done | bytes 13856 | tf_op jit(solution)/shard_map/ppermute | solution.py:15
  39.4 0.6 %slice_add_fusion = f32[2,1152]{1,0:T(2,128)} fusion(f32[3,1152]{1,0:T(4,128)S(1)} %collective-permute-done.15, f32[3,1152]{1,0:T(4,128)S(1)} %add.6), kind=kLoop, calls=%fused_computation | loop fusion | flops 2304 | bytes 27648 | tf_op jit(solution)/shard_map/add | solution.py:71
  (40 shorter events, 0.2 us)
Async XLA Ops:
  0.6 7.1 %collective-permute-start.1 = (bf16[1,64,1152]{2,1,0:T(8,128)(2,1)}, bf16[1,64,1152]{2,1,0:T(8,128)(2,1)S(1)}, u32[]{:S(2)}, u32[]{:S(2)}) collective-permute-start(bf16[1,64,1152]{2,1,0:T(8,128)(2,1)} %refs_7_.1), channel_id=1, source_target_pairs={{0,16},{4,20},{8,24},{12,28},{16,0},{20,4},{24,8},{28,12},{1,17},{... | collective-permute-start | bytes 442376 | tf_op jit(solution)/shard_map/ppermute | solution.py:15
  3.7 6.0 %collective-permute-start = (bf16[1,64,1152]{2,1,0:T(8,128)(2,1)}, bf16[1,64,1152]{2,1,0:T(8,128)(2,1)S(1)}, u32[]{:S(2)}, u32[]{:S(2)}) collective-permute-start(bf16[1,64,1152]{2,1,0:T(8,128)(2,1)} %refs_7_.1), channel_id=1, source_target_pairs={{0,8},{4,12},{8,0},{12,4},{16,24},{20,28},{24,16},{28,20},{1,9},{5... | collective-permute-start | bytes 442376 | tf_op jit(solution)/shard_map/ppermute | solution.py:15
  5.2 4.6 %collective-permute-start.3 = (bf16[1,64,1152]{2,1,0:T(8,128)(2,1)}, bf16[1,64,1152]{2,1,0:T(8,128)(2,1)S(1)}, u32[]{:S(2)}, u32[]{:S(2)}) collective-permute-start(bf16[1,64,1152]{2,1,0:T(8,128)(2,1)} %refs_7_.1), channel_id=1, source_target_pairs={{0,4},{4,0},{8,12},{12,8},{16,20},{20,16},{24,28},{28,24},{1,5},{5... | collective-permute-start | bytes 442376 | tf_op jit(solution)/shard_map/ppermute | solution.py:15
  5.2 6.5 %collective-permute-start.7 = (bf16[1,64,1152]{2,1,0:T(8,128)(2,1)}, bf16[1,64,1152]{2,1,0:T(8,128)(2,1)S(1)}, u32[]{:S(2)}, u32[]{:S(2)}) collective-permute-start(bf16[1,64,1152]{2,1,0:T(8,128)(2,1)} %refs_15_.1), channel_id=1, source_target_pairs={{0,16},{4,20},{8,24},{12,28},{16,0},{20,4},{24,8},{28,12},{1,17},{... | collective-permute-start | bytes 442376 | tf_op jit(solution)/shard_map/ppermute | solution.py:15
  5.7 7.0 %collective-permute-start.8 = (bf16[1,64,1152]{2,1,0:T(8,128)(2,1)}, bf16[1,64,1152]{2,1,0:T(8,128)(2,1)S(1)}, u32[]{:S(2)}, u32[]{:S(2)}) collective-permute-start(bf16[1,64,1152]{2,1,0:T(8,128)(2,1)} %refs_15_.1), channel_id=1, source_target_pairs={{0,8},{4,12},{8,0},{12,4},{16,24},{20,28},{24,16},{28,20},{1,9},{5... | collective-permute-start | bytes 442376 | tf_op jit(solution)/shard_map/ppermute | solution.py:15
  7.8 11.4 %copy-start = (bf16[1,64,1152]{2,1,0:T(8,128)(2,1)}, bf16[1,64,1152]{2,1,0:T(8,128)(2,1)S(1)}, u32[]{:S(2)}) copy-start(bf16[1,64,1152]{2,1,0:T(8,128)(2,1)S(1)} %collective-permute-done.1.refs_9_) | copy-start | bytes 442372
  7.8 4.9 %collective-permute-start.10 = (bf16[1,64,1152]{2,1,0:T(8,128)(2,1)}, bf16[1,64,1152]{2,1,0:T(8,128)(2,1)S(1)}, u32[]{:S(2)}, u32[]{:S(2)}) collective-permute-start(bf16[1,64,1152]{2,1,0:T(8,128)(2,1)} %refs_15_.1), channel_id=1, source_target_pairs={{0,4},{4,0},{8,12},{12,8},{16,20},{20,16},{24,28},{28,24},{1,5},{5... | collective-permute-start | bytes 442376 | tf_op jit(solution)/shard_map/ppermute | solution.py:15
  9.7 9.4 %copy-start.1 = (bf16[1,64,1152]{2,1,0:T(8,128)(2,1)}, bf16[1,64,1152]{2,1,0:T(8,128)(2,1)S(1)}, u32[]{:S(2)}) copy-start(bf16[1,64,1152]{2,1,0:T(8,128)(2,1)S(1)} %collective-permute-done.refs_8_) | copy-start | bytes 442372
  9.7 3.4 %collective-permute-start.5 = (bf16[1,64,1152]{2,1,0:T(8,128)(2,1)S(1)}, bf16[1,64,1152]{2,1,0:T(8,128)(2,1)S(1)}, u32[]{:S(2)}, u32[]{:S(2)}) collective-permute-start(bf16[1,64,1152]{2,1,0:T(8,128)(2,1)S(1)} %collective-permute-done.1.refs_9_), channel_id=1, source_target_pairs={{0,4},{4,0},{8,12},{12,8},{16,20},{20,16},{24,28},{28,24},{1,5},{5... | collective-permute-start | bytes 442376 | tf_op jit(solution)/shard_map/ppermute | solution.py:15
  9.7 9.4 %copy-start.2 = (bf16[1,64,1152]{2,1,0:T(8,128)(2,1)}, bf16[1,64,1152]{2,1,0:T(8,128)(2,1)S(1)}, u32[]{:S(2)}) copy-start(bf16[1,64,1152]{2,1,0:T(8,128)(2,1)S(1)} %collective-permute-done.3.refs_11_) | copy-start | bytes 442372
  9.8 6.3 %collective-permute-start.2 = (bf16[1,64,1152]{2,1,0:T(8,128)(2,1)S(1)}, bf16[1,64,1152]{2,1,0:T(8,128)(2,1)S(1)}, u32[]{:S(2)}, u32[]{:S(2)}) collective-permute-start(bf16[1,64,1152]{2,1,0:T(8,128)(2,1)S(1)} %collective-permute-done.refs_8_), channel_id=1, source_target_pairs={{0,16},{4,20},{8,24},{12,28},{16,0},{20,4},{24,8},{28,12},{1,17},{... | collective-permute-start | bytes 442376 | tf_op jit(solution)/shard_map/ppermute | solution.py:15
  11.7 7.5 %copy-start.3 = (bf16[1,64,1152]{2,1,0:T(8,128)(2,1)}, bf16[1,64,1152]{2,1,0:T(8,128)(2,1)S(1)}, u32[]{:S(2)}) copy-start(bf16[1,64,1152]{2,1,0:T(8,128)(2,1)S(1)} %collective-permute-done.7.refs_16_) | copy-start | bytes 442372
  11.7 5.4 %collective-permute-start.9 = (bf16[1,64,1152]{2,1,0:T(8,128)(2,1)S(1)}, bf16[1,64,1152]{2,1,0:T(8,128)(2,1)S(1)}, u32[]{:S(2)}, u32[]{:S(2)}) collective-permute-start(bf16[1,64,1152]{2,1,0:T(8,128)(2,1)S(1)} %collective-permute-done.7.refs_16_), channel_id=1, source_target_pairs={{0,8},{4,12},{8,0},{12,4},{16,24},{20,28},{24,16},{28,20},{1,9},{5... | collective-permute-start | bytes 442376 | tf_op jit(solution)/shard_map/ppermute | solution.py:15
  12.6 6.5 %copy-start.4 = (bf16[1,64,1152]{2,1,0:T(8,128)(2,1)}, bf16[1,64,1152]{2,1,0:T(8,128)(2,1)S(1)}, u32[]{:S(2)}) copy-start(bf16[1,64,1152]{2,1,0:T(8,128)(2,1)S(1)} %collective-permute-done.8.refs_17_) | copy-start | bytes 442372
  12.7 6.4 %collective-permute-start.4 = (bf16[1,64,1152]{2,1,0:T(8,128)(2,1)S(1)}, bf16[1,64,1152]{2,1,0:T(8,128)(2,1)S(1)}, u32[]{:S(2)}, u32[]{:S(2)}) collective-permute-start(bf16[1,64,1152]{2,1,0:T(8,128)(2,1)S(1)} %collective-permute-done.refs_8_), channel_id=1, source_target_pairs={{0,4},{4,0},{8,12},{12,8},{16,20},{20,16},{24,28},{28,24},{1,5},{5... | collective-permute-start | bytes 442376 | tf_op jit(solution)/shard_map/ppermute | solution.py:15
  12.7 6.5 %copy-start.5 = (bf16[1,64,1152]{2,1,0:T(8,128)(2,1)}, bf16[1,64,1152]{2,1,0:T(8,128)(2,1)S(1)}, u32[]{:S(2)}) copy-start(bf16[1,64,1152]{2,1,0:T(8,128)(2,1)S(1)} %collective-permute-done.10.refs_19_) | copy-start | bytes 442372
  12.7 6.4 %collective-permute-start.11 = (bf16[1,64,1152]{2,1,0:T(8,128)(2,1)S(1)}, bf16[1,64,1152]{2,1,0:T(8,128)(2,1)S(1)}, u32[]{:S(2)}, u32[]{:S(2)}) collective-permute-start(bf16[1,64,1152]{2,1,0:T(8,128)(2,1)S(1)} %collective-permute-done.7.refs_16_), channel_id=1, source_target_pairs={{0,4},{4,0},{8,12},{12,8},{16,20},{20,16},{24,28},{28,24},{1,5},{5... | collective-permute-start | bytes 442376 | tf_op jit(solution)/shard_map/ppermute | solution.py:15
  13.2 6.0 %copy-start.6 = (bf16[1,64,1152]{2,1,0:T(8,128)(2,1)}, bf16[1,64,1152]{2,1,0:T(8,128)(2,1)S(1)}, u32[]{:S(2)}) copy-start(bf16[1,64,1152]{2,1,0:T(8,128)(2,1)S(1)} %collective-permute-done.5.refs_13_) | copy-start | bytes 442372
  13.2 5.9 %collective-permute-start.12 = (bf16[1,64,1152]{2,1,0:T(8,128)(2,1)S(1)}, bf16[1,64,1152]{2,1,0:T(8,128)(2,1)S(1)}, u32[]{:S(2)}, u32[]{:S(2)}) collective-permute-start(bf16[1,64,1152]{2,1,0:T(8,128)(2,1)S(1)} %collective-permute-done.8.refs_17_), channel_id=1, source_target_pairs={{0,4},{4,0},{8,12},{12,8},{16,20},{20,16},{24,28},{28,24},{1,5},{5... | collective-permute-start | bytes 442376 | tf_op jit(solution)/shard_map/ppermute | solution.py:15
  16.0 3.2 %copy-start.7 = (bf16[1,64,1152]{2,1,0:T(8,128)(2,1)}, bf16[1,64,1152]{2,1,0:T(8,128)(2,1)S(1)}, u32[]{:S(2)}) copy-start(bf16[1,64,1152]{2,1,0:T(8,128)(2,1)S(1)} %collective-permute-done.2.refs_10_) | copy-start | bytes 442372
  16.0 3.1 %collective-permute-start.6 = (bf16[1,64,1152]{2,1,0:T(8,128)(2,1)S(1)}, bf16[1,64,1152]{2,1,0:T(8,128)(2,1)S(1)}, u32[]{:S(2)}, u32[]{:S(2)}) collective-permute-start(bf16[1,64,1152]{2,1,0:T(8,128)(2,1)S(1)} %collective-permute-done.2.refs_10_), channel_id=1, source_target_pairs={{0,4},{4,0},{8,12},{12,8},{16,20},{20,16},{24,28},{28,24},{1,5},{5... | collective-permute-start | bytes 442376 | tf_op jit(solution)/shard_map/ppermute | solution.py:15
  17.1 2.0 %collective-permute-start.13 = (bf16[1,64,1152]{2,1,0:T(8,128)(2,1)S(1)}, bf16[1,64,1152]{2,1,0:T(8,128)(2,1)S(1)}, u32[]{:S(2)}, u32[]{:S(2)}) collective-permute-start(bf16[1,64,1152]{2,1,0:T(8,128)(2,1)S(1)} %collective-permute-done.9.refs_18_), channel_id=1, source_target_pairs={{0,4},{4,0},{8,12},{12,8},{16,20},{20,16},{24,28},{28,24},{1,5},{5... | collective-permute-start | bytes 442376 | tf_op jit(solution)/shard_map/ppermute | solution.py:15
  30.0 4.0 %collective-permute-start.14 = (f32[3,1152]{1,0:T(4,128)}, f32[3,1152]{1,0:T(4,128)S(1)}, u32[]{:S(2)}, u32[]{:S(2)}) collective-permute-start(f32[3,1152]{1,0:T(4,128)} %get-tuple-element.9), channel_id=1, source_target_pairs={{0,1},{1,0},{2,3},{3,2},{4,5},{5,4},{6,7},{7,6},{8,9},{9,8},{10,11... | collective-permute-start | bytes 41480 | tf_op jit(solution)/shard_map/ppermute | solution.py:15
  34.8 4.7 %collective-permute-start.15 = (f32[3,1152]{1,0:T(4,128)S(1)}, f32[3,1152]{1,0:T(4,128)S(1)}, u32[]{:S(2)}, u32[]{:S(2)}) collective-permute-start(f32[3,1152]{1,0:T(4,128)S(1)} %add.6), channel_id=1, source_target_pairs={{0,2},{1,3},{2,0},{3,1},{4,6},{5,7},{6,4},{7,5},{8,10},{9,11},{10,... | collective-permute-start | bytes 41480 | tf_op jit(solution)/shard_map/ppermute | solution.py:15
  (6 other events, 5.7 us)

commit v11 on v10

--- a/solution.py
+++ b/solution.py
@@ -242,13 +242,16 @@
         jnp.where(natural == image_row, partner_ref[...].astype(jnp.float32), 0.0), axis=1, keepdims=True
     ).astype(jnp.int32)
 
-    for arrival in arrivals:
-        arrival.wait()
     gains = (picture_gain_ref[...][None, :], caption_gain_ref[...][None, :])
     chunk = min(128, group_rows)
+    waited = set()
     for tower in range(2):
         for first in range(0, group_rows, chunk):
             rows = pl.ds(first, chunk)
+            for slot in range(first // block_rows, (first + chunk - 1) // block_rows + 1):
+                if tower * count + slot not in waited:
+                    waited.add(tower * count + slot)
+                    arrivals[tower * count + slot].wait()
             values = raw_ref[tower, rows, :].astype(jnp.float32)
             centred = values - jnp.mean(values, axis=-1, keepdims=True)
             inverse = lax.rsqrt(jnp.mean(centred * centred, axis=-1, keepdims=True) + epsilon)

time: 40.3 us -> 40.5 us (level)
  no operation moved by 1% of the time
where the time goes in v11:
time: 40.5 us; the launch traced here: 40.3 us
  waiting for transfers between devices  12.2 us (30%)
  starting transfers between devices  11.7 us (29%)
  Pallas kernels  9.66 us (24%)
  between operations  2.77 us (7%)
  local copies, waits for them, and re-layouts  2.59 us (6%)
  other arithmetic  1.33 us (3%)
    ppermute x16, waiting for transfers between devices, xor_swap(): lax.ppermute(value, axis, [(source, source ^ bit) for source in range(cou...  12.2 us
    ppermute x16, starting transfers between devices, xor_swap(): lax.ppermute(value, axis, [(source, source ^ bit) for source in range(cou...  11.7 us
    pallas_call x1, Pallas kernels, whole_group(): pl.pallas_call(functools.partial(group_kernel, tuple(masks[:count]), tupl...  9.66 us
    unnamed x28, local copies, waits for them, and re-layouts  1.41 us
    slice x1, local copies, waits for them, and re-layouts, whole_group(): group_loss = sums[2, 0:1]  1.18 us
  transfers between devices with their start and end apart: 16, of which 7 were waited for; matrix products, arithmetic and copies ran while one was open for 3% of the time, Pallas kernels for 0%

profile of v11, /device:TPU:0, one launch (start us, length us, event | category | flops | bytes accessed | tf_op | source)
XLA Modules:
  0.0 40.3 jit_solution(16067541359435170922)
XLA Ops:
  0.6 3.1 %collective-permute-start.1 = (bf16[1,64,1152]{2,1,0:T(8,128)(2,1)}, bf16[1,64,1152]{2,1,0:T(8,128)(2,1)S(1)}, u32[]{:S(2)}, u32[]{:S(2)}) collective-permute-start(bf16[1,64,1152]{2,1,0:T(8,128)(2,1)} %refs_7_.1), channel_id=1, source_target_pairs={{0,16},{4,20},{8,24},{12,28},{16,0},{20,4},{24,8},{28,12},{1,17},{... | collective-permute-start | bytes 442376 | tf_op jit(solution)/shard_map/ppermute | solution.py:15
  3.7 1.5 %collective-permute-start = (bf16[1,64,1152]{2,1,0:T(8,128)(2,1)}, bf16[1,64,1152]{2,1,0:T(8,128)(2,1)S(1)}, u32[]{:S(2)}, u32[]{:S(2)}) collective-permute-start(bf16[1,64,1152]{2,1,0:T(8,128)(2,1)} %refs_7_.1), channel_id=1, source_target_pairs={{0,8},{4,12},{8,0},{12,4},{16,24},{20,28},{24,16},{28,20},{1,9},{5... | collective-permute-start | bytes 442376 | tf_op jit(solution)/shard_map/ppermute | solution.py:15
  5.2 0.5 %collective-permute-start.7 = (bf16[1,64,1152]{2,1,0:T(8,128)(2,1)}, bf16[1,64,1152]{2,1,0:T(8,128)(2,1)S(1)}, u32[]{:S(2)}, u32[]{:S(2)}) collective-permute-start(bf16[1,64,1152]{2,1,0:T(8,128)(2,1)} %refs_15_.1), channel_id=1, source_target_pairs={{0,16},{4,20},{8,24},{12,28},{16,0},{20,4},{24,8},{28,12},{1,17},{... | collective-permute-start | bytes 442376 | tf_op jit(solution)/shard_map/ppermute | solution.py:15
  5.7 0.1 collective-permute-start.8
  5.8 1.9 %collective-permute-done.1.refs_9_ = bf16[1,64,1152]{2,1,0:T(8,128)(2,1)S(1)} collective-permute-done((bf16[1,64,1152]{2,1,0:T(8,128)(2,1)}, bf16[1,64,1152]{2,1,0:T(8,128)(2,1)S(1)}, u32[]{:S(2)}, u32[]{:S(2)}) %collective-permute-start.1) | collective-permute-done | bytes 147488 | tf_op jit(solution)/shard_map/ppermute | solution.py:15
  7.8 2.0 %collective-permute-done.refs_8_ = bf16[1,64,1152]{2,1,0:T(8,128)(2,1)S(1)} collective-permute-done((bf16[1,64,1152]{2,1,0:T(8,128)(2,1)}, bf16[1,64,1152]{2,1,0:T(8,128)(2,1)S(1)}, u32[]{:S(2)}, u32[]{:S(2)}) %collective-permute-start) | collective-permute-done | bytes 147488 | tf_op jit(solution)/shard_map/ppermute | solution.py:15
  9.8 0.7 %collective-permute-start.2 = (bf16[1,64,1152]{2,1,0:T(8,128)(2,1)S(1)}, bf16[1,64,1152]{2,1,0:T(8,128)(2,1)S(1)}, u32[]{:S(2)}, u32[]{:S(2)}) collective-permute-start(bf16[1,64,1152]{2,1,0:T(8,128)(2,1)S(1)} %collective-permute-done.refs_8_), channel_id=1, source_target_pairs={{0,16},{4,20},{8,24},{12,28},{16,0},{20,4},{24,8},{28,12},{1,17},{... | collective-permute-start | bytes 442376 | tf_op jit(solution)/shard_map/ppermute | solution.py:15
  10.5 1.2 %collective-permute-done.7.refs_16_ = bf16[1,64,1152]{2,1,0:T(8,128)(2,1)S(1)} collective-permute-done((bf16[1,64,1152]{2,1,0:T(8,128)(2,1)}, bf16[1,64,1152]{2,1,0:T(8,128)(2,1)S(1)}, u32[]{:S(2)}, u32[]{:S(2)}) %collective-permute-start.7) | collective-permute-done | bytes 147488 | tf_op jit(solution)/shard_map/ppermute | solution.py:15
  11.7 1.0 %collective-permute-start.9 = (bf16[1,64,1152]{2,1,0:T(8,128)(2,1)S(1)}, bf16[1,64,1152]{2,1,0:T(8,128)(2,1)S(1)}, u32[]{:S(2)}, u32[]{:S(2)}) collective-permute-start(bf16[1,64,1152]{2,1,0:T(8,128)(2,1)S(1)} %collective-permute-done.7.refs_16_), channel_id=1, source_target_pairs={{0,8},{4,12},{8,0},{12,4},{16,24},{20,28},{24,16},{28,20},{1,9},{5... | collective-permute-start | bytes 442376 | tf_op jit(solution)/shard_map/ppermute | solution.py:15
  12.7 0.5 %collective-permute-start.11 = (bf16[1,64,1152]{2,1,0:T(8,128)(2,1)S(1)}, bf16[1,64,1152]{2,1,0:T(8,128)(2,1)S(1)}, u32[]{:S(2)}, u32[]{:S(2)}) collective-permute-start(bf16[1,64,1152]{2,1,0:T(8,128)(2,1)S(1)} %collective-permute-done.7.refs_16_), channel_id=1, source_target_pairs={{0,4},{4,0},{8,12},{12,8},{16,20},{20,16},{24,28},{28,24},{1,5},{5... | collective-permute-start | bytes 442376 | tf_op jit(solution)/shard_map/ppermute | solution.py:15
  13.2 0.1 collective-permute-start.12
  13.3 2.8 %collective-permute-done.2.refs_10_ = bf16[1,64,1152]{2,1,0:T(8,128)(2,1)S(1)} collective-permute-done((bf16[1,64,1152]{2,1,0:T(8,128)(2,1)S(1)}, bf16[1,64,1152]{2,1,0:T(8,128)(2,1)S(1)}, u32[]{:S(2)}, u32[]{:S(2)}) %collective-permute-start.2) | collective-permute-done | bytes 147488 | tf_op jit(solution)/shard_map/ppermute | solution.py:15
  16.0 1.0 %collective-permute-done.9.refs_18_ = bf16[1,64,1152]{2,1,0:T(8,128)(2,1)S(1)} collective-permute-done((bf16[1,64,1152]{2,1,0:T(8,128)(2,1)S(1)}, bf16[1,64,1152]{2,1,0:T(8,128)(2,1)S(1)}, u32[]{:S(2)}, u32[]{:S(2)}) %collective-permute-start.9) | collective-permute-done | bytes 147488 | tf_op jit(solution)/shard_map/ppermute | solution.py:15
  19.2 0.5 %copy-done.9 = bf16[1,64,1152]{2,1,0:T(8,128)(2,1)} copy-done((bf16[1,64,1152]{2,1,0:T(8,128)(2,1)}, bf16[1,64,1152]{2,1,0:T(8,128)(2,1)S(1)}, u32[]{:S(2)}) %copy-start.9) | copy-done | bytes 147480
  19.8 0.1 copy-done.12
  19.9 0.7 %copy-done.13 = bf16[1,64,1152]{2,1,0:T(8,128)(2,1)} copy-done((bf16[1,64,1152]{2,1,0:T(8,128)(2,1)}, bf16[1,64,1152]{2,1,0:T(8,128)(2,1)S(1)}, u32[]{:S(2)}) %copy-start.13) | copy-done | bytes 147480
  20.6 9.7 %shard_map.120 = (bf16[1,64,1152]{2,1,0:T(8,128)(2,1)}, bf16[1,64,1152]{2,1,0:T(8,128)(2,1)}, f32[3,1152]{1,0:T(4,128)}) custom-call(f32[1]{0:T(128)S(6)} %copy.13.refs_0_, f32[1]{0:T(128)S(6)} %copy.14.refs_1_, f32[1]{0:T(128)S(6)} %copy.15.refs_2_, s32[1,8]{1,0:T(1,128)} %refs_3_.1, f32[1152]{0:T(1024)} %refs_4_.1, f32[1152]{0:T(1024)} %refs_5_.1, ...), custom_call_target="tpu_custom_call" | custom-call | tf_op jit(solution)/shard_map/pallas_call | solution.py:338
  30.2 1.6 %collective-permute-start.14 = (f32[3,1152]{1,0:T(4,128)}, f32[3,1152]{1,0:T(4,128)S(1)}, u32[]{:S(2)}, u32[]{:S(2)}) collective-permute-start(f32[3,1152]{1,0:T(4,128)} %get-tuple-element.9), channel_id=1, source_target_pairs={{0,1},{1,0},{2,3},{3,2},{4,5},{5,4},{6,7},{7,6},{8,9},{9,8},{10,11... | collective-permute-start | bytes 41480 | tf_op jit(solution)/shard_map/ppermute | solution.py:15
  31.9 2.4 %collective-permute-done.14 = f32[3,1152]{1,0:T(4,128)S(1)} collective-permute-done((f32[3,1152]{1,0:T(4,128)}, f32[3,1152]{1,0:T(4,128)S(1)}, u32[]{:S(2)}, u32[]{:S(2)}) %collective-permute-start.14) | collective-permute-done | bytes 13856 | tf_op jit(solution)/shard_map/ppermute | solution.py:15
  34.3 0.7 %add.6 = f32[3,1152]{1,0:T(4,128)S(1)} add(f32[3,1152]{1,0:T(4,128)} %get-tuple-element.9, f32[3,1152]{1,0:T(4,128)S(1)} %collective-permute-done.14) | non-fusion elementwise | flops 3456 | bytes 41472 | tf_op jit(solution)/shard_map/add | solution.py:69
  35.0 2.6 %collective-permute-start.15 = (f32[3,1152]{1,0:T(4,128)S(1)}, f32[3,1152]{1,0:T(4,128)S(1)}, u32[]{:S(2)}, u32[]{:S(2)}) collective-permute-start(f32[3,1152]{1,0:T(4,128)S(1)} %add.6), channel_id=1, source_target_pairs={{0,2},{1,3},{2,0},{3,1},{4,6},{5,7},{6,4},{7,5},{8,10},{9,11},{10,... | collective-permute-start | bytes 41480 | tf_op jit(solution)/shard_map/ppermute | solution.py:15
  37.6 1.2 %slice.11 = f32[1,1]{1,0:T(1,128)} slice(f32[3,1152]{1,0:T(4,128)} %get-tuple-element.9), slice={[2:3], [0:1]} | slice | bytes 8 | tf_op jit(solution)/shard_map/slice | solution.py:365
  38.8 0.9 %collective-permute-done.15 = f32[3,1152]{1,0:T(4,128)S(1)} collective-permute-done((f32[3,1152]{1,0:T(4,128)S(1)}, f32[3,1152]{1,0:T(4,128)S(1)}, u32[]{:S(2)}, u32[]{:S(2)}) %collective-permute-start.15) | collective-permute-done | bytes 13856 | tf_op jit(solution)/shard_map/ppermute | solution.py:15
  39.7 0.6 %slice_add_fusion = f32[2,1152]{1,0:T(2,128)} fusion(f32[3,1152]{1,0:T(4,128)S(1)} %collective-permute-done.15, f32[3,1152]{1,0:T(4,128)S(1)} %add.6), kind=kLoop, calls=%fused_computation | loop fusion | flops 2304 | bytes 27648 | tf_op jit(solution)/shard_map/add | solution.py:71
  (40 shorter events, 0.2 us)
Async XLA Ops:
  0.6 7.1 %collective-permute-start.1 = (bf16[1,64,1152]{2,1,0:T(8,128)(2,1)}, bf16[1,64,1152]{2,1,0:T(8,128)(2,1)S(1)}, u32[]{:S(2)}, u32[]{:S(2)}) collective-permute-start(bf16[1,64,1152]{2,1,0:T(8,128)(2,1)} %refs_7_.1), channel_id=1, source_target_pairs={{0,16},{4,20},{8,24},{12,28},{16,0},{20,4},{24,8},{28,12},{1,17},{... | collective-permute-start | bytes 442376 | tf_op jit(solution)/shard_map/ppermute | solution.py:15
  3.7 6.0 %collective-permute-start = (bf16[1,64,1152]{2,1,0:T(8,128)(2,1)}, bf16[1,64,1152]{2,1,0:T(8,128)(2,1)S(1)}, u32[]{:S(2)}, u32[]{:S(2)}) collective-permute-start(bf16[1,64,1152]{2,1,0:T(8,128)(2,1)} %refs_7_.1), channel_id=1, source_target_pairs={{0,8},{4,12},{8,0},{12,4},{16,24},{20,28},{24,16},{28,20},{1,9},{5... | collective-permute-start | bytes 442376 | tf_op jit(solution)/shard_map/ppermute | solution.py:15
  5.2 4.6 %collective-permute-start.3 = (bf16[1,64,1152]{2,1,0:T(8,128)(2,1)}, bf16[1,64,1152]{2,1,0:T(8,128)(2,1)S(1)}, u32[]{:S(2)}, u32[]{:S(2)}) collective-permute-start(bf16[1,64,1152]{2,1,0:T(8,128)(2,1)} %refs_7_.1), channel_id=1, source_target_pairs={{0,4},{4,0},{8,12},{12,8},{16,20},{20,16},{24,28},{28,24},{1,5},{5... | collective-permute-start | bytes 442376 | tf_op jit(solution)/shard_map/ppermute | solution.py:15
  5.2 6.5 %collective-permute-start.7 = (bf16[1,64,1152]{2,1,0:T(8,128)(2,1)}, bf16[1,64,1152]{2,1,0:T(8,128)(2,1)S(1)}, u32[]{:S(2)}, u32[]{:S(2)}) collective-permute-start(bf16[1,64,1152]{2,1,0:T(8,128)(2,1)} %refs_15_.1), channel_id=1, source_target_pairs={{0,16},{4,20},{8,24},{12,28},{16,0},{20,4},{24,8},{28,12},{1,17},{... | collective-permute-start | bytes 442376 | tf_op jit(solution)/shard_map/ppermute | solution.py:15
  5.7 7.0 %collective-permute-start.8 = (bf16[1,64,1152]{2,1,0:T(8,128)(2,1)}, bf16[1,64,1152]{2,1,0:T(8,128)(2,1)S(1)}, u32[]{:S(2)}, u32[]{:S(2)}) collective-permute-start(bf16[1,64,1152]{2,1,0:T(8,128)(2,1)} %refs_15_.1), channel_id=1, source_target_pairs={{0,8},{4,12},{8,0},{12,4},{16,24},{20,28},{24,16},{28,20},{1,9},{5... | collective-permute-start | bytes 442376 | tf_op jit(solution)/shard_map/ppermute | solution.py:15
  7.8 11.4 %copy-start = (bf16[1,64,1152]{2,1,0:T(8,128)(2,1)}, bf16[1,64,1152]{2,1,0:T(8,128)(2,1)S(1)}, u32[]{:S(2)}) copy-start(bf16[1,64,1152]{2,1,0:T(8,128)(2,1)S(1)} %collective-permute-done.1.refs_9_) | copy-start | bytes 442372
  7.8 4.9 %collective-permute-start.10 = (bf16[1,64,1152]{2,1,0:T(8,128)(2,1)}, bf16[1,64,1152]{2,1,0:T(8,128)(2,1)S(1)}, u32[]{:S(2)}, u32[]{:S(2)}) collective-permute-start(bf16[1,64,1152]{2,1,0:T(8,128)(2,1)} %refs_15_.1), channel_id=1, source_target_pairs={{0,4},{4,0},{8,12},{12,8},{16,20},{20,16},{24,28},{28,24},{1,5},{5... | collective-permute-start | bytes 442376 | tf_op jit(solution)/shard_map/ppermute | solution.py:15
  9.7 9.4 %copy-start.1 = (bf16[1,64,1152]{2,1,0:T(8,128)(2,1)}, bf16[1,64,1152]{2,1,0:T(8,128)(2,1)S(1)}, u32[]{:S(2)}) copy-start(bf16[1,64,1152]{2,1,0:T(8,128)(2,1)S(1)} %collective-permute-done.refs_8_) | copy-start | bytes 442372
  9.7 3.4 %collective-permute-start.5 = (bf16[1,64,1152]{2,1,0:T(8,128)(2,1)S(1)}, bf16[1,64,1152]{2,1,0:T(8,128)(2,1)S(1)}, u32[]{:S(2)}, u32[]{:S(2)}) collective-permute-start(bf16[1,64,1152]{2,1,0:T(8,128)(2,1)S(1)} %collective-permute-done.1.refs_9_), channel_id=1, source_target_pairs={{0,4},{4,0},{8,12},{12,8},{16,20},{20,16},{24,28},{28,24},{1,5},{5... | collective-permute-start | bytes 442376 | tf_op jit(solution)/shard_map/ppermute | solution.py:15
  9.7 9.4 %copy-start.2 = (bf16[1,64,1152]{2,1,0:T(8,128)(2,1)}, bf16[1,64,1152]{2,1,0:T(8,128)(2,1)S(1)}, u32[]{:S(2)}) copy-start(bf16[1,64,1152]{2,1,0:T(8,128)(2,1)S(1)} %collective-permute-done.3.refs_11_) | copy-start | bytes 442372
  9.8 6.3 %collective-permute-start.2 = (bf16[1,64,1152]{2,1,0:T(8,128)(2,1)S(1)}, bf16[1,64,1152]{2,1,0:T(8,128)(2,1)S(1)}, u32[]{:S(2)}, u32[]{:S(2)}) collective-permute-start(bf16[1,64,1152]{2,1,0:T(8,128)(2,1)S(1)} %collective-permute-done.refs_8_), channel_id=1, source_target_pairs={{0,16},{4,20},{8,24},{12,28},{16,0},{20,4},{24,8},{28,12},{1,17},{... | collective-permute-start | bytes 442376 | tf_op jit(solution)/shard_map/ppermute | solution.py:15
  11.7 7.5 %copy-start.3 = (bf16[1,64,1152]{2,1,0:T(8,128)(2,1)}, bf16[1,64,1152]{2,1,0:T(8,128)(2,1)S(1)}, u32[]{:S(2)}) copy-start(bf16[1,64,1152]{2,1,0:T(8,128)(2,1)S(1)} %collective-permute-done.7.refs_16_) | copy-start | bytes 442372
  11.7 5.4 %collective-permute-start.9 = (bf16[1,64,1152]{2,1,0:T(8,128)(2,1)S(1)}, bf16[1,64,1152]{2,1,0:T(8,128)(2,1)S(1)}, u32[]{:S(2)}, u32[]{:S(2)}) collective-permute-start(bf16[1,64,1152]{2,1,0:T(8,128)(2,1)S(1)} %collective-permute-done.7.refs_16_), channel_id=1, source_target_pairs={{0,8},{4,12},{8,0},{12,4},{16,24},{20,28},{24,16},{28,20},{1,9},{5... | collective-permute-start | bytes 442376 | tf_op jit(solution)/shard_map/ppermute | solution.py:15
  12.6 6.5 %copy-start.4 = (bf16[1,64,1152]{2,1,0:T(8,128)(2,1)}, bf16[1,64,1152]{2,1,0:T(8,128)(2,1)S(1)}, u32[]{:S(2)}) copy-start(bf16[1,64,1152]{2,1,0:T(8,128)(2,1)S(1)} %collective-permute-done.8.refs_17_) | copy-start | bytes 442372
  12.7 6.4 %collective-permute-start.4 = (bf16[1,64,1152]{2,1,0:T(8,128)(2,1)S(1)}, bf16[1,64,1152]{2,1,0:T(8,128)(2,1)S(1)}, u32[]{:S(2)}, u32[]{:S(2)}) collective-permute-start(bf16[1,64,1152]{2,1,0:T(8,128)(2,1)S(1)} %collective-permute-done.refs_8_), channel_id=1, source_target_pairs={{0,4},{4,0},{8,12},{12,8},{16,20},{20,16},{24,28},{28,24},{1,5},{5... | collective-permute-start | bytes 442376 | tf_op jit(solution)/shard_map/ppermute | solution.py:15
  12.7 6.5 %copy-start.5 = (bf16[1,64,1152]{2,1,0:T(8,128)(2,1)}, bf16[1,64,1152]{2,1,0:T(8,128)(2,1)S(1)}, u32[]{:S(2)}) copy-start(bf16[1,64,1152]{2,1,0:T(8,128)(2,1)S(1)} %collective-permute-done.10.refs_19_) | copy-start | bytes 442372
  12.7 6.4 %collective-permute-start.11 = (bf16[1,64,1152]{2,1,0:T(8,128)(2,1)S(1)}, bf16[1,64,1152]{2,1,0:T(8,128)(2,1)S(1)}, u32[]{:S(2)}, u32[]{:S(2)}) collective-permute-start(bf16[1,64,1152]{2,1,0:T(8,128)(2,1)S(1)} %collective-permute-done.7.refs_16_), channel_id=1, source_target_pairs={{0,4},{4,0},{8,12},{12,8},{16,20},{20,16},{24,28},{28,24},{1,5},{5... | collective-permute-start | bytes 442376 | tf_op jit(solution)/shard_map/ppermute | solution.py:15
  13.2 6.0 %copy-start.6 = (bf16[1,64,1152]{2,1,0:T(8,128)(2,1)}, bf16[1,64,1152]{2,1,0:T(8,128)(2,1)S(1)}, u32[]{:S(2)}) copy-start(bf16[1,64,1152]{2,1,0:T(8,128)(2,1)S(1)} %collective-permute-done.5.refs_13_) | copy-start | bytes 442372
  13.2 5.9 %collective-permute-start.12 = (bf16[1,64,1152]{2,1,0:T(8,128)(2,1)S(1)}, bf16[1,64,1152]{2,1,0:T(8,128)(2,1)S(1)}, u32[]{:S(2)}, u32[]{:S(2)}) collective-permute-start(bf16[1,64,1152]{2,1,0:T(8,128)(2,1)S(1)} %collective-permute-done.8.refs_17_), channel_id=1, source_target_pairs={{0,4},{4,0},{8,12},{12,8},{16,20},{20,16},{24,28},{28,24},{1,5},{5... | collective-permute-start | bytes 442376 | tf_op jit(solution)/shard_map/ppermute | solution.py:15
  16.0 3.2 %copy-start.7 = (bf16[1,64,1152]{2,1,0:T(8,128)(2,1)}, bf16[1,64,1152]{2,1,0:T(8,128)(2,1)S(1)}, u32[]{:S(2)}) copy-start(bf16[1,64,1152]{2,1,0:T(8,128)(2,1)S(1)} %collective-permute-done.2.refs_10_) | copy-start | bytes 442372
  16.0 3.1 %collective-permute-start.6 = (bf16[1,64,1152]{2,1,0:T(8,128)(2,1)S(1)}, bf16[1,64,1152]{2,1,0:T(8,128)(2,1)S(1)}, u32[]{:S(2)}, u32[]{:S(2)}) collective-permute-start(bf16[1,64,1152]{2,1,0:T(8,128)(2,1)S(1)} %collective-permute-done.2.refs_10_), channel_id=1, source_target_pairs={{0,4},{4,0},{8,12},{12,8},{16,20},{20,16},{24,28},{28,24},{1,5},{5... | collective-permute-start | bytes 442376 | tf_op jit(solution)/shard_map/ppermute | solution.py:15
  17.1 2.0 %collective-permute-start.13 = (bf16[1,64,1152]{2,1,0:T(8,128)(2,1)S(1)}, bf16[1,64,1152]{2,1,0:T(8,128)(2,1)S(1)}, u32[]{:S(2)}, u32[]{:S(2)}) collective-permute-start(bf16[1,64,1152]{2,1,0:T(8,128)(2,1)S(1)} %collective-permute-done.9.refs_18_), channel_id=1, source_target_pairs={{0,4},{4,0},{8,12},{12,8},{16,20},{20,16},{24,28},{28,24},{1,5},{5... | collective-permute-start | bytes 442376 | tf_op jit(solution)/shard_map/ppermute | solution.py:15
  30.2 4.0 %collective-permute-start.14 = (f32[3,1152]{1,0:T(4,128)}, f32[3,1152]{1,0:T(4,128)S(1)}, u32[]{:S(2)}, u32[]{:S(2)}) collective-permute-start(f32[3,1152]{1,0:T(4,128)} %get-tuple-element.9), channel_id=1, source_target_pairs={{0,1},{1,0},{2,3},{3,2},{4,5},{5,4},{6,7},{7,6},{8,9},{9,8},{10,11... | collective-permute-start | bytes 41480 | tf_op jit(solution)/shard_map/ppermute | solution.py:15
  35.0 4.7 %collective-permute-start.15 = (f32[3,1152]{1,0:T(4,128)S(1)}, f32[3,1152]{1,0:T(4,128)S(1)}, u32[]{:S(2)}, u32[]{:S(2)}) collective-permute-start(f32[3,1152]{1,0:T(4,128)S(1)} %add.6), channel_id=1, source_target_pairs={{0,2},{1,3},{2,0},{3,1},{4,6},{5,7},{6,4},{7,5},{8,10},{9,11},{10,... | collective-permute-start | bytes 41480 | tf_op jit(solution)/shard_map/ppermute | solution.py:15
  (6 other events, 5.7 us)

commit v12 on v10

--- a/solution.py
+++ b/solution.py
@@ -202,19 +202,28 @@
     count = len(image_masks)
     pieces = refs[7 : 7 + 2 * count]
     (image_grad_ref, text_grad_ref, sums_ref, raw_ref, unit_ref, short_ref, normed_ref, inverse_ref,
-     length_ref, weights_ref, copy_sems) = refs[7 + 2 * count :]
+     length_ref, weights_ref, tangent_ref, copy_sems) = refs[7 + 2 * count :]
     block_rows = pieces[0].shape[1]
     group_rows = raw_ref.shape[1]
     width = raw_ref.shape[2]
+    own_block = lax.axis_index("blk")
+
+    def block_of(mask):
+        block = own_block
+        for bit in range(mask.bit_length()):
+            if mask >> bit & 1:
+                block = block + (1 - 2 * (own_block // (1 << bit) % 2)) * (1 << bit)
+        return block
+
     arrivals = []
     for position, source in enumerate(pieces):
         tower, slot = divmod(position, count)
-        rows = pl.ds(slot * block_rows, block_rows)
+        masks = image_masks if tower == 0 else text_masks
+        rows = pl.ds(pl.multiple_of(block_of(masks[slot]) * block_rows, block_rows), block_rows)
         arrival = pltpu.make_async_copy(source.at[0], raw_ref.at[tower, rows, :], copy_sems.at[position])
         arrival.start()
         arrivals.append(arrival)
 
-    own_block = lax.axis_index("blk")
     blocks = counts_ref.shape[1]
     total = counts_ref[0, 0]
     for block in range(1, blocks):
@@ -224,19 +233,15 @@
     score_shift_amount = jnp.full((1, 1), shift_ref[0], jnp.float32)
     grad_factor = jnp.full((1, 1), multiplier_ref[0], jnp.float32) / real_count
 
-    def held(masks, shape, dim):
-        place = lax.broadcasted_iota(jnp.int32, shape, dim)
-        row = jnp.zeros(shape, jnp.int32)
+    def held(shape, dim):
+        row = lax.broadcasted_iota(jnp.int32, shape, dim)
         limit = jnp.zeros(shape, jnp.int32)
-        for slot, mask in enumerate(masks):
-            block = own_block ^ mask
-            here = place // block_rows == slot
-            row = jnp.where(here, block * block_rows + place % block_rows, row)
-            limit = jnp.where(here, counts_ref[0, block], limit)
+        for block in range(blocks):
+            limit = jnp.where(row // block_rows == block, counts_ref[0, block], limit)
         return row, (row % block_rows) < limit
 
-    image_row, image_real = held(image_masks, (group_rows, 1), 0)
-    text_row, text_real = held(text_masks, (1, group_rows), 1)
+    image_row, image_real = held((group_rows, 1), 0)
+    text_row, text_real = held((1, group_rows), 1)
     natural = lax.broadcasted_iota(jnp.int32, (group_rows, group_rows), 1)
     partner_of_image = jnp.sum(
         jnp.where(natural == image_row, partner_ref[...].astype(jnp.float32), 0.0), axis=1, keepdims=True
@@ -298,16 +303,17 @@
                 direction - unit_rows * jnp.sum(unit_rows * direction, axis=-1, keepdims=True)
             ) * length_ref[tower, rows, :]
             gain_sum = gain_sum + jnp.sum(tangent * normed, axis=0, keepdims=True)
-            if first == 0:
-                own = slice(0, block_rows)
-                scaled_back = tangent[own] * gains[tower]
-                gradient = (
-                    scaled_back
-                    - jnp.mean(scaled_back, axis=-1, keepdims=True)
-                    - normed[own] * jnp.mean(scaled_back * normed[own], axis=-1, keepdims=True)
-                ) * inverse_ref[tower, 0:block_rows, :]
-                grad_ref[0] = gradient.astype(grad_ref.dtype)
+            tangent_ref[rows, :] = tangent
         sums_ref[tower : tower + 1, :] = gain_sum
+        own = pl.ds(pl.multiple_of(own_block * block_rows, block_rows), block_rows)
+        normed = normed_ref[tower, own, :]
+        scaled_back = tangent_ref[own, :] * gains[tower]
+        gradient = (
+            scaled_back
+            - jnp.mean(scaled_back, axis=-1, keepdims=True)
+            - normed * jnp.mean(scaled_back * normed, axis=-1, keepdims=True)
+        ) * inverse_ref[tower, own, :]
+        grad_ref[0] = gradient.astype(grad_ref.dtype)
     first_lane = lax.broadcasted_iota(jnp.int32, (1, width), 1) == 0
     sums_ref[2:3, :] = jnp.where(first_lane, loss / real_count, 0.0)
 
@@ -347,6 +353,7 @@
             pltpu.VMEM(column, jnp.float32),
             pltpu.VMEM(column, jnp.float32),
             pltpu.VMEM((group_rows, group_rows), jnp.bfloat16),
+            pltpu.VMEM((group_rows, width), jnp.float32),
             pltpu.SemaphoreType.DMA((len(pieces),)),
         ],
     )(

time: 40.3 us -> 40.6 us (level)
  no operation moved by 1% of the time
where the time goes in v12:
time: 40.6 us; the launch traced here: 40.3 us
  waiting for transfers between devices  12.2 us (30%)
  starting transfers between devices  11.7 us (29%)
  Pallas kernels  9.73 us (24%)
  between operations  2.77 us (7%)
  local copies, waits for them, and re-layouts  2.59 us (6%)
  other arithmetic  1.33 us (3%)
    ppermute x16, waiting for transfers between devices, xor_swap(): lax.ppermute(value, axis, [(source, source ^ bit) for source in range(cou...  12.2 us
    ppermute x16, starting transfers between devices, xor_swap(): lax.ppermute(value, axis, [(source, source ^ bit) for source in range(cou...  11.7 us
    pallas_call x1, Pallas kernels, whole_group(): pl.pallas_call(functools.partial(group_kernel, tuple(masks[:count]), tupl...  9.73 us
    unnamed x28, local copies, waits for them, and re-layouts  1.41 us
    slice x1, local copies, waits for them, and re-layouts, whole_group(): group_loss = sums[2, 0:1]  1.18 us
  transfers between devices with their start and end apart: 16, of which 7 were waited for; matrix products, arithmetic and copies ran while one was open for 3% of the time, Pallas kernels for 0%

profile of v12, /device:TPU:0, one launch (start us, length us, event | category | flops | bytes accessed | tf_op | source)
XLA Modules:
  0.0 40.3 jit_solution(13913189831648702518)
XLA Ops:
  0.6 3.1 %collective-permute-start.1 = (bf16[1,64,1152]{2,1,0:T(8,128)(2,1)}, bf16[1,64,1152]{2,1,0:T(8,128)(2,1)S(1)}, u32[]{:S(2)}, u32[]{:S(2)}) collective-permute-start(bf16[1,64,1152]{2,1,0:T(8,128)(2,1)} %refs_7_.1), channel_id=1, source_target_pairs={{0,16},{4,20},{8,24},{12,28},{16,0},{20,4},{24,8},{28,12},{1,17},{... | collective-permute-start | bytes 442376 | tf_op jit(solution)/shard_map/ppermute | solution.py:15
  3.7 1.5 %collective-permute-start = (bf16[1,64,1152]{2,1,0:T(8,128)(2,1)}, bf16[1,64,1152]{2,1,0:T(8,128)(2,1)S(1)}, u32[]{:S(2)}, u32[]{:S(2)}) collective-permute-start(bf16[1,64,1152]{2,1,0:T(8,128)(2,1)} %refs_7_.1), channel_id=1, source_target_pairs={{0,8},{4,12},{8,0},{12,4},{16,24},{20,28},{24,16},{28,20},{1,9},{5... | collective-permute-start | bytes 442376 | tf_op jit(solution)/shard_map/ppermute | solution.py:15
  5.2 0.5 %collective-permute-start.7 = (bf16[1,64,1152]{2,1,0:T(8,128)(2,1)}, bf16[1,64,1152]{2,1,0:T(8,128)(2,1)S(1)}, u32[]{:S(2)}, u32[]{:S(2)}) collective-permute-start(bf16[1,64,1152]{2,1,0:T(8,128)(2,1)} %refs_15_.1), channel_id=1, source_target_pairs={{0,16},{4,20},{8,24},{12,28},{16,0},{20,4},{24,8},{28,12},{1,17},{... | collective-permute-start | bytes 442376 | tf_op jit(solution)/shard_map/ppermute | solution.py:15
  5.7 0.1 collective-permute-start.8
  5.8 1.9 %collective-permute-done.1.refs_9_ = bf16[1,64,1152]{2,1,0:T(8,128)(2,1)S(1)} collective-permute-done((bf16[1,64,1152]{2,1,0:T(8,128)(2,1)}, bf16[1,64,1152]{2,1,0:T(8,128)(2,1)S(1)}, u32[]{:S(2)}, u32[]{:S(2)}) %collective-permute-start.1) | collective-permute-done | bytes 147488 | tf_op jit(solution)/shard_map/ppermute | solution.py:15
  7.8 2.0 %collective-permute-done.refs_8_ = bf16[1,64,1152]{2,1,0:T(8,128)(2,1)S(1)} collective-permute-done((bf16[1,64,1152]{2,1,0:T(8,128)(2,1)}, bf16[1,64,1152]{2,1,0:T(8,128)(2,1)S(1)}, u32[]{:S(2)}, u32[]{:S(2)}) %collective-permute-start) | collective-permute-done | bytes 147488 | tf_op jit(solution)/shard_map/ppermute | solution.py:15
  9.8 0.7 %collective-permute-start.2 = (bf16[1,64,1152]{2,1,0:T(8,128)(2,1)S(1)}, bf16[1,64,1152]{2,1,0:T(8,128)(2,1)S(1)}, u32[]{:S(2)}, u32[]{:S(2)}) collective-permute-start(bf16[1,64,1152]{2,1,0:T(8,128)(2,1)S(1)} %collective-permute-done.refs_8_), channel_id=1, source_target_pairs={{0,16},{4,20},{8,24},{12,28},{16,0},{20,4},{24,8},{28,12},{1,17},{... | collective-permute-start | bytes 442376 | tf_op jit(solution)/shard_map/ppermute | solution.py:15
  10.5 1.2 %collective-permute-done.7.refs_16_ = bf16[1,64,1152]{2,1,0:T(8,128)(2,1)S(1)} collective-permute-done((bf16[1,64,1152]{2,1,0:T(8,128)(2,1)}, bf16[1,64,1152]{2,1,0:T(8,128)(2,1)S(1)}, u32[]{:S(2)}, u32[]{:S(2)}) %collective-permute-start.7) | collective-permute-done | bytes 147488 | tf_op jit(solution)/shard_map/ppermute | solution.py:15
  11.7 1.0 %collective-permute-start.9 = (bf16[1,64,1152]{2,1,0:T(8,128)(2,1)S(1)}, bf16[1,64,1152]{2,1,0:T(8,128)(2,1)S(1)}, u32[]{:S(2)}, u32[]{:S(2)}) collective-permute-start(bf16[1,64,1152]{2,1,0:T(8,128)(2,1)S(1)} %collective-permute-done.7.refs_16_), channel_id=1, source_target_pairs={{0,8},{4,12},{8,0},{12,4},{16,24},{20,28},{24,16},{28,20},{1,9},{5... | collective-permute-start | bytes 442376 | tf_op jit(solution)/shard_map/ppermute | solution.py:15
  12.7 0.5 %collective-permute-start.11 = (bf16[1,64,1152]{2,1,0:T(8,128)(2,1)S(1)}, bf16[1,64,1152]{2,1,0:T(8,128)(2,1)S(1)}, u32[]{:S(2)}, u32[]{:S(2)}) collective-permute-start(bf16[1,64,1152]{2,1,0:T(8,128)(2,1)S(1)} %collective-permute-done.7.refs_16_), channel_id=1, source_target_pairs={{0,4},{4,0},{8,12},{12,8},{16,20},{20,16},{24,28},{28,24},{1,5},{5... | collective-permute-start | bytes 442376 | tf_op jit(solution)/shard_map/ppermute | solution.py:15
  13.2 0.1 collective-permute-start.12
  13.3 2.8 %collective-permute-done.2.refs_10_ = bf16[1,64,1152]{2,1,0:T(8,128)(2,1)S(1)} collective-permute-done((bf16[1,64,1152]{2,1,0:T(8,128)(2,1)S(1)}, bf16[1,64,1152]{2,1,0:T(8,128)(2,1)S(1)}, u32[]{:S(2)}, u32[]{:S(2)}) %collective-permute-start.2) | collective-permute-done | bytes 147488 | tf_op jit(solution)/shard_map/ppermute | solution.py:15
  16.0 1.0 %collective-permute-done.9.refs_18_ = bf16[1,64,1152]{2,1,0:T(8,128)(2,1)S(1)} collective-permute-done((bf16[1,64,1152]{2,1,0:T(8,128)(2,1)S(1)}, bf16[1,64,1152]{2,1,0:T(8,128)(2,1)S(1)}, u32[]{:S(2)}, u32[]{:S(2)}) %collective-permute-start.9) | collective-permute-done | bytes 147488 | tf_op jit(solution)/shard_map/ppermute | solution.py:15
  19.2 0.5 %copy-done.9 = bf16[1,64,1152]{2,1,0:T(8,128)(2,1)} copy-done((bf16[1,64,1152]{2,1,0:T(8,128)(2,1)}, bf16[1,64,1152]{2,1,0:T(8,128)(2,1)S(1)}, u32[]{:S(2)}) %copy-start.9) | copy-done | bytes 147480
  19.8 0.1 copy-done.12
  19.9 0.7 %copy-done.13 = bf16[1,64,1152]{2,1,0:T(8,128)(2,1)} copy-done((bf16[1,64,1152]{2,1,0:T(8,128)(2,1)}, bf16[1,64,1152]{2,1,0:T(8,128)(2,1)S(1)}, u32[]{:S(2)}) %copy-start.13) | copy-done | bytes 147480
  20.6 9.7 %shard_map.120 = (bf16[1,64,1152]{2,1,0:T(8,128)(2,1)}, bf16[1,64,1152]{2,1,0:T(8,128)(2,1)}, f32[3,1152]{1,0:T(4,128)}) custom-call(f32[1]{0:T(128)S(6)} %copy.13.refs_0_, f32[1]{0:T(128)S(6)} %copy.14.refs_1_, f32[1]{0:T(128)S(6)} %copy.15.refs_2_, s32[1,8]{1,0:T(1,128)} %refs_3_.1, f32[1152]{0:T(1024)} %refs_4_.1, f32[1152]{0:T(1024)} %refs_5_.1, ...), custom_call_target="tpu_custom_call" | custom-call | tf_op jit(solution)/shard_map/pallas_call | solution.py:341
  30.3 1.6 %collective-permute-start.14 = (f32[3,1152]{1,0:T(4,128)}, f32[3,1152]{1,0:T(4,128)S(1)}, u32[]{:S(2)}, u32[]{:S(2)}) collective-permute-start(f32[3,1152]{1,0:T(4,128)} %get-tuple-element.9), channel_id=1, source_target_pairs={{0,1},{1,0},{2,3},{3,2},{4,5},{5,4},{6,7},{7,6},{8,9},{9,8},{10,11... | collective-permute-start | bytes 41480 | tf_op jit(solution)/shard_map/ppermute | solution.py:15
  32.0 2.4 %collective-permute-done.14 = f32[3,1152]{1,0:T(4,128)S(1)} collective-permute-done((f32[3,1152]{1,0:T(4,128)}, f32[3,1152]{1,0:T(4,128)S(1)}, u32[]{:S(2)}, u32[]{:S(2)}) %collective-permute-start.14) | collective-permute-done | bytes 13856 | tf_op jit(solution)/shard_map/ppermute | solution.py:15
  34.3 0.7 %add.6 = f32[3,1152]{1,0:T(4,128)S(1)} add(f32[3,1152]{1,0:T(4,128)} %get-tuple-element.9, f32[3,1152]{1,0:T(4,128)S(1)} %collective-permute-done.14) | non-fusion elementwise | flops 3456 | bytes 41472 | tf_op jit(solution)/shard_map/add | solution.py:69
  35.1 2.6 %collective-permute-start.15 = (f32[3,1152]{1,0:T(4,128)S(1)}, f32[3,1152]{1,0:T(4,128)S(1)}, u32[]{:S(2)}, u32[]{:S(2)}) collective-permute-start(f32[3,1152]{1,0:T(4,128)S(1)} %add.6), channel_id=1, source_target_pairs={{0,2},{1,3},{2,0},{3,1},{4,6},{5,7},{6,4},{7,5},{8,10},{9,11},{10,... | collective-permute-start | bytes 41480 | tf_op jit(solution)/shard_map/ppermute | solution.py:15
  37.7 1.2 %slice.11 = f32[1,1]{1,0:T(1,128)} slice(f32[3,1152]{1,0:T(4,128)} %get-tuple-element.9), slice={[2:3], [0:1]} | slice | bytes 8 | tf_op jit(solution)/shard_map/slice | solution.py:369
  38.8 0.9 %collective-permute-done.15 = f32[3,1152]{1,0:T(4,128)S(1)} collective-permute-done((f32[3,1152]{1,0:T(4,128)S(1)}, f32[3,1152]{1,0:T(4,128)S(1)}, u32[]{:S(2)}, u32[]{:S(2)}) %collective-permute-start.15) | collective-permute-done | bytes 13856 | tf_op jit(solution)/shard_map/ppermute | solution.py:15
  39.7 0.6 %slice_add_fusion = f32[2,1152]{1,0:T(2,128)} fusion(f32[3,1152]{1,0:T(4,128)S(1)} %collective-permute-done.15, f32[3,1152]{1,0:T(4,128)S(1)} %add.6), kind=kLoop, calls=%fused_computation | loop fusion | flops 2304 | bytes 27648 | tf_op jit(solution)/shard_map/add | solution.py:71
  (40 shorter events, 0.2 us)
Async XLA Ops:
  0.6 7.1 %collective-permute-start.1 = (bf16[1,64,1152]{2,1,0:T(8,128)(2,1)}, bf16[1,64,1152]{2,1,0:T(8,128)(2,1)S(1)}, u32[]{:S(2)}, u32[]{:S(2)}) collective-permute-start(bf16[1,64,1152]{2,1,0:T(8,128)(2,1)} %refs_7_.1), channel_id=1, source_target_pairs={{0,16},{4,20},{8,24},{12,28},{16,0},{20,4},{24,8},{28,12},{1,17},{... | collective-permute-start | bytes 442376 | tf_op jit(solution)/shard_map/ppermute | solution.py:15
  3.7 6.0 %collective-permute-start = (bf16[1,64,1152]{2,1,0:T(8,128)(2,1)}, bf16[1,64,1152]{2,1,0:T(8,128)(2,1)S(1)}, u32[]{:S(2)}, u32[]{:S(2)}) collective-permute-start(bf16[1,64,1152]{2,1,0:T(8,128)(2,1)} %refs_7_.1), channel_id=1, source_target_pairs={{0,8},{4,12},{8,0},{12,4},{16,24},{20,28},{24,16},{28,20},{1,9},{5... | collective-permute-start | bytes 442376 | tf_op jit(solution)/shard_map/ppermute | solution.py:15
  5.2 4.6 %collective-permute-start.3 = (bf16[1,64,1152]{2,1,0:T(8,128)(2,1)}, bf16[1,64,1152]{2,1,0:T(8,128)(2,1)S(1)}, u32[]{:S(2)}, u32[]{:S(2)}) collective-permute-start(bf16[1,64,1152]{2,1,0:T(8,128)(2,1)} %refs_7_.1), channel_id=1, source_target_pairs={{0,4},{4,0},{8,12},{12,8},{16,20},{20,16},{24,28},{28,24},{1,5},{5... | collective-permute-start | bytes 442376 | tf_op jit(solution)/shard_map/ppermute | solution.py:15
  5.2 6.5 %collective-permute-start.7 = (bf16[1,64,1152]{2,1,0:T(8,128)(2,1)}, bf16[1,64,1152]{2,1,0:T(8,128)(2,1)S(1)}, u32[]{:S(2)}, u32[]{:S(2)}) collective-permute-start(bf16[1,64,1152]{2,1,0:T(8,128)(2,1)} %refs_15_.1), channel_id=1, source_target_pairs={{0,16},{4,20},{8,24},{12,28},{16,0},{20,4},{24,8},{28,12},{1,17},{... | collective-permute-start | bytes 442376 | tf_op jit(solution)/shard_map/ppermute | solution.py:15
  5.7 7.0 %collective-permute-start.8 = (bf16[1,64,1152]{2,1,0:T(8,128)(2,1)}, bf16[1,64,1152]{2,1,0:T(8,128)(2,1)S(1)}, u32[]{:S(2)}, u32[]{:S(2)}) collective-permute-start(bf16[1,64,1152]{2,1,0:T(8,128)(2,1)} %refs_15_.1), channel_id=1, source_target_pairs={{0,8},{4,12},{8,0},{12,4},{16,24},{20,28},{24,16},{28,20},{1,9},{5... | collective-permute-start | bytes 442376 | tf_op jit(solution)/shard_map/ppermute | solution.py:15
  7.8 11.4 %copy-start = (bf16[1,64,1152]{2,1,0:T(8,128)(2,1)}, bf16[1,64,1152]{2,1,0:T(8,128)(2,1)S(1)}, u32[]{:S(2)}) copy-start(bf16[1,64,1152]{2,1,0:T(8,128)(2,1)S(1)} %collective-permute-done.1.refs_9_) | copy-start | bytes 442372
  7.8 4.9 %collective-permute-start.10 = (bf16[1,64,1152]{2,1,0:T(8,128)(2,1)}, bf16[1,64,1152]{2,1,0:T(8,128)(2,1)S(1)}, u32[]{:S(2)}, u32[]{:S(2)}) collective-permute-start(bf16[1,64,1152]{2,1,0:T(8,128)(2,1)} %refs_15_.1), channel_id=1, source_target_pairs={{0,4},{4,0},{8,12},{12,8},{16,20},{20,16},{24,28},{28,24},{1,5},{5... | collective-permute-start | bytes 442376 | tf_op jit(solution)/shard_map/ppermute | solution.py:15
  9.7 9.4 %copy-start.1 = (bf16[1,64,1152]{2,1,0:T(8,128)(2,1)}, bf16[1,64,1152]{2,1,0:T(8,128)(2,1)S(1)}, u32[]{:S(2)}) copy-start(bf16[1,64,1152]{2,1,0:T(8,128)(2,1)S(1)} %collective-permute-done.refs_8_) | copy-start | bytes 442372
  9.7 3.4 %collective-permute-start.5 = (bf16[1,64,1152]{2,1,0:T(8,128)(2,1)S(1)}, bf16[1,64,1152]{2,1,0:T(8,128)(2,1)S(1)}, u32[]{:S(2)}, u32[]{:S(2)}) collective-permute-start(bf16[1,64,1152]{2,1,0:T(8,128)(2,1)S(1)} %collective-permute-done.1.refs_9_), channel_id=1, source_target_pairs={{0,4},{4,0},{8,12},{12,8},{16,20},{20,16},{24,28},{28,24},{1,5},{5... | collective-permute-start | bytes 442376 | tf_op jit(solution)/shard_map/ppermute | solution.py:15
  9.7 9.4 %copy-start.2 = (bf16[1,64,1152]{2,1,0:T(8,128)(2,1)}, bf16[1,64,1152]{2,1,0:T(8,128)(2,1)S(1)}, u32[]{:S(2)}) copy-start(bf16[1,64,1152]{2,1,0:T(8,128)(2,1)S(1)} %collective-permute-done.3.refs_11_) | copy-start | bytes 442372
  9.8 6.3 %collective-permute-start.2 = (bf16[1,64,1152]{2,1,0:T(8,128)(2,1)S(1)}, bf16[1,64,1152]{2,1,0:T(8,128)(2,1)S(1)}, u32[]{:S(2)}, u32[]{:S(2)}) collective-permute-start(bf16[1,64,1152]{2,1,0:T(8,128)(2,1)S(1)} %collective-permute-done.refs_8_), channel_id=1, source_target_pairs={{0,16},{4,20},{8,24},{12,28},{16,0},{20,4},{24,8},{28,12},{1,17},{... | collective-permute-start | bytes 442376 | tf_op jit(solution)/shard_map/ppermute | solution.py:15
  11.7 7.5 %copy-start.3 = (bf16[1,64,1152]{2,1,0:T(8,128)(2,1)}, bf16[1,64,1152]{2,1,0:T(8,128)(2,1)S(1)}, u32[]{:S(2)}) copy-start(bf16[1,64,1152]{2,1,0:T(8,128)(2,1)S(1)} %collective-permute-done.7.refs_16_) | copy-start | bytes 442372
  11.7 5.4 %collective-permute-start.9 = (bf16[1,64,1152]{2,1,0:T(8,128)(2,1)S(1)}, bf16[1,64,1152]{2,1,0:T(8,128)(2,1)S(1)}, u32[]{:S(2)}, u32[]{:S(2)}) collective-permute-start(bf16[1,64,1152]{2,1,0:T(8,128)(2,1)S(1)} %collective-permute-done.7.refs_16_), channel_id=1, source_target_pairs={{0,8},{4,12},{8,0},{12,4},{16,24},{20,28},{24,16},{28,20},{1,9},{5... | collective-permute-start | bytes 442376 | tf_op jit(solution)/shard_map/ppermute | solution.py:15
  12.6 6.5 %copy-start.4 = (bf16[1,64,1152]{2,1,0:T(8,128)(2,1)}, bf16[1,64,1152]{2,1,0:T(8,128)(2,1)S(1)}, u32[]{:S(2)}) copy-start(bf16[1,64,1152]{2,1,0:T(8,128)(2,1)S(1)} %collective-permute-done.8.refs_17_) | copy-start | bytes 442372
  12.7 6.4 %collective-permute-start.4 = (bf16[1,64,1152]{2,1,0:T(8,128)(2,1)S(1)}, bf16[1,64,1152]{2,1,0:T(8,128)(2,1)S(1)}, u32[]{:S(2)}, u32[]{:S(2)}) collective-permute-start(bf16[1,64,1152]{2,1,0:T(8,128)(2,1)S(1)} %collective-permute-done.refs_8_), channel_id=1, source_target_pairs={{0,4},{4,0},{8,12},{12,8},{16,20},{20,16},{24,28},{28,24},{1,5},{5... | collective-permute-start | bytes 442376 | tf_op jit(solution)/shard_map/ppermute | solution.py:15
  12.7 6.5 %copy-start.5 = (bf16[1,64,1152]{2,1,0:T(8,128)(2,1)}, bf16[1,64,1152]{2,1,0:T(8,128)(2,1)S(1)}, u32[]{:S(2)}) copy-start(bf16[1,64,1152]{2,1,0:T(8,128)(2,1)S(1)} %collective-permute-done.10.refs_19_) | copy-start | bytes 442372
  12.7 6.4 %collective-permute-start.11 = (bf16[1,64,1152]{2,1,0:T(8,128)(2,1)S(1)}, bf16[1,64,1152]{2,1,0:T(8,128)(2,1)S(1)}, u32[]{:S(2)}, u32[]{:S(2)}) collective-permute-start(bf16[1,64,1152]{2,1,0:T(8,128)(2,1)S(1)} %collective-permute-done.7.refs_16_), channel_id=1, source_target_pairs={{0,4},{4,0},{8,12},{12,8},{16,20},{20,16},{24,28},{28,24},{1,5},{5... | collective-permute-start | bytes 442376 | tf_op jit(solution)/shard_map/ppermute | solution.py:15
  13.2 6.0 %copy-start.6 = (bf16[1,64,1152]{2,1,0:T(8,128)(2,1)}, bf16[1,64,1152]{2,1,0:T(8,128)(2,1)S(1)}, u32[]{:S(2)}) copy-start(bf16[1,64,1152]{2,1,0:T(8,128)(2,1)S(1)} %collective-permute-done.5.refs_13_) | copy-start | bytes 442372
  13.2 5.9 %collective-permute-start.12 = (bf16[1,64,1152]{2,1,0:T(8,128)(2,1)S(1)}, bf16[1,64,1152]{2,1,0:T(8,128)(2,1)S(1)}, u32[]{:S(2)}, u32[]{:S(2)}) collective-permute-start(bf16[1,64,1152]{2,1,0:T(8,128)(2,1)S(1)} %collective-permute-done.8.refs_17_), channel_id=1, source_target_pairs={{0,4},{4,0},{8,12},{12,8},{16,20},{20,16},{24,28},{28,24},{1,5},{5... | collective-permute-start | bytes 442376 | tf_op jit(solution)/shard_map/ppermute | solution.py:15
  16.0 3.2 %copy-start.7 = (bf16[1,64,1152]{2,1,0:T(8,128)(2,1)}, bf16[1,64,1152]{2,1,0:T(8,128)(2,1)S(1)}, u32[]{:S(2)}) copy-start(bf16[1,64,1152]{2,1,0:T(8,128)(2,1)S(1)} %collective-permute-done.2.refs_10_) | copy-start | bytes 442372
  16.0 3.1 %collective-permute-start.6 = (bf16[1,64,1152]{2,1,0:T(8,128)(2,1)S(1)}, bf16[1,64,1152]{2,1,0:T(8,128)(2,1)S(1)}, u32[]{:S(2)}, u32[]{:S(2)}) collective-permute-start(bf16[1,64,1152]{2,1,0:T(8,128)(2,1)S(1)} %collective-permute-done.2.refs_10_), channel_id=1, source_target_pairs={{0,4},{4,0},{8,12},{12,8},{16,20},{20,16},{24,28},{28,24},{1,5},{5... | collective-permute-start | bytes 442376 | tf_op jit(solution)/shard_map/ppermute | solution.py:15
  17.1 2.0 %collective-permute-start.13 = (bf16[1,64,1152]{2,1,0:T(8,128)(2,1)S(1)}, bf16[1,64,1152]{2,1,0:T(8,128)(2,1)S(1)}, u32[]{:S(2)}, u32[]{:S(2)}) collective-permute-start(bf16[1,64,1152]{2,1,0:T(8,128)(2,1)S(1)} %collective-permute-done.9.refs_18_), channel_id=1, source_target_pairs={{0,4},{4,0},{8,12},{12,8},{16,20},{20,16},{24,28},{28,24},{1,5},{5... | collective-permute-start | bytes 442376 | tf_op jit(solution)/shard_map/ppermute | solution.py:15
  30.3 4.0 %collective-permute-start.14 = (f32[3,1152]{1,0:T(4,128)}, f32[3,1152]{1,0:T(4,128)S(1)}, u32[]{:S(2)}, u32[]{:S(2)}) collective-permute-start(f32[3,1152]{1,0:T(4,128)} %get-tuple-element.9), channel_id=1, source_target_pairs={{0,1},{1,0},{2,3},{3,2},{4,5},{5,4},{6,7},{7,6},{8,9},{9,8},{10,11... | collective-permute-start | bytes 41480 | tf_op jit(solution)/shard_map/ppermute | solution.py:15
  35.1 4.7 %collective-permute-start.15 = (f32[3,1152]{1,0:T(4,128)S(1)}, f32[3,1152]{1,0:T(4,128)S(1)}, u32[]{:S(2)}, u32[]{:S(2)}) collective-permute-start(f32[3,1152]{1,0:T(4,128)S(1)} %add.6), channel_id=1, source_target_pairs={{0,2},{1,3},{2,0},{3,1},{4,6},{5,7},{6,4},{7,5},{8,10},{9,11},{10,... | collective-permute-start | bytes 41480 | tf_op jit(solution)/shard_map/ppermute | solution.py:15
  (6 other events, 5.7 us)

commit v13 on v12

--- a/solution.py
+++ b/solution.py
@@ -61,6 +61,20 @@
 def all_sum(value, axis, keep=None):
     keep = value.shape[0] if keep is None else keep
     count = lax.axis_size(axis)
+    if 1 < count <= 4:
+        held = [value[:keep]] + [
+            lax.ppermute(value, axis, [(source, (source + shift) % count) for source in range(count)])[:keep]
+            for shift in range(1, count)
+        ]
+        own = lax.axis_index(axis)
+        total = None
+        for member in range(count):
+            shift = (own - member) % count
+            part = held[0]
+            for other in range(1, count):
+                part = jnp.where(shift == other, held[other], part)
+            total = part if total is None else total + part
+        return total
     if not power_of_two(count):
         return lax.psum(value, axis)[:keep]
     bit = 1
@@ -303,7 +317,10 @@
                 direction - unit_rows * jnp.sum(unit_rows * direction, axis=-1, keepdims=True)
             ) * length_ref[tower, rows, :]
             gain_sum = gain_sum + jnp.sum(tangent * normed, axis=0, keepdims=True)
-            tangent_ref[rows, :] = tangent
+
+            @pl.when((own_block * block_rows >= first) & (own_block * block_rows < first + chunk))
+            def _():
+                tangent_ref[rows, :] = tangent
         sums_ref[tower : tower + 1, :] = gain_sum
         own = pl.ds(pl.multiple_of(own_block * block_rows, block_rows), block_rows)
         normed = normed_ref[tower, own, :]

time: 40.6 us -> 43.6 us (1.074)
  Pallas kernels: 9.73 us -> 11.4 us
  starting transfers between devices: 11.7 us -> 13.1 us
  other arithmetic: 1.33 us -> 0.62 us
  waiting for transfers between devices: 12.2 us -> 12.7 us
    ppermute x0 -> x3, starting transfers between devices: none -> 4.64 us  [all_sum(): lax.ppermute(value, axis, [(source, (source + shift) % count) for source...]
    ppermute x0 -> x3, waiting for transfers between devices: none -> 3.49 us  [all_sum(): lax.ppermute(value, axis, [(source, (source + shift) % count) for source...]
    ppermute x16 -> x14, starting transfers between devices: 11.7 us -> 8.45 us  [xor_swap(): lax.ppermute(value, axis, [(source, source ^ bit) for source in range(cou...]
    ppermute x16 -> x14, waiting for transfers between devices: 12.2 us -> 9.25 us  [xor_swap(): lax.ppermute(value, axis, [(source, source ^ bit) for source in range(cou...]
    pallas_call x1, Pallas kernels: 9.73 us -> 11.4 us  [whole_group(): pl.pallas_call(functools.partial(group_kernel, tuple(masks[:count]), tupl...]
    unnamed x28 -> x30, local copies, waits for them, and re-layouts: 1.41 us -> 2.14 us
    add x2 -> x1, other arithmetic: 1.33 us -> 0.62 us  [all_sum(): total = part if total is None else total + part]
    slice x1, local copies, waits for them, and re-layouts: 1.18 us -> 0.51 us  [whole_group(): group_loss = sums[2, 0:1]]
  transfers between devices with their start and end apart: 16 -> 17, of which waited for: 7 -> 7; matrix products, arithmetic and copies ran while one was open for 3% -> 1% of each run, Pallas kernels for 0% -> 0%
where the time goes in v13:
time: 43.6 us; the launch traced here: 43.3 us
  starting transfers between devices  13.1 us (30%)
  waiting for transfers between devices  12.7 us (29%)
  Pallas kernels  11.4 us (26%)
  between operations  2.79 us (6%)
  local copies, waits for them, and re-layouts  2.65 us (6%)
  other arithmetic  0.62 us (1%)
    pallas_call x1, Pallas kernels, whole_group(): pl.pallas_call(functools.partial(group_kernel, tuple(masks[:count]), tupl...  11.4 us
    ppermute x14, waiting for transfers between devices, xor_swap(): lax.ppermute(value, axis, [(source, source ^ bit) for source in range(cou...  9.25 us
    ppermute x14, starting transfers between devices, xor_swap(): lax.ppermute(value, axis, [(source, source ^ bit) for source in range(cou...  8.45 us
    ppermute x3, starting transfers between devices, all_sum(): lax.ppermute(value, axis, [(source, (source + shift) % count) for source...  4.64 us
    ppermute x3, waiting for transfers between devices, all_sum(): lax.ppermute(value, axis, [(source, (source + shift) % count) for source...  3.49 us
    unnamed x30, local copies, waits for them, and re-layouts  2.14 us
  transfers between devices with their start and end apart: 17, of which 7 were waited for; matrix products, arithmetic and copies ran while one was open for 1% of the time, Pallas kernels for 0%

profile of v13, /device:TPU:0, one launch (start us, length us, event | category | flops | bytes accessed | tf_op | source)
XLA Modules:
  0.0 43.3 jit_solution(2153326189003708968)
XLA Ops:
  0.6 3.0 %collective-permute-start = (bf16[1,64,1152]{2,1,0:T(8,128)(2,1)}, bf16[1,64,1152]{2,1,0:T(8,128)(2,1)S(1)}, u32[]{:S(2)}, u32[]{:S(2)}) collective-permute-start(bf16[1,64,1152]{2,1,0:T(8,128)(2,1)} %refs_7_.1), channel_id=1, source_target_pairs={{0,8},{4,12},{8,0},{12,4},{16,24},{20,28},{24,16},{28,20},{1,9},{5... | collective-permute-start | bytes 442376 | tf_op jit(solution)/shard_map/ppermute | solution.py:15
  3.7 1.5 %collective-permute-start.1 = (bf16[1,64,1152]{2,1,0:T(8,128)(2,1)}, bf16[1,64,1152]{2,1,0:T(8,128)(2,1)S(1)}, u32[]{:S(2)}, u32[]{:S(2)}) collective-permute-start(bf16[1,64,1152]{2,1,0:T(8,128)(2,1)} %refs_7_.1), channel_id=1, source_target_pairs={{0,16},{4,20},{8,24},{12,28},{16,0},{20,4},{24,8},{28,12},{1,17},{... | collective-permute-start | bytes 442376 | tf_op jit(solution)/shard_map/ppermute | solution.py:15
  5.2 0.5 %collective-permute-start.7 = (bf16[1,64,1152]{2,1,0:T(8,128)(2,1)}, bf16[1,64,1152]{2,1,0:T(8,128)(2,1)S(1)}, u32[]{:S(2)}, u32[]{:S(2)}) collective-permute-start(bf16[1,64,1152]{2,1,0:T(8,128)(2,1)} %refs_15_.1), channel_id=1, source_target_pairs={{0,16},{4,20},{8,24},{12,28},{16,0},{20,4},{24,8},{28,12},{1,17},{... | collective-permute-start | bytes 442376 | tf_op jit(solution)/shard_map/ppermute | solution.py:15
  5.7 0.1 collective-permute-start.8
  5.8 1.9 %collective-permute-done.refs_8_ = bf16[1,64,1152]{2,1,0:T(8,128)(2,1)S(1)} collective-permute-done((bf16[1,64,1152]{2,1,0:T(8,128)(2,1)}, bf16[1,64,1152]{2,1,0:T(8,128)(2,1)S(1)}, u32[]{:S(2)}, u32[]{:S(2)}) %collective-permute-start) | collective-permute-done | bytes 147488 | tf_op jit(solution)/shard_map/ppermute | solution.py:15
  7.7 2.1 %collective-permute-done.1.refs_9_ = bf16[1,64,1152]{2,1,0:T(8,128)(2,1)S(1)} collective-permute-done((bf16[1,64,1152]{2,1,0:T(8,128)(2,1)}, bf16[1,64,1152]{2,1,0:T(8,128)(2,1)S(1)}, u32[]{:S(2)}, u32[]{:S(2)}) %collective-permute-start.1) | collective-permute-done | bytes 147488 | tf_op jit(solution)/shard_map/ppermute | solution.py:15
  9.9 2.2 %collective-permute-start.2 = (bf16[1,64,1152]{2,1,0:T(8,128)(2,1)S(1)}, bf16[1,64,1152]{2,1,0:T(8,128)(2,1)S(1)}, u32[]{:S(2)}, u32[]{:S(2)}) collective-permute-start(bf16[1,64,1152]{2,1,0:T(8,128)(2,1)S(1)} %collective-permute-done.refs_8_), channel_id=1, source_target_pairs={{0,16},{4,20},{8,24},{12,28},{16,0},{20,4},{24,8},{28,12},{1,17},{... | collective-permute-start | bytes 442376 | tf_op jit(solution)/shard_map/ppermute | solution.py:15
  12.1 0.9 %collective-permute-done.7.refs_16_ = bf16[1,64,1152]{2,1,0:T(8,128)(2,1)S(1)} collective-permute-done((bf16[1,64,1152]{2,1,0:T(8,128)(2,1)}, bf16[1,64,1152]{2,1,0:T(8,128)(2,1)S(1)}, u32[]{:S(2)}, u32[]{:S(2)}) %collective-permute-start.7) | collective-permute-done | bytes 147488 | tf_op jit(solution)/shard_map/ppermute | solution.py:15
  13.0 0.1 collective-permute-start.11
  13.1 0.5 %collective-permute-start.5 = (bf16[1,64,1152]{2,1,0:T(8,128)(2,1)S(1)}, bf16[1,64,1152]{2,1,0:T(8,128)(2,1)S(1)}, u32[]{:S(2)}, u32[]{:S(2)}) collective-permute-start(bf16[1,64,1152]{2,1,0:T(8,128)(2,1)S(1)} %collective-permute-done.1.refs_9_), channel_id=1, source_target_pairs={{0,4},{4,0},{8,12},{12,8},{16,20},{20,16},{24,28},{28,24},{1,5},{5... | collective-permute-start | bytes 442376 | tf_op jit(solution)/shard_map/ppermute | solution.py:15
  13.6 1.9 %collective-permute-done.2.refs_10_ = bf16[1,64,1152]{2,1,0:T(8,128)(2,1)S(1)} collective-permute-done((bf16[1,64,1152]{2,1,0:T(8,128)(2,1)S(1)}, bf16[1,64,1152]{2,1,0:T(8,128)(2,1)S(1)}, u32[]{:S(2)}, u32[]{:S(2)}) %collective-permute-start.2) | collective-permute-done | bytes 147488 | tf_op jit(solution)/shard_map/ppermute | solution.py:15
  15.5 0.5 %collective-permute-start.6 = (bf16[1,64,1152]{2,1,0:T(8,128)(2,1)S(1)}, bf16[1,64,1152]{2,1,0:T(8,128)(2,1)S(1)}, u32[]{:S(2)}, u32[]{:S(2)}) collective-permute-start(bf16[1,64,1152]{2,1,0:T(8,128)(2,1)S(1)} %collective-permute-done.2.refs_10_), channel_id=1, source_target_pairs={{0,4},{4,0},{8,12},{12,8},{16,20},{20,16},{24,28},{28,24},{1,5},{5... | collective-permute-start | bytes 442376 | tf_op jit(solution)/shard_map/ppermute | solution.py:15
  16.0 2.4 %collective-permute-done.9.refs_18_ = bf16[1,64,1152]{2,1,0:T(8,128)(2,1)S(1)} collective-permute-done((bf16[1,64,1152]{2,1,0:T(8,128)(2,1)S(1)}, bf16[1,64,1152]{2,1,0:T(8,128)(2,1)S(1)}, u32[]{:S(2)}, u32[]{:S(2)}) %collective-permute-start.9) | collective-permute-done | bytes 147488 | tf_op jit(solution)/shard_map/ppermute | solution.py:15
  20.5 0.5 %copy-done.10 = bf16[1,64,1152]{2,1,0:T(8,128)(2,1)} copy-done((bf16[1,64,1152]{2,1,0:T(8,128)(2,1)}, bf16[1,64,1152]{2,1,0:T(8,128)(2,1)S(1)}, u32[]{:S(2)}) %copy-start.10) | copy-done | bytes 147480
  21.0 0.1 copy-done.9
  21.2 0.7 %copy-done.13 = bf16[1,64,1152]{2,1,0:T(8,128)(2,1)} copy-done((bf16[1,64,1152]{2,1,0:T(8,128)(2,1)}, bf16[1,64,1152]{2,1,0:T(8,128)(2,1)S(1)}, u32[]{:S(2)}) %copy-start.13) | copy-done | bytes 147480
  21.9 11.4 %shard_map.120 = (bf16[1,64,1152]{2,1,0:T(8,128)(2,1)}, bf16[1,64,1152]{2,1,0:T(8,128)(2,1)}, f32[3,1152]{1,0:T(4,128)}) custom-call(f32[1]{0:T(128)S(6)} %copy.13.refs_0_, f32[1]{0:T(128)S(6)} %copy.14.refs_1_, f32[1]{0:T(128)S(6)} %copy.15.refs_2_, s32[1,8]{1,0:T(1,128)} %refs_3_.1, f32[1152]{0:T(1024)} %refs_4_.1, f32[1152]{0:T(1024)} %refs_5_.1, ...), custom_call_target="tpu_custom_call" | custom-call | tf_op jit(solution)/shard_map/pallas_call | solution.py:358
  33.3 3.6 %collective-permute-start.14 = (f32[3,1152]{1,0:T(4,128)}, f32[3,1152]{1,0:T(4,128)S(1)}, u32[]{:S(2)}, u32[]{:S(2)}) collective-permute-start(f32[3,1152]{1,0:T(4,128)} %get-tuple-element.9), channel_id=1, source_target_pairs={{0,3},{1,0},{2,1},{3,2},{4,7},{5,4},{6,5},{7,6},{8,11},{9,8},{10,9... | collective-permute-start | bytes 41480 | tf_op jit(solution)/shard_map/ppermute | solution.py:66
  37.0 1.0 %collective-permute-start.16 = (f32[3,1152]{1,0:T(4,128)}, f32[3,1152]{1,0:T(4,128)S(1)}, u32[]{:S(2)}, u32[]{:S(2)}) collective-permute-start(f32[3,1152]{1,0:T(4,128)} %get-tuple-element.9), channel_id=1, source_target_pairs={{0,1},{1,2},{2,3},{3,0},{4,5},{5,6},{6,7},{7,4},{8,9},{9,10},{10,1... | collective-permute-start | bytes 41480 | tf_op jit(solution)/shard_map/ppermute | solution.py:66
  38.0 0.8 %copy-done.14 = f32[3,1152]{1,0:T(4,128)S(1)} copy-done((f32[3,1152]{1,0:T(4,128)S(1)}, f32[3,1152]{1,0:T(4,128)}, u32[]{:S(2)}) %copy-start.14) | copy-done | bytes 13848
  38.7 0.5 %slice.19 = f32[1,1]{1,0:T(1,128)} slice(f32[3,1152]{1,0:T(4,128)S(1)} %copy-done.14), slice={[2:3], [0:1]} | slice | bytes 8 | tf_op jit(solution)/shard_map/slice | solution.py:386
  39.2 2.6 %collective-permute-done.15 = f32[3,1152]{1,0:T(4,128)S(1)} collective-permute-done((f32[3,1152]{1,0:T(4,128)}, f32[3,1152]{1,0:T(4,128)S(1)}, u32[]{:S(2)}, u32[]{:S(2)}) %collective-permute-start.15) | collective-permute-done | bytes 13856 | tf_op jit(solution)/shard_map/ppermute | solution.py:66
  41.8 0.9 %collective-permute-done.16 = f32[3,1152]{1,0:T(4,128)S(1)} collective-permute-done((f32[3,1152]{1,0:T(4,128)}, f32[3,1152]{1,0:T(4,128)S(1)}, u32[]{:S(2)}, u32[]{:S(2)}) %collective-permute-start.16) | collective-permute-done | bytes 13856 | tf_op jit(solution)/shard_map/ppermute | solution.py:66
  42.7 0.6 %select_add_fusion = f32[2,1152]{1,0:T(2,128)} fusion(f32[3,1152]{1,0:T(4,128)S(1)} %collective-permute-done.14, f32[3,1152]{1,0:T(4,128)S(1)} %collective-permute-done.15, f32[3,1152]{1,0:T(4,128)S(1)} %collective-permute-done.16, f32[3,1152]{1,0:T(4,128)S(1)} %copy-done.14, pred[]{:T(512)S(6)} %eq.52, pred[]{:T(512)S(6)} %eq.51, pred[]{:T(512)S(6)} %eq.50, ...), kind=kLoop, calls=%fused_computation | loop fusion | flops 34560 | bytes 46092 | tf_op jit(solution)/shard_map/add | solution.py:76
  (43 shorter events, 0.2 us)
Async XLA Ops:
  0.6 7.1 %collective-permute-start = (bf16[1,64,1152]{2,1,0:T(8,128)(2,1)}, bf16[1,64,1152]{2,1,0:T(8,128)(2,1)S(1)}, u32[]{:S(2)}, u32[]{:S(2)}) collective-permute-start(bf16[1,64,1152]{2,1,0:T(8,128)(2,1)} %refs_7_.1), channel_id=1, source_target_pairs={{0,8},{4,12},{8,0},{12,4},{16,24},{20,28},{24,16},{28,20},{1,9},{5... | collective-permute-start | bytes 442376 | tf_op jit(solution)/shard_map/ppermute | solution.py:15
  3.7 6.2 %collective-permute-start.1 = (bf16[1,64,1152]{2,1,0:T(8,128)(2,1)}, bf16[1,64,1152]{2,1,0:T(8,128)(2,1)S(1)}, u32[]{:S(2)}, u32[]{:S(2)}) collective-permute-start(bf16[1,64,1152]{2,1,0:T(8,128)(2,1)} %refs_7_.1), channel_id=1, source_target_pairs={{0,16},{4,20},{8,24},{12,28},{16,0},{20,4},{24,8},{28,12},{1,17},{... | collective-permute-start | bytes 442376 | tf_op jit(solution)/shard_map/ppermute | solution.py:15
  5.2 6.9 %collective-permute-start.3 = (bf16[1,64,1152]{2,1,0:T(8,128)(2,1)}, bf16[1,64,1152]{2,1,0:T(8,128)(2,1)S(1)}, u32[]{:S(2)}, u32[]{:S(2)}) collective-permute-start(bf16[1,64,1152]{2,1,0:T(8,128)(2,1)} %refs_7_.1), channel_id=1, source_target_pairs={{0,4},{4,0},{8,12},{12,8},{16,20},{20,16},{24,28},{28,24},{1,5},{5... | collective-permute-start | bytes 442376 | tf_op jit(solution)/shard_map/ppermute | solution.py:15
  5.2 7.8 %collective-permute-start.7 = (bf16[1,64,1152]{2,1,0:T(8,128)(2,1)}, bf16[1,64,1152]{2,1,0:T(8,128)(2,1)S(1)}, u32[]{:S(2)}, u32[]{:S(2)}) collective-permute-start(bf16[1,64,1152]{2,1,0:T(8,128)(2,1)} %refs_15_.1), channel_id=1, source_target_pairs={{0,16},{4,20},{8,24},{12,28},{16,0},{20,4},{24,8},{28,12},{1,17},{... | collective-permute-start | bytes 442376 | tf_op jit(solution)/shard_map/ppermute | solution.py:15
  5.7 7.3 %collective-permute-start.8 = (bf16[1,64,1152]{2,1,0:T(8,128)(2,1)}, bf16[1,64,1152]{2,1,0:T(8,128)(2,1)S(1)}, u32[]{:S(2)}, u32[]{:S(2)}) collective-permute-start(bf16[1,64,1152]{2,1,0:T(8,128)(2,1)} %refs_15_.1), channel_id=1, source_target_pairs={{0,8},{4,12},{8,0},{12,4},{16,24},{20,28},{24,16},{28,20},{1,9},{5... | collective-permute-start | bytes 442376 | tf_op jit(solution)/shard_map/ppermute | solution.py:15
  7.7 12.7 %copy-start = (bf16[1,64,1152]{2,1,0:T(8,128)(2,1)}, bf16[1,64,1152]{2,1,0:T(8,128)(2,1)S(1)}, u32[]{:S(2)}) copy-start(bf16[1,64,1152]{2,1,0:T(8,128)(2,1)S(1)} %collective-permute-done.refs_8_) | copy-start | bytes 442372
  7.7 5.4 %collective-permute-start.10 = (bf16[1,64,1152]{2,1,0:T(8,128)(2,1)}, bf16[1,64,1152]{2,1,0:T(8,128)(2,1)S(1)}, u32[]{:S(2)}, u32[]{:S(2)}) collective-permute-start(bf16[1,64,1152]{2,1,0:T(8,128)(2,1)} %refs_15_.1), channel_id=1, source_target_pairs={{0,4},{4,0},{8,12},{12,8},{16,20},{20,16},{24,28},{28,24},{1,5},{5... | collective-permute-start | bytes 442376 | tf_op jit(solution)/shard_map/ppermute | solution.py:15
  9.9 10.6 %copy-start.1 = (bf16[1,64,1152]{2,1,0:T(8,128)(2,1)}, bf16[1,64,1152]{2,1,0:T(8,128)(2,1)S(1)}, u32[]{:S(2)}) copy-start(bf16[1,64,1152]{2,1,0:T(8,128)(2,1)S(1)} %collective-permute-done.1.refs_9_) | copy-start | bytes 442372
  9.9 5.6 %collective-permute-start.2 = (bf16[1,64,1152]{2,1,0:T(8,128)(2,1)S(1)}, bf16[1,64,1152]{2,1,0:T(8,128)(2,1)S(1)}, u32[]{:S(2)}, u32[]{:S(2)}) collective-permute-start(bf16[1,64,1152]{2,1,0:T(8,128)(2,1)S(1)} %collective-permute-done.refs_8_), channel_id=1, source_target_pairs={{0,16},{4,20},{8,24},{12,28},{16,0},{20,4},{24,8},{28,12},{1,17},{... | collective-permute-start | bytes 442376 | tf_op jit(solution)/shard_map/ppermute | solution.py:15
  12.1 8.3 %copy-start.2 = (bf16[1,64,1152]{2,1,0:T(8,128)(2,1)}, bf16[1,64,1152]{2,1,0:T(8,128)(2,1)S(1)}, u32[]{:S(2)}) copy-start(bf16[1,64,1152]{2,1,0:T(8,128)(2,1)S(1)} %collective-permute-done.3.refs_11_) | copy-start | bytes 442372
  12.1 3.4 %collective-permute-start.4 = (bf16[1,64,1152]{2,1,0:T(8,128)(2,1)S(1)}, bf16[1,64,1152]{2,1,0:T(8,128)(2,1)S(1)}, u32[]{:S(2)}, u32[]{:S(2)}) collective-permute-start(bf16[1,64,1152]{2,1,0:T(8,128)(2,1)S(1)} %collective-permute-done.refs_8_), channel_id=1, source_target_pairs={{0,4},{4,0},{8,12},{12,8},{16,20},{20,16},{24,28},{28,24},{1,5},{5... | collective-permute-start | bytes 442376 | tf_op jit(solution)/shard_map/ppermute | solution.py:15
  13.0 7.4 %copy-start.3 = (bf16[1,64,1152]{2,1,0:T(8,128)(2,1)}, bf16[1,64,1152]{2,1,0:T(8,128)(2,1)S(1)}, u32[]{:S(2)}) copy-start(bf16[1,64,1152]{2,1,0:T(8,128)(2,1)S(1)} %collective-permute-done.7.refs_16_) | copy-start | bytes 442372
  13.0 5.4 %collective-permute-start.9 = (bf16[1,64,1152]{2,1,0:T(8,128)(2,1)S(1)}, bf16[1,64,1152]{2,1,0:T(8,128)(2,1)S(1)}, u32[]{:S(2)}, u32[]{:S(2)}) collective-permute-start(bf16[1,64,1152]{2,1,0:T(8,128)(2,1)S(1)} %collective-permute-done.7.refs_16_), channel_id=1, source_target_pairs={{0,8},{4,12},{8,0},{12,4},{16,24},{20,28},{24,16},{28,20},{1,9},{5... | collective-permute-start | bytes 442376 | tf_op jit(solution)/shard_map/ppermute | solution.py:15
  13.0 7.4 %copy-start.4 = (bf16[1,64,1152]{2,1,0:T(8,128)(2,1)}, bf16[1,64,1152]{2,1,0:T(8,128)(2,1)S(1)}, u32[]{:S(2)}) copy-start(bf16[1,64,1152]{2,1,0:T(8,128)(2,1)S(1)} %collective-permute-done.8.refs_17_) | copy-start | bytes 442372
  13.0 7.3 %collective-permute-start.11 = (bf16[1,64,1152]{2,1,0:T(8,128)(2,1)S(1)}, bf16[1,64,1152]{2,1,0:T(8,128)(2,1)S(1)}, u32[]{:S(2)}, u32[]{:S(2)}) collective-permute-start(bf16[1,64,1152]{2,1,0:T(8,128)(2,1)S(1)} %collective-permute-done.7.refs_16_), channel_id=1, source_target_pairs={{0,4},{4,0},{8,12},{12,8},{16,20},{20,16},{24,28},{28,24},{1,5},{5... | collective-permute-start | bytes 442376 | tf_op jit(solution)/shard_map/ppermute | solution.py:15
  13.1 7.3 %copy-start.5 = (bf16[1,64,1152]{2,1,0:T(8,128)(2,1)}, bf16[1,64,1152]{2,1,0:T(8,128)(2,1)S(1)}, u32[]{:S(2)}) copy-start(bf16[1,64,1152]{2,1,0:T(8,128)(2,1)S(1)} %collective-permute-done.10.refs_19_) | copy-start | bytes 442372
  13.1 7.2 %collective-permute-start.5 = (bf16[1,64,1152]{2,1,0:T(8,128)(2,1)S(1)}, bf16[1,64,1152]{2,1,0:T(8,128)(2,1)S(1)}, u32[]{:S(2)}, u32[]{:S(2)}) collective-permute-start(bf16[1,64,1152]{2,1,0:T(8,128)(2,1)S(1)} %collective-permute-done.1.refs_9_), channel_id=1, source_target_pairs={{0,4},{4,0},{8,12},{12,8},{16,20},{20,16},{24,28},{28,24},{1,5},{5... | collective-permute-start | bytes 442376 | tf_op jit(solution)/shard_map/ppermute | solution.py:15
  15.5 5.0 %copy-start.6 = (bf16[1,64,1152]{2,1,0:T(8,128)(2,1)}, bf16[1,64,1152]{2,1,0:T(8,128)(2,1)S(1)}, u32[]{:S(2)}) copy-start(bf16[1,64,1152]{2,1,0:T(8,128)(2,1)S(1)} %collective-permute-done.2.refs_10_) | copy-start | bytes 442372
  15.5 4.9 %collective-permute-start.12 = (bf16[1,64,1152]{2,1,0:T(8,128)(2,1)S(1)}, bf16[1,64,1152]{2,1,0:T(8,128)(2,1)S(1)}, u32[]{:S(2)}, u32[]{:S(2)}) collective-permute-start(bf16[1,64,1152]{2,1,0:T(8,128)(2,1)S(1)} %collective-permute-done.8.refs_17_), channel_id=1, source_target_pairs={{0,4},{4,0},{8,12},{12,8},{16,20},{20,16},{24,28},{28,24},{1,5},{5... | collective-permute-start | bytes 442376 | tf_op jit(solution)/shard_map/ppermute | solution.py:15
  15.5 4.9 %collective-permute-start.6 = (bf16[1,64,1152]{2,1,0:T(8,128)(2,1)S(1)}, bf16[1,64,1152]{2,1,0:T(8,128)(2,1)S(1)}, u32[]{:S(2)}, u32[]{:S(2)}) collective-permute-start(bf16[1,64,1152]{2,1,0:T(8,128)(2,1)S(1)} %collective-permute-done.2.refs_10_), channel_id=1, source_target_pairs={{0,4},{4,0},{8,12},{12,8},{16,20},{20,16},{24,28},{28,24},{1,5},{5... | collective-permute-start | bytes 442376 | tf_op jit(solution)/shard_map/ppermute | solution.py:15
  18.4 2.0 %collective-permute-start.13 = (bf16[1,64,1152]{2,1,0:T(8,128)(2,1)S(1)}, bf16[1,64,1152]{2,1,0:T(8,128)(2,1)S(1)}, u32[]{:S(2)}, u32[]{:S(2)}) collective-permute-start(bf16[1,64,1152]{2,1,0:T(8,128)(2,1)S(1)} %collective-permute-done.9.refs_18_), channel_id=1, source_target_pairs={{0,4},{4,0},{8,12},{12,8},{16,20},{20,16},{24,28},{28,24},{1,5},{5... | collective-permute-start | bytes 442376 | tf_op jit(solution)/shard_map/ppermute | solution.py:15
  33.3 5.9 %collective-permute-start.14 = (f32[3,1152]{1,0:T(4,128)}, f32[3,1152]{1,0:T(4,128)S(1)}, u32[]{:S(2)}, u32[]{:S(2)}) collective-permute-start(f32[3,1152]{1,0:T(4,128)} %get-tuple-element.9), channel_id=1, source_target_pairs={{0,3},{1,0},{2,1},{3,2},{4,7},{5,4},{6,5},{7,6},{8,11},{9,8},{10,9... | collective-permute-start | bytes 41480 | tf_op jit(solution)/shard_map/ppermute | solution.py:66
  37.0 4.9 %collective-permute-start.15 = (f32[3,1152]{1,0:T(4,128)}, f32[3,1152]{1,0:T(4,128)S(1)}, u32[]{:S(2)}, u32[]{:S(2)}) collective-permute-start(f32[3,1152]{1,0:T(4,128)} %get-tuple-element.9), channel_id=1, source_target_pairs={{0,2},{1,3},{2,0},{3,1},{4,6},{5,7},{6,4},{7,5},{8,10},{9,11},{10,... | collective-permute-start | bytes 41480 | tf_op jit(solution)/shard_map/ppermute | solution.py:66
  37.0 5.8 %collective-permute-start.16 = (f32[3,1152]{1,0:T(4,128)}, f32[3,1152]{1,0:T(4,128)S(1)}, u32[]{:S(2)}, u32[]{:S(2)}) collective-permute-start(f32[3,1152]{1,0:T(4,128)} %get-tuple-element.9), channel_id=1, source_target_pairs={{0,1},{1,2},{2,3},{3,0},{4,5},{5,6},{6,7},{7,4},{8,9},{9,10},{10,1... | collective-permute-start | bytes 41480 | tf_op jit(solution)/shard_map/ppermute | solution.py:66
  (8 other events, 11.5 us)

commit v14 on v12

--- a/solution.py
+++ b/solution.py
@@ -364,7 +364,7 @@
         picture_rescale_factor,
         caption_rescale_factor,
         matching_caption_index,
-        *pieces,
+        *[pltpu.with_memory_space_constraint(piece, pltpu.VMEM) for piece in pieces],
     )
     group_loss = sums[2, 0:1]
     gain_grads = all_sum(sums, "rep", keep=2)

time: 40.6 us -> 42.8 us (1.054)
  Pallas kernels: 9.73 us -> 11.6 us
    pallas_call x1, Pallas kernels: 9.73 us -> 11.6 us  [whole_group(): pl.pallas_call(functools.partial(group_kernel, tuple(masks[:count]), tupl...]
    unnamed x28 -> x4, local copies, waits for them, and re-layouts: 1.41 us -> 1.81 us
where the time goes in v14:
time: 42.8 us; the launch traced here: 42.5 us
  waiting for transfers between devices  12.2 us (29%)
  starting transfers between devices  11.7 us (27%)
  Pallas kernels  11.6 us (27%)
  local copies, waits for them, and re-layouts  3 us (7%)
  between operations  2.65 us (6%)
  other arithmetic  1.33 us (3%)
    ppermute x16, waiting for transfers between devices, xor_swap(): lax.ppermute(value, axis, [(source, source ^ bit) for source in range(cou...  12.2 us
    ppermute x16, starting transfers between devices, xor_swap(): lax.ppermute(value, axis, [(source, source ^ bit) for source in range(cou...  11.7 us
    pallas_call x1, Pallas kernels, whole_group(): pl.pallas_call(functools.partial(group_kernel, tuple(masks[:count]), tupl...  11.6 us
    unnamed x4, local copies, waits for them, and re-layouts  1.81 us
    slice x1, local copies, waits for them, and re-layouts, whole_group(): group_loss = sums[2, 0:1]  1.19 us
  transfers between devices with their start and end apart: 16, of which 7 were waited for; matrix products, arithmetic and copies ran while one was open for 3% of the time, Pallas kernels for 0%

profile of v14, /device:TPU:0, one launch (start us, length us, event | category | flops | bytes accessed | tf_op | source)
XLA Modules:
  0.0 42.5 jit_solution(13389250557132681494)
XLA Ops:
  0.6 3.1 %collective-permute-start.1 = (bf16[1,64,1152]{2,1,0:T(8,128)(2,1)}, bf16[1,64,1152]{2,1,0:T(8,128)(2,1)S(1)}, u32[]{:S(2)}, u32[]{:S(2)}) collective-permute-start(bf16[1,64,1152]{2,1,0:T(8,128)(2,1)} %refs_7_.1), channel_id=1, source_target_pairs={{0,16},{4,20},{8,24},{12,28},{16,0},{20,4},{24,8},{28,12},{1,17},{... | collective-permute-start | bytes 442376 | tf_op jit(solution)/shard_map/ppermute | solution.py:15
  3.7 1.5 %collective-permute-start = (bf16[1,64,1152]{2,1,0:T(8,128)(2,1)}, bf16[1,64,1152]{2,1,0:T(8,128)(2,1)S(1)}, u32[]{:S(2)}, u32[]{:S(2)}) collective-permute-start(bf16[1,64,1152]{2,1,0:T(8,128)(2,1)} %refs_7_.1), channel_id=1, source_target_pairs={{0,8},{4,12},{8,0},{12,4},{16,24},{20,28},{24,16},{28,20},{1,9},{5... | collective-permute-start | bytes 442376 | tf_op jit(solution)/shard_map/ppermute | solution.py:15
  5.2 0.5 %collective-permute-start.7 = (bf16[1,64,1152]{2,1,0:T(8,128)(2,1)}, bf16[1,64,1152]{2,1,0:T(8,128)(2,1)S(1)}, u32[]{:S(2)}, u32[]{:S(2)}) collective-permute-start(bf16[1,64,1152]{2,1,0:T(8,128)(2,1)} %refs_15_.1), channel_id=1, source_target_pairs={{0,16},{4,20},{8,24},{12,28},{16,0},{20,4},{24,8},{28,12},{1,17},{... | collective-permute-start | bytes 442376 | tf_op jit(solution)/shard_map/ppermute | solution.py:15
  5.7 0.1 collective-permute-start.8
  5.8 1.9 %collective-permute-done.1.refs_9_ = bf16[1,64,1152]{2,1,0:T(8,128)(2,1)S(1)} collective-permute-done((bf16[1,64,1152]{2,1,0:T(8,128)(2,1)}, bf16[1,64,1152]{2,1,0:T(8,128)(2,1)S(1)}, u32[]{:S(2)}, u32[]{:S(2)}) %collective-permute-start.1) | collective-permute-done | bytes 147488 | tf_op jit(solution)/shard_map/ppermute | solution.py:15
  7.8 0.0 collective-permute-start.10
  7.8 2.0 %collective-permute-done.refs_8_ = bf16[1,64,1152]{2,1,0:T(8,128)(2,1)S(1)} collective-permute-done((bf16[1,64,1152]{2,1,0:T(8,128)(2,1)}, bf16[1,64,1152]{2,1,0:T(8,128)(2,1)S(1)}, u32[]{:S(2)}, u32[]{:S(2)}) %collective-permute-start) | collective-permute-done | bytes 147488 | tf_op jit(solution)/shard_map/ppermute | solution.py:15
  9.7 0.7 %collective-permute-start.2 = (bf16[1,64,1152]{2,1,0:T(8,128)(2,1)S(1)}, bf16[1,64,1152]{2,1,0:T(8,128)(2,1)S(1)}, u32[]{:S(2)}, u32[]{:S(2)}) collective-permute-start(bf16[1,64,1152]{2,1,0:T(8,128)(2,1)S(1)} %collective-permute-done.refs_8_), channel_id=1, source_target_pairs={{0,16},{4,20},{8,24},{12,28},{16,0},{20,4},{24,8},{28,12},{1,17},{... | collective-permute-start | bytes 442376 | tf_op jit(solution)/shard_map/ppermute | solution.py:15
  10.5 1.2 %collective-permute-done.7.refs_16_ = bf16[1,64,1152]{2,1,0:T(8,128)(2,1)S(1)} collective-permute-done((bf16[1,64,1152]{2,1,0:T(8,128)(2,1)}, bf16[1,64,1152]{2,1,0:T(8,128)(2,1)S(1)}, u32[]{:S(2)}, u32[]{:S(2)}) %collective-permute-start.7) | collective-permute-done | bytes 147488 | tf_op jit(solution)/shard_map/ppermute | solution.py:15
  11.7 1.0 %collective-permute-start.9 = (bf16[1,64,1152]{2,1,0:T(8,128)(2,1)S(1)}, bf16[1,64,1152]{2,1,0:T(8,128)(2,1)S(1)}, u32[]{:S(2)}, u32[]{:S(2)}) collective-permute-start(bf16[1,64,1152]{2,1,0:T(8,128)(2,1)S(1)} %collective-permute-done.7.refs_16_), channel_id=1, source_target_pairs={{0,8},{4,12},{8,0},{12,4},{16,24},{20,28},{24,16},{28,20},{1,9},{5... | collective-permute-start | bytes 442376 | tf_op jit(solution)/shard_map/ppermute | solution.py:15
  12.6 0.5 %collective-permute-start.11 = (bf16[1,64,1152]{2,1,0:T(8,128)(2,1)S(1)}, bf16[1,64,1152]{2,1,0:T(8,128)(2,1)S(1)}, u32[]{:S(2)}, u32[]{:S(2)}) collective-permute-start(bf16[1,64,1152]{2,1,0:T(8,128)(2,1)S(1)} %collective-permute-done.7.refs_16_), channel_id=1, source_target_pairs={{0,4},{4,0},{8,12},{12,8},{16,20},{20,16},{24,28},{28,24},{1,5},{5... | collective-permute-start | bytes 442376 | tf_op jit(solution)/shard_map/ppermute | solution.py:15
  13.2 0.1 collective-permute-start.12
  13.2 2.8 %collective-permute-done.2.refs_10_ = bf16[1,64,1152]{2,1,0:T(8,128)(2,1)S(1)} collective-permute-done((bf16[1,64,1152]{2,1,0:T(8,128)(2,1)S(1)}, bf16[1,64,1152]{2,1,0:T(8,128)(2,1)S(1)}, u32[]{:S(2)}, u32[]{:S(2)}) %collective-permute-start.2) | collective-permute-done | bytes 147488 | tf_op jit(solution)/shard_map/ppermute | solution.py:15
  16.0 1.1 %collective-permute-done.9.refs_18_ = bf16[1,64,1152]{2,1,0:T(8,128)(2,1)S(1)} collective-permute-done((bf16[1,64,1152]{2,1,0:T(8,128)(2,1)S(1)}, bf16[1,64,1152]{2,1,0:T(8,128)(2,1)S(1)}, u32[]{:S(2)}, u32[]{:S(2)}) %collective-permute-start.9) | collective-permute-done | bytes 147488 | tf_op jit(solution)/shard_map/ppermute | solution.py:15
  19.1 0.9 %copy-done = bf16[1,64,1152]{2,1,0:T(8,128)(2,1)S(1)} copy-done((bf16[1,64,1152]{2,1,0:T(8,128)(2,1)S(1)}, bf16[1,64,1152]{2,1,0:T(8,128)(2,1)}, u32[]{:S(2)}) %copy-start) | copy-done | bytes 147480
  20.0 0.9 %copy-done.1 = bf16[1,64,1152]{2,1,0:T(8,128)(2,1)S(1)} copy-done((bf16[1,64,1152]{2,1,0:T(8,128)(2,1)S(1)}, bf16[1,64,1152]{2,1,0:T(8,128)(2,1)}, u32[]{:S(2)}) %copy-start.1) | copy-done | bytes 147480
  20.9 11.6 %shard_map.120 = (bf16[1,64,1152]{2,1,0:T(8,128)(2,1)}, bf16[1,64,1152]{2,1,0:T(8,128)(2,1)}, f32[3,1152]{1,0:T(4,128)}) custom-call(f32[1]{0:T(128)S(6)} %copy.13.refs_0_, f32[1]{0:T(128)S(6)} %copy.14.refs_1_, f32[1]{0:T(128)S(6)} %copy.15.refs_2_, s32[1,8]{1,0:T(1,128)} %refs_3_.1, f32[1152]{0:T(1024)} %refs_4_.1, f32[1152]{0:T(1024)} %refs_5_.1, ...), custom_call_target="tpu_custom_call" | custom-call | tf_op jit(solution)/shard_map/pallas_call | solution.py:341
  32.5 1.6 %collective-permute-start.14 = (f32[3,1152]{1,0:T(4,128)}, f32[3,1152]{1,0:T(4,128)S(1)}, u32[]{:S(2)}, u32[]{:S(2)}) collective-permute-start(f32[3,1152]{1,0:T(4,128)} %get-tuple-element.9), channel_id=1, source_target_pairs={{0,1},{1,0},{2,3},{3,2},{4,5},{5,4},{6,7},{7,6},{8,9},{9,8},{10,11... | collective-permute-start | bytes 41480 | tf_op jit(solution)/shard_map/ppermute | solution.py:15
  34.1 2.4 %collective-permute-done.14 = f32[3,1152]{1,0:T(4,128)S(1)} collective-permute-done((f32[3,1152]{1,0:T(4,128)}, f32[3,1152]{1,0:T(4,128)S(1)}, u32[]{:S(2)}, u32[]{:S(2)}) %collective-permute-start.14) | collective-permute-done | bytes 13856 | tf_op jit(solution)/shard_map/ppermute | solution.py:15
  36.5 0.7 %add.6 = f32[3,1152]{1,0:T(4,128)S(1)} add(f32[3,1152]{1,0:T(4,128)} %get-tuple-element.9, f32[3,1152]{1,0:T(4,128)S(1)} %collective-permute-done.14) | non-fusion elementwise | flops 3456 | bytes 41472 | tf_op jit(solution)/shard_map/add | solution.py:69
  37.2 2.6 %collective-permute-start.15 = (f32[3,1152]{1,0:T(4,128)S(1)}, f32[3,1152]{1,0:T(4,128)S(1)}, u32[]{:S(2)}, u32[]{:S(2)}) collective-permute-start(f32[3,1152]{1,0:T(4,128)S(1)} %add.6), channel_id=1, source_target_pairs={{0,2},{1,3},{2,0},{3,1},{4,6},{5,7},{6,4},{7,5},{8,10},{9,11},{10,... | collective-permute-start | bytes 41480 | tf_op jit(solution)/shard_map/ppermute | solution.py:15
  39.8 1.2 %slice.11 = f32[1,1]{1,0:T(1,128)} slice(f32[3,1152]{1,0:T(4,128)} %get-tuple-element.9), slice={[2:3], [0:1]} | slice | bytes 8 | tf_op jit(solution)/shard_map/slice | solution.py:369
  41.0 0.9 %collective-permute-done.15 = f32[3,1152]{1,0:T(4,128)S(1)} collective-permute-done((f32[3,1152]{1,0:T(4,128)S(1)}, f32[3,1152]{1,0:T(4,128)S(1)}, u32[]{:S(2)}, u32[]{:S(2)}) %collective-permute-start.15) | collective-permute-done | bytes 13856 | tf_op jit(solution)/shard_map/ppermute | solution.py:15
  41.9 0.6 %slice_add_fusion = f32[2,1152]{1,0:T(2,128)} fusion(f32[3,1152]{1,0:T(4,128)S(1)} %collective-permute-done.15, f32[3,1152]{1,0:T(4,128)S(1)} %add.6), kind=kLoop, calls=%fused_computation | loop fusion | flops 2304 | bytes 27648 | tf_op jit(solution)/shard_map/add | solution.py:71
  (16 shorter events, 0.0 us)
Async XLA Ops:
  0.6 7.1 %collective-permute-start.1 = (bf16[1,64,1152]{2,1,0:T(8,128)(2,1)}, bf16[1,64,1152]{2,1,0:T(8,128)(2,1)S(1)}, u32[]{:S(2)}, u32[]{:S(2)}) collective-permute-start(bf16[1,64,1152]{2,1,0:T(8,128)(2,1)} %refs_7_.1), channel_id=1, source_target_pairs={{0,16},{4,20},{8,24},{12,28},{16,0},{20,4},{24,8},{28,12},{1,17},{... | collective-permute-start | bytes 442376 | tf_op jit(solution)/shard_map/ppermute | solution.py:15
  3.7 6.0 %collective-permute-start = (bf16[1,64,1152]{2,1,0:T(8,128)(2,1)}, bf16[1,64,1152]{2,1,0:T(8,128)(2,1)S(1)}, u32[]{:S(2)}, u32[]{:S(2)}) collective-permute-start(bf16[1,64,1152]{2,1,0:T(8,128)(2,1)} %refs_7_.1), channel_id=1, source_target_pairs={{0,8},{4,12},{8,0},{12,4},{16,24},{20,28},{24,16},{28,20},{1,9},{5... | collective-permute-start | bytes 442376 | tf_op jit(solution)/shard_map/ppermute | solution.py:15
  5.2 4.6 %collective-permute-start.3 = (bf16[1,64,1152]{2,1,0:T(8,128)(2,1)}, bf16[1,64,1152]{2,1,0:T(8,128)(2,1)S(1)}, u32[]{:S(2)}, u32[]{:S(2)}) collective-permute-start(bf16[1,64,1152]{2,1,0:T(8,128)(2,1)} %refs_7_.1), channel_id=1, source_target_pairs={{0,4},{4,0},{8,12},{12,8},{16,20},{20,16},{24,28},{28,24},{1,5},{5... | collective-permute-start | bytes 442376 | tf_op jit(solution)/shard_map/ppermute | solution.py:15
  5.2 6.5 %collective-permute-start.7 = (bf16[1,64,1152]{2,1,0:T(8,128)(2,1)}, bf16[1,64,1152]{2,1,0:T(8,128)(2,1)S(1)}, u32[]{:S(2)}, u32[]{:S(2)}) collective-permute-start(bf16[1,64,1152]{2,1,0:T(8,128)(2,1)} %refs_15_.1), channel_id=1, source_target_pairs={{0,16},{4,20},{8,24},{12,28},{16,0},{20,4},{24,8},{28,12},{1,17},{... | collective-permute-start | bytes 442376 | tf_op jit(solution)/shard_map/ppermute | solution.py:15
  5.7 6.9 %collective-permute-start.8 = (bf16[1,64,1152]{2,1,0:T(8,128)(2,1)}, bf16[1,64,1152]{2,1,0:T(8,128)(2,1)S(1)}, u32[]{:S(2)}, u32[]{:S(2)}) collective-permute-start(bf16[1,64,1152]{2,1,0:T(8,128)(2,1)} %refs_15_.1), channel_id=1, source_target_pairs={{0,8},{4,12},{8,0},{12,4},{16,24},{20,28},{24,16},{28,20},{1,9},{5... | collective-permute-start | bytes 442376 | tf_op jit(solution)/shard_map/ppermute | solution.py:15
  7.8 4.9 %collective-permute-start.10 = (bf16[1,64,1152]{2,1,0:T(8,128)(2,1)}, bf16[1,64,1152]{2,1,0:T(8,128)(2,1)S(1)}, u32[]{:S(2)}, u32[]{:S(2)}) collective-permute-start(bf16[1,64,1152]{2,1,0:T(8,128)(2,1)} %refs_15_.1), channel_id=1, source_target_pairs={{0,4},{4,0},{8,12},{12,8},{16,20},{20,16},{24,28},{28,24},{1,5},{5... | collective-permute-start | bytes 442376 | tf_op jit(solution)/shard_map/ppermute | solution.py:15
  9.7 3.4 %collective-permute-start.5 = (bf16[1,64,1152]{2,1,0:T(8,128)(2,1)S(1)}, bf16[1,64,1152]{2,1,0:T(8,128)(2,1)S(1)}, u32[]{:S(2)}, u32[]{:S(2)}) collective-permute-start(bf16[1,64,1152]{2,1,0:T(8,128)(2,1)S(1)} %collective-permute-done.1.refs_9_), channel_id=1, source_target_pairs={{0,4},{4,0},{8,12},{12,8},{16,20},{20,16},{24,28},{28,24},{1,5},{5... | collective-permute-start | bytes 442376 | tf_op jit(solution)/shard_map/ppermute | solution.py:15
  9.7 6.3 %collective-permute-start.2 = (bf16[1,64,1152]{2,1,0:T(8,128)(2,1)S(1)}, bf16[1,64,1152]{2,1,0:T(8,128)(2,1)S(1)}, u32[]{:S(2)}, u32[]{:S(2)}) collective-permute-start(bf16[1,64,1152]{2,1,0:T(8,128)(2,1)S(1)} %collective-permute-done.refs_8_), channel_id=1, source_target_pairs={{0,16},{4,20},{8,24},{12,28},{16,0},{20,4},{24,8},{28,12},{1,17},{... | collective-permute-start | bytes 442376 | tf_op jit(solution)/shard_map/ppermute | solution.py:15
  11.7 5.4 %collective-permute-start.9 = (bf16[1,64,1152]{2,1,0:T(8,128)(2,1)S(1)}, bf16[1,64,1152]{2,1,0:T(8,128)(2,1)S(1)}, u32[]{:S(2)}, u32[]{:S(2)}) collective-permute-start(bf16[1,64,1152]{2,1,0:T(8,128)(2,1)S(1)} %collective-permute-done.7.refs_16_), channel_id=1, source_target_pairs={{0,8},{4,12},{8,0},{12,4},{16,24},{20,28},{24,16},{28,20},{1,9},{5... | collective-permute-start | bytes 442376 | tf_op jit(solution)/shard_map/ppermute | solution.py:15
  12.6 6.4 %collective-permute-start.4 = (bf16[1,64,1152]{2,1,0:T(8,128)(2,1)S(1)}, bf16[1,64,1152]{2,1,0:T(8,128)(2,1)S(1)}, u32[]{:S(2)}, u32[]{:S(2)}) collective-permute-start(bf16[1,64,1152]{2,1,0:T(8,128)(2,1)S(1)} %collective-permute-done.refs_8_), channel_id=1, source_target_pairs={{0,4},{4,0},{8,12},{12,8},{16,20},{20,16},{24,28},{28,24},{1,5},{5... | collective-permute-start | bytes 442376 | tf_op jit(solution)/shard_map/ppermute | solution.py:15
  12.6 6.4 %collective-permute-start.11 = (bf16[1,64,1152]{2,1,0:T(8,128)(2,1)S(1)}, bf16[1,64,1152]{2,1,0:T(8,128)(2,1)S(1)}, u32[]{:S(2)}, u32[]{:S(2)}) collective-permute-start(bf16[1,64,1152]{2,1,0:T(8,128)(2,1)S(1)} %collective-permute-done.7.refs_16_), channel_id=1, source_target_pairs={{0,4},{4,0},{8,12},{12,8},{16,20},{20,16},{24,28},{28,24},{1,5},{5... | collective-permute-start | bytes 442376 | tf_op jit(solution)/shard_map/ppermute | solution.py:15
  13.2 5.9 %collective-permute-start.12 = (bf16[1,64,1152]{2,1,0:T(8,128)(2,1)S(1)}, bf16[1,64,1152]{2,1,0:T(8,128)(2,1)S(1)}, u32[]{:S(2)}, u32[]{:S(2)}) collective-permute-start(bf16[1,64,1152]{2,1,0:T(8,128)(2,1)S(1)} %collective-permute-done.8.refs_17_), channel_id=1, source_target_pairs={{0,4},{4,0},{8,12},{12,8},{16,20},{20,16},{24,28},{28,24},{1,5},{5... | collective-permute-start | bytes 442376 | tf_op jit(solution)/shard_map/ppermute | solution.py:15
  16.0 3.0 %collective-permute-start.6 = (bf16[1,64,1152]{2,1,0:T(8,128)(2,1)S(1)}, bf16[1,64,1152]{2,1,0:T(8,128)(2,1)S(1)}, u32[]{:S(2)}, u32[]{:S(2)}) collective-permute-start(bf16[1,64,1152]{2,1,0:T(8,128)(2,1)S(1)} %collective-permute-done.2.refs_10_), channel_id=1, source_target_pairs={{0,4},{4,0},{8,12},{12,8},{16,20},{20,16},{24,28},{28,24},{1,5},{5... | collective-permute-start | bytes 442376 | tf_op jit(solution)/shard_map/ppermute | solution.py:15
  17.1 2.0 %collective-permute-start.13 = (bf16[1,64,1152]{2,1,0:T(8,128)(2,1)S(1)}, bf16[1,64,1152]{2,1,0:T(8,128)(2,1)S(1)}, u32[]{:S(2)}, u32[]{:S(2)}) collective-permute-start(bf16[1,64,1152]{2,1,0:T(8,128)(2,1)S(1)} %collective-permute-done.9.refs_18_), channel_id=1, source_target_pairs={{0,4},{4,0},{8,12},{12,8},{16,20},{20,16},{24,28},{28,24},{1,5},{5... | collective-permute-start | bytes 442376 | tf_op jit(solution)/shard_map/ppermute | solution.py:15
  19.1 0.9 %copy-start = (bf16[1,64,1152]{2,1,0:T(8,128)(2,1)S(1)}, bf16[1,64,1152]{2,1,0:T(8,128)(2,1)}, u32[]{:S(2)}) copy-start(bf16[1,64,1152]{2,1,0:T(8,128)(2,1)} %refs_7_.1) | copy-start | bytes 442372
  20.0 0.9 %copy-start.1 = (bf16[1,64,1152]{2,1,0:T(8,128)(2,1)S(1)}, bf16[1,64,1152]{2,1,0:T(8,128)(2,1)}, u32[]{:S(2)}) copy-start(bf16[1,64,1152]{2,1,0:T(8,128)(2,1)} %refs_15_.1) | copy-start | bytes 442372
  32.5 4.0 %collective-permute-start.14 = (f32[3,1152]{1,0:T(4,128)}, f32[3,1152]{1,0:T(4,128)S(1)}, u32[]{:S(2)}, u32[]{:S(2)}) collective-permute-start(f32[3,1152]{1,0:T(4,128)} %get-tuple-element.9), channel_id=1, source_target_pairs={{0,1},{1,0},{2,3},{3,2},{4,5},{5,4},{6,7},{7,6},{8,9},{9,8},{10,11... | collective-permute-start | bytes 41480 | tf_op jit(solution)/shard_map/ppermute | solution.py:15
  37.2 4.7 %collective-permute-start.15 = (f32[3,1152]{1,0:T(4,128)S(1)}, f32[3,1152]{1,0:T(4,128)S(1)}, u32[]{:S(2)}, u32[]{:S(2)}) collective-permute-start(f32[3,1152]{1,0:T(4,128)S(1)} %add.6), channel_id=1, source_target_pairs={{0,2},{1,3},{2,0},{3,1},{4,6},{5,7},{6,4},{7,5},{8,10},{9,11},{10,... | collective-permute-start | bytes 41480 | tf_op jit(solution)/shard_map/ppermute | solution.py:15

commit v15 on v14

--- a/solution.py
+++ b/solution.py
@@ -204,8 +204,8 @@
     (image_grad_ref, text_grad_ref, sums_ref, raw_ref, unit_ref, short_ref, normed_ref, inverse_ref,
      length_ref, weights_ref, tangent_ref, copy_sems) = refs[7 + 2 * count :]
     block_rows = pieces[0].shape[1]
-    group_rows = raw_ref.shape[1]
-    width = raw_ref.shape[2]
+    group_rows = count * block_rows
+    width = pieces[0].shape[2]
     own_block = lax.axis_index("blk")
 
     def block_of(mask):
@@ -215,14 +215,6 @@
                 block = block + (1 - 2 * (own_block // (1 << bit) % 2)) * (1 << bit)
         return block
 
-    arrivals = []
-    for position, source in enumerate(pieces):
-        tower, slot = divmod(position, count)
-        masks = image_masks if tower == 0 else text_masks
-        rows = pl.ds(pl.multiple_of(block_of(masks[slot]) * block_rows, block_rows), block_rows)
-        arrival = pltpu.make_async_copy(source.at[0], raw_ref.at[tower, rows, :], copy_sems.at[position])
-        arrival.start()
-        arrivals.append(arrival)
 
     blocks = counts_ref.shape[1]
     total = counts_ref[0, 0]
@@ -247,14 +239,14 @@
         jnp.where(natural == image_row, partner_ref[...].astype(jnp.float32), 0.0), axis=1, keepdims=True
     ).astype(jnp.int32)
 
-    for arrival in arrivals:
-        arrival.wait()
     gains = (picture_gain_ref[...][None, :], caption_gain_ref[...][None, :])
     chunk = min(128, group_rows)
-    for tower in range(2):
-        for first in range(0, group_rows, chunk):
-            rows = pl.ds(first, chunk)
-            values = raw_ref[tower, rows, :].astype(jnp.float32)
+    for position, source in enumerate(pieces):
+        tower, slot = divmod(position, count)
+        masks = image_masks if tower == 0 else text_masks
+        rows = pl.ds(pl.multiple_of(block_of(masks[slot]) * block_rows, block_rows), block_rows)
+        if source is not None:
+            values = source[0].astype(jnp.float32)
             centred = values - jnp.mean(values, axis=-1, keepdims=True)
             inverse = lax.rsqrt(jnp.mean(centred * centred, axis=-1, keepdims=True) + epsilon)
             normed = centred * inverse
@@ -343,7 +335,7 @@
         out_shape=(grad_shape, grad_shape, jax.ShapeDtypeStruct((3, width), jnp.float32)),
         in_specs=[pl.BlockSpec(memory_space=smem)] * 4
         + [pl.BlockSpec(memory_space=vmem)] * 3
-        + [pl.BlockSpec(memory_space=pl.ANY)] * len(pieces),
+        + [pl.BlockSpec(memory_space=vmem)] * len(pieces),
         out_specs=(pl.BlockSpec(memory_space=vmem),) * 3,
         scratch_shapes=[
             pltpu.VMEM(full, jnp.bfloat16),

time: 42.8 us -> 40.3 us (0.942)
  Pallas kernels: 11.6 us -> 9.11 us
    pallas_call x1, Pallas kernels: 11.6 us -> 9.11 us  [whole_group(): pl.pallas_call(functools.partial(group_kernel, tuple(masks[:count]), tupl...]
where the time goes in v15:
time: 40.3 us; the launch traced here: 40 us
  waiting for transfers between devices  12.2 us (30%)
  starting transfers between devices  11.7 us (29%)
  Pallas kernels  9.11 us (23%)
  local copies, waits for them, and re-layouts  3 us (7%)
  between operations  2.65 us (7%)
  other arithmetic  1.33 us (3%)
    ppermute x16, waiting for transfers between devices, xor_swap(): lax.ppermute(value, axis, [(source, source ^ bit) for source in range(cou...  12.2 us
    ppermute x16, starting transfers between devices, xor_swap(): lax.ppermute(value, axis, [(source, source ^ bit) for source in range(cou...  11.7 us
    pallas_call x1, Pallas kernels, whole_group(): pl.pallas_call(functools.partial(group_kernel, tuple(masks[:count]), tupl...  9.11 us
    unnamed x4, local copies, waits for them, and re-layouts  1.81 us
    slice x1, local copies, waits for them, and re-layouts, whole_group(): group_loss = sums[2, 0:1]  1.19 us
  transfers between devices with their start and end apart: 16, of which 7 were waited for; matrix products, arithmetic and copies ran while one was open for 3% of the time, Pallas kernels for 0%

profile of v15, /device:TPU:0, one launch (start us, length us, event | category | flops | bytes accessed | tf_op | source)
XLA Modules:
  0.0 40.0 jit_solution(10101260886314946308)
XLA Ops:
  0.6 3.1 %collective-permute-start.1 = (bf16[1,64,1152]{2,1,0:T(8,128)(2,1)}, bf16[1,64,1152]{2,1,0:T(8,128)(2,1)S(1)}, u32[]{:S(2)}, u32[]{:S(2)}) collective-permute-start(bf16[1,64,1152]{2,1,0:T(8,128)(2,1)} %refs_7_.1), channel_id=1, source_target_pairs={{0,16},{4,20},{8,24},{12,28},{16,0},{20,4},{24,8},{28,12},{1,17},{... | collective-permute-start | bytes 442376 | tf_op jit(solution)/shard_map/ppermute | solution.py:15
  3.7 1.5 %collective-permute-start = (bf16[1,64,1152]{2,1,0:T(8,128)(2,1)}, bf16[1,64,1152]{2,1,0:T(8,128)(2,1)S(1)}, u32[]{:S(2)}, u32[]{:S(2)}) collective-permute-start(bf16[1,64,1152]{2,1,0:T(8,128)(2,1)} %refs_7_.1), channel_id=1, source_target_pairs={{0,8},{4,12},{8,0},{12,4},{16,24},{20,28},{24,16},{28,20},{1,9},{5... | collective-permute-start | bytes 442376 | tf_op jit(solution)/shard_map/ppermute | solution.py:15
  5.2 0.5 %collective-permute-start.7 = (bf16[1,64,1152]{2,1,0:T(8,128)(2,1)}, bf16[1,64,1152]{2,1,0:T(8,128)(2,1)S(1)}, u32[]{:S(2)}, u32[]{:S(2)}) collective-permute-start(bf16[1,64,1152]{2,1,0:T(8,128)(2,1)} %refs_15_.1), channel_id=1, source_target_pairs={{0,16},{4,20},{8,24},{12,28},{16,0},{20,4},{24,8},{28,12},{1,17},{... | collective-permute-start | bytes 442376 | tf_op jit(solution)/shard_map/ppermute | solution.py:15
  5.7 0.1 collective-permute-start.8
  5.8 1.9 %collective-permute-done.1.refs_9_ = bf16[1,64,1152]{2,1,0:T(8,128)(2,1)S(1)} collective-permute-done((bf16[1,64,1152]{2,1,0:T(8,128)(2,1)}, bf16[1,64,1152]{2,1,0:T(8,128)(2,1)S(1)}, u32[]{:S(2)}, u32[]{:S(2)}) %collective-permute-start.1) | collective-permute-done | bytes 147488 | tf_op jit(solution)/shard_map/ppermute | solution.py:15
  7.8 0.0 collective-permute-start.10
  7.8 2.0 %collective-permute-done.refs_8_ = bf16[1,64,1152]{2,1,0:T(8,128)(2,1)S(1)} collective-permute-done((bf16[1,64,1152]{2,1,0:T(8,128)(2,1)}, bf16[1,64,1152]{2,1,0:T(8,128)(2,1)S(1)}, u32[]{:S(2)}, u32[]{:S(2)}) %collective-permute-start) | collective-permute-done | bytes 147488 | tf_op jit(solution)/shard_map/ppermute | solution.py:15
  9.7 0.7 %collective-permute-start.2 = (bf16[1,64,1152]{2,1,0:T(8,128)(2,1)S(1)}, bf16[1,64,1152]{2,1,0:T(8,128)(2,1)S(1)}, u32[]{:S(2)}, u32[]{:S(2)}) collective-permute-start(bf16[1,64,1152]{2,1,0:T(8,128)(2,1)S(1)} %collective-permute-done.refs_8_), channel_id=1, source_target_pairs={{0,16},{4,20},{8,24},{12,28},{16,0},{20,4},{24,8},{28,12},{1,17},{... | collective-permute-start | bytes 442376 | tf_op jit(solution)/shard_map/ppermute | solution.py:15
  10.5 1.2 %collective-permute-done.7.refs_16_ = bf16[1,64,1152]{2,1,0:T(8,128)(2,1)S(1)} collective-permute-done((bf16[1,64,1152]{2,1,0:T(8,128)(2,1)}, bf16[1,64,1152]{2,1,0:T(8,128)(2,1)S(1)}, u32[]{:S(2)}, u32[]{:S(2)}) %collective-permute-start.7) | collective-permute-done | bytes 147488 | tf_op jit(solution)/shard_map/ppermute | solution.py:15
  11.7 1.0 %collective-permute-start.9 = (bf16[1,64,1152]{2,1,0:T(8,128)(2,1)S(1)}, bf16[1,64,1152]{2,1,0:T(8,128)(2,1)S(1)}, u32[]{:S(2)}, u32[]{:S(2)}) collective-permute-start(bf16[1,64,1152]{2,1,0:T(8,128)(2,1)S(1)} %collective-permute-done.7.refs_16_), channel_id=1, source_target_pairs={{0,8},{4,12},{8,0},{12,4},{16,24},{20,28},{24,16},{28,20},{1,9},{5... | collective-permute-start | bytes 442376 | tf_op jit(solution)/shard_map/ppermute | solution.py:15
  12.6 0.5 %collective-permute-start.11 = (bf16[1,64,1152]{2,1,0:T(8,128)(2,1)S(1)}, bf16[1,64,1152]{2,1,0:T(8,128)(2,1)S(1)}, u32[]{:S(2)}, u32[]{:S(2)}) collective-permute-start(bf16[1,64,1152]{2,1,0:T(8,128)(2,1)S(1)} %collective-permute-done.7.refs_16_), channel_id=1, source_target_pairs={{0,4},{4,0},{8,12},{12,8},{16,20},{20,16},{24,28},{28,24},{1,5},{5... | collective-permute-start | bytes 442376 | tf_op jit(solution)/shard_map/ppermute | solution.py:15
  13.2 0.1 collective-permute-start.12
  13.2 2.8 %collective-permute-done.2.refs_10_ = bf16[1,64,1152]{2,1,0:T(8,128)(2,1)S(1)} collective-permute-done((bf16[1,64,1152]{2,1,0:T(8,128)(2,1)S(1)}, bf16[1,64,1152]{2,1,0:T(8,128)(2,1)S(1)}, u32[]{:S(2)}, u32[]{:S(2)}) %collective-permute-start.2) | collective-permute-done | bytes 147488 | tf_op jit(solution)/shard_map/ppermute | solution.py:15
  16.0 1.1 %collective-permute-done.9.refs_18_ = bf16[1,64,1152]{2,1,0:T(8,128)(2,1)S(1)} collective-permute-done((bf16[1,64,1152]{2,1,0:T(8,128)(2,1)S(1)}, bf16[1,64,1152]{2,1,0:T(8,128)(2,1)S(1)}, u32[]{:S(2)}, u32[]{:S(2)}) %collective-permute-start.9) | collective-permute-done | bytes 147488 | tf_op jit(solution)/shard_map/ppermute | solution.py:15
  19.1 0.9 %copy-done = bf16[1,64,1152]{2,1,0:T(8,128)(2,1)S(1)} copy-done((bf16[1,64,1152]{2,1,0:T(8,128)(2,1)S(1)}, bf16[1,64,1152]{2,1,0:T(8,128)(2,1)}, u32[]{:S(2)}) %copy-start) | copy-done | bytes 147480
  20.0 0.9 %copy-done.1 = bf16[1,64,1152]{2,1,0:T(8,128)(2,1)S(1)} copy-done((bf16[1,64,1152]{2,1,0:T(8,128)(2,1)S(1)}, bf16[1,64,1152]{2,1,0:T(8,128)(2,1)}, u32[]{:S(2)}) %copy-start.1) | copy-done | bytes 147480
  20.9 9.1 %shard_map.120 = (bf16[1,64,1152]{2,1,0:T(8,128)(2,1)}, bf16[1,64,1152]{2,1,0:T(8,128)(2,1)}, f32[3,1152]{1,0:T(4,128)}) custom-call(f32[1]{0:T(128)S(6)} %copy.13.refs_0_, f32[1]{0:T(128)S(6)} %copy.14.refs_1_, f32[1]{0:T(128)S(6)} %copy.15.refs_2_, s32[1,8]{1,0:T(1,128)} %refs_3_.1, f32[1152]{0:T(1024)} %refs_4_.1, f32[1152]{0:T(1024)} %refs_5_.1, ...), custom_call_target="tpu_custom_call" | custom-call | tf_op jit(solution)/shard_map/pallas_call | solution.py:333
  30.0 1.6 %collective-permute-start.14 = (f32[3,1152]{1,0:T(4,128)}, f32[3,1152]{1,0:T(4,128)S(1)}, u32[]{:S(2)}, u32[]{:S(2)}) collective-permute-start(f32[3,1152]{1,0:T(4,128)} %get-tuple-element.9), channel_id=1, source_target_pairs={{0,1},{1,0},{2,3},{3,2},{4,5},{5,4},{6,7},{7,6},{8,9},{9,8},{10,11... | collective-permute-start | bytes 41480 | tf_op jit(solution)/shard_map/ppermute | solution.py:15
  31.6 2.4 %collective-permute-done.14 = f32[3,1152]{1,0:T(4,128)S(1)} collective-permute-done((f32[3,1152]{1,0:T(4,128)}, f32[3,1152]{1,0:T(4,128)S(1)}, u32[]{:S(2)}, u32[]{:S(2)}) %collective-permute-start.14) | collective-permute-done | bytes 13856 | tf_op jit(solution)/shard_map/ppermute | solution.py:15
  34.0 0.7 %add.6 = f32[3,1152]{1,0:T(4,128)S(1)} add(f32[3,1152]{1,0:T(4,128)} %get-tuple-element.9, f32[3,1152]{1,0:T(4,128)S(1)} %collective-permute-done.14) | non-fusion elementwise | flops 3456 | bytes 41472 | tf_op jit(solution)/shard_map/add | solution.py:69
  34.8 2.6 %collective-permute-start.15 = (f32[3,1152]{1,0:T(4,128)S(1)}, f32[3,1152]{1,0:T(4,128)S(1)}, u32[]{:S(2)}, u32[]{:S(2)}) collective-permute-start(f32[3,1152]{1,0:T(4,128)S(1)} %add.6), channel_id=1, source_target_pairs={{0,2},{1,3},{2,0},{3,1},{4,6},{5,7},{6,4},{7,5},{8,10},{9,11},{10,... | collective-permute-start | bytes 41480 | tf_op jit(solution)/shard_map/ppermute | solution.py:15
  37.4 1.2 %slice.11 = f32[1,1]{1,0:T(1,128)} slice(f32[3,1152]{1,0:T(4,128)} %get-tuple-element.9), slice={[2:3], [0:1]} | slice | bytes 8 | tf_op jit(solution)/shard_map/slice | solution.py:361
  38.6 0.9 %collective-permute-done.15 = f32[3,1152]{1,0:T(4,128)S(1)} collective-permute-done((f32[3,1152]{1,0:T(4,128)S(1)}, f32[3,1152]{1,0:T(4,128)S(1)}, u32[]{:S(2)}, u32[]{:S(2)}) %collective-permute-start.15) | collective-permute-done | bytes 13856 | tf_op jit(solution)/shard_map/ppermute | solution.py:15
  39.4 0.6 %slice_add_fusion = f32[2,1152]{1,0:T(2,128)} fusion(f32[3,1152]{1,0:T(4,128)S(1)} %collective-permute-done.15, f32[3,1152]{1,0:T(4,128)S(1)} %add.6), kind=kLoop, calls=%fused_computation | loop fusion | flops 2304 | bytes 27648 | tf_op jit(solution)/shard_map/add | solution.py:71
  (16 shorter events, 0.0 us)
Async XLA Ops:
  0.6 7.1 %collective-permute-start.1 = (bf16[1,64,1152]{2,1,0:T(8,128)(2,1)}, bf16[1,64,1152]{2,1,0:T(8,128)(2,1)S(1)}, u32[]{:S(2)}, u32[]{:S(2)}) collective-permute-start(bf16[1,64,1152]{2,1,0:T(8,128)(2,1)} %refs_7_.1), channel_id=1, source_target_pairs={{0,16},{4,20},{8,24},{12,28},{16,0},{20,4},{24,8},{28,12},{1,17},{... | collective-permute-start | bytes 442376 | tf_op jit(solution)/shard_map/ppermute | solution.py:15
  3.7 6.0 %collective-permute-start = (bf16[1,64,1152]{2,1,0:T(8,128)(2,1)}, bf16[1,64,1152]{2,1,0:T(8,128)(2,1)S(1)}, u32[]{:S(2)}, u32[]{:S(2)}) collective-permute-start(bf16[1,64,1152]{2,1,0:T(8,128)(2,1)} %refs_7_.1), channel_id=1, source_target_pairs={{0,8},{4,12},{8,0},{12,4},{16,24},{20,28},{24,16},{28,20},{1,9},{5... | collective-permute-start | bytes 442376 | tf_op jit(solution)/shard_map/ppermute | solution.py:15
  5.2 4.6 %collective-permute-start.3 = (bf16[1,64,1152]{2,1,0:T(8,128)(2,1)}, bf16[1,64,1152]{2,1,0:T(8,128)(2,1)S(1)}, u32[]{:S(2)}, u32[]{:S(2)}) collective-permute-start(bf16[1,64,1152]{2,1,0:T(8,128)(2,1)} %refs_7_.1), channel_id=1, source_target_pairs={{0,4},{4,0},{8,12},{12,8},{16,20},{20,16},{24,28},{28,24},{1,5},{5... | collective-permute-start | bytes 442376 | tf_op jit(solution)/shard_map/ppermute | solution.py:15
  5.2 6.5 %collective-permute-start.7 = (bf16[1,64,1152]{2,1,0:T(8,128)(2,1)}, bf16[1,64,1152]{2,1,0:T(8,128)(2,1)S(1)}, u32[]{:S(2)}, u32[]{:S(2)}) collective-permute-start(bf16[1,64,1152]{2,1,0:T(8,128)(2,1)} %refs_15_.1), channel_id=1, source_target_pairs={{0,16},{4,20},{8,24},{12,28},{16,0},{20,4},{24,8},{28,12},{1,17},{... | collective-permute-start | bytes 442376 | tf_op jit(solution)/shard_map/ppermute | solution.py:15
  5.7 6.9 %collective-permute-start.8 = (bf16[1,64,1152]{2,1,0:T(8,128)(2,1)}, bf16[1,64,1152]{2,1,0:T(8,128)(2,1)S(1)}, u32[]{:S(2)}, u32[]{:S(2)}) collective-permute-start(bf16[1,64,1152]{2,1,0:T(8,128)(2,1)} %refs_15_.1), channel_id=1, source_target_pairs={{0,8},{4,12},{8,0},{12,4},{16,24},{20,28},{24,16},{28,20},{1,9},{5... | collective-permute-start | bytes 442376 | tf_op jit(solution)/shard_map/ppermute | solution.py:15
  7.8 4.9 %collective-permute-start.10 = (bf16[1,64,1152]{2,1,0:T(8,128)(2,1)}, bf16[1,64,1152]{2,1,0:T(8,128)(2,1)S(1)}, u32[]{:S(2)}, u32[]{:S(2)}) collective-permute-start(bf16[1,64,1152]{2,1,0:T(8,128)(2,1)} %refs_15_.1), channel_id=1, source_target_pairs={{0,4},{4,0},{8,12},{12,8},{16,20},{20,16},{24,28},{28,24},{1,5},{5... | collective-permute-start | bytes 442376 | tf_op jit(solution)/shard_map/ppermute | solution.py:15
  9.7 3.4 %collective-permute-start.5 = (bf16[1,64,1152]{2,1,0:T(8,128)(2,1)S(1)}, bf16[1,64,1152]{2,1,0:T(8,128)(2,1)S(1)}, u32[]{:S(2)}, u32[]{:S(2)}) collective-permute-start(bf16[1,64,1152]{2,1,0:T(8,128)(2,1)S(1)} %collective-permute-done.1.refs_9_), channel_id=1, source_target_pairs={{0,4},{4,0},{8,12},{12,8},{16,20},{20,16},{24,28},{28,24},{1,5},{5... | collective-permute-start | bytes 442376 | tf_op jit(solution)/shard_map/ppermute | solution.py:15
  9.7 6.3 %collective-permute-start.2 = (bf16[1,64,1152]{2,1,0:T(8,128)(2,1)S(1)}, bf16[1,64,1152]{2,1,0:T(8,128)(2,1)S(1)}, u32[]{:S(2)}, u32[]{:S(2)}) collective-permute-start(bf16[1,64,1152]{2,1,0:T(8,128)(2,1)S(1)} %collective-permute-done.refs_8_), channel_id=1, source_target_pairs={{0,16},{4,20},{8,24},{12,28},{16,0},{20,4},{24,8},{28,12},{1,17},{... | collective-permute-start | bytes 442376 | tf_op jit(solution)/shard_map/ppermute | solution.py:15
  11.7 5.4 %collective-permute-start.9 = (bf16[1,64,1152]{2,1,0:T(8,128)(2,1)S(1)}, bf16[1,64,1152]{2,1,0:T(8,128)(2,1)S(1)}, u32[]{:S(2)}, u32[]{:S(2)}) collective-permute-start(bf16[1,64,1152]{2,1,0:T(8,128)(2,1)S(1)} %collective-permute-done.7.refs_16_), channel_id=1, source_target_pairs={{0,8},{4,12},{8,0},{12,4},{16,24},{20,28},{24,16},{28,20},{1,9},{5... | collective-permute-start | bytes 442376 | tf_op jit(solution)/shard_map/ppermute | solution.py:15
  12.6 6.4 %collective-permute-start.4 = (bf16[1,64,1152]{2,1,0:T(8,128)(2,1)S(1)}, bf16[1,64,1152]{2,1,0:T(8,128)(2,1)S(1)}, u32[]{:S(2)}, u32[]{:S(2)}) collective-permute-start(bf16[1,64,1152]{2,1,0:T(8,128)(2,1)S(1)} %collective-permute-done.refs_8_), channel_id=1, source_target_pairs={{0,4},{4,0},{8,12},{12,8},{16,20},{20,16},{24,28},{28,24},{1,5},{5... | collective-permute-start | bytes 442376 | tf_op jit(solution)/shard_map/ppermute | solution.py:15
  12.6 6.4 %collective-permute-start.11 = (bf16[1,64,1152]{2,1,0:T(8,128)(2,1)S(1)}, bf16[1,64,1152]{2,1,0:T(8,128)(2,1)S(1)}, u32[]{:S(2)}, u32[]{:S(2)}) collective-permute-start(bf16[1,64,1152]{2,1,0:T(8,128)(2,1)S(1)} %collective-permute-done.7.refs_16_), channel_id=1, source_target_pairs={{0,4},{4,0},{8,12},{12,8},{16,20},{20,16},{24,28},{28,24},{1,5},{5... | collective-permute-start | bytes 442376 | tf_op jit(solution)/shard_map/ppermute | solution.py:15
  13.2 5.9 %collective-permute-start.12 = (bf16[1,64,1152]{2,1,0:T(8,128)(2,1)S(1)}, bf16[1,64,1152]{2,1,0:T(8,128)(2,1)S(1)}, u32[]{:S(2)}, u32[]{:S(2)}) collective-permute-start(bf16[1,64,1152]{2,1,0:T(8,128)(2,1)S(1)} %collective-permute-done.8.refs_17_), channel_id=1, source_target_pairs={{0,4},{4,0},{8,12},{12,8},{16,20},{20,16},{24,28},{28,24},{1,5},{5... | collective-permute-start | bytes 442376 | tf_op jit(solution)/shard_map/ppermute | solution.py:15
  16.0 3.0 %collective-permute-start.6 = (bf16[1,64,1152]{2,1,0:T(8,128)(2,1)S(1)}, bf16[1,64,1152]{2,1,0:T(8,128)(2,1)S(1)}, u32[]{:S(2)}, u32[]{:S(2)}) collective-permute-start(bf16[1,64,1152]{2,1,0:T(8,128)(2,1)S(1)} %collective-permute-done.2.refs_10_), channel_id=1, source_target_pairs={{0,4},{4,0},{8,12},{12,8},{16,20},{20,16},{24,28},{28,24},{1,5},{5... | collective-permute-start | bytes 442376 | tf_op jit(solution)/shard_map/ppermute | solution.py:15
  17.1 2.0 %collective-permute-start.13 = (bf16[1,64,1152]{2,1,0:T(8,128)(2,1)S(1)}, bf16[1,64,1152]{2,1,0:T(8,128)(2,1)S(1)}, u32[]{:S(2)}, u32[]{:S(2)}) collective-permute-start(bf16[1,64,1152]{2,1,0:T(8,128)(2,1)S(1)} %collective-permute-done.9.refs_18_), channel_id=1, source_target_pairs={{0,4},{4,0},{8,12},{12,8},{16,20},{20,16},{24,28},{28,24},{1,5},{5... | collective-permute-start | bytes 442376 | tf_op jit(solution)/shard_map/ppermute | solution.py:15
  19.1 0.9 %copy-start = (bf16[1,64,1152]{2,1,0:T(8,128)(2,1)S(1)}, bf16[1,64,1152]{2,1,0:T(8,128)(2,1)}, u32[]{:S(2)}) copy-start(bf16[1,64,1152]{2,1,0:T(8,128)(2,1)} %refs_7_.1) | copy-start | bytes 442372
  20.0 0.9 %copy-start.1 = (bf16[1,64,1152]{2,1,0:T(8,128)(2,1)S(1)}, bf16[1,64,1152]{2,1,0:T(8,128)(2,1)}, u32[]{:S(2)}) copy-start(bf16[1,64,1152]{2,1,0:T(8,128)(2,1)} %refs_15_.1) | copy-start | bytes 442372
  30.0 4.0 %collective-permute-start.14 = (f32[3,1152]{1,0:T(4,128)}, f32[3,1152]{1,0:T(4,128)S(1)}, u32[]{:S(2)}, u32[]{:S(2)}) collective-permute-start(f32[3,1152]{1,0:T(4,128)} %get-tuple-element.9), channel_id=1, source_target_pairs={{0,1},{1,0},{2,3},{3,2},{4,5},{5,4},{6,7},{7,6},{8,9},{9,8},{10,11... | collective-permute-start | bytes 41480 | tf_op jit(solution)/shard_map/ppermute | solution.py:15
  34.8 4.7 %collective-permute-start.15 = (f32[3,1152]{1,0:T(4,128)S(1)}, f32[3,1152]{1,0:T(4,128)S(1)}, u32[]{:S(2)}, u32[]{:S(2)}) collective-permute-start(f32[3,1152]{1,0:T(4,128)S(1)} %add.6), channel_id=1, source_target_pairs={{0,2},{1,3},{2,0},{3,1},{4,6},{5,7},{6,4},{7,5},{8,10},{9,11},{10,... | collective-permute-start | bytes 41480 | tf_op jit(solution)/shard_map/ppermute | solution.py:15

commit v16 on v15

--- a/solution.py
+++ b/solution.py
@@ -356,7 +356,7 @@
         picture_rescale_factor,
         caption_rescale_factor,
         matching_caption_index,
-        *[pltpu.with_memory_space_constraint(piece, pltpu.VMEM) for piece in pieces],
+        *[piece if slot % count == 0 else pltpu.with_memory_space_constraint(piece, pltpu.VMEM) for slot, piece in enumerate(pieces)],
     )
     group_loss = sums[2, 0:1]
     gain_grads = all_sum(sums, "rep", keep=2)

time: 40.3 us -> 38.7 us (0.960)
  local copies, waits for them, and re-layouts: 3 us -> 1.18 us
    unnamed x4 -> x0, local copies, waits for them, and re-layouts: 1.81 us -> none
where the time goes in v16:
time: 38.7 us; the launch traced here: 38.5 us
  waiting for transfers between devices  12.2 us (32%)
  starting transfers between devices  11.7 us (30%)
  Pallas kernels  9.35 us (24%)
  between operations  2.64 us (7%)
  other arithmetic  1.33 us (3%)
  local copies, waits for them, and re-layouts  1.18 us (3%)
    ppermute x16, waiting for transfers between devices, xor_swap(): lax.ppermute(value, axis, [(source, source ^ bit) for source in range(cou...  12.2 us
    ppermute x16, starting transfers between devices, xor_swap(): lax.ppermute(value, axis, [(source, source ^ bit) for source in range(cou...  11.7 us
    pallas_call x1, Pallas kernels, whole_group(): pl.pallas_call(functools.partial(group_kernel, tuple(masks[:count]), tupl...  9.35 us
    slice x1, local copies, waits for them, and re-layouts, whole_group(): group_loss = sums[2, 0:1]  1.18 us
  transfers between devices with their start and end apart: 16, of which 7 were waited for; matrix products, arithmetic and copies ran while one was open for 3% of the time, Pallas kernels for 0%

profile of v16, /device:TPU:0, one launch (start us, length us, event | category | flops | bytes accessed | tf_op | source)
XLA Modules:
  0.0 38.5 jit_solution(14534092063139848047)
XLA Ops:
  0.6 3.1 %collective-permute-start.1 = (bf16[1,64,1152]{2,1,0:T(8,128)(2,1)}, bf16[1,64,1152]{2,1,0:T(8,128)(2,1)S(1)}, u32[]{:S(2)}, u32[]{:S(2)}) collective-permute-start(bf16[1,64,1152]{2,1,0:T(8,128)(2,1)} %refs_7_.1), channel_id=1, source_target_pairs={{0,16},{4,20},{8,24},{12,28},{16,0},{20,4},{24,8},{28,12},{1,17},{... | collective-permute-start | bytes 442376 | tf_op jit(solution)/shard_map/ppermute | solution.py:15
  3.7 1.5 %collective-permute-start = (bf16[1,64,1152]{2,1,0:T(8,128)(2,1)}, bf16[1,64,1152]{2,1,0:T(8,128)(2,1)S(1)}, u32[]{:S(2)}, u32[]{:S(2)}) collective-permute-start(bf16[1,64,1152]{2,1,0:T(8,128)(2,1)} %refs_7_.1), channel_id=1, source_target_pairs={{0,8},{4,12},{8,0},{12,4},{16,24},{20,28},{24,16},{28,20},{1,9},{5... | collective-permute-start | bytes 442376 | tf_op jit(solution)/shard_map/ppermute | solution.py:15
  5.2 0.5 %collective-permute-start.7 = (bf16[1,64,1152]{2,1,0:T(8,128)(2,1)}, bf16[1,64,1152]{2,1,0:T(8,128)(2,1)S(1)}, u32[]{:S(2)}, u32[]{:S(2)}) collective-permute-start(bf16[1,64,1152]{2,1,0:T(8,128)(2,1)} %refs_15_.1), channel_id=1, source_target_pairs={{0,16},{4,20},{8,24},{12,28},{16,0},{20,4},{24,8},{28,12},{1,17},{... | collective-permute-start | bytes 442376 | tf_op jit(solution)/shard_map/ppermute | solution.py:15
  5.7 0.1 collective-permute-start.8
  5.8 1.9 %collective-permute-done.1.refs_9_ = bf16[1,64,1152]{2,1,0:T(8,128)(2,1)S(1)} collective-permute-done((bf16[1,64,1152]{2,1,0:T(8,128)(2,1)}, bf16[1,64,1152]{2,1,0:T(8,128)(2,1)S(1)}, u32[]{:S(2)}, u32[]{:S(2)}) %collective-permute-start.1) | collective-permute-done | bytes 147488 | tf_op jit(solution)/shard_map/ppermute | solution.py:15
  7.8 0.0 collective-permute-start.10
  7.8 2.0 %collective-permute-done.refs_8_ = bf16[1,64,1152]{2,1,0:T(8,128)(2,1)S(1)} collective-permute-done((bf16[1,64,1152]{2,1,0:T(8,128)(2,1)}, bf16[1,64,1152]{2,1,0:T(8,128)(2,1)S(1)}, u32[]{:S(2)}, u32[]{:S(2)}) %collective-permute-start) | collective-permute-done | bytes 147488 | tf_op jit(solution)/shard_map/ppermute | solution.py:15
  9.7 0.0 collective-permute-start.5
  9.7 0.0 collective-permute-done.3.refs_11_
  9.7 0.7 %collective-permute-start.2 = (bf16[1,64,1152]{2,1,0:T(8,128)(2,1)S(1)}, bf16[1,64,1152]{2,1,0:T(8,128)(2,1)S(1)}, u32[]{:S(2)}, u32[]{:S(2)}) collective-permute-start(bf16[1,64,1152]{2,1,0:T(8,128)(2,1)S(1)} %collective-permute-done.refs_8_), channel_id=1, source_target_pairs={{0,16},{4,20},{8,24},{12,28},{16,0},{20,4},{24,8},{28,12},{1,17},{... | collective-permute-start | bytes 442376 | tf_op jit(solution)/shard_map/ppermute | solution.py:15
  10.5 1.2 %collective-permute-done.7.refs_16_ = bf16[1,64,1152]{2,1,0:T(8,128)(2,1)S(1)} collective-permute-done((bf16[1,64,1152]{2,1,0:T(8,128)(2,1)}, bf16[1,64,1152]{2,1,0:T(8,128)(2,1)S(1)}, u32[]{:S(2)}, u32[]{:S(2)}) %collective-permute-start.7) | collective-permute-done | bytes 147488 | tf_op jit(solution)/shard_map/ppermute | solution.py:15
  11.7 1.0 %collective-permute-start.9 = (bf16[1,64,1152]{2,1,0:T(8,128)(2,1)S(1)}, bf16[1,64,1152]{2,1,0:T(8,128)(2,1)S(1)}, u32[]{:S(2)}, u32[]{:S(2)}) collective-permute-start(bf16[1,64,1152]{2,1,0:T(8,128)(2,1)S(1)} %collective-permute-done.7.refs_16_), channel_id=1, source_target_pairs={{0,8},{4,12},{8,0},{12,4},{16,24},{20,28},{24,16},{28,20},{1,9},{5... | collective-permute-start | bytes 442376 | tf_op jit(solution)/shard_map/ppermute | solution.py:15
  12.6 0.5 %collective-permute-start.11 = (bf16[1,64,1152]{2,1,0:T(8,128)(2,1)S(1)}, bf16[1,64,1152]{2,1,0:T(8,128)(2,1)S(1)}, u32[]{:S(2)}, u32[]{:S(2)}) collective-permute-start(bf16[1,64,1152]{2,1,0:T(8,128)(2,1)S(1)} %collective-permute-done.7.refs_16_), channel_id=1, source_target_pairs={{0,4},{4,0},{8,12},{12,8},{16,20},{20,16},{24,28},{28,24},{1,5},{5... | collective-permute-start | bytes 442376 | tf_op jit(solution)/shard_map/ppermute | solution.py:15
  13.2 0.1 collective-permute-start.12
  13.2 2.8 %collective-permute-done.2.refs_10_ = bf16[1,64,1152]{2,1,0:T(8,128)(2,1)S(1)} collective-permute-done((bf16[1,64,1152]{2,1,0:T(8,128)(2,1)S(1)}, bf16[1,64,1152]{2,1,0:T(8,128)(2,1)S(1)}, u32[]{:S(2)}, u32[]{:S(2)}) %collective-permute-start.2) | collective-permute-done | bytes 147488 | tf_op jit(solution)/shard_map/ppermute | solution.py:15
  16.0 1.1 %collective-permute-done.9.refs_18_ = bf16[1,64,1152]{2,1,0:T(8,128)(2,1)S(1)} collective-permute-done((bf16[1,64,1152]{2,1,0:T(8,128)(2,1)S(1)}, bf16[1,64,1152]{2,1,0:T(8,128)(2,1)S(1)}, u32[]{:S(2)}, u32[]{:S(2)}) %collective-permute-start.9) | collective-permute-done | bytes 147488 | tf_op jit(solution)/shard_map/ppermute | solution.py:15
  19.1 9.4 %shard_map.120 = (bf16[1,64,1152]{2,1,0:T(8,128)(2,1)}, bf16[1,64,1152]{2,1,0:T(8,128)(2,1)}, f32[3,1152]{1,0:T(4,128)}) custom-call(f32[1]{0:T(128)S(6)} %copy.13.refs_0_, f32[1]{0:T(128)S(6)} %copy.14.refs_1_, f32[1]{0:T(128)S(6)} %copy.15.refs_2_, s32[1,8]{1,0:T(1,128)} %refs_3_.1, f32[1152]{0:T(1024)} %refs_4_.1, f32[1152]{0:T(1024)} %refs_5_.1, ...), custom_call_target="tpu_custom_call" | custom-call | tf_op jit(solution)/shard_map/pallas_call | solution.py:333
  28.4 1.6 %collective-permute-start.14 = (f32[3,1152]{1,0:T(4,128)}, f32[3,1152]{1,0:T(4,128)S(1)}, u32[]{:S(2)}, u32[]{:S(2)}) collective-permute-start(f32[3,1152]{1,0:T(4,128)} %get-tuple-element.9), channel_id=1, source_target_pairs={{0,1},{1,0},{2,3},{3,2},{4,5},{5,4},{6,7},{7,6},{8,9},{9,8},{10,11... | collective-permute-start | bytes 41480 | tf_op jit(solution)/shard_map/ppermute | solution.py:15
  30.1 2.4 %collective-permute-done.14 = f32[3,1152]{1,0:T(4,128)S(1)} collective-permute-done((f32[3,1152]{1,0:T(4,128)}, f32[3,1152]{1,0:T(4,128)S(1)}, u32[]{:S(2)}, u32[]{:S(2)}) %collective-permute-start.14) | collective-permute-done | bytes 13856 | tf_op jit(solution)/shard_map/ppermute | solution.py:15
  32.5 0.7 %add.6 = f32[3,1152]{1,0:T(4,128)S(1)} add(f32[3,1152]{1,0:T(4,128)} %get-tuple-element.9, f32[3,1152]{1,0:T(4,128)S(1)} %collective-permute-done.14) | non-fusion elementwise | flops 3456 | bytes 41472 | tf_op jit(solution)/shard_map/add | solution.py:69
  33.2 2.6 %collective-permute-start.15 = (f32[3,1152]{1,0:T(4,128)S(1)}, f32[3,1152]{1,0:T(4,128)S(1)}, u32[]{:S(2)}, u32[]{:S(2)}) collective-permute-start(f32[3,1152]{1,0:T(4,128)S(1)} %add.6), channel_id=1, source_target_pairs={{0,2},{1,3},{2,0},{3,1},{4,6},{5,7},{6,4},{7,5},{8,10},{9,11},{10,... | collective-permute-start | bytes 41480 | tf_op jit(solution)/shard_map/ppermute | solution.py:15
  35.8 1.2 %slice.11 = f32[1,1]{1,0:T(1,128)} slice(f32[3,1152]{1,0:T(4,128)} %get-tuple-element.9), slice={[2:3], [0:1]} | slice | bytes 8 | tf_op jit(solution)/shard_map/slice | solution.py:361
  37.0 0.9 %collective-permute-done.15 = f32[3,1152]{1,0:T(4,128)S(1)} collective-permute-done((f32[3,1152]{1,0:T(4,128)S(1)}, f32[3,1152]{1,0:T(4,128)S(1)}, u32[]{:S(2)}, u32[]{:S(2)}) %collective-permute-start.15) | collective-permute-done | bytes 13856 | tf_op jit(solution)/shard_map/ppermute | solution.py:15
  37.8 0.6 %slice_add_fusion = f32[2,1152]{1,0:T(2,128)} fusion(f32[3,1152]{1,0:T(4,128)S(1)} %collective-permute-done.15, f32[3,1152]{1,0:T(4,128)S(1)} %add.6), kind=kLoop, calls=%fused_computation | loop fusion | flops 2304 | bytes 27648 | tf_op jit(solution)/shard_map/add | solution.py:71
  (12 shorter events, 0.0 us)
Async XLA Ops:
  0.6 7.1 %collective-permute-start.1 = (bf16[1,64,1152]{2,1,0:T(8,128)(2,1)}, bf16[1,64,1152]{2,1,0:T(8,128)(2,1)S(1)}, u32[]{:S(2)}, u32[]{:S(2)}) collective-permute-start(bf16[1,64,1152]{2,1,0:T(8,128)(2,1)} %refs_7_.1), channel_id=1, source_target_pairs={{0,16},{4,20},{8,24},{12,28},{16,0},{20,4},{24,8},{28,12},{1,17},{... | collective-permute-start | bytes 442376 | tf_op jit(solution)/shard_map/ppermute | solution.py:15
  3.7 6.0 %collective-permute-start = (bf16[1,64,1152]{2,1,0:T(8,128)(2,1)}, bf16[1,64,1152]{2,1,0:T(8,128)(2,1)S(1)}, u32[]{:S(2)}, u32[]{:S(2)}) collective-permute-start(bf16[1,64,1152]{2,1,0:T(8,128)(2,1)} %refs_7_.1), channel_id=1, source_target_pairs={{0,8},{4,12},{8,0},{12,4},{16,24},{20,28},{24,16},{28,20},{1,9},{5... | collective-permute-start | bytes 442376 | tf_op jit(solution)/shard_map/ppermute | solution.py:15
  5.2 4.6 %collective-permute-start.3 = (bf16[1,64,1152]{2,1,0:T(8,128)(2,1)}, bf16[1,64,1152]{2,1,0:T(8,128)(2,1)S(1)}, u32[]{:S(2)}, u32[]{:S(2)}) collective-permute-start(bf16[1,64,1152]{2,1,0:T(8,128)(2,1)} %refs_7_.1), channel_id=1, source_target_pairs={{0,4},{4,0},{8,12},{12,8},{16,20},{20,16},{24,28},{28,24},{1,5},{5... | collective-permute-start | bytes 442376 | tf_op jit(solution)/shard_map/ppermute | solution.py:15
  5.2 6.5 %collective-permute-start.7 = (bf16[1,64,1152]{2,1,0:T(8,128)(2,1)}, bf16[1,64,1152]{2,1,0:T(8,128)(2,1)S(1)}, u32[]{:S(2)}, u32[]{:S(2)}) collective-permute-start(bf16[1,64,1152]{2,1,0:T(8,128)(2,1)} %refs_15_.1), channel_id=1, source_target_pairs={{0,16},{4,20},{8,24},{12,28},{16,0},{20,4},{24,8},{28,12},{1,17},{... | collective-permute-start | bytes 442376 | tf_op jit(solution)/shard_map/ppermute | solution.py:15
  5.7 6.9 %collective-permute-start.8 = (bf16[1,64,1152]{2,1,0:T(8,128)(2,1)}, bf16[1,64,1152]{2,1,0:T(8,128)(2,1)S(1)}, u32[]{:S(2)}, u32[]{:S(2)}) collective-permute-start(bf16[1,64,1152]{2,1,0:T(8,128)(2,1)} %refs_15_.1), channel_id=1, source_target_pairs={{0,8},{4,12},{8,0},{12,4},{16,24},{20,28},{24,16},{28,20},{1,9},{5... | collective-permute-start | bytes 442376 | tf_op jit(solution)/shard_map/ppermute | solution.py:15
  7.8 4.9 %collective-permute-start.10 = (bf16[1,64,1152]{2,1,0:T(8,128)(2,1)}, bf16[1,64,1152]{2,1,0:T(8,128)(2,1)S(1)}, u32[]{:S(2)}, u32[]{:S(2)}) collective-permute-start(bf16[1,64,1152]{2,1,0:T(8,128)(2,1)} %refs_15_.1), channel_id=1, source_target_pairs={{0,4},{4,0},{8,12},{12,8},{16,20},{20,16},{24,28},{28,24},{1,5},{5... | collective-permute-start | bytes 442376 | tf_op jit(solution)/shard_map/ppermute | solution.py:15
  9.7 3.4 %collective-permute-start.5 = (bf16[1,64,1152]{2,1,0:T(8,128)(2,1)S(1)}, bf16[1,64,1152]{2,1,0:T(8,128)(2,1)S(1)}, u32[]{:S(2)}, u32[]{:S(2)}) collective-permute-start(bf16[1,64,1152]{2,1,0:T(8,128)(2,1)S(1)} %collective-permute-done.1.refs_9_), channel_id=1, source_target_pairs={{0,4},{4,0},{8,12},{12,8},{16,20},{20,16},{24,28},{28,24},{1,5},{5... | collective-permute-start | bytes 442376 | tf_op jit(solution)/shard_map/ppermute | solution.py:15
  9.7 6.3 %collective-permute-start.2 = (bf16[1,64,1152]{2,1,0:T(8,128)(2,1)S(1)}, bf16[1,64,1152]{2,1,0:T(8,128)(2,1)S(1)}, u32[]{:S(2)}, u32[]{:S(2)}) collective-permute-start(bf16[1,64,1152]{2,1,0:T(8,128)(2,1)S(1)} %collective-permute-done.refs_8_), channel_id=1, source_target_pairs={{0,16},{4,20},{8,24},{12,28},{16,0},{20,4},{24,8},{28,12},{1,17},{... | collective-permute-start | bytes 442376 | tf_op jit(solution)/shard_map/ppermute | solution.py:15
  11.7 5.4 %collective-permute-start.9 = (bf16[1,64,1152]{2,1,0:T(8,128)(2,1)S(1)}, bf16[1,64,1152]{2,1,0:T(8,128)(2,1)S(1)}, u32[]{:S(2)}, u32[]{:S(2)}) collective-permute-start(bf16[1,64,1152]{2,1,0:T(8,128)(2,1)S(1)} %collective-permute-done.7.refs_16_), channel_id=1, source_target_pairs={{0,8},{4,12},{8,0},{12,4},{16,24},{20,28},{24,16},{28,20},{1,9},{5... | collective-permute-start | bytes 442376 | tf_op jit(solution)/shard_map/ppermute | solution.py:15
  12.6 6.4 %collective-permute-start.4 = (bf16[1,64,1152]{2,1,0:T(8,128)(2,1)S(1)}, bf16[1,64,1152]{2,1,0:T(8,128)(2,1)S(1)}, u32[]{:S(2)}, u32[]{:S(2)}) collective-permute-start(bf16[1,64,1152]{2,1,0:T(8,128)(2,1)S(1)} %collective-permute-done.refs_8_), channel_id=1, source_target_pairs={{0,4},{4,0},{8,12},{12,8},{16,20},{20,16},{24,28},{28,24},{1,5},{5... | collective-permute-start | bytes 442376 | tf_op jit(solution)/shard_map/ppermute | solution.py:15
  12.6 6.4 %collective-permute-start.11 = (bf16[1,64,1152]{2,1,0:T(8,128)(2,1)S(1)}, bf16[1,64,1152]{2,1,0:T(8,128)(2,1)S(1)}, u32[]{:S(2)}, u32[]{:S(2)}) collective-permute-start(bf16[1,64,1152]{2,1,0:T(8,128)(2,1)S(1)} %collective-permute-done.7.refs_16_), channel_id=1, source_target_pairs={{0,4},{4,0},{8,12},{12,8},{16,20},{20,16},{24,28},{28,24},{1,5},{5... | collective-permute-start | bytes 442376 | tf_op jit(solution)/shard_map/ppermute | solution.py:15
  13.2 5.9 %collective-permute-start.12 = (bf16[1,64,1152]{2,1,0:T(8,128)(2,1)S(1)}, bf16[1,64,1152]{2,1,0:T(8,128)(2,1)S(1)}, u32[]{:S(2)}, u32[]{:S(2)}) collective-permute-start(bf16[1,64,1152]{2,1,0:T(8,128)(2,1)S(1)} %collective-permute-done.8.refs_17_), channel_id=1, source_target_pairs={{0,4},{4,0},{8,12},{12,8},{16,20},{20,16},{24,28},{28,24},{1,5},{5... | collective-permute-start | bytes 442376 | tf_op jit(solution)/shard_map/ppermute | solution.py:15
  16.0 3.0 %collective-permute-start.6 = (bf16[1,64,1152]{2,1,0:T(8,128)(2,1)S(1)}, bf16[1,64,1152]{2,1,0:T(8,128)(2,1)S(1)}, u32[]{:S(2)}, u32[]{:S(2)}) collective-permute-start(bf16[1,64,1152]{2,1,0:T(8,128)(2,1)S(1)} %collective-permute-done.2.refs_10_), channel_id=1, source_target_pairs={{0,4},{4,0},{8,12},{12,8},{16,20},{20,16},{24,28},{28,24},{1,5},{5... | collective-permute-start | bytes 442376 | tf_op jit(solution)/shard_map/ppermute | solution.py:15
  17.1 2.0 %collective-permute-start.13 = (bf16[1,64,1152]{2,1,0:T(8,128)(2,1)S(1)}, bf16[1,64,1152]{2,1,0:T(8,128)(2,1)S(1)}, u32[]{:S(2)}, u32[]{:S(2)}) collective-permute-start(bf16[1,64,1152]{2,1,0:T(8,128)(2,1)S(1)} %collective-permute-done.9.refs_18_), channel_id=1, source_target_pairs={{0,4},{4,0},{8,12},{12,8},{16,20},{20,16},{24,28},{28,24},{1,5},{5... | collective-permute-start | bytes 442376 | tf_op jit(solution)/shard_map/ppermute | solution.py:15
  28.4 4.0 %collective-permute-start.14 = (f32[3,1152]{1,0:T(4,128)}, f32[3,1152]{1,0:T(4,128)S(1)}, u32[]{:S(2)}, u32[]{:S(2)}) collective-permute-start(f32[3,1152]{1,0:T(4,128)} %get-tuple-element.9), channel_id=1, source_target_pairs={{0,1},{1,0},{2,3},{3,2},{4,5},{5,4},{6,7},{7,6},{8,9},{9,8},{10,11... | collective-permute-start | bytes 41480 | tf_op jit(solution)/shard_map/ppermute | solution.py:15
  33.2 4.7 %collective-permute-start.15 = (f32[3,1152]{1,0:T(4,128)S(1)}, f32[3,1152]{1,0:T(4,128)S(1)}, u32[]{:S(2)}, u32[]{:S(2)}) collective-permute-start(f32[3,1152]{1,0:T(4,128)S(1)} %add.6), channel_id=1, source_target_pairs={{0,2},{1,3},{2,0},{3,1},{4,6},{5,7},{6,4},{7,5},{8,10},{9,11},{10,... | collective-permute-start | bytes 41480 | tf_op jit(solution)/shard_map/ppermute | solution.py:15

commit v17 on v16

--- a/solution.py
+++ b/solution.py
@@ -240,7 +240,7 @@
     ).astype(jnp.int32)
 
     gains = (picture_gain_ref[...][None, :], caption_gain_ref[...][None, :])
-    chunk = min(128, group_rows)
+    chunk = min(256, group_rows)
     for position, source in enumerate(pieces):
         tower, slot = divmod(position, count)
         masks = image_masks if tower == 0 else text_masks

time: 38.7 us -> 38.3 us (0.990)
  Pallas kernels: 9.35 us -> 8.95 us
    pallas_call x1, Pallas kernels: 9.35 us -> 8.95 us  [whole_group(): pl.pallas_call(functools.partial(group_kernel, tuple(masks[:count]), tupl...]
where the time goes in v17:
time: 38.3 us; the launch traced here: 38.1 us
  waiting for transfers between devices  12.2 us (32%)
  starting transfers between devices  11.7 us (31%)
  Pallas kernels  8.95 us (23%)
  between operations  2.64 us (7%)
  other arithmetic  1.33 us (3%)
  local copies, waits for them, and re-layouts  1.18 us (3%)
    ppermute x16, waiting for transfers between devices, xor_swap(): lax.ppermute(value, axis, [(source, source ^ bit) for source in range(cou...  12.2 us
    ppermute x16, starting transfers between devices, xor_swap(): lax.ppermute(value, axis, [(source, source ^ bit) for source in range(cou...  11.7 us
    pallas_call x1, Pallas kernels, whole_group(): pl.pallas_call(functools.partial(group_kernel, tuple(masks[:count]), tupl...  8.95 us
    slice x1, local copies, waits for them, and re-layouts, whole_group(): group_loss = sums[2, 0:1]  1.18 us
  transfers between devices with their start and end apart: 16, of which 7 were waited for; matrix products, arithmetic and copies ran while one was open for 3% of the time, Pallas kernels for 0%

profile of v17, /device:TPU:0, one launch (start us, length us, event | category | flops | bytes accessed | tf_op | source)
XLA Modules:
  0.0 38.1 jit_solution(1410078059699288852)
XLA Ops:
  0.6 3.1 %collective-permute-start.1 = (bf16[1,64,1152]{2,1,0:T(8,128)(2,1)}, bf16[1,64,1152]{2,1,0:T(8,128)(2,1)S(1)}, u32[]{:S(2)}, u32[]{:S(2)}) collective-permute-start(bf16[1,64,1152]{2,1,0:T(8,128)(2,1)} %refs_7_.1), channel_id=1, source_target_pairs={{0,16},{4,20},{8,24},{12,28},{16,0},{20,4},{24,8},{28,12},{1,17},{... | collective-permute-start | bytes 442376 | tf_op jit(solution)/shard_map/ppermute | solution.py:15
  3.7 1.5 %collective-permute-start = (bf16[1,64,1152]{2,1,0:T(8,128)(2,1)}, bf16[1,64,1152]{2,1,0:T(8,128)(2,1)S(1)}, u32[]{:S(2)}, u32[]{:S(2)}) collective-permute-start(bf16[1,64,1152]{2,1,0:T(8,128)(2,1)} %refs_7_.1), channel_id=1, source_target_pairs={{0,8},{4,12},{8,0},{12,4},{16,24},{20,28},{24,16},{28,20},{1,9},{5... | collective-permute-start | bytes 442376 | tf_op jit(solution)/shard_map/ppermute | solution.py:15
  5.2 0.5 %collective-permute-start.7 = (bf16[1,64,1152]{2,1,0:T(8,128)(2,1)}, bf16[1,64,1152]{2,1,0:T(8,128)(2,1)S(1)}, u32[]{:S(2)}, u32[]{:S(2)}) collective-permute-start(bf16[1,64,1152]{2,1,0:T(8,128)(2,1)} %refs_15_.1), channel_id=1, source_target_pairs={{0,16},{4,20},{8,24},{12,28},{16,0},{20,4},{24,8},{28,12},{1,17},{... | collective-permute-start | bytes 442376 | tf_op jit(solution)/shard_map/ppermute | solution.py:15
  5.7 0.1 collective-permute-start.8
  5.8 1.9 %collective-permute-done.1.refs_9_ = bf16[1,64,1152]{2,1,0:T(8,128)(2,1)S(1)} collective-permute-done((bf16[1,64,1152]{2,1,0:T(8,128)(2,1)}, bf16[1,64,1152]{2,1,0:T(8,128)(2,1)S(1)}, u32[]{:S(2)}, u32[]{:S(2)}) %collective-permute-start.1) | collective-permute-done | bytes 147488 | tf_op jit(solution)/shard_map/ppermute | solution.py:15
  7.8 0.0 collective-permute-start.10
  7.8 2.0 %collective-permute-done.refs_8_ = bf16[1,64,1152]{2,1,0:T(8,128)(2,1)S(1)} collective-permute-done((bf16[1,64,1152]{2,1,0:T(8,128)(2,1)}, bf16[1,64,1152]{2,1,0:T(8,128)(2,1)S(1)}, u32[]{:S(2)}, u32[]{:S(2)}) %collective-permute-start) | collective-permute-done | bytes 147488 | tf_op jit(solution)/shard_map/ppermute | solution.py:15
  9.7 0.0 collective-permute-start.5
  9.7 0.0 collective-permute-done.3.refs_11_
  9.7 0.7 %collective-permute-start.2 = (bf16[1,64,1152]{2,1,0:T(8,128)(2,1)S(1)}, bf16[1,64,1152]{2,1,0:T(8,128)(2,1)S(1)}, u32[]{:S(2)}, u32[]{:S(2)}) collective-permute-start(bf16[1,64,1152]{2,1,0:T(8,128)(2,1)S(1)} %collective-permute-done.refs_8_), channel_id=1, source_target_pairs={{0,16},{4,20},{8,24},{12,28},{16,0},{20,4},{24,8},{28,12},{1,17},{... | collective-permute-start | bytes 442376 | tf_op jit(solution)/shard_map/ppermute | solution.py:15
  10.5 1.2 %collective-permute-done.7.refs_16_ = bf16[1,64,1152]{2,1,0:T(8,128)(2,1)S(1)} collective-permute-done((bf16[1,64,1152]{2,1,0:T(8,128)(2,1)}, bf16[1,64,1152]{2,1,0:T(8,128)(2,1)S(1)}, u32[]{:S(2)}, u32[]{:S(2)}) %collective-permute-start.7) | collective-permute-done | bytes 147488 | tf_op jit(solution)/shard_map/ppermute | solution.py:15
  11.7 1.0 %collective-permute-start.9 = (bf16[1,64,1152]{2,1,0:T(8,128)(2,1)S(1)}, bf16[1,64,1152]{2,1,0:T(8,128)(2,1)S(1)}, u32[]{:S(2)}, u32[]{:S(2)}) collective-permute-start(bf16[1,64,1152]{2,1,0:T(8,128)(2,1)S(1)} %collective-permute-done.7.refs_16_), channel_id=1, source_target_pairs={{0,8},{4,12},{8,0},{12,4},{16,24},{20,28},{24,16},{28,20},{1,9},{5... | collective-permute-start | bytes 442376 | tf_op jit(solution)/shard_map/ppermute | solution.py:15
  12.6 0.5 %collective-permute-start.11 = (bf16[1,64,1152]{2,1,0:T(8,128)(2,1)S(1)}, bf16[1,64,1152]{2,1,0:T(8,128)(2,1)S(1)}, u32[]{:S(2)}, u32[]{:S(2)}) collective-permute-start(bf16[1,64,1152]{2,1,0:T(8,128)(2,1)S(1)} %collective-permute-done.7.refs_16_), channel_id=1, source_target_pairs={{0,4},{4,0},{8,12},{12,8},{16,20},{20,16},{24,28},{28,24},{1,5},{5... | collective-permute-start | bytes 442376 | tf_op jit(solution)/shard_map/ppermute | solution.py:15
  13.2 0.1 collective-permute-start.12
  13.2 2.8 %collective-permute-done.2.refs_10_ = bf16[1,64,1152]{2,1,0:T(8,128)(2,1)S(1)} collective-permute-done((bf16[1,64,1152]{2,1,0:T(8,128)(2,1)S(1)}, bf16[1,64,1152]{2,1,0:T(8,128)(2,1)S(1)}, u32[]{:S(2)}, u32[]{:S(2)}) %collective-permute-start.2) | collective-permute-done | bytes 147488 | tf_op jit(solution)/shard_map/ppermute | solution.py:15
  16.0 1.1 %collective-permute-done.9.refs_18_ = bf16[1,64,1152]{2,1,0:T(8,128)(2,1)S(1)} collective-permute-done((bf16[1,64,1152]{2,1,0:T(8,128)(2,1)S(1)}, bf16[1,64,1152]{2,1,0:T(8,128)(2,1)S(1)}, u32[]{:S(2)}, u32[]{:S(2)}) %collective-permute-start.9) | collective-permute-done | bytes 147488 | tf_op jit(solution)/shard_map/ppermute | solution.py:15
  19.1 9.0 %shard_map.120 = (bf16[1,64,1152]{2,1,0:T(8,128)(2,1)}, bf16[1,64,1152]{2,1,0:T(8,128)(2,1)}, f32[3,1152]{1,0:T(4,128)}) custom-call(f32[1]{0:T(128)S(6)} %copy.13.refs_0_, f32[1]{0:T(128)S(6)} %copy.14.refs_1_, f32[1]{0:T(128)S(6)} %copy.15.refs_2_, s32[1,8]{1,0:T(1,128)} %refs_3_.1, f32[1152]{0:T(1024)} %refs_4_.1, f32[1152]{0:T(1024)} %refs_5_.1, ...), custom_call_target="tpu_custom_call" | custom-call | tf_op jit(solution)/shard_map/pallas_call | solution.py:333
  28.0 1.6 %collective-permute-start.14 = (f32[3,1152]{1,0:T(4,128)}, f32[3,1152]{1,0:T(4,128)S(1)}, u32[]{:S(2)}, u32[]{:S(2)}) collective-permute-start(f32[3,1152]{1,0:T(4,128)} %get-tuple-element.9), channel_id=1, source_target_pairs={{0,1},{1,0},{2,3},{3,2},{4,5},{5,4},{6,7},{7,6},{8,9},{9,8},{10,11... | collective-permute-start | bytes 41480 | tf_op jit(solution)/shard_map/ppermute | solution.py:15
  29.7 2.4 %collective-permute-done.14 = f32[3,1152]{1,0:T(4,128)S(1)} collective-permute-done((f32[3,1152]{1,0:T(4,128)}, f32[3,1152]{1,0:T(4,128)S(1)}, u32[]{:S(2)}, u32[]{:S(2)}) %collective-permute-start.14) | collective-permute-done | bytes 13856 | tf_op jit(solution)/shard_map/ppermute | solution.py:15
  32.1 0.7 %add.6 = f32[3,1152]{1,0:T(4,128)S(1)} add(f32[3,1152]{1,0:T(4,128)} %get-tuple-element.9, f32[3,1152]{1,0:T(4,128)S(1)} %collective-permute-done.14) | non-fusion elementwise | flops 3456 | bytes 41472 | tf_op jit(solution)/shard_map/add | solution.py:69
  32.8 2.6 %collective-permute-start.15 = (f32[3,1152]{1,0:T(4,128)S(1)}, f32[3,1152]{1,0:T(4,128)S(1)}, u32[]{:S(2)}, u32[]{:S(2)}) collective-permute-start(f32[3,1152]{1,0:T(4,128)S(1)} %add.6), channel_id=1, source_target_pairs={{0,2},{1,3},{2,0},{3,1},{4,6},{5,7},{6,4},{7,5},{8,10},{9,11},{10,... | collective-permute-start | bytes 41480 | tf_op jit(solution)/shard_map/ppermute | solution.py:15
  35.4 1.2 %slice.11 = f32[1,1]{1,0:T(1,128)} slice(f32[3,1152]{1,0:T(4,128)} %get-tuple-element.9), slice={[2:3], [0:1]} | slice | bytes 8 | tf_op jit(solution)/shard_map/slice | solution.py:361
  36.6 0.9 %collective-permute-done.15 = f32[3,1152]{1,0:T(4,128)S(1)} collective-permute-done((f32[3,1152]{1,0:T(4,128)S(1)}, f32[3,1152]{1,0:T(4,128)S(1)}, u32[]{:S(2)}, u32[]{:S(2)}) %collective-permute-start.15) | collective-permute-done | bytes 13856 | tf_op jit(solution)/shard_map/ppermute | solution.py:15
  37.4 0.6 %slice_add_fusion = f32[2,1152]{1,0:T(2,128)} fusion(f32[3,1152]{1,0:T(4,128)S(1)} %collective-permute-done.15, f32[3,1152]{1,0:T(4,128)S(1)} %add.6), kind=kLoop, calls=%fused_computation | loop fusion | flops 2304 | bytes 27648 | tf_op jit(solution)/shard_map/add | solution.py:71
  (12 shorter events, 0.0 us)
Async XLA Ops:
  0.6 7.1 %collective-permute-start.1 = (bf16[1,64,1152]{2,1,0:T(8,128)(2,1)}, bf16[1,64,1152]{2,1,0:T(8,128)(2,1)S(1)}, u32[]{:S(2)}, u32[]{:S(2)}) collective-permute-start(bf16[1,64,1152]{2,1,0:T(8,128)(2,1)} %refs_7_.1), channel_id=1, source_target_pairs={{0,16},{4,20},{8,24},{12,28},{16,0},{20,4},{24,8},{28,12},{1,17},{... | collective-permute-start | bytes 442376 | tf_op jit(solution)/shard_map/ppermute | solution.py:15
  3.7 6.0 %collective-permute-start = (bf16[1,64,1152]{2,1,0:T(8,128)(2,1)}, bf16[1,64,1152]{2,1,0:T(8,128)(2,1)S(1)}, u32[]{:S(2)}, u32[]{:S(2)}) collective-permute-start(bf16[1,64,1152]{2,1,0:T(8,128)(2,1)} %refs_7_.1), channel_id=1, source_target_pairs={{0,8},{4,12},{8,0},{12,4},{16,24},{20,28},{24,16},{28,20},{1,9},{5... | collective-permute-start | bytes 442376 | tf_op jit(solution)/shard_map/ppermute | solution.py:15
  5.2 4.6 %collective-permute-start.3 = (bf16[1,64,1152]{2,1,0:T(8,128)(2,1)}, bf16[1,64,1152]{2,1,0:T(8,128)(2,1)S(1)}, u32[]{:S(2)}, u32[]{:S(2)}) collective-permute-start(bf16[1,64,1152]{2,1,0:T(8,128)(2,1)} %refs_7_.1), channel_id=1, source_target_pairs={{0,4},{4,0},{8,12},{12,8},{16,20},{20,16},{24,28},{28,24},{1,5},{5... | collective-permute-start | bytes 442376 | tf_op jit(solution)/shard_map/ppermute | solution.py:15
  5.2 6.5 %collective-permute-start.7 = (bf16[1,64,1152]{2,1,0:T(8,128)(2,1)}, bf16[1,64,1152]{2,1,0:T(8,128)(2,1)S(1)}, u32[]{:S(2)}, u32[]{:S(2)}) collective-permute-start(bf16[1,64,1152]{2,1,0:T(8,128)(2,1)} %refs_15_.1), channel_id=1, source_target_pairs={{0,16},{4,20},{8,24},{12,28},{16,0},{20,4},{24,8},{28,12},{1,17},{... | collective-permute-start | bytes 442376 | tf_op jit(solution)/shard_map/ppermute | solution.py:15
  5.7 6.9 %collective-permute-start.8 = (bf16[1,64,1152]{2,1,0:T(8,128)(2,1)}, bf16[1,64,1152]{2,1,0:T(8,128)(2,1)S(1)}, u32[]{:S(2)}, u32[]{:S(2)}) collective-permute-start(bf16[1,64,1152]{2,1,0:T(8,128)(2,1)} %refs_15_.1), channel_id=1, source_target_pairs={{0,8},{4,12},{8,0},{12,4},{16,24},{20,28},{24,16},{28,20},{1,9},{5... | collective-permute-start | bytes 442376 | tf_op jit(solution)/shard_map/ppermute | solution.py:15
  7.8 4.9 %collective-permute-start.10 = (bf16[1,64,1152]{2,1,0:T(8,128)(2,1)}, bf16[1,64,1152]{2,1,0:T(8,128)(2,1)S(1)}, u32[]{:S(2)}, u32[]{:S(2)}) collective-permute-start(bf16[1,64,1152]{2,1,0:T(8,128)(2,1)} %refs_15_.1), channel_id=1, source_target_pairs={{0,4},{4,0},{8,12},{12,8},{16,20},{20,16},{24,28},{28,24},{1,5},{5... | collective-permute-start | bytes 442376 | tf_op jit(solution)/shard_map/ppermute | solution.py:15
  9.7 3.4 %collective-permute-start.5 = (bf16[1,64,1152]{2,1,0:T(8,128)(2,1)S(1)}, bf16[1,64,1152]{2,1,0:T(8,128)(2,1)S(1)}, u32[]{:S(2)}, u32[]{:S(2)}) collective-permute-start(bf16[1,64,1152]{2,1,0:T(8,128)(2,1)S(1)} %collective-permute-done.1.refs_9_), channel_id=1, source_target_pairs={{0,4},{4,0},{8,12},{12,8},{16,20},{20,16},{24,28},{28,24},{1,5},{5... | collective-permute-start | bytes 442376 | tf_op jit(solution)/shard_map/ppermute | solution.py:15
  9.7 6.3 %collective-permute-start.2 = (bf16[1,64,1152]{2,1,0:T(8,128)(2,1)S(1)}, bf16[1,64,1152]{2,1,0:T(8,128)(2,1)S(1)}, u32[]{:S(2)}, u32[]{:S(2)}) collective-permute-start(bf16[1,64,1152]{2,1,0:T(8,128)(2,1)S(1)} %collective-permute-done.refs_8_), channel_id=1, source_target_pairs={{0,16},{4,20},{8,24},{12,28},{16,0},{20,4},{24,8},{28,12},{1,17},{... | collective-permute-start | bytes 442376 | tf_op jit(solution)/shard_map/ppermute | solution.py:15
  11.7 5.4 %collective-permute-start.9 = (bf16[1,64,1152]{2,1,0:T(8,128)(2,1)S(1)}, bf16[1,64,1152]{2,1,0:T(8,128)(2,1)S(1)}, u32[]{:S(2)}, u32[]{:S(2)}) collective-permute-start(bf16[1,64,1152]{2,1,0:T(8,128)(2,1)S(1)} %collective-permute-done.7.refs_16_), channel_id=1, source_target_pairs={{0,8},{4,12},{8,0},{12,4},{16,24},{20,28},{24,16},{28,20},{1,9},{5... | collective-permute-start | bytes 442376 | tf_op jit(solution)/shard_map/ppermute | solution.py:15
  12.6 6.4 %collective-permute-start.4 = (bf16[1,64,1152]{2,1,0:T(8,128)(2,1)S(1)}, bf16[1,64,1152]{2,1,0:T(8,128)(2,1)S(1)}, u32[]{:S(2)}, u32[]{:S(2)}) collective-permute-start(bf16[1,64,1152]{2,1,0:T(8,128)(2,1)S(1)} %collective-permute-done.refs_8_), channel_id=1, source_target_pairs={{0,4},{4,0},{8,12},{12,8},{16,20},{20,16},{24,28},{28,24},{1,5},{5... | collective-permute-start | bytes 442376 | tf_op jit(solution)/shard_map/ppermute | solution.py:15
  12.6 6.4 %collective-permute-start.11 = (bf16[1,64,1152]{2,1,0:T(8,128)(2,1)S(1)}, bf16[1,64,1152]{2,1,0:T(8,128)(2,1)S(1)}, u32[]{:S(2)}, u32[]{:S(2)}) collective-permute-start(bf16[1,64,1152]{2,1,0:T(8,128)(2,1)S(1)} %collective-permute-done.7.refs_16_), channel_id=1, source_target_pairs={{0,4},{4,0},{8,12},{12,8},{16,20},{20,16},{24,28},{28,24},{1,5},{5... | collective-permute-start | bytes 442376 | tf_op jit(solution)/shard_map/ppermute | solution.py:15
  13.2 5.9 %collective-permute-start.12 = (bf16[1,64,1152]{2,1,0:T(8,128)(2,1)S(1)}, bf16[1,64,1152]{2,1,0:T(8,128)(2,1)S(1)}, u32[]{:S(2)}, u32[]{:S(2)}) collective-permute-start(bf16[1,64,1152]{2,1,0:T(8,128)(2,1)S(1)} %collective-permute-done.8.refs_17_), channel_id=1, source_target_pairs={{0,4},{4,0},{8,12},{12,8},{16,20},{20,16},{24,28},{28,24},{1,5},{5... | collective-permute-start | bytes 442376 | tf_op jit(solution)/shard_map/ppermute | solution.py:15
  16.0 3.0 %collective-permute-start.6 = (bf16[1,64,1152]{2,1,0:T(8,128)(2,1)S(1)}, bf16[1,64,1152]{2,1,0:T(8,128)(2,1)S(1)}, u32[]{:S(2)}, u32[]{:S(2)}) collective-permute-start(bf16[1,64,1152]{2,1,0:T(8,128)(2,1)S(1)} %collective-permute-done.2.refs_10_), channel_id=1, source_target_pairs={{0,4},{4,0},{8,12},{12,8},{16,20},{20,16},{24,28},{28,24},{1,5},{5... | collective-permute-start | bytes 442376 | tf_op jit(solution)/shard_map/ppermute | solution.py:15
  17.1 2.0 %collective-permute-start.13 = (bf16[1,64,1152]{2,1,0:T(8,128)(2,1)S(1)}, bf16[1,64,1152]{2,1,0:T(8,128)(2,1)S(1)}, u32[]{:S(2)}, u32[]{:S(2)}) collective-permute-start(bf16[1,64,1152]{2,1,0:T(8,128)(2,1)S(1)} %collective-permute-done.9.refs_18_), channel_id=1, source_target_pairs={{0,4},{4,0},{8,12},{12,8},{16,20},{20,16},{24,28},{28,24},{1,5},{5... | collective-permute-start | bytes 442376 | tf_op jit(solution)/shard_map/ppermute | solution.py:15
  28.0 4.0 %collective-permute-start.14 = (f32[3,1152]{1,0:T(4,128)}, f32[3,1152]{1,0:T(4,128)S(1)}, u32[]{:S(2)}, u32[]{:S(2)}) collective-permute-start(f32[3,1152]{1,0:T(4,128)} %get-tuple-element.9), channel_id=1, source_target_pairs={{0,1},{1,0},{2,3},{3,2},{4,5},{5,4},{6,7},{7,6},{8,9},{9,8},{10,11... | collective-permute-start | bytes 41480 | tf_op jit(solution)/shard_map/ppermute | solution.py:15
  32.8 4.7 %collective-permute-start.15 = (f32[3,1152]{1,0:T(4,128)S(1)}, f32[3,1152]{1,0:T(4,128)S(1)}, u32[]{:S(2)}, u32[]{:S(2)}) collective-permute-start(f32[3,1152]{1,0:T(4,128)S(1)} %add.6), channel_id=1, source_target_pairs={{0,2},{1,3},{2,0},{3,1},{4,6},{5,7},{6,4},{7,5},{8,10},{9,11},{10,... | collective-permute-start | bytes 41480 | tf_op jit(solution)/shard_map/ppermute | solution.py:15
